TPU v7x, 32 devices: a whole 2x2x4 slice. The times are simulated.
32 devices in a mesh: clip: 4 (over z), seg: 8 (over y, x, core).
Axes of the slice: x: 2, y: 2, z: 4, core: 2. Of those that a mesh axis runs over, the one named last changes fastest.
Arguments:
- spectra: bfloat16 [16, 2, 1024, 192], P('clip', None, 'seg'), may hold values from -6 to 6
- target: bfloat16 [16, 98304], P('clip', 'seg'), may hold values from -12 to 12
- lengths: int32 [16], P('clip'), may hold values from 96 to 192, as said below
Outputs:
- loss: float32 [], replicated
- spec_grad: bfloat16 [16, 2, 1024, 192], P('clip', None, 'seg')
Inputs may be any that keep to these rules, and one draw needn't show every extreme that they name: `lengths`: some clip has all 192 frames.
All inputs are finite; a program needn't handle non-finite values.
Results may differ from a plain program's by a relative error of at most 0.0092.
Values may be sent and summed in bfloat16 or wider, within the bound.
No kernel may reach another device: no remote copies, remote signals or barrier semaphores. Data moves between devices by JAX's collectives and lax.ppermute only.
A program may use at most 128 MiB of HBM per device.

v0:
```python
import math

import jax
import jax.numpy as jnp
from jax import lax
from jax.sharding import PartitionSpec as P

BINS = 1024
NFFT = 2048
HOP = 512


EPS_MAG = 0.1
EPS_RATIO = 1e-05


def shifted(block, axis, distance):
    devices = range(lax.axis_size(axis))
    route = [(i - distance, i) for i in devices if i - distance in devices]
    return lax.ppermute(block, axis, route)


def angle_pair(index, points):
    angles = (index % points).astype(jnp.float32) * (2.0 * math.pi / points)
    return jnp.cos(angles), jnp.sin(angles)


def window_of(time_index, points):
    return 0.5 - 0.5 * jnp.cos(time_index.astype(jnp.float32) * (2.0 * math.pi / points))


def analysis_table(points):
    halfway = points // 2
    lanes = min(128, halfway)
    groups = halfway // lanes
    time_index = jnp.arange(points, dtype=jnp.int32)[:, None]
    coarse_cos, coarse_sin = angle_pair(
        (jnp.arange(groups, dtype=jnp.int32)[None, :] * lanes) * time_index, points
    )
    fine_cos, fine_sin = angle_pair(jnp.arange(lanes, dtype=jnp.int32)[None, :] * time_index, points)
    cos_full = (
        coarse_cos[:, :, None] * fine_cos[:, None, :] - coarse_sin[:, :, None] * fine_sin[:, None, :]
    )
    sin_full = (
        coarse_sin[:, :, None] * fine_cos[:, None, :] + coarse_cos[:, :, None] * fine_sin[:, None, :]
    )
    window = window_of(time_index, points)[:, :, None]
    factor = 1.0 / math.sqrt(points)
    real = (cos_full * window * factor).astype(jnp.bfloat16).reshape(points, halfway)
    imag = (-sin_full * window * factor).astype(jnp.bfloat16).reshape(points, halfway)
    return jnp.concatenate([real, imag], axis=1)


def synthesis_rows(first_bin, band_count):
    sub = 8 if band_count % 8 == 0 else 1
    time_index = jnp.arange(NFFT, dtype=jnp.int32)[None, :]
    coarse_bins = first_bin + sub * jnp.arange(band_count // sub, dtype=jnp.int32)[:, None]
    coarse_cos, coarse_sin = angle_pair(coarse_bins * time_index, NFFT)
    fine_cos, fine_sin = angle_pair(jnp.arange(sub, dtype=jnp.int32)[:, None] * time_index, NFFT)
    cos_full = (
        coarse_cos[:, None, :] * fine_cos[None, :, :] - coarse_sin[:, None, :] * fine_sin[None, :, :]
    )
    sin_full = (
        coarse_sin[:, None, :] * fine_cos[None, :, :] + coarse_cos[:, None, :] * fine_sin[None, :, :]
    )
    window = window_of(time_index, NFFT)[None, :, :]
    factor = 1.0 / math.sqrt(BINS)
    real = (cos_full * window * factor).astype(jnp.bfloat16).reshape(band_count, NFFT)
    imag = (-sin_full * window * factor).astype(jnp.bfloat16).reshape(band_count, NFFT)
    return jnp.stack([real, imag])


def spread_parts(quarters):
    return sum(
        (
            jnp.pad(quarters[:, :, quarter], ((0, 0), (quarter, 3 - quarter), (0, 0)))
            for quarter in range(4)
        )
    )


def framed(signal, beyond, stride):
    frame_count = signal.shape[1] // stride
    padded = jnp.concatenate([signal, beyond], axis=1).reshape(
        signal.shape[0], frame_count + 3, stride
    )
    return jnp.concatenate(
        [padded[:, quarter : quarter + frame_count] for quarter in range(4)], axis=2
    )


def body(spectra, target, lengths):
    clip_count = spectra.shape[0]
    band_count = spectra.shape[2]
    frames_all = spectra.shape[3]
    samples = target.shape[1]
    rows_here = samples // HOP
    seg_index = lax.axis_index("seg")
    start_sample = seg_index * samples
    local_table = synthesis_rows(seg_index * band_count, band_count)
    padded_spec = jnp.pad(spectra, ((0, 0), (0, 0), (0, 0), (3, 0)))
    framed_sig = jnp.einsum(
        "crbf,rbm->fcm", padded_spec, local_table, preferred_element_type=jnp.float32
    )
    hop_rows = lax.psum_scatter(
        sum(
            (
                framed_sig[
                    3 - quarter : 3 - quarter + rows_here * lax.axis_size("seg"),
                    :,
                    quarter * HOP : (quarter + 1) * HOP,
                ]
                for quarter in range(4)
            )
        ),
        "seg",
        scatter_dimension=0,
        tiled=True,
    )
    estimate = jnp.transpose(hop_rows, (1, 0, 2)).reshape(clip_count, samples)
    sample_index = start_sample + jnp.arange(samples, dtype=jnp.int32)
    inside = sample_index[None, :] < (lengths * HOP)[:, None]
    est_wave = jnp.where(inside, estimate, 0.0).astype(jnp.bfloat16)
    clean = jnp.where(inside, target, jnp.zeros_like(target))
    sizes_list = (NFFT // 4, NFFT // 2, NFFT)
    beyond_list = [
        shifted((est_wave[:, : 3 * NFFT // 16], clean[:, : 3 * NFFT // 16]), "seg", -1),
        shifted((est_wave[:, : 3 * NFFT // 8], clean[:, : 3 * NFFT // 8]), "seg", -1),
        shifted((est_wave[:, : 3 * NFFT // 4], clean[:, : 3 * NFFT // 4]), "seg", -1),
    ]
    saved = []
    spread_list = []
    energy_list = []
    logterm_list = []
    for points, beyond_pair in zip(sizes_list, beyond_list):
        stride = points // 4
        halfway = points // 2
        frame_count = samples // stride
        paired = jnp.stack(
            [framed(est_wave, beyond_pair[0], stride), framed(clean, beyond_pair[1], stride)]
        )
        table = analysis_table(points)
        spectra_pair = jnp.einsum(
            "ecfm,mj->ecfj", paired, table, preferred_element_type=jnp.float32
        )
        est_real = spectra_pair[0, :, :, :halfway]
        est_imag = spectra_pair[0, :, :, halfway:]
        tgt_real = spectra_pair[1, :, :, :halfway]
        tgt_imag = spectra_pair[1, :, :, halfway:]
        est_mag = jnp.sqrt(est_real * est_real + est_imag * est_imag + EPS_MAG)
        tgt_mag = jnp.sqrt(tgt_real * tgt_real + tgt_imag * tgt_imag + EPS_MAG)
        usable_count = lengths * (HOP // stride)
        frame_index = start_sample // stride + jnp.arange(frame_count, dtype=jnp.int32)
        usable = frame_index[None, :, None] < usable_count[:, None, None]
        mag_gap = est_mag - tgt_mag
        log_gap = jnp.log(est_mag) - jnp.log(tgt_mag)
        entries = (usable_count * halfway).astype(jnp.float32)
        spread_list.append(jnp.sum(jnp.where(usable, mag_gap * mag_gap, 0.0), axis=(1, 2)))
        energy_list.append(jnp.sum(jnp.where(usable, tgt_mag * tgt_mag, 0.0), axis=(1, 2)))
        logterm_list.append(
            jnp.sum(jnp.where(usable, log_gap * log_gap, 0.0), axis=(1, 2)) / entries
        )
        saved.append((est_real, est_imag, est_mag, mag_gap, log_gap, usable, entries, table))
    spreads = jnp.stack(spread_list)
    energies = jnp.stack(energy_list)
    logterms = jnp.stack(logterm_list)
    spreads, energies, logterms = lax.psum((spreads, energies, logterms), "seg")
    own_loss = jnp.sum(jnp.sqrt((spreads + EPS_RATIO) / energies) + logterms)
    loss = lax.psum(own_loss, "clip") / (3 * clip_count * lax.axis_size("clip"))
    ratio_weight = 1.0 / jnp.sqrt((spreads + EPS_RATIO) * energies)
    gradient = jnp.zeros((clip_count, samples), jnp.float32)
    extras = []
    for level, points in enumerate(sizes_list):
        stride = points // 4
        frame_count = samples // stride
        est_real, est_imag, est_mag, mag_gap, log_gap, usable, entries, table = saved[level]
        grad_mag = jnp.where(
            usable,
            mag_gap * ratio_weight[level][:, None, None]
            + 2.0 * log_gap / (est_mag * entries[:, None, None]),
            0.0,
        ) * (frames_all * BINS)
        grad_x = jnp.concatenate(
            [grad_mag * est_real / est_mag, grad_mag * est_imag / est_mag], axis=2
        ).astype(jnp.bfloat16)
        grad_frames = jnp.einsum(
            "cfj,mj->cfm", grad_x, table, preferred_element_type=jnp.float32
        )
        spread_back = spread_parts(grad_frames.reshape(clip_count, frame_count, 4, stride))
        gradient = gradient + spread_back[:, :frame_count].reshape(clip_count, samples)
        extras.append(spread_back[:, frame_count:].reshape(clip_count, 3 * stride))
    received_short = shifted(extras[0], "seg", 1)
    received_middle = shifted(extras[1], "seg", 1)
    received_long = shifted(extras[2], "seg", 1)
    for received in (received_short, received_middle, received_long):
        gradient = gradient + jnp.pad(received, ((0, 0), (0, samples - received.shape[1])))
    grad_wave = jnp.where(inside, gradient, 0.0).astype(jnp.bfloat16)
    grad_hops = grad_wave.reshape(clip_count, rows_here, HOP)
    initial = jnp.zeros((clip_count, 2, band_count, frames_all + 3), jnp.float32)
    running = initial
    portion = lax.all_gather(grad_hops, "seg", axis=1, tiled=True)
    first_row = jnp.int32(0)
    for quarter in range(4):
        contrib = jnp.einsum(
            "cjm,rbm->crbj",
            portion,
            local_table[:, :, quarter * HOP : (quarter + 1) * HOP],
            preferred_element_type=jnp.float32,
        )
        offset = first_row + 3 - quarter
        current = lax.dynamic_slice_in_dim(running, offset, portion.shape[1], 3)
        running = lax.dynamic_update_slice_in_dim(running, current + contrib, offset, 3)
    spec_grad = running[:, :, :, 3:].astype(jnp.bfloat16)
    return (loss, spec_grad)


def solution(mesh):
    return jax.shard_map(
        body,
        mesh=mesh,
        in_specs=(P("clip", None, "seg", None), P("clip", "seg"), P("clip")),
        out_specs=(P(), P("clip", None, "seg", None)),
        check_vma=False,
    )
```

profile of v0, /device:TPU:0, one launch (start us, length us, event | category | flops | bytes accessed | tf_op | source)
XLA Modules:
  0.0 186.7 jit_solution(12123341868288833466)
XLA Ops:
  7.6 0.6 fusion.129
  8.2 0.4 fusion.28
  8.6 2.0 %convolution_bitcast_fusion = f32[195,4,2048]{2,0,1:T(8,128)S(1)} fusion(bf16[1,128,2048]{2,1,0:T(8,128)(2,1)S(1)} %get-tuple-element.51, bf16[1,128,2048]{2,1,0:T(8,128)(2,1)S(1)} %get-tuple-element.50, bf16[4,2,128,192]{2,3,1,0:T(8,128)(2,1)} %param.3), kind=kOutput, calls=%fused_computation.13 | convolution fusion | flops 819986432 | bytes 7831552 | tf_op jit(solution)/shard_map/crbf,rbm->fcm/dot_general | solution.py:102
  10.6 2.0 %slice_add_fusion = f32[192,4,512]{2,0,1:T(8,128)} fusion(f32[195,4,2048]{2,0,1:T(8,128)S(1)} %convolution_bitcast_fusion), kind=kLoop, calls=%fused_computation.36 | loop fusion | flops 1179648 | bytes 7864320 | tf_op jit(solution)/shard_map/add | solution.py:106
  12.6 5.5 %fusion.56 = (f32[2048,128]{1,0:T(8,128)S(1)}, f32[2048,128]{1,0:T(8,128)}) fusion(), kind=kLoop, calls=%fused_computation.94 | loop fusion | flops 3670016 | bytes 2097152 | tf_op jit(solution)/shard_map/sin | solution.py:25
  18.1 2.1 %fusion.98 = (f32[1024,128]{1,0:T(8,128)S(1)}, f32[1024,128]{1,0:T(8,128)S(1)}) fusion(), kind=kLoop, calls=%fused_computation.182 | loop fusion | flops 1835008 | bytes 1048576 | tf_op jit(solution)/shard_map/sin | solution.py:25
  20.2 1.7 fusion.113
  22.0 1.0 fusion.133
  23.0 2.2 %copy.32 = f32[2048,8]{1,0:T(8,128)} copy(f32[2048,8]{0,1:T(8,128)} %get-tuple-element.102) | data formatting | bytes 131072 | tf_op jit(solution)/shard_map/cos | solution.py:25
  25.1 2.2 %copy.33 = f32[2048,8]{1,0:T(8,128)} copy(f32[2048,8]{0,1:T(8,128)} %get-tuple-element.103) | data formatting | bytes 131072 | tf_op jit(solution)/shard_map/sin | solution.py:25
  27.3 0.6 broadcast_compare_fusion
  28.2 1.0 copy.30
  29.2 1.0 copy.31
  30.4 0.9 copy.28
  31.2 0.9 copy.29
  32.1 0.6 broadcast_compare_fusion.1
  32.7 5.3 %multiply_subtract_fusion.1 = (f32[1024,4,128]{2,1,0:T(4,128)S(1)}, f32[1024,4,128]{2,1,0:T(4,128)S(1)}) fusion(f32[1024,128]{1,0:T(8,128)S(1)} %get-tuple-element.108, f32[1024,4]{1,0:T(8,128)} %copy.31, f32[1024,128]{1,0:T(8,128)S(1)} %get-tuple-element.109, f32[1024,4]{1,0:T(8,128)} %copy.30), kind=kLoop, calls=%fused_computation.26 | loop fusion | flops 3670016 | bytes 5275648 | tf_op jit(solution)/shard_map/sub | solution.py:42
  38.1 1.8 fusion.11
  39.9 1.4 multiply_subtract_fusion.2
  41.3 1.0 fusion.52
  42.3 10.3 %multiply_subtract_fusion = (f32[2048,8,128]{2,1,0:T(8,128)S(1)}, f32[2048,8,128]{2,1,0:T(8,128)S(1)}) fusion(f32[2048,128]{1,0:T(8,128)S(1)} %get-tuple-element.110, f32[2048,8]{1,0:T(8,128)S(1)} %copy-done.2, f32[2048,128]{1,0:T(8,128)S(1)} %copy-done, f32[2048,8]{1,0:T(8,128)S(1)} %copy-done.1), kind=kLoop, calls=%fused_computation.12 | loop fusion | flops 14680064 | bytes 19005440 | tf_op jit(solution)/shard_map/sub | solution.py:42
  52.6 4.9 %fusion.3 = (bf16[2048,1024]{1,0:T(8,128)(2,1)}, bf16[2048,1024]{1,0:T(8,128)(2,1)}) fusion(f32[256,8,8,128]{3,2,1,0:T(8,128)S(1)} %bitcast.335, f32[2048]{0:T(1024)S(1)} %multiply_subtract_fusion.3, f32[256,8,8,128]{3,2,1,0:T(8,128)S(1)} %bitcast.336), kind=kLoop, calls=%fused_computation.5 | loop fusion | flops 12582912 | bytes 25174016 | tf_op jit(solution)/shard_map/convert_element_type | solution.py:49
  57.5 1.1 copy.67
  58.8 1.3 collective-permute-start
  60.2 0.6 slice.312
  60.8 1.3 collective-permute-start.4
  62.1 1.3 collective-permute-start.5
  63.4 1.3 collective-permute-start.2
  64.7 1.3 collective-permute-start.3
  66.0 1.5 collective-permute-start.1
  67.7 4.5 %collective-permute-done.1 = bf16[4,384]{1,0:T(4,128)(2,1)S(1)} collective-permute-done((bf16[4,384]{1,0:T(4,128)(2,1)S(1)}, bf16[4,384]{1,0:T(4,128)(2,1)S(1)}, u32[]{:S(2)}, u32[]{:S(2)}) %collective-permute-start.1) | collective-permute-done | bytes 3104 | tf_op jit(solution)/shard_map/ppermute | solution.py:20
  72.5 1.6 fusion.32
  74.1 2.0 %select_reduce_fusion.5 = (f32[4]{0:T(128)}, f32[4]{0:T(128)}, f32[4]{0:T(128)}, f32[4,96,256]{2,1,0:T(8,128)}, f32[1,4,96,256]{3,2,1,0:T(8,128)}) fusion(pred[4,96]{1,0:T(4,128)(4,1)S(1)} %broadcast_compare_fusion.2, f32[2,4,96,512]{3,2,1,0:T(8,128)S(1)} %fusion.32), kind=kLoop, calls=%fused_computation.166 | loop fusion | flops 2064372 | bytes 2359728 | tf_op jit(solution)/shard_map/reduce_sum | solution.py:158
  76.6 2.5 %fusion.12 = f32[2,4,48,1024]{3,2,1,0:T(8,128)S(1)} fusion(bf16[1024,512]{1,0:T(8,128)(2,1)} %get-tuple-element.83, bf16[1024,512]{1,0:T(8,128)(2,1)} %get-tuple-element.82, bf16[1,4,48,1024]{3,2,1,0:T(8,128)(2,1)S(1)} %maximum_bitcast_fusion.3, bf16[1,4,48,1024]{3,2,1,0:T(8,128)(2,1)S(1)} %maximum_bitcast_fusion.2), kind=kOutput, calls=%fused_computation.21 | convolution fusion | flops 809893888 | bytes 4456448 | tf_op jit(solution)/shard_map/ecfm,mj->ecfj/dot_general | solution.py:143
  79.1 1.1 copy-done.4
  80.3 1.9 %select_reduce_fusion.4 = (f32[4]{0:T(128)}, f32[4]{0:T(128)}, f32[4]{0:T(128)}, f32[4,48,512]{2,1,0:T(8,128)S(1)}, f32[1,4,48,512]{3,2,1,0:T(8,128)}) fusion(pred[4,48]{1,0:T(4,128)(4,1)S(1)} %copy-done.26, f32[2,4,48,1024]{3,2,1,0:T(8,128)S(1)} %fusion.12), kind=kLoop, calls=%fused_computation.164 | loop fusion | flops 2064372 | bytes 2359536 | tf_op jit(solution)/shard_map/reduce_sum | solution.py:158
  82.3 0.7 fusion.164
  83.2 1.0 maximum_bitcast_fusion.4
  84.4 4.6 %fusion.4 = f32[2,4,24,2048]{3,2,1,0:T(8,128)S(1)} fusion(bf16[2048,1024]{1,0:T(8,128)(2,1)} %get-tuple-element.79, bf16[2048,1024]{1,0:T(8,128)(2,1)} %get-tuple-element.78, bf16[1,4,24,2048]{3,2,1,0:T(8,128)(2,1)S(1)} %maximum_bitcast_fusion.5, bf16[1,4,24,2048]{3,2,1,0:T(8,128)(2,1)S(1)} %maximum_bitcast_fusion.4), kind=kOutput, calls=%fused_computation.7 | convolution fusion | flops 1627783168 | bytes 10747904 | tf_op jit(solution)/shard_map/ecfm,mj->ecfj/dot_general | solution.py:143
  89.0 1.1 copy-done.5
  90.1 1.3 select_reduce_fusion.3
  91.6 17.9 %all-reduce.17 = (f32[3,4]{1,0:T(4,128)S(1)}, f32[3,4]{1,0:T(4,128)S(1)}, f32[3,4]{1,0:T(4,128)S(1)}) all-reduce(f32[3,4]{1,0:T(4,128)S(1)} %pad_maximum_fusion.18, f32[3,4]{1,0:T(4,128)S(1)} %pad_maximum_fusion.17, f32[3,4]{1,0:T(4,128)S(1)} %pad_maximum_fusion.16), channel_id=1, replica_groups=mesh['clip'=4,'seg'=8] {'seg'}, use_global_device_ids=true, to_apply=%region_12.13 | all-reduce | flops 36 | bytes 288 | tf_op jit(solution)/shard_map/psum | solution.py:167
  109.4 0.6 multiply_rsqrt_fusion
  110.0 1.7 divide_convert_fusion.3
  111.8 3.3 %fusion.14 = f32[4,48,1024]{2,1,0:T(8,128)} fusion(bf16[1024,512]{1,0:T(8,128)(2,1)} %get-tuple-element.83, bf16[1024,512]{1,0:T(8,128)(2,1)} %get-tuple-element.82, bf16[4,48,512]{2,1,0:T(8,128)(2,1)S(1)} %get-tuple-element.31, bf16[4,48,512]{2,1,0:T(8,128)(2,1)S(1)} %get-tuple-element.30), kind=kOutput, calls=%fused_computation.23 | convolution fusion | flops 407633920 | bytes 3276800 | tf_op jit(solution)/shard_map/cfj,mj->cfm/dot_general | solution.py:186
  115.1 1.5 reshape.822
  116.6 0.7 fusion.162
  117.8 0.8 pad_add_fusion.1
  118.6 1.7 divide_convert_fusion.1
  120.3 5.7 %fusion.6 = f32[4,24,2048]{2,1,0:T(8,128)} fusion(bf16[2048,1024]{1,0:T(8,128)(2,1)} %get-tuple-element.79, bf16[2048,1024]{1,0:T(8,128)(2,1)S(1)} %copy-done.3, bf16[4,24,1024]{2,1,0:T(8,128)(2,1)S(1)} %get-tuple-element.33, bf16[4,24,1024]{2,1,0:T(8,128)(2,1)S(1)} %get-tuple-element.32), kind=kOutput, calls=%fused_computation.9 | convolution fusion | flops 822870016 | bytes 9568256 | tf_op jit(solution)/shard_map/cfj,mj->cfm/dot_general | solution.py:186
  126.0 1.7 reshape.824
  127.7 0.7 fusion.163
  129.1 0.5 divide_convert_fusion.5
  129.6 1.3 fusion.54
  130.9 1.4 reshape.820
  132.3 0.6 fusion.161
  133.5 1.3 collective-permute-start.6
  134.8 1.8 collective-permute-start.7
  136.6 2.6 %collective-permute-start.8 = (f32[4,1536]{1,0:T(4,128)S(1)}, f32[4,1536]{1,0:T(4,128)S(1)}, u32[]{:S(2)}, u32[]{:S(2)}) collective-permute-start(f32[4,1536]{1,0:T(4,128)S(1)} %bitcast.371), channel_id=1, source_target_pairs={{0,1},{1,2},{2,3},{3,4},{4,5},{5,6},{6,7},{8,9},{9,10},{10,11},{11... | collective-permute-start | bytes 73736 | tf_op jit(solution)/shard_map/ppermute | solution.py:20
  139.2 13.2 %psum.31 = f32[]{:T(128)} all-reduce(f32[]{:T(128)} %get-tuple-element.81), channel_id=1, replica_groups=mesh['clip'=4,'seg'=8] {'clip'}, use_global_device_ids=true, to_apply=%region_14.15 | all-reduce | flops 1 | bytes 8 | tf_op jit(solution)/shard_map/psum | solution.py:169
  153.3 12.2 %all_gather.3 = bf16[4,192,512]{2,1,0:T(8,128)(2,1)S(1)} all-gather(bf16[4,24,512]{2,1,0:T(8,128)(2,1)S(1)} %bitcast.367), channel_id=1, replica_groups=mesh['clip'=4,'seg'=8] {'seg'}, dimensions={1}, use_global_device_ids=true | all-gather | bytes 884736 | tf_op jit(solution)/shard_map/all_gather | solution.py:201
  166.4 5.3 %dynamic_update_slice.13 = f32[4,2,128,195]{2,3,0,1:T(8,128)S(1)} dynamic-update-slice(f32[4,2,128,195]{2,3,0,1:T(8,128)S(1)} %dynamic_update_slice.12, f32[4,2,128,192]{2,3,0,1:T(8,128)S(1)} %fusion.16, s32[]{:T(128)} %constant.170.clone.1, s32[]{:T(128)} %constant.170.clone.1, s32[]{:T(128)} %constant.170.clone.1, s32[]{:T(128)} %constant.190.clone.1) | dynamic-update-slice | bytes 1572868 | tf_op jit(solution)/shard_map/dynamic_update_slice | solution.py:212
  172.2 5.3 %dynamic_update_slice.14 = f32[4,2,128,195]{2,3,0,1:T(8,128)S(1)} dynamic-update-slice(f32[4,2,128,195]{2,3,0,1:T(8,128)S(1)} %dynamic_update_slice.13, f32[4,2,128,192]{2,3,0,1:T(8,128)S(1)} %fusion.17, s32[]{:T(128)} %constant.170.clone.1, s32[]{:T(128)} %constant.170.clone.1, s32[]{:T(128)} %constant.170.clone.1, s32[]{:T(128)} %constant.169.clone.1) | dynamic-update-slice | bytes 1572868 | tf_op jit(solution)/shard_map/dynamic_update_slice | solution.py:212
  178.0 0.8 copy.46
  (142 shorter events, 6.2 us)
Async XLA Ops:
  7.2 50.3 %reduce-scatter.2.cloned.1.call-start = ((), (), s32[]{:S(2)}) async-start(), calls=%async_computation.1 | async-start | bytes 1769472 | tf_op jit(solution)/shard_map/reduce_scatter | solution.py:105
  12.6 9.4 %copy-start.15 = (s32[4]{0:T(128)S(1)}, s32[4]{0:T(128)}, u32[]{:S(2)}) copy-start(s32[4]{0:T(128)} %param.5) | copy-start | bytes 52
  38.0 1.9 copy-start.9
  38.0 1.8 copy-start.10
  38.1 1.8 copy-start.11
  38.1 4.2 %copy-start = (f32[2048,128]{1,0:T(8,128)S(1)}, f32[2048,128]{1,0:T(8,128)}, u32[]{:S(2)}) copy-start(f32[2048,128]{1,0:T(8,128)} %get-tuple-element.111) | copy-start | bytes 3145732
  38.1 4.2 %copy-start.1 = (f32[2048,8]{1,0:T(8,128)S(1)}, f32[2048,8]{1,0:T(8,128)}, u32[]{:S(2)}) copy-start(f32[2048,8]{1,0:T(8,128)} %copy.32) | copy-start | bytes 196612
  38.1 4.2 %copy-start.2 = (f32[2048,8]{1,0:T(8,128)S(1)}, f32[2048,8]{1,0:T(8,128)}, u32[]{:S(2)}) copy-start(f32[2048,8]{1,0:T(8,128)} %copy.33) | copy-start | bytes 196612
  52.6 6.0 %copy-start.14 = (bf16[4,12288]{1,0:T(4,128)(2,1)S(1)}, bf16[4,12288]{1,0:T(4,128)(2,1)}, u32[]{:S(2)}) copy-start(bf16[4,12288]{1,0:T(4,128)(2,1)} %param.4) | copy-start | bytes 294916
  58.8 7.2 %collective-permute-start = (bf16[4,384]{1,0:T(4,128)(2,1)S(1)}, bf16[4,384]{1,0:T(4,128)(2,1)S(1)}, u32[]{:S(2)}, u32[]{:S(2)}) collective-permute-start(bf16[4,384]{1,0:T(4,128)(2,1)S(1)} %slice.293), channel_id=1, source_target_pairs={{1,0},{2,1},{3,2},{4,3},{5,4},{6,5},{7,6},{9,8},{10,9},{11,10},{12... | collective-permute-start | bytes 9224 | tf_op jit(solution)/shard_map/ppermute | solution.py:20
  60.1 16.0 %copy-start.24 = (pred[4,96]{1,0:T(4,128)(4,1)}, pred[4,96]{1,0:T(4,128)(4,1)S(1)}, u32[]{:S(2)}) copy-start(pred[4,96]{1,0:T(4,128)(4,1)S(1)} %broadcast_compare_fusion.2) | copy-start | bytes 1156
  60.8 21.4 %collective-permute-start.4 = (bf16[4,1536]{1,0:T(4,128)(2,1)S(1)}, bf16[4,1536]{1,0:T(4,128)(2,1)S(1)}, u32[]{:S(2)}, u32[]{:S(2)}) collective-permute-start(bf16[4,1536]{1,0:T(4,128)(2,1)S(1)} %slice.321), channel_id=1, source_target_pairs={{1,0},{2,1},{3,2},{4,3},{5,4},{6,5},{7,6},{9,8},{10,9},{11,10},{12... | collective-permute-start | bytes 36872 | tf_op jit(solution)/shard_map/ppermute | solution.py:20
  62.1 21.0 %collective-permute-start.5 = (bf16[4,1536]{1,0:T(4,128)(2,1)S(1)}, bf16[4,1536]{1,0:T(4,128)(2,1)S(1)}, u32[]{:S(2)}, u32[]{:S(2)}) collective-permute-start(bf16[4,1536]{1,0:T(4,128)(2,1)S(1)} %slice.326), channel_id=1, source_target_pairs={{1,0},{2,1},{3,2},{4,3},{5,4},{6,5},{7,6},{9,8},{10,9},{11,10},{12... | collective-permute-start | bytes 36872 | tf_op jit(solution)/shard_map/ppermute | solution.py:20
  63.4 12.7 %collective-permute-start.2 = (bf16[4,768]{1,0:T(4,128)(2,1)S(1)}, bf16[4,768]{1,0:T(4,128)(2,1)S(1)}, u32[]{:S(2)}, u32[]{:S(2)}) collective-permute-start(bf16[4,768]{1,0:T(4,128)(2,1)S(1)} %slice.307), channel_id=1, source_target_pairs={{1,0},{2,1},{3,2},{4,3},{5,4},{6,5},{7,6},{9,8},{10,9},{11,10},{12... | collective-permute-start | bytes 18440 | tf_op jit(solution)/shard_map/ppermute | solution.py:20
  64.7 11.6 %collective-permute-start.3 = (bf16[4,768]{1,0:T(4,128)(2,1)}, bf16[4,768]{1,0:T(4,128)(2,1)S(1)}, u32[]{:S(2)}, u32[]{:S(2)}) collective-permute-start(bf16[4,768]{1,0:T(4,128)(2,1)} %slice.312), channel_id=1, source_target_pairs={{1,0},{2,1},{3,2},{4,3},{5,4},{6,5},{7,6},{9,8},{10,9},{11,10},{12... | collective-permute-start | bytes 18440 | tf_op jit(solution)/shard_map/ppermute | solution.py:20
  66.0 6.2 %collective-permute-start.1 = (bf16[4,384]{1,0:T(4,128)(2,1)S(1)}, bf16[4,384]{1,0:T(4,128)(2,1)S(1)}, u32[]{:S(2)}, u32[]{:S(2)}) collective-permute-start(bf16[4,384]{1,0:T(4,128)(2,1)S(1)} %slice.298), channel_id=1, source_target_pairs={{1,0},{2,1},{3,2},{4,3},{5,4},{6,5},{7,6},{9,8},{10,9},{11,10},{12... | collective-permute-start | bytes 9224 | tf_op jit(solution)/shard_map/ppermute | solution.py:20
  76.5 3.8 %copy-start.26 = (pred[4,48]{1,0:T(4,128)(4,1)S(1)}, pred[4,48]{1,0:T(4,128)(4,1)}, u32[]{:S(2)}) copy-start(pred[4,48]{1,0:T(4,128)(4,1)} %broadcast_compare_fusion.1) | copy-start | bytes 580
  79.1 1.2 copy-start.4
  84.3 5.8 %copy-start.23 = (pred[4,24]{1,0:T(4,128)(4,1)S(1)}, pred[4,24]{1,0:T(4,128)(4,1)}, u32[]{:S(2)}) copy-start(pred[4,24]{1,0:T(4,128)(4,1)} %broadcast_compare_fusion) | copy-start | bytes 292
  84.3 7.2 %copy-start.19 = (f32[4]{0:T(128)S(1)}, f32[4]{0:T(128)}, u32[]{:S(2)}) copy-start(f32[4]{0:T(128)} %get-tuple-element.8) | copy-start | bytes 52
  84.3 7.1 %copy-start.22 = (f32[4]{0:T(128)S(1)}, f32[4]{0:T(128)}, u32[]{:S(2)}) copy-start(f32[4]{0:T(128)} %get-tuple-element.10) | copy-start | bytes 52
  84.3 7.2 %copy-start.18 = (f32[4]{0:T(128)S(1)}, f32[4]{0:T(128)}, u32[]{:S(2)}) copy-start(f32[4]{0:T(128)} %get-tuple-element.14) | copy-start | bytes 52
  84.3 7.2 %copy-start.21 = (f32[4]{0:T(128)S(1)}, f32[4]{0:T(128)}, u32[]{:S(2)}) copy-start(f32[4]{0:T(128)} %get-tuple-element.15) | copy-start | bytes 52
  84.3 7.2 %copy-start.16 = (s32[4]{0:T(128)S(1)}, s32[4]{0:T(128)}, u32[]{:S(2)}) copy-start(s32[4]{0:T(128)} %param.5) | copy-start | bytes 52
  84.3 7.2 %copy-start.17 = (f32[4]{0:T(128)S(1)}, f32[4]{0:T(128)}, u32[]{:S(2)}) copy-start(f32[4]{0:T(128)} %get-tuple-element.9) | copy-start | bytes 52
  84.3 7.2 %copy-start.20 = (f32[4]{0:T(128)S(1)}, f32[4]{0:T(128)}, u32[]{:S(2)}) copy-start(f32[4]{0:T(128)} %get-tuple-element.11) | copy-start | bytes 52
  84.4 25.7 %copy-start.27 = (pred[4,48]{1,0:T(4,128)(4,1)S(1)}, pred[4,48]{1,0:T(4,128)(4,1)}, u32[]{:S(2)}) copy-start(pred[4,48]{1,0:T(4,128)(4,1)} %broadcast_compare_fusion.1) | copy-start | bytes 580
  89.0 1.1 copy-start.5
  116.6 2.0 %copy-start.8 = (f32[4,24,1024]{2,1,0:T(8,128)S(1)}, f32[4,24,1024]{2,1,0:T(8,128)}, u32[]{:S(2)}) copy-start(f32[4,24,1024]{2,1,0:T(8,128)} %get-tuple-element.24) | copy-start | bytes 1179652
  116.6 3.7 %copy-start.3 = (bf16[2048,1024]{1,0:T(8,128)(2,1)S(1)}, bf16[2048,1024]{1,0:T(8,128)(2,1)}, u32[]{:S(2)}) copy-start(bf16[2048,1024]{1,0:T(8,128)(2,1)} %get-tuple-element.78) | copy-start | bytes 12582916
  126.0 3.0 %copy-start.25 = (pred[4,96]{1,0:T(4,128)(4,1)S(1)}, pred[4,96]{1,0:T(4,128)(4,1)}, u32[]{:S(2)}) copy-start(pred[4,96]{1,0:T(4,128)(4,1)} %copy-done.24) | copy-start | bytes 1156
  127.7 1.4 copy-start.6
  127.7 1.4 copy-start.7
  127.7 1.9 %copy-start.12 = (bf16[512,256]{1,0:T(8,128)(2,1)S(1)}, bf16[512,256]{1,0:T(8,128)(2,1)}, u32[]{:S(2)}) copy-start(bf16[512,256]{1,0:T(8,128)(2,1)} %get-tuple-element.87) | copy-start | bytes 786436
  127.7 1.9 %copy-start.13 = (bf16[512,256]{1,0:T(8,128)(2,1)S(1)}, bf16[512,256]{1,0:T(8,128)(2,1)}, u32[]{:S(2)}) copy-start(bf16[512,256]{1,0:T(8,128)(2,1)} %get-tuple-element.88) | copy-start | bytes 786436
  129.6 23.5 %slice-start = ((f32[4,51,256]{2,0,1:T(4,128)}), f32[4,48,256]{2,0,1:T(4,128)S(1)}, s32[]{:S(2)}) async-start(f32[4,51,256]{2,0,1:T(4,128)} %pad_add_fusion.1), calls=%async_computation.2 | async-start | bytes 393216 | tf_op jit(solution)/shard_map/slice | solution.py:190
  133.5 19.7 %collective-permute-start.6 = (f32[4,384]{1,0:T(4,128)S(1)}, f32[4,384]{1,0:T(4,128)S(1)}, u32[]{:S(2)}, u32[]{:S(2)}) collective-permute-start(f32[4,384]{1,0:T(4,128)S(1)} %add_bitcast_fusion), channel_id=1, source_target_pairs={{0,1},{1,2},{2,3},{3,4},{4,5},{5,6},{6,7},{8,9},{9,10},{10,11},{11... | collective-permute-start | bytes 18440 | tf_op jit(solution)/shard_map/ppermute | solution.py:20
  134.8 18.4 %collective-permute-start.7 = (f32[4,768]{1,0:T(4,128)S(1)}, f32[4,768]{1,0:T(4,128)S(1)}, u32[]{:S(2)}, u32[]{:S(2)}) collective-permute-start(f32[4,768]{1,0:T(4,128)S(1)} %bitcast.372), channel_id=1, source_target_pairs={{0,1},{1,2},{2,3},{3,4},{4,5},{5,6},{6,7},{8,9},{9,10},{10,11},{11... | collective-permute-start | bytes 36872 | tf_op jit(solution)/shard_map/ppermute | solution.py:20
  136.6 16.6 %collective-permute-start.8 = (f32[4,1536]{1,0:T(4,128)S(1)}, f32[4,1536]{1,0:T(4,128)S(1)}, u32[]{:S(2)}, u32[]{:S(2)}) collective-permute-start(f32[4,1536]{1,0:T(4,128)S(1)} %bitcast.371), channel_id=1, source_target_pairs={{0,1},{1,2},{2,3},{3,4},{4,5},{5,6},{6,7},{8,9},{9,10},{10,11},{11... | collective-permute-start | bytes 73736 | tf_op jit(solution)/shard_map/ppermute | solution.py:20
Sparse Core Ops, SparseCore 0:
  12.7 41.1 reduce-scatter.1
where the time goes:
time: 188 us; the launch traced here: 187 us
  other arithmetic  52.6 us (28%)
  blocking collectives  43.3 us (23%)
  local copies, waits for them, and re-layouts  33.1 us (18%)
  matrix products  22.7 us (12%)
  between operations  16.8 us (9%)
  starting transfers between devices  13.7 us (7%)
  waiting for transfers between devices  4.5 us (2%)
    psum x1, blocking collectives, body(): spreads, energies, logterms = lax.psum((spreads, energies, logterms), 'seg')  17.9 us
    sub x3, other arithmetic, analysis_table(): coarse_cos[:, :, None] * fine_cos[:, None, :]  17 us
    ppermute x9, starting transfers between devices, shifted(): return lax.ppermute(block, axis, route)  13.6 us
    psum x1, blocking collectives, body(): loss = lax.psum(own_loss, 'clip') / (3 * clip_count * lax.axis_size('clip'))  13.2 us
    all_gather x1, blocking collectives, body(): portion = lax.all_gather(grad_hops, 'seg', axis=1, tiled=True)  12.2 us
    dynamic_update_slice x3, local copies, waits for them, and re-layouts, body(): lax.dynamic_update_slice_in_dim(running, current + contrib, offset, 3)  10.6 us
    dot_general x3, matrix products, body(): jnp.einsum('cfj,mj->cfm', grad_x, table, preferred_element_type=jnp.float32)  10.3 us
    sin x4, other arithmetic, angle_pair(): return (jnp.cos(angles), jnp.sin(angles))  9.53 us
  transfers between devices with their start and end apart: 10, of which 1 were waited for; matrix products, arithmetic and copies ran while one was open for 30% of the time, Pallas kernels for 0%

commit v1 on v0

--- a/solution.py
+++ b/solution.py
@@ -29,26 +29,22 @@
     return 0.5 - 0.5 * jnp.cos(time_index.astype(jnp.float32) * (2.0 * math.pi / points))
 
 
-def analysis_table(points):
+def analysis_table(points, fine):
     halfway = points // 2
-    lanes = min(128, halfway)
+    lanes = fine[0].shape[1]
     groups = halfway // lanes
     time_index = jnp.arange(points, dtype=jnp.int32)[:, None]
     coarse_cos, coarse_sin = angle_pair(
         (jnp.arange(groups, dtype=jnp.int32)[None, :] * lanes) * time_index, points
     )
-    fine_cos, fine_sin = angle_pair(jnp.arange(lanes, dtype=jnp.int32)[None, :] * time_index, points)
-    cos_full = (
-        coarse_cos[:, :, None] * fine_cos[:, None, :] - coarse_sin[:, :, None] * fine_sin[:, None, :]
-    )
-    sin_full = (
-        coarse_sin[:, :, None] * fine_cos[:, None, :] + coarse_cos[:, :, None] * fine_sin[:, None, :]
-    )
+    first = jnp.concatenate([coarse_cos, -coarse_sin], axis=1)
+    second = jnp.concatenate([-coarse_sin, -coarse_cos], axis=1)
+    fine_cos, fine_sin = fine
     window = window_of(time_index, points)[:, :, None]
-    factor = 1.0 / math.sqrt(points)
-    real = (cos_full * window * factor).astype(jnp.bfloat16).reshape(points, halfway)
-    imag = (-sin_full * window * factor).astype(jnp.bfloat16).reshape(points, halfway)
-    return jnp.concatenate([real, imag], axis=1)
+    entry_value = first[:, :, None] * fine_cos[:, None, :] + second[:, :, None] * fine_sin[:, None, :]
+    return (entry_value * window * (1.0 / math.sqrt(points))).astype(jnp.bfloat16).reshape(
+        points, points
+    )
 
 
 def synthesis_rows(first_bin, band_count):
@@ -57,17 +53,16 @@
     coarse_bins = first_bin + sub * jnp.arange(band_count // sub, dtype=jnp.int32)[:, None]
     coarse_cos, coarse_sin = angle_pair(coarse_bins * time_index, NFFT)
     fine_cos, fine_sin = angle_pair(jnp.arange(sub, dtype=jnp.int32)[:, None] * time_index, NFFT)
-    cos_full = (
-        coarse_cos[:, None, :] * fine_cos[None, :, :] - coarse_sin[:, None, :] * fine_sin[None, :, :]
-    )
-    sin_full = (
-        coarse_sin[:, None, :] * fine_cos[None, :, :] + coarse_cos[:, None, :] * fine_sin[None, :, :]
-    )
-    window = window_of(time_index, NFFT)[None, :, :]
-    factor = 1.0 / math.sqrt(BINS)
-    real = (cos_full * window * factor).astype(jnp.bfloat16).reshape(band_count, NFFT)
-    imag = (-sin_full * window * factor).astype(jnp.bfloat16).reshape(band_count, NFFT)
-    return jnp.stack([real, imag])
+    first = jnp.stack([coarse_cos, -coarse_sin])
+    second = jnp.stack([-coarse_sin, -coarse_cos])
+    window = window_of(time_index, NFFT)[None, None, :, :]
+    entry_value = (
+        first[:, :, None, :] * fine_cos[None, None, :, :]
+        + second[:, :, None, :] * fine_sin[None, None, :, :]
+    )
+    return (entry_value * window * (1.0 / math.sqrt(BINS))).astype(jnp.bfloat16).reshape(
+        2, band_count, NFFT
+    )
 
 
 def spread_parts(quarters):
@@ -123,11 +118,13 @@
     est_wave = jnp.where(inside, estimate, 0.0).astype(jnp.bfloat16)
     clean = jnp.where(inside, target, jnp.zeros_like(target))
     sizes_list = (NFFT // 4, NFFT // 2, NFFT)
-    beyond_list = [
-        shifted((est_wave[:, : 3 * NFFT // 16], clean[:, : 3 * NFFT // 16]), "seg", -1),
-        shifted((est_wave[:, : 3 * NFFT // 8], clean[:, : 3 * NFFT // 8]), "seg", -1),
-        shifted((est_wave[:, : 3 * NFFT // 4], clean[:, : 3 * NFFT // 4]), "seg", -1),
-    ]
+    halo = 3 * NFFT // 4
+    beyond_all = shifted(jnp.stack([est_wave[:, :halo], clean[:, :halo]]), "seg", -1)
+    beyond_list = [beyond_all[:, :, : 3 * points // 4] for points in sizes_list]
+    lanes = min(128, NFFT // 4)
+    fine_all = angle_pair(
+        jnp.arange(lanes, dtype=jnp.int32)[None, :] * jnp.arange(NFFT, dtype=jnp.int32)[:, None], NFFT
+    )
     saved = []
     spread_list = []
     energy_list = []
@@ -139,7 +136,8 @@
         paired = jnp.stack(
             [framed(est_wave, beyond_pair[0], stride), framed(clean, beyond_pair[1], stride)]
         )
-        table = analysis_table(points)
+        step = NFFT // points
+        table = analysis_table(points, (fine_all[0][::step], fine_all[1][::step]))
         spectra_pair = jnp.einsum(
             "ecfm,mj->ecfj", paired, table, preferred_element_type=jnp.float32
         )
@@ -164,9 +162,19 @@
     spreads = jnp.stack(spread_list)
     energies = jnp.stack(energy_list)
     logterms = jnp.stack(logterm_list)
-    spreads, energies, logterms = lax.psum((spreads, energies, logterms), "seg")
-    own_loss = jnp.sum(jnp.sqrt((spreads + EPS_RATIO) / energies) + logterms)
-    loss = lax.psum(own_loss, "clip") / (3 * clip_count * lax.axis_size("clip"))
+    clip_index = lax.axis_index("clip")
+    clip_groups = lax.axis_size("clip")
+    stats = jnp.stack([spreads, energies, logterms])
+    slots = jnp.where(
+        (jnp.arange(clip_groups, dtype=jnp.int32) == clip_index)[:, None, None, None],
+        stats[None],
+        0.0,
+    )
+    slots = lax.psum(slots, ("clip", "seg"))
+    loss = jnp.sum(jnp.sqrt((slots[:, 0] + EPS_RATIO) / slots[:, 1]) + slots[:, 2]) / (
+        3 * clip_count * clip_groups
+    )
+    spreads, energies, logterms = slots[clip_index]
     ratio_weight = 1.0 / jnp.sqrt((spreads + EPS_RATIO) * energies)
     gradient = jnp.zeros((clip_count, samples), jnp.float32)
     extras = []
@@ -189,28 +197,20 @@
         spread_back = spread_parts(grad_frames.reshape(clip_count, frame_count, 4, stride))
         gradient = gradient + spread_back[:, :frame_count].reshape(clip_count, samples)
         extras.append(spread_back[:, frame_count:].reshape(clip_count, 3 * stride))
-    received_short = shifted(extras[0], "seg", 1)
-    received_middle = shifted(extras[1], "seg", 1)
-    received_long = shifted(extras[2], "seg", 1)
-    for received in (received_short, received_middle, received_long):
-        gradient = gradient + jnp.pad(received, ((0, 0), (0, samples - received.shape[1])))
+    halo = 3 * NFFT // 4
+    spill = sum(jnp.pad(extra, ((0, 0), (0, halo - extra.shape[1]))) for extra in extras)
+    received = shifted(spill, "seg", 1)
+    gradient = gradient + jnp.pad(received, ((0, 0), (0, samples - halo)))
     grad_wave = jnp.where(inside, gradient, 0.0).astype(jnp.bfloat16)
     grad_hops = grad_wave.reshape(clip_count, rows_here, HOP)
-    initial = jnp.zeros((clip_count, 2, band_count, frames_all + 3), jnp.float32)
-    running = initial
     portion = lax.all_gather(grad_hops, "seg", axis=1, tiled=True)
-    first_row = jnp.int32(0)
-    for quarter in range(4):
-        contrib = jnp.einsum(
-            "cjm,rbm->crbj",
-            portion,
-            local_table[:, :, quarter * HOP : (quarter + 1) * HOP],
-            preferred_element_type=jnp.float32,
-        )
-        offset = first_row + 3 - quarter
-        current = lax.dynamic_slice_in_dim(running, offset, portion.shape[1], 3)
-        running = lax.dynamic_update_slice_in_dim(running, current + contrib, offset, 3)
-    spec_grad = running[:, :, :, 3:].astype(jnp.bfloat16)
+    padded = jnp.concatenate([portion, jnp.zeros((clip_count, 3, HOP), portion.dtype)], axis=1)
+    grad_signals = jnp.concatenate(
+        [padded[:, quarter : quarter + frames_all] for quarter in range(4)], axis=2
+    )
+    spec_grad = jnp.einsum(
+        "ctm,rbm->crbt", grad_signals, local_table, preferred_element_type=jnp.float32
+    ).astype(jnp.bfloat16)
     return (loss, spec_grad)
 
 

time: 188 us -> 187 us (level)
  blocking collectives: 43.3 us -> 57.2 us
  other arithmetic: 52.6 us -> 40.5 us
  starting transfers between devices: 13.7 us -> 2.75 us
  local copies, waits for them, and re-layouts: 33.1 us -> 42.8 us
  waiting for transfers between devices: 4.5 us -> 0.2 us
  matrix products: 22.7 us -> 25.5 us
    add x0 -> x3, local copies, waits for them, and re-layouts: none -> 24.3 us  [analysis_table(): first[:, :, None] * fine_cos[:, None, :]]
    add x0 -> x4, other arithmetic: none -> 23.5 us  [the longest x3 23.5 us: analysis_table(): first[:, :, None] * fine_cos[:, None, :]]
    sub x3 -> x0, other arithmetic: 17 us -> none  [analysis_table(): coarse_cos[:, :, None] * fine_cos[:, None, :]]
    psum x2 -> x1, blocking collectives: 31.1 us -> 42.8 us  [body(): slots = lax.psum(slots, ('clip', 'seg'))]
    ppermute x9 -> x2, starting transfers between devices: 13.6 us -> 2.71 us  [shifted(): return lax.ppermute(block, axis, route)]
    dynamic_update_slice x3 -> x0, local copies, waits for them, and re-layouts: 10.6 us -> none  [body(): lax.dynamic_update_slice_in_dim(running, current + contrib, offset, 3)]
    convert_element_type x4 -> x0, other arithmetic: 8.06 us -> none  [the longest x3 7.64 us: analysis_table(): (cos_full * window * factor).astype(jnp.bfloat16).reshape(points, halfway)]
    concatenate x0 -> x6, local copies, waits for them, and re-layouts: none -> 6.38 us  [the longest x3 3.19 us: analysis_table(): first = jnp.concatenate([coarse_cos, -coarse_sin], axis=1)]
  transfers between devices with their start and end apart: 10 -> 3, of which waited for: 1 -> 1; matrix products, arithmetic and copies ran while one was open for 30% -> 36% of each run, Pallas kernels for 0% -> 0%
where the time goes in v1:
time: 187 us; the launch traced here: 186 us
  blocking collectives  57.2 us (31%)
  local copies, waits for them, and re-layouts  42.8 us (23%)
  other arithmetic  40.5 us (22%)
  matrix products  25.5 us (14%)
  between operations  16.8 us (9%)
  starting transfers between devices  2.75 us (1%)
    psum x1, blocking collectives, body(): slots = lax.psum(slots, ('clip', 'seg'))  42.8 us
    add x3, local copies, waits for them, and re-layouts, analysis_table(): first[:, :, None] * fine_cos[:, None, :]  24.3 us
    add x3, other arithmetic, analysis_table(): first[:, :, None] * fine_cos[:, None, :]  23.5 us
    all_gather x1, blocking collectives, body(): portion = lax.all_gather(grad_hops, 'seg', axis=1, tiled=True)  14.4 us
    dot_general x3, matrix products, body(): jnp.einsum('ecfm,mj->ecfj', paired, table, preferred_element_type=jnp.flo...  13.2 us
    dot_general x3, matrix products, body(): jnp.einsum('cfj,mj->cfm', grad_x, table, preferred_element_type=jnp.float32)  8.74 us
    slice x4, local copies, waits for them, and re-layouts, body(): table = analysis_table(points, (fine_all[0][::step], fine_all[1][::step]))  5.72 us
    unnamed x57, local copies, waits for them, and re-layouts  4.73 us
  transfers between devices with their start and end apart: 3, of which 1 were waited for; matrix products, arithmetic and copies ran while one was open for 36% of the time, Pallas kernels for 0%

profile of v1, /device:TPU:0, one launch (start us, length us, event | category | flops | bytes accessed | tf_op | source)
XLA Modules:
  0.0 185.8 jit_solution(4532744503190446467)
XLA Ops:
  7.3 0.3 fusion.110
  7.5 0.3 fusion.109
  7.8 0.6 fusion.104
  8.4 0.2 broadcast_bitcast_fusion
  8.7 2.4 %convolution_bitcast_fusion = f32[195,4,2048]{2,0,1:T(8,128)S(1)} fusion(bf16[4,2,128,192]{2,3,1,0:T(8,128)(2,1)} %param.3, f32[2048]{0:T(1024)S(1)} %multiply_subtract_fusion.1, f32[128,2048]{1,0:T(8,128)S(1)} %get-tuple-element.106, f32[2,16,2048]{2,1,0:T(8,128)S(1)} %get-tuple-element.53, f32[128,2048]{1,0:T(8,128)S(1)} %get-tuple-element.107, ...), kind=kOutput, calls=%fused_computation.16 | convolution fusion | flops 821035008 | bytes 9412608 | tf_op jit(solution)/shard_map/crbf,rbm->fcm/dot_general | solution.py:97
  11.2 2.0 %slice_add_fusion = f32[192,4,512]{2,0,1:T(8,128)} fusion(f32[195,4,2048]{2,0,1:T(8,128)S(1)} %convolution_bitcast_fusion), kind=kLoop, calls=%fused_computation.38 | loop fusion | flops 1179648 | bytes 7864320 | tf_op jit(solution)/shard_map/add | solution.py:101
  13.4 0.1 multiply_subtract_fusion
  13.5 4.1 %fusion.63 = (f32[2048,128]{1,0:T(8,128)S(1)}, f32[2048,128]{1,0:T(8,128)S(1)}) fusion(), kind=kLoop, calls=%fused_computation.79 | loop fusion | flops 3670016 | bytes 2097152 | tf_op jit(solution)/shard_map/sin | solution.py:25
  17.7 0.1 broadcast_compare_fusion
  17.8 0.2 fusion.122
  17.9 0.2 fusion.116
  18.1 0.3 fusion.108
  18.5 0.1 broadcast_compare_fusion.1
  18.8 1.1 slice.265
  19.9 0.7 slice.281
  20.6 1.9 %slice.264 = f32[512,128]{1,0:T(8,128)} slice(f32[2048,128]{1,0:T(8,128)S(1)} %get-tuple-element.109), slice={[0:2048:4], [0:128:1]} | slice | bytes 524288 | tf_op jit(solution)/shard_map/slice | solution.py:140
  22.5 2.0 %slice.280 = f32[1024,128]{1,0:T(8,128)} slice(f32[2048,128]{1,0:T(8,128)S(1)} %get-tuple-element.109), slice={[0:2048:2], [0:128:1]} | slice | bytes 1048576 | tf_op jit(solution)/shard_map/slice | solution.py:140
  24.5 0.9 copy.25
  25.4 0.9 copy.26
  26.2 1.0 copy.27
  27.2 1.0 copy.28
  28.3 1.3 copy.29
  29.6 1.3 copy.30
  30.9 4.2 %multiply_add_fusion.2 = f32[512,4,128]{2,1,0:T(4,128)S(1)} fusion(f32[512,128]{1,0:T(8,128)S(1)} %slice.265, f32[512,4]{1,0:T(8,128)} %copy.26, f32[512,128]{1,0:T(8,128)} %slice.264, f32[512,4]{1,0:T(8,128)} %copy.25), kind=kLoop, calls=%fused_computation.55 | loop fusion | flops 786432 | bytes 1589248 | tf_op jit(solution)/shard_map/add | solution.py:44
  35.1 8.3 %multiply_add_fusion.1 = f32[1024,8,128]{2,1,0:T(8,128)} fusion(f32[1024,128]{1,0:T(8,128)S(1)} %slice.281, f32[1024,8]{1,0:T(8,128)} %copy.28, f32[1024,128]{1,0:T(8,128)} %slice.280, f32[1024,8]{1,0:T(8,128)} %copy.27), kind=kLoop, calls=%fused_computation.15 | loop fusion | flops 3145728 | bytes 5308416 | tf_op jit(solution)/shard_map/add | solution.py:44
  43.4 11.0 %multiply_add_fusion = f32[2048,16,128]{2,1,0:T(8,128)} fusion(f32[2048,128]{1,0:T(8,128)S(1)} %get-tuple-element.108, f32[2048,16]{1,0:T(8,128)S(1)} %copy-done.5, f32[2048,128]{1,0:T(8,128)S(1)} %copy-done.3, f32[2048,16]{1,0:T(8,128)S(1)} %copy-done.4), kind=kLoop, calls=%fused_computation.4 | loop fusion | flops 12582912 | bytes 19136512 | tf_op jit(solution)/shard_map/add | solution.py:44
  54.4 0.2 reduce-scatter.2.cloned.1.call-done
  54.6 1.1 copy.58
  55.6 0.2 fusion.84
  55.8 1.3 collective-permute-start
  57.2 1.4 add.391
  58.5 4.9 %add.396 = f32[4,256,1024]{2,1,0:T(8,128)} reshape(f32[1024,8,128]{2,1,0:T(8,128)} %multiply_add_fusion.1) | data formatting | bytes 8388608 | tf_op jit(solution)/shard_map/add | solution.py:44
  63.5 18.0 %add.402 = f32[4,512,2048]{2,1,0:T(8,128)} reshape(f32[2048,16,128]{2,1,0:T(8,128)} %multiply_add_fusion) | data formatting | bytes 33554432 | tf_op jit(solution)/shard_map/add | solution.py:44
  81.7 0.1 reshape.574
  81.9 0.1 reshape.575
  82.5 0.1 fusion.148
  82.6 0.1 fusion.147
  82.8 0.7 fusion.44
  83.5 1.5 select_reduce_fusion.5
  85.1 1.3 fusion.21
  86.3 1.5 select_reduce_fusion.4
  87.9 11.3 %fusion.4 = f32[2,4,24,2048]{3,2,1,0:T(8,128)S(1)} fusion(f32[256,8,16,128]{3,2,1,0:T(8,128)} %bitcast.359, f32[2048]{0:T(1024)S(1)} %multiply_subtract_fusion.1, bf16[1,4,24,2048]{3,2,1,0:T(8,128)(2,1)S(1)} %maximum_bitcast_fusion.11, bf16[1,4,24,2048]{3,2,1,0:T(8,128)(2,1)S(1)} %maximum_bitcast_fusion.10), kind=kOutput, calls=%fused_computation.7 | convolution fusion | flops 1623588864 | bytes 19144704 | tf_op jit(solution)/shard_map/ecfm,mj->ecfj/dot_general | solution.py:141
  99.2 1.2 copy-done.11
  100.4 0.8 select_reduce_fusion.3
  101.3 0.1 broadcast_select_fusion
  101.3 42.8 %psum.7 = f32[4,3,3,4]{3,2,1,0:T(4,128)S(1)} all-reduce(f32[4,3,3,4]{3,2,1,0:T(4,128)S(1)} %broadcast_select_fusion), channel_id=1, replica_groups=mesh['clip'=4,'seg'=8] {'clip','seg'}, use_global_device_ids=true, to_apply=%region_10.11 | all-reduce | flops 144 | bytes 1152 | tf_op jit(solution)/shard_map/psum | solution.py:173
  144.3 1.7 divide_convert_fusion.5
  146.0 0.5 fusion.55
  146.7 0.5 divide_convert_fusion.3
  147.2 1.0 copy-done
  148.2 0.9 fusion.27
  149.3 0.3 copy-done.12
  149.6 0.5 divide_convert_fusion.1
  150.1 7.3 %fusion.8 = f32[4,24,4,512]{3,1,2,0:T(8,128)S(1)} fusion(f32[4,512,2048]{2,1,0:T(8,128)} %add.402, f32[4,512]{1,0:T(4,128)S(1)} %multiply_subtract_fusion, bf16[4,24,1024]{2,1,0:T(8,128)(2,1)S(1)} %get-tuple-element.28, bf16[4,24,1024]{2,1,0:T(8,128)(2,1)S(1)} %get-tuple-element.27), kind=kOutput, calls=%fused_computation.10 | convolution fusion | flops 818675712 | bytes 17965056 | tf_op jit(solution)/shard_map/cfj,mj->cfm/dot_general | solution.py:194
  157.6 0.1 pad_add_fusion
  157.8 1.4 collective-permute-start.1
  159.2 0.6 fusion.115
  159.8 0.1 copy.63
  160.0 0.1 copy.64
  160.8 0.2 fusion.85
  161.0 14.4 %all_gather.3 = bf16[4,192,512]{2,1,0:T(8,128)(2,1)S(1)} all-gather(bf16[4,24,512]{2,1,0:T(8,128)(2,1)S(1)} %bitcast.364), channel_id=1, replica_groups=mesh['clip'=4,'seg'=8] {'seg'}, dimensions={1}, use_global_device_ids=true | all-gather | bytes 884736 | tf_op jit(solution)/shard_map/all_gather | solution.py:206
  175.4 0.5 pad_slice_fusion.2
  175.9 1.1 fusion.33
  177.0 0.8 copy.40
  (116 shorter events, 2.2 us)
Async XLA Ops:
  7.2 47.4 %reduce-scatter.2.cloned.1.call-start = ((), (), s32[]{:S(2)}) async-start(), calls=%async_computation.1 | async-start | bytes 1769472 | tf_op jit(solution)/shard_map/reduce_scatter | solution.py:100
  8.7 2.5 %copy-start.7 = (f32[128,2048]{1,0:T(8,128)}, f32[128,2048]{1,0:T(8,128)S(1)}, u32[]{:S(2)}) copy-start(f32[128,2048]{1,0:T(8,128)S(1)} %get-tuple-element.106) | copy-start | bytes 3145732
  8.7 2.5 %copy-start.9 = (f32[128,2048]{1,0:T(8,128)}, f32[128,2048]{1,0:T(8,128)S(1)}, u32[]{:S(2)}) copy-start(f32[128,2048]{1,0:T(8,128)S(1)} %get-tuple-element.107) | copy-start | bytes 3145732
  8.7 2.5 %copy-start.17 = (f32[2,16,2048]{2,1,0:T(8,128)}, f32[2,16,2048]{2,1,0:T(8,128)S(1)}, u32[]{:S(2)}) copy-start(f32[2,16,2048]{2,1,0:T(8,128)S(1)} %get-tuple-element.52) | copy-start | bytes 786436
  8.7 2.5 %copy-start.19 = (f32[2,16,2048]{2,1,0:T(8,128)}, f32[2,16,2048]{2,1,0:T(8,128)S(1)}, u32[]{:S(2)}) copy-start(f32[2,16,2048]{2,1,0:T(8,128)S(1)} %get-tuple-element.53) | copy-start | bytes 786436
  11.2 6.5 %copy-start.22 = (s32[4]{0:T(128)S(1)}, s32[4]{0:T(128)}, u32[]{:S(2)}) copy-start(s32[4]{0:T(128)} %param.5) | copy-start | bytes 52
  17.6 12.0 %copy-start.2 = (f32[2048,128]{1,0:T(8,128)}, f32[2048,128]{1,0:T(8,128)S(1)}, u32[]{:S(2)}) copy-start(f32[2048,128]{1,0:T(8,128)S(1)} %get-tuple-element.109) | copy-start | bytes 3145732
  30.9 12.5 %copy-start.3 = (f32[2048,128]{1,0:T(8,128)S(1)}, f32[2048,128]{1,0:T(8,128)}, u32[]{:S(2)}) copy-start(f32[2048,128]{1,0:T(8,128)} %copy-done.2) | copy-start | bytes 3145732
  30.9 12.5 %copy-start.4 = (f32[2048,16]{1,0:T(8,128)S(1)}, f32[2048,16]{1,0:T(8,128)}, u32[]{:S(2)}) copy-start(f32[2048,16]{1,0:T(8,128)} %copy.29) | copy-start | bytes 393220
  30.9 12.5 %copy-start.5 = (f32[2048,16]{1,0:T(8,128)S(1)}, f32[2048,16]{1,0:T(8,128)}, u32[]{:S(2)}) copy-start(f32[2048,16]{1,0:T(8,128)} %copy.30) | copy-start | bytes 393220
  43.4 12.2 %copy-start.21 = (bf16[4,12288]{1,0:T(4,128)(2,1)S(1)}, bf16[4,12288]{1,0:T(4,128)(2,1)}, u32[]{:S(2)}) copy-start(bf16[4,12288]{1,0:T(4,128)(2,1)} %param.4) | copy-start | bytes 294916
  55.8 25.6 %collective-permute-start = (bf16[2,4,1536]{2,1,0:T(4,128)(2,1)S(1)}, bf16[2,4,1536]{2,1,0:T(4,128)(2,1)S(1)}, u32[]{:S(2)}, u32[]{:S(2)}) collective-permute-start(bf16[2,4,1536]{2,1,0:T(4,128)(2,1)S(1)} %pad_maximum_fusion.12), channel_id=1, source_target_pairs={{1,0},{2,1},{3,2},{4,3},{5,4},{6,5},{7,6},{9,8},{10,9},{11,10},{12... | collective-permute-start | bytes 73736 | tf_op jit(solution)/shard_map/ppermute | solution.py:20
  82.8 2.3 %copy-start.1 = (f32[1024,8,128]{2,1,0:T(8,128)S(1)}, f32[1024,8,128]{2,1,0:T(8,128)}, u32[]{:S(2)}) copy-start(f32[1024,8,128]{2,1,0:T(8,128)} %multiply_add_fusion.1) | copy-start | bytes 12582916
  86.3 1.5 copy-start.13
  99.2 1.2 copy-start.11
  100.4 45.7 %copy-start.6 = (f32[4,128,512]{2,1,0:T(8,128)S(1)}, f32[4,128,512]{2,1,0:T(8,128)}, u32[]{:S(2)}) copy-start(f32[4,128,512]{2,1,0:T(8,128)} %add.391) | copy-start | bytes 3145732
  144.2 2.5 %copy-start.14 = (f32[2,4,48,1024]{3,2,1,0:T(8,128)S(1)}, f32[2,4,48,1024]{3,2,1,0:T(8,128)}, u32[]{:S(2)}) copy-start(f32[2,4,48,1024]{3,2,1,0:T(8,128)} %copy-done.13) | copy-start | bytes 4718596
  144.2 2.5 %copy-start.15 = (f32[4,48,512]{2,1,0:T(8,128)S(1)}, f32[4,48,512]{2,1,0:T(8,128)}, u32[]{:S(2)}) copy-start(f32[4,48,512]{2,1,0:T(8,128)} %get-tuple-element.19) | copy-start | bytes 1179652
  144.2 2.5 %copy-start.16 = (f32[1,4,48,512]{3,2,1,0:T(8,128)S(1)}, f32[1,4,48,512]{3,2,1,0:T(8,128)}, u32[]{:S(2)}) copy-start(f32[1,4,48,512]{3,2,1,0:T(8,128)} %get-tuple-element.20) | copy-start | bytes 1179652
  146.0 2.2 %copy-start = (f32[4,256,1024]{2,1,0:T(8,128)S(1)}, f32[4,256,1024]{2,1,0:T(8,128)}, u32[]{:S(2)}) copy-start(f32[4,256,1024]{2,1,0:T(8,128)} %add.396) | copy-start | bytes 12582916
  148.2 1.4 copy-start.12
  157.5 18.4 %copy-start.8 = (f32[128,2048]{1,0:T(8,128)S(1)}, f32[128,2048]{1,0:T(8,128)}, u32[]{:S(2)}) copy-start(f32[128,2048]{1,0:T(8,128)} %copy-done.7) | copy-start | bytes 3145732
  157.5 18.4 %copy-start.10 = (f32[128,2048]{1,0:T(8,128)S(1)}, f32[128,2048]{1,0:T(8,128)}, u32[]{:S(2)}) copy-start(f32[128,2048]{1,0:T(8,128)} %copy-done.9) | copy-start | bytes 3145732
  157.5 18.4 %copy-start.18 = (f32[2,16,2048]{2,1,0:T(8,128)S(1)}, f32[2,16,2048]{2,1,0:T(8,128)}, u32[]{:S(2)}) copy-start(f32[2,16,2048]{2,1,0:T(8,128)} %copy-done.17) | copy-start | bytes 786436
  157.5 18.4 %copy-start.20 = (f32[2,16,2048]{2,1,0:T(8,128)S(1)}, f32[2,16,2048]{2,1,0:T(8,128)}, u32[]{:S(2)}) copy-start(f32[2,16,2048]{2,1,0:T(8,128)} %copy-done.19) | copy-start | bytes 786436
  157.8 3.0 %collective-permute-start.1 = (f32[4,1536]{1,0:T(4,128)S(1)}, f32[4,1536]{1,0:T(4,128)S(1)}, u32[]{:S(2)}, u32[]{:S(2)}) collective-permute-start(f32[4,1536]{1,0:T(4,128)S(1)} %add_add_fusion.3), channel_id=1, source_target_pairs={{0,1},{1,2},{2,3},{3,4},{4,5},{5,6},{6,7},{8,9},{9,10},{10,11},{11... | collective-permute-start | bytes 73736 | tf_op jit(solution)/shard_map/ppermute | solution.py:20
Sparse Core Ops, SparseCore 0:
  13.3 41.1 reduce-scatter.1

commit v2 on v1

--- a/solution.py
+++ b/solution.py
@@ -31,38 +31,58 @@
 
 def analysis_table(points, fine):
     halfway = points // 2
-    lanes = fine[0].shape[1]
+    lanes = fine[0].shape[0]
     groups = halfway // lanes
-    time_index = jnp.arange(points, dtype=jnp.int32)[:, None]
-    coarse_cos, coarse_sin = angle_pair(
-        (jnp.arange(groups, dtype=jnp.int32)[None, :] * lanes) * time_index, points
-    )
-    first = jnp.concatenate([coarse_cos, -coarse_sin], axis=1)
-    second = jnp.concatenate([-coarse_sin, -coarse_cos], axis=1)
-    fine_cos, fine_sin = fine
-    window = window_of(time_index, points)[:, :, None]
-    entry_value = first[:, :, None] * fine_cos[:, None, :] + second[:, :, None] * fine_sin[:, None, :]
-    return (entry_value * window * (1.0 / math.sqrt(points))).astype(jnp.bfloat16).reshape(
-        points, points
-    )
+    time_index = jnp.arange(points, dtype=jnp.int32)[None, :]
+    row = jnp.arange(2 * groups, dtype=jnp.int32)[:, None]
+    is_sine = row >= groups
+    coarse_cos, coarse_sin = angle_pair(((row % groups) * lanes) * time_index, points)
+    first = jnp.where(is_sine, -coarse_sin, coarse_cos)
+    second = jnp.where(is_sine, -coarse_cos, -coarse_sin)
+    scale = window_of(time_index, points) * (1.0 / math.sqrt(points))
+    fine_cos, fine_sin = (part * scale for part in fine)
+    entry_value = first[:, None, :] * fine_cos[None, :, :] + second[:, None, :] * fine_sin[None, :, :]
+    table = entry_value.astype(jnp.bfloat16)
+    return lax.optimization_barrier(table.reshape(points, points))
 
 
 def synthesis_rows(first_bin, band_count):
-    sub = 8 if band_count % 8 == 0 else 1
+    sub = 16 if band_count % 16 == 0 else 1
     time_index = jnp.arange(NFFT, dtype=jnp.int32)[None, :]
-    coarse_bins = first_bin + sub * jnp.arange(band_count // sub, dtype=jnp.int32)[:, None]
+    row = jnp.arange(2 * (band_count // sub), dtype=jnp.int32)[:, None]
+    is_sine = row >= band_count // sub
+    coarse_bins = first_bin + sub * (row % (band_count // sub))
     coarse_cos, coarse_sin = angle_pair(coarse_bins * time_index, NFFT)
-    fine_cos, fine_sin = angle_pair(jnp.arange(sub, dtype=jnp.int32)[:, None] * time_index, NFFT)
-    first = jnp.stack([coarse_cos, -coarse_sin])
-    second = jnp.stack([-coarse_sin, -coarse_cos])
-    window = window_of(time_index, NFFT)[None, None, :, :]
-    entry_value = (
-        first[:, :, None, :] * fine_cos[None, None, :, :]
-        + second[:, :, None, :] * fine_sin[None, None, :, :]
-    )
-    return (entry_value * window * (1.0 / math.sqrt(BINS))).astype(jnp.bfloat16).reshape(
-        2, band_count, NFFT
-    )
+    scale = window_of(time_index, NFFT) * (1.0 / math.sqrt(BINS))
+    fine_cos, fine_sin = (
+        part * scale
+        for part in angle_pair(jnp.arange(sub, dtype=jnp.int32)[:, None] * time_index, NFFT)
+    )
+    first = jnp.where(is_sine, -coarse_sin, coarse_cos)
+    second = jnp.where(is_sine, -coarse_cos, -coarse_sin)
+    entry_value = first[:, None, :] * fine_cos[None, :, :] + second[:, None, :] * fine_sin[None, :, :]
+    table = entry_value.astype(jnp.bfloat16)
+    return lax.optimization_barrier(table.reshape(2, band_count, NFFT))
+
+
+def gathered_sum(value, axis):
+    size = lax.axis_size(axis)
+    here = lax.axis_index(axis)
+    devices = range(size)
+    slots = jnp.zeros((size,) + value.shape, value.dtype)
+    for distance in range(size):
+        if distance == 0:
+            arrived = value
+        else:
+            route = [(i, (i + distance) % size) for i in devices]
+            arrived = lax.ppermute(value, axis, route)
+        source = (here - distance) % size
+        slots = slots + jnp.where(
+            (jnp.arange(size, dtype=jnp.int32) == source).reshape((size,) + (1,) * value.ndim),
+            arrived[None],
+            0.0,
+        )
+    return jnp.sum(slots, axis=0)
 
 
 def spread_parts(quarters):
@@ -123,7 +143,7 @@
     beyond_list = [beyond_all[:, :, : 3 * points // 4] for points in sizes_list]
     lanes = min(128, NFFT // 4)
     fine_all = angle_pair(
-        jnp.arange(lanes, dtype=jnp.int32)[None, :] * jnp.arange(NFFT, dtype=jnp.int32)[:, None], NFFT
+        jnp.arange(lanes, dtype=jnp.int32)[:, None] * jnp.arange(NFFT, dtype=jnp.int32)[None, :], NFFT
     )
     saved = []
     spread_list = []
@@ -137,9 +157,9 @@
             [framed(est_wave, beyond_pair[0], stride), framed(clean, beyond_pair[1], stride)]
         )
         step = NFFT // points
-        table = analysis_table(points, (fine_all[0][::step], fine_all[1][::step]))
+        table = analysis_table(points, (fine_all[0][:, ::step], fine_all[1][:, ::step]))
         spectra_pair = jnp.einsum(
-            "ecfm,mj->ecfj", paired, table, preferred_element_type=jnp.float32
+            "ecfm,jm->ecfj", paired, table, preferred_element_type=jnp.float32
         )
         est_real = spectra_pair[0, :, :, :halfway]
         est_imag = spectra_pair[0, :, :, halfway:]
@@ -162,19 +182,9 @@
     spreads = jnp.stack(spread_list)
     energies = jnp.stack(energy_list)
     logterms = jnp.stack(logterm_list)
-    clip_index = lax.axis_index("clip")
-    clip_groups = lax.axis_size("clip")
-    stats = jnp.stack([spreads, energies, logterms])
-    slots = jnp.where(
-        (jnp.arange(clip_groups, dtype=jnp.int32) == clip_index)[:, None, None, None],
-        stats[None],
-        0.0,
-    )
-    slots = lax.psum(slots, ("clip", "seg"))
-    loss = jnp.sum(jnp.sqrt((slots[:, 0] + EPS_RATIO) / slots[:, 1]) + slots[:, 2]) / (
-        3 * clip_count * clip_groups
-    )
-    spreads, energies, logterms = slots[clip_index]
+    spreads, energies, logterms = lax.psum((spreads, energies, logterms), "seg")
+    own_loss = jnp.sum(jnp.sqrt((spreads + EPS_RATIO) / energies) + logterms)
+    loss = gathered_sum(own_loss, "clip") / (3 * clip_count * lax.axis_size("clip"))
     ratio_weight = 1.0 / jnp.sqrt((spreads + EPS_RATIO) * energies)
     gradient = jnp.zeros((clip_count, samples), jnp.float32)
     extras = []
@@ -192,7 +202,7 @@
             [grad_mag * est_real / est_mag, grad_mag * est_imag / est_mag], axis=2
         ).astype(jnp.bfloat16)
         grad_frames = jnp.einsum(
-            "cfj,mj->cfm", grad_x, table, preferred_element_type=jnp.float32
+            "cfj,jm->cfm", grad_x, table, preferred_element_type=jnp.float32
         )
         spread_back = spread_parts(grad_frames.reshape(clip_count, frame_count, 4, stride))
         gradient = gradient + spread_back[:, :frame_count].reshape(clip_count, samples)

time: 187 us -> 201 us (1.075); the launches traced: 186 us -> 197 us
  local copies, waits for them, and re-layouts: 42.8 us -> 81.8 us
  blocking collectives: 57.2 us -> 29.7 us
  matrix products: 25.5 us -> 15.4 us
  starting transfers between devices: 2.75 us -> 7.66 us
  other arithmetic: 40.5 us -> 43.5 us
    slice x4 -> x11, local copies, waits for them, and re-layouts: 5.72 us -> 68.1 us  [the longest x2 31.5 us: body(): fine_all[0][:, ::step]]
    psum x1, blocking collectives: 42.8 us -> 16.3 us  [body(): spreads, energies, logterms = lax.psum((spreads, energies, logterms), 'seg')]
    add x3 -> x0, local copies, waits for them, and re-layouts: 24.3 us -> none  [analysis_table(): first[:, :, None] * fine_cos[:, None, :]]
    add x4 -> x1, other arithmetic: 23.5 us -> 0.01 us  [synthesis_rows(): coarse_bins = first_bin + sub * (row % (band_count // sub))]
    dot_general x6, matrix products: 22 us -> 12.2 us  [the longest x3 7.7 us: body(): jnp.einsum('cfj,jm->cfm', grad_x, table, preferred_element_type=jnp.float32)]
    convert_element_type x0 -> x4, other arithmetic: none -> 7.97 us  [the longest x3 7.72 us: analysis_table(): table = entry_value.astype(jnp.bfloat16)]
    concatenate x6 -> x0, local copies, waits for them, and re-layouts: 6.38 us -> none  [the longest x3 3.19 us: analysis_table(): first = jnp.concatenate([coarse_cos, -coarse_sin], axis=1)]
    mul x3 -> x10, other arithmetic: 0.01 us -> 6.1 us  [the longest x3 5.35 us: analysis_table(): fine_cos, fine_sin = (part * scale for part in fine)]
  transfers between devices with their start and end apart: 3 -> 6, of which waited for: 1 -> 1; matrix products, arithmetic and copies ran while one was open for 36% -> 59% of each run, Pallas kernels for 0% -> 0%
where the time goes in v2:
time: 201 us; the launch traced here: 197 us
  local copies, waits for them, and re-layouts  81.8 us (41%)
  other arithmetic  43.5 us (22%)
  blocking collectives  29.7 us (15%)
  between operations  17.2 us (9%)
  matrix products  15.4 us (8%)
  starting transfers between devices  7.66 us (4%)
    slice x2, local copies, waits for them, and re-layouts, body(): fine_all[0][:, ::step]  31.5 us
    slice x2, local copies, waits for them, and re-layouts, body(): fine_all[1][:, ::step]  30 us
    psum x1, blocking collectives, body(): spreads, energies, logterms = lax.psum((spreads, energies, logterms), 'seg')  16.3 us
    all_gather x1, blocking collectives, body(): portion = lax.all_gather(grad_hops, 'seg', axis=1, tiled=True)  13.4 us
    convert_element_type x3, other arithmetic, analysis_table(): table = entry_value.astype(jnp.bfloat16)  7.72 us
    dot_general x3, matrix products, body(): jnp.einsum('cfj,jm->cfm', grad_x, table, preferred_element_type=jnp.float32)  7.7 us
    slice x3, local copies, waits for them, and re-layouts, spread_parts(): quarters[:, :, quarter]  6.61 us
    mul x3, other arithmetic, analysis_table(): fine_cos, fine_sin = (part * scale for part in fine)  5.35 us
  transfers between devices with their start and end apart: 6, of which 1 were waited for; matrix products, arithmetic and copies ran while one was open for 59% of the time, Pallas kernels for 0%

profile of v2, /device:TPU:0, one launch (start us, length us, event | category | flops | bytes accessed | tf_op | source)
XLA Modules:
  0.0 196.8 jit_solution(11377015044252097905)
XLA Ops:
  7.3 0.5 cosine_multiply_fusion
  7.8 1.1 fusion.85
  9.0 0.2 add_convert_fusion.2
  9.2 2.0 %convolution_bitcast_fusion = f32[195,4,2048]{2,0,1:T(8,128)S(1)} fusion(bf16[2,128,2048]{2,1,0:T(8,128)(2,1)S(1)} %bitcast.273, bf16[4,2,128,192]{2,3,1,0:T(8,128)(2,1)} %param.3), kind=kOutput, calls=%fused_computation.6 | convolution fusion | flops 817889280 | bytes 7831552 | tf_op jit(solution)/shard_map/crbf,rbm->fcm/dot_general | solution.py:117
  11.3 2.0 slice_add_fusion
  13.3 4.9 %fusion.39 = f32[128,2048]{1,0:T(8,128)} fusion(), kind=kLoop, calls=%fused_computation.56 | loop fusion | flops 3670016 | bytes 1048576 | tf_op jit(solution)/shard_map/cos | solution.py:25
  18.2 3.8 %fusion.38 = f32[128,2048]{1,0:T(8,128)S(1)} fusion(), kind=kLoop, calls=%fused_computation.55 | loop fusion | flops 3670016 | bytes 1048576 | tf_op jit(solution)/shard_map/sin | solution.py:25
  22.2 0.6 multiply_convert_fusion
  22.8 0.6 broadcast_compare_fusion
  23.4 0.6 broadcast_compare_fusion.2
  24.0 0.2 fusion.102
  24.2 0.2 fusion.95
  24.4 0.6 iota_add_fusion.2
  25.0 12.6 %slice.250 = f32[128,512]{1,0:T(8,128)S(1)} slice(f32[128,2048]{1,0:T(8,128)} %fusion.39), slice={[0:128:1], [0:2048:4]} | slice | bytes 524288 | tf_op jit(solution)/shard_map/slice | solution.py:160
  37.5 19.0 %slice.266 = f32[128,1024]{1,0:T(8,128)S(1)} slice(f32[128,2048]{1,0:T(8,128)} %fusion.39), slice={[0:128:1], [0:2048:2]} | slice | bytes 1048576 | tf_op jit(solution)/shard_map/slice | solution.py:160
  56.5 11.7 %slice.251 = f32[128,512]{1,0:T(8,128)S(1)} slice(f32[128,2048]{1,0:T(8,128)S(1)} %fusion.38), slice={[0:128:1], [0:2048:4]} | slice | bytes 524288 | tf_op jit(solution)/shard_map/slice | solution.py:160
  68.2 18.3 %slice.267 = f32[128,1024]{1,0:T(8,128)} slice(f32[128,2048]{1,0:T(8,128)S(1)} %fusion.38), slice={[0:128:1], [0:2048:2]} | slice | bytes 1048576 | tf_op jit(solution)/shard_map/slice | solution.py:160
  86.6 0.1 add_convert_fusion.3
  86.7 1.2 broadcast_multiply_fusion.3
  87.9 1.9 add_convert_fusion.1
  89.8 4.1 %broadcast_multiply_fusion.1 = (f32[128,2048]{1,0:T(8,128)S(1)}, f32[128,2048]{1,0:T(8,128)S(1)}) fusion(f32[2048]{0:T(1024)S(1)} %fusion.100), kind=kLoop, calls=%fused_computation.54 | loop fusion | flops 4194304 | bytes 2105344 | tf_op jit(solution)/shard_map/mul | solution.py:43
  94.0 5.7 %add_convert_fusion = bf16[16,128,2048]{2,1,0:T(8,128)(2,1)} fusion(f32[128,2048]{1,0:T(8,128)S(1)} %get-tuple-element.80, f32[16,2048]{1,0:T(8,128)S(1)} %get-tuple-element.105, f32[128,2048]{1,0:T(8,128)S(1)} %get-tuple-element.79, f32[16,2048]{1,0:T(8,128)S(1)} %get-tuple-element.106), kind=kLoop, calls=%fused_computation | loop fusion | flops 16777216 | bytes 10747904 | tf_op jit(solution)/shard_map/convert_element_type | solution.py:45
  99.6 1.1 copy.45
  100.7 0.2 fusion.62
  101.0 1.5 collective-permute-start
  102.6 1.5 collective-permute-done
  104.6 0.8 fusion.127
  105.5 0.8 fusion.126
  106.4 0.8 fusion.125
  107.6 0.6 fusion.25
  108.2 1.3 select_reduce_fusion.5
  109.7 1.0 fusion.11
  110.8 1.4 select_reduce_fusion.4
  112.3 0.9 slice-done.1
  113.2 2.9 %fusion = f32[2,4,24,2048]{3,2,1,0:T(8,128)S(1)} fusion(bf16[2048,2048]{1,0:T(8,128)(2,1)S(1)} %bitcast.268, bf16[1,4,24,2048]{3,2,1,0:T(8,128)(2,1)S(1)} %maximum_bitcast_fusion.11, bf16[1,4,24,2048]{3,2,1,0:T(8,128)(2,1)S(1)} %maximum_bitcast_fusion.10), kind=kOutput, calls=%fused_computation.1 | convolution fusion | flops 1611005952 | bytes 10747904 | tf_op jit(solution)/shard_map/ecfm,jm->ecfj/dot_general | solution.py:161
  116.1 1.4 select_reduce_fusion.3
  117.6 16.3 %all-reduce.17 = (f32[3,4]{1,0:T(4,128)}, f32[3,4]{1,0:T(4,128)}, f32[3,4]{1,0:T(4,128)}) all-reduce(f32[3,4]{1,0:T(4,128)S(1)} %pad_maximum_fusion.9, f32[3,4]{1,0:T(4,128)S(1)} %pad_maximum_fusion.8, f32[3,4]{1,0:T(4,128)S(1)} %pad_maximum_fusion.7), channel_id=1, replica_groups=mesh['clip'=4,'seg'=8] {'seg'}, use_global_device_ids=true, to_apply=%region_12.13 | all-reduce | flops 36 | bytes 288 | tf_op jit(solution)/shard_map/psum | solution.py:185
  134.0 1.4 multiply_rsqrt_fusion
  135.4 3.6 %collective-permute-start.3 = (f32[]{:T(128)}, f32[]{:T(128)}, u32[]{:S(2)}, u32[]{:S(2)}) collective-permute-start(f32[]{:T(128)} %get-tuple-element.82), channel_id=1, source_target_pairs={{0,24},{8,0},{16,8},{24,16},{1,25},{9,1},{17,9},{25,17},{2,26},{10... | collective-permute-start | bytes 20 | tf_op jit(solution)/shard_map/ppermute | solution.py:78
  139.0 1.2 collective-permute-start.1
  140.2 0.5 slice_bitcast_fusion.17
  140.7 1.8 divide_convert_fusion.1
  142.6 5.8 %fusion.2 = f32[4,24,2048]{2,1,0:T(8,128)} fusion(bf16[2048,2048]{1,0:T(8,128)(2,1)} %bitcast.265, bf16[4,24,1024]{2,1,0:T(8,128)(2,1)S(1)} %get-tuple-element.29, bf16[4,24,1024]{2,1,0:T(8,128)(2,1)S(1)} %get-tuple-element.28), kind=kOutput, calls=%fused_computation.3 | convolution fusion | flops 806092800 | bytes 9568256 | tf_op jit(solution)/shard_map/cfj,jm->cfm/dot_general | solution.py:204
  148.4 2.6 %reshape.796 = f32[4,24,4,512]{3,2,1,0:T(4,128)} reshape(f32[4,24,2048]{2,1,0:T(8,128)} %fusion.2) | data formatting | bytes 1572864 | tf_op jit(solution)/shard_map/reshape | solution.py:207
  151.0 3.0 %fusion.123 = (f32[4,24,1,512]{3,2,1,0:T(1,128)S(1)}, f32[4,24,1,512]{3,2,1,0:T(1,128)S(1)}, f32[4,24,1,512]{3,2,1,0:T(1,128)S(1)}, f32[4,24,1,512]{3,2,1,0:T(1,128)S(1)}) fusion(f32[4,24,4,512]{3,2,1,0:T(4,128)} %reshape.796), kind=kLoop, calls=%fused_computation.287 | loop fusion | bytes 1572864 | tf_op jit(solution)/shard_map/slice | solution.py:91
  154.0 0.1 copy.60
  154.2 0.1 copy.61
  154.6 0.8 pad_add_fusion
  155.4 0.6 pad_add_fusion.3
  156.0 0.5 divide_convert_fusion.3
  156.5 1.5 fusion.13
  158.0 2.4 %reshape.794 = f32[4,48,4,256]{3,2,1,0:T(4,128)} reshape(f32[4,48,1024]{2,1,0:T(8,128)} %fusion.13) | data formatting | bytes 1572864 | tf_op jit(solution)/shard_map/reshape | solution.py:207
  160.4 3.0 %fusion.122 = (f32[4,48,1,256]{3,2,1,0:T(1,128)S(1)}, f32[4,48,1,256]{3,2,1,0:T(1,128)S(1)}, f32[4,48,1,256]{3,2,1,0:T(1,128)S(1)}, f32[4,48,1,256]{3,2,1,0:T(1,128)S(1)}) fusion(f32[4,48,4,256]{3,2,1,0:T(4,128)} %reshape.794), kind=kLoop, calls=%fused_computation.286 | loop fusion | bytes 1572864 | tf_op jit(solution)/shard_map/slice | solution.py:91
  163.9 0.8 pad_add_fusion.1
  164.7 0.5 divide_convert_fusion.5
  165.2 0.4 fusion.36
  165.6 0.3 reshape.792
  165.9 0.6 fusion.121
  167.1 1.3 collective-permute-start.4
  168.5 3.3 %fusion.109 = f32[]{:T(128)} fusion(f32[]{:T(128)} %collective-permute-done.3, s32[]{:T(128)S(6)} %select_n.308, f32[]{:T(128)} %collective-permute-done.2, s32[]{:T(128)S(6)} %select_n.306, f32[]{:T(128)} %collective-permute-done.1, s32[]{:T(128)S(6)} %select_n.304, f32[]{:T(128)} %get-tuple-element.82, s32[]{:T(128)S(6)} %select_n.271), kind=kLoop, calls=%fused_computation.261 | loop fusion | flops 47 | bytes 36 | tf_op jit(solution)/shard_map/reduce_sum | solution.py:85
  172.6 13.4 %all_gather.3 = bf16[4,192,512]{2,1,0:T(8,128)(2,1)S(1)} all-gather(bf16[4,24,512]{2,1,0:T(8,128)(2,1)S(1)} %bitcast.301), channel_id=1, replica_groups=mesh['clip'=4,'seg'=8] {'seg'}, dimensions={1}, use_global_device_ids=true | all-gather | bytes 884736 | tf_op jit(solution)/shard_map/all_gather | solution.py:216
  186.0 0.5 pad_slice_fusion.2
  186.5 1.3 fusion.16
  187.8 0.8 copy.27
  (152 shorter events, 3.4 us)
Async XLA Ops:
  7.2 92.5 %reduce-scatter.2.cloned.1.call-start = ((), (), s32[]{:S(2)}) async-start(), calls=%async_computation.1 | async-start | bytes 1769472 | tf_op jit(solution)/shard_map/reduce_scatter | solution.py:120
  13.2 8.9 %copy-start.27 = (s32[4]{0:T(128)S(1)}, s32[4]{0:T(128)}, u32[]{:S(2)}) copy-start(s32[4]{0:T(128)} %param.5) | copy-start | bytes 52
  13.3 87.4 %copy-start.8 = (s32[12288]{0:T(1024)}, s32[12288]{0:T(1024)S(1)}, u32[]{:S(2)}) copy-start(s32[12288]{0:T(1024)S(1)} %iota_add_fusion) | copy-start | bytes 147460
  93.9 6.8 %copy-start.23 = (bf16[4,12288]{1,0:T(4,128)(2,1)S(1)}, bf16[4,12288]{1,0:T(4,128)(2,1)}, u32[]{:S(2)}) copy-start(bf16[4,12288]{1,0:T(4,128)(2,1)} %param.4) | copy-start | bytes 294916
  93.9 6.8 %copy-start.25 = (s32[4]{0:T(128)S(1)}, s32[4]{0:T(128)}, u32[]{:S(2)}) copy-start(s32[4]{0:T(128)} %get-tuple-element.100) | copy-start | bytes 52
  93.9 8.5 %copy-start.35 = (s32[4]{0:T(128)S(1)}, s32[4]{0:T(128)}, u32[]{:S(2)}) copy-start(s32[4]{0:T(128)} %get-tuple-element.99) | copy-start | bytes 52
  93.9 8.5 %copy-start.36 = (s32[48]{0:T(128)S(1)}, s32[48]{0:T(128)}, u32[]{:S(2)}) copy-start(s32[48]{0:T(128)} %iota_add_fusion.2) | copy-start | bytes 580
  101.0 3.1 %collective-permute-start = (bf16[2,4,1536]{2,1,0:T(4,128)(2,1)S(1)}, bf16[2,4,1536]{2,1,0:T(4,128)(2,1)S(1)}, u32[]{:S(2)}, u32[]{:S(2)}) collective-permute-start(bf16[2,4,1536]{2,1,0:T(4,128)(2,1)S(1)} %pad_maximum_fusion.6), channel_id=1, source_target_pairs={{1,0},{2,1},{3,2},{4,3},{5,4},{6,5},{7,6},{9,8},{10,9},{11,10},{12... | collective-permute-start | bytes 73736 | tf_op jit(solution)/shard_map/ppermute | solution.py:20
  102.6 8.2 %copy-start.33 = (pred[4,48]{1,0:T(4,128)(4,1)}, pred[4,48]{1,0:T(4,128)(4,1)S(1)}, u32[]{:S(2)}) copy-start(pred[4,48]{1,0:T(4,128)(4,1)S(1)} %broadcast_compare_fusion.1) | copy-start | bytes 580
  106.4 1.8 copy-start.30
  107.5 2.1 %copy-start.10 = (bf16[4,48,256]{2,1,0:T(8,128)(2,1)S(1)}, bf16[4,48,256]{2,1,0:T(8,128)(2,1)}, u32[]{:S(2)}) copy-start(bf16[4,48,256]{2,1,0:T(8,128)(2,1)} %get-tuple-element.57) | copy-start | bytes 294916
  107.5 2.1 %copy-start.11 = (bf16[4,48,256]{2,1,0:T(8,128)(2,1)S(1)}, bf16[4,48,256]{2,1,0:T(8,128)(2,1)}, u32[]{:S(2)}) copy-start(bf16[4,48,256]{2,1,0:T(8,128)(2,1)} %get-tuple-element.58) | copy-start | bytes 294916
  107.5 2.1 %copy-start.12 = (bf16[4,48,256]{2,1,0:T(8,128)(2,1)S(1)}, bf16[4,48,256]{2,1,0:T(8,128)(2,1)}, u32[]{:S(2)}) copy-start(bf16[4,48,256]{2,1,0:T(8,128)(2,1)} %get-tuple-element.59) | copy-start | bytes 294916
  107.5 2.1 %copy-start.13 = (bf16[4,48,256]{2,1,0:T(8,128)(2,1)S(1)}, bf16[4,48,256]{2,1,0:T(8,128)(2,1)}, u32[]{:S(2)}) copy-start(bf16[4,48,256]{2,1,0:T(8,128)(2,1)} %get-tuple-element.60) | copy-start | bytes 294916
  107.5 2.1 %copy-start.14 = (bf16[4,48,256]{2,1,0:T(8,128)(2,1)S(1)}, bf16[4,48,256]{2,1,0:T(8,128)(2,1)}, u32[]{:S(2)}) copy-start(bf16[4,48,256]{2,1,0:T(8,128)(2,1)} %get-tuple-element.53) | copy-start | bytes 294916
  107.5 2.1 %copy-start.15 = (bf16[4,48,256]{2,1,0:T(8,128)(2,1)S(1)}, bf16[4,48,256]{2,1,0:T(8,128)(2,1)}, u32[]{:S(2)}) copy-start(bf16[4,48,256]{2,1,0:T(8,128)(2,1)} %get-tuple-element.54) | copy-start | bytes 294916
  107.5 2.1 %copy-start.16 = (bf16[4,48,256]{2,1,0:T(8,128)(2,1)S(1)}, bf16[4,48,256]{2,1,0:T(8,128)(2,1)}, u32[]{:S(2)}) copy-start(bf16[4,48,256]{2,1,0:T(8,128)(2,1)} %get-tuple-element.55) | copy-start | bytes 294916
  107.5 2.1 %copy-start.17 = (bf16[4,48,256]{2,1,0:T(8,128)(2,1)S(1)}, bf16[4,48,256]{2,1,0:T(8,128)(2,1)}, u32[]{:S(2)}) copy-start(bf16[4,48,256]{2,1,0:T(8,128)(2,1)} %get-tuple-element.56) | copy-start | bytes 294916
  107.6 2.1 %copy-start = (bf16[8,128,1024]{2,1,0:T(8,128)(2,1)S(1)}, bf16[8,128,1024]{2,1,0:T(8,128)(2,1)}, u32[]{:S(2)}) copy-start(bf16[8,128,1024]{2,1,0:T(8,128)(2,1)} %add_convert_fusion.1) | copy-start | bytes 6291460
  107.6 4.7 %slice-start = ((s8[8388608]{0:T(1024)(128)(4,1)}), s8[4194304]{0:T(1024)(128)(4,1)S(1)}, s32[]{:S(2)}) async-start(s8[8388608]{0:T(1024)(128)(4,1)} %bitcast.266), calls=%async_computation.2 | async-start | bytes 8388608
  109.7 2.5 %copy-start.18 = (bf16[4,24,512]{2,1,0:T(8,128)(2,1)S(1)}, bf16[4,24,512]{2,1,0:T(8,128)(2,1)}, u32[]{:S(2)}) copy-start(bf16[4,24,512]{2,1,0:T(8,128)(2,1)} %get-tuple-element.49) | copy-start | bytes 294916
  109.7 2.5 %copy-start.19 = (bf16[4,24,512]{2,1,0:T(8,128)(2,1)S(1)}, bf16[4,24,512]{2,1,0:T(8,128)(2,1)}, u32[]{:S(2)}) copy-start(bf16[4,24,512]{2,1,0:T(8,128)(2,1)} %get-tuple-element.50) | copy-start | bytes 294916
  109.7 2.5 %copy-start.20 = (bf16[4,24,512]{2,1,0:T(8,128)(2,1)S(1)}, bf16[4,24,512]{2,1,0:T(8,128)(2,1)}, u32[]{:S(2)}) copy-start(bf16[4,24,512]{2,1,0:T(8,128)(2,1)} %get-tuple-element.51) | copy-start | bytes 294916
  109.7 2.5 %copy-start.21 = (bf16[4,24,512]{2,1,0:T(8,128)(2,1)S(1)}, bf16[4,24,512]{2,1,0:T(8,128)(2,1)}, u32[]{:S(2)}) copy-start(bf16[4,24,512]{2,1,0:T(8,128)(2,1)} %get-tuple-element.52) | copy-start | bytes 294916
  109.7 3.5 %slice-start.1 = ((s8[8388608]{0:T(1024)(128)(4,1)}), s8[4194304]{0:T(1024)(128)(4,1)S(1)}, s32[]{:S(2)}) async-start(s8[8388608]{0:T(1024)(128)(4,1)} %bitcast.266), calls=%async_computation.3 | async-start | bytes 8388608
  110.8 5.3 %copy-start.2 = (f32[2,4,48,1024]{3,2,1,0:T(8,128)}, f32[2,4,48,1024]{3,2,1,0:T(8,128)S(1)}, u32[]{:S(2)}) copy-start(f32[2,4,48,1024]{3,2,1,0:T(8,128)S(1)} %fusion.11) | copy-start | bytes 4718596
  113.2 2.9 %copy-start.32 = (pred[4,24]{1,0:T(4,128)(4,1)S(1)}, pred[4,24]{1,0:T(4,128)(4,1)}, u32[]{:S(2)}) copy-start(pred[4,24]{1,0:T(4,128)(4,1)} %broadcast_compare_fusion) | copy-start | bytes 292
  113.2 4.3 %copy-start.28 = (s32[4]{0:T(128)S(1)}, s32[4]{0:T(128)}, u32[]{:S(2)}) copy-start(s32[4]{0:T(128)} %param.5) | copy-start | bytes 52
  113.2 27.5 %copy-start.24 = (f32[4]{0:T(128)S(1)}, f32[4]{0:T(128)}, u32[]{:S(2)}) copy-start(f32[4]{0:T(128)} %get-tuple-element.98) | copy-start | bytes 52
  116.1 1.4 copy-start.4
  135.4 33.1 %collective-permute-start.3 = (f32[]{:T(128)}, f32[]{:T(128)}, u32[]{:S(2)}, u32[]{:S(2)}) collective-permute-start(f32[]{:T(128)} %get-tuple-element.82), channel_id=1, source_target_pairs={{0,24},{8,0},{16,8},{24,16},{1,25},{9,1},{17,9},{25,17},{2,26},{10... | collective-permute-start | bytes 20 | tf_op jit(solution)/shard_map/ppermute | solution.py:78
  139.0 29.5 %collective-permute-start.2 = (f32[]{:T(128)}, f32[]{:T(128)}, u32[]{:S(2)}, u32[]{:S(2)}) collective-permute-start(f32[]{:T(128)} %get-tuple-element.82), channel_id=1, source_target_pairs={{0,16},{8,24},{16,0},{24,8},{1,17},{9,25},{17,1},{25,9},{2,18},{10... | collective-permute-start | bytes 20 | tf_op jit(solution)/shard_map/ppermute | solution.py:78
  139.0 29.5 %collective-permute-start.1 = (f32[]{:T(128)}, f32[]{:T(128)}, u32[]{:S(2)}, u32[]{:S(2)}) collective-permute-start(f32[]{:T(128)} %get-tuple-element.82), channel_id=1, source_target_pairs={{0,8},{8,16},{16,24},{24,0},{1,9},{9,17},{17,25},{25,1},{2,10},{10... | collective-permute-start | bytes 20 | tf_op jit(solution)/shard_map/ppermute | solution.py:78
  148.4 7.6 %copy-start.34 = (pred[4,48]{1,0:T(4,128)(4,1)S(1)}, pred[4,48]{1,0:T(4,128)(4,1)}, u32[]{:S(2)}) copy-start(pred[4,48]{1,0:T(4,128)(4,1)} %copy-done.33) | copy-start | bytes 580
  151.0 5.0 %copy-start.3 = (f32[2,4,48,1024]{3,2,1,0:T(8,128)S(1)}, f32[2,4,48,1024]{3,2,1,0:T(8,128)}, u32[]{:S(2)}) copy-start(f32[2,4,48,1024]{3,2,1,0:T(8,128)} %copy-done.2) | copy-start | bytes 4718596
  151.0 5.0 %copy-start.6 = (f32[4,48,512]{2,1,0:T(8,128)S(1)}, f32[4,48,512]{2,1,0:T(8,128)}, u32[]{:S(2)}) copy-start(f32[4,48,512]{2,1,0:T(8,128)} %get-tuple-element.20) | copy-start | bytes 1179652
  151.0 5.0 %copy-start.7 = (f32[1,4,48,512]{3,2,1,0:T(8,128)S(1)}, f32[1,4,48,512]{3,2,1,0:T(8,128)}, u32[]{:S(2)}) copy-start(f32[1,4,48,512]{3,2,1,0:T(8,128)} %get-tuple-element.21) | copy-start | bytes 1179652
  151.0 5.5 %copy-start.1 = (bf16[8,128,1024]{2,1,0:T(8,128)(2,1)S(1)}, bf16[8,128,1024]{2,1,0:T(8,128)(2,1)}, u32[]{:S(2)}) copy-start(bf16[8,128,1024]{2,1,0:T(8,128)(2,1)} %add_convert_fusion.1) | copy-start | bytes 6291460
  160.4 4.3 %copy-start.5 = (f32[1,4,96,256]{3,2,1,0:T(8,128)S(1)}, f32[1,4,96,256]{3,2,1,0:T(8,128)}, u32[]{:S(2)}) copy-start(f32[1,4,96,256]{3,2,1,0:T(8,128)} %get-tuple-element.19) | copy-start | bytes 1179652
  160.4 4.3 %copy-start.29 = (f32[4]{0:T(128)S(1)}, f32[4]{0:T(128)}, u32[]{:S(2)}) copy-start(f32[4]{0:T(128)} %get-tuple-element.85) | copy-start | bytes 52
  160.4 4.3 %copy-start.31 = (pred[4,96]{1,0:T(4,128)(4,1)S(1)}, pred[4,96]{1,0:T(4,128)(4,1)}, u32[]{:S(2)}) copy-start(pred[4,96]{1,0:T(4,128)(4,1)} %broadcast_compare_fusion.2) | copy-start | bytes 1156
  165.6 1.5 copy-start.22
  165.9 6.6 %slice-start.2 = ((f32[4,27,512]{2,0,1:T(4,128)}), f32[4,24,512]{2,0,1:T(4,128)S(1)}, s32[]{:S(2)}) async-start(f32[4,27,512]{2,0,1:T(4,128)} %pad_add_fusion), calls=%async_computation.4 | async-start | bytes 393216 | tf_op jit(solution)/shard_map/slice | solution.py:208
  165.9 6.6 %slice-start.3 = ((f32[4,51,256]{2,0,1:T(4,128)}), f32[4,48,256]{2,0,1:T(4,128)S(1)}, s32[]{:S(2)}) async-start(f32[4,51,256]{2,0,1:T(4,128)} %pad_add_fusion.1), calls=%async_computation.5 | async-start | bytes 393216 | tf_op jit(solution)/shard_map/slice | solution.py:208
  165.9 6.6 %copy-start.9 = (s32[12288]{0:T(1024)S(1)}, s32[12288]{0:T(1024)}, u32[]{:S(2)}) copy-start(s32[12288]{0:T(1024)} %copy-done.8) | copy-start | bytes 147460
  165.9 6.6 %copy-start.26 = (s32[4]{0:T(128)S(1)}, s32[4]{0:T(128)}, u32[]{:S(2)}) copy-start(s32[4]{0:T(128)} %get-tuple-element.100) | copy-start | bytes 52
  167.1 5.4 %collective-permute-start.4 = (f32[4,1536]{1,0:T(4,128)S(1)}, f32[4,1536]{1,0:T(4,128)S(1)}, u32[]{:S(2)}, u32[]{:S(2)}) collective-permute-start(f32[4,1536]{1,0:T(4,128)S(1)} %add_add_fusion.3), channel_id=1, source_target_pairs={{0,1},{1,2},{2,3},{3,4},{4,5},{5,6},{6,7},{8,9},{9,10},{10,11},{11... | collective-permute-start | bytes 73736 | tf_op jit(solution)/shard_map/ppermute | solution.py:20
Sparse Core Ops, SparseCore 0:
  13.4 41.1 reduce-scatter.1

commit v3 on v2

--- a/solution.py
+++ b/solution.py
@@ -29,11 +29,12 @@
     return 0.5 - 0.5 * jnp.cos(time_index.astype(jnp.float32) * (2.0 * math.pi / points))
 
 
-def analysis_table(points, fine):
+def analysis_table(points):
     halfway = points // 2
-    lanes = fine[0].shape[0]
+    lanes = min(128, halfway)
     groups = halfway // lanes
     time_index = jnp.arange(points, dtype=jnp.int32)[None, :]
+    fine = angle_pair(jnp.arange(lanes, dtype=jnp.int32)[:, None] * time_index, points)
     row = jnp.arange(2 * groups, dtype=jnp.int32)[:, None]
     is_sine = row >= groups
     coarse_cos, coarse_sin = angle_pair(((row % groups) * lanes) * time_index, points)
@@ -141,10 +142,6 @@
     halo = 3 * NFFT // 4
     beyond_all = shifted(jnp.stack([est_wave[:, :halo], clean[:, :halo]]), "seg", -1)
     beyond_list = [beyond_all[:, :, : 3 * points // 4] for points in sizes_list]
-    lanes = min(128, NFFT // 4)
-    fine_all = angle_pair(
-        jnp.arange(lanes, dtype=jnp.int32)[:, None] * jnp.arange(NFFT, dtype=jnp.int32)[None, :], NFFT
-    )
     saved = []
     spread_list = []
     energy_list = []
@@ -156,8 +153,7 @@
         paired = jnp.stack(
             [framed(est_wave, beyond_pair[0], stride), framed(clean, beyond_pair[1], stride)]
         )
-        step = NFFT // points
-        table = analysis_table(points, (fine_all[0][:, ::step], fine_all[1][:, ::step]))
+        table = analysis_table(points)
         spectra_pair = jnp.einsum(
             "ecfm,jm->ecfj", paired, table, preferred_element_type=jnp.float32
         )

time: 201 us -> 150 us (0.75); the launches traced: 197 us -> 150 us
  local copies, waits for them, and re-layouts: 81.8 us -> 20.5 us
  waiting for transfers between devices: 1.5 us -> 26.5 us
  other arithmetic: 43.5 us -> 34.9 us
    slice x4 -> x0, local copies, waits for them, and re-layouts: 61.5 us -> none  [the longest x2 31.5 us: body(): fine_all[0][:, ::step]]
    reduce_scatter x1, waiting for transfers between devices: 0.01 us -> 25.2 us  [body(): lax.psum_scatter(sum((framed_sig[3 - quarter:3 - quarter + rows_here * la...]
    cos x1 -> x0, other arithmetic: 4.86 us -> none  [angle_pair(): return (jnp.cos(angles), jnp.sin(angles))]
    sin x1 -> x0, other arithmetic: 3.8 us -> none  [angle_pair(): return (jnp.cos(angles), jnp.sin(angles))]
    mul x3, other arithmetic: 5.35 us -> 7.44 us  [analysis_table(): fine_cos, fine_sin = (part * scale for part in fine)]
    unnamed x93 -> x85, local copies, waits for them, and re-layouts: 4.47 us -> 4.46 us
  transfers between devices with their start and end apart: 6 -> 6, of which waited for: 1 -> 2; matrix products, arithmetic and copies ran while one was open for 59% -> 31% of each run, Pallas kernels for 0% -> 0%
where the time goes in v3:
time: 150 us
  other arithmetic  34.9 us (23%)
  blocking collectives  28.4 us (19%)
  waiting for transfers between devices  26.5 us (18%)
  local copies, waits for them, and re-layouts  20.5 us (14%)
  between operations  16.9 us (11%)
  matrix products  15.4 us (10%)
  starting transfers between devices  7.07 us (5%)
    reduce_scatter x1, waiting for transfers between devices, body(): lax.psum_scatter(sum((framed_sig[3 - quarter:3 - quarter + rows_here * la...  25.2 us
    psum x1, blocking collectives, body(): spreads, energies, logterms = lax.psum((spreads, energies, logterms), 'seg')  14.5 us
    all_gather x1, blocking collectives, body(): portion = lax.all_gather(grad_hops, 'seg', axis=1, tiled=True)  13.9 us
    convert_element_type x3, other arithmetic, analysis_table(): table = entry_value.astype(jnp.bfloat16)  7.76 us
    dot_general x3, matrix products, body(): jnp.einsum('cfj,jm->cfm', grad_x, table, preferred_element_type=jnp.float32)  7.69 us
    mul x3, other arithmetic, analysis_table(): fine_cos, fine_sin = (part * scale for part in fine)  7.44 us
    slice x3, local copies, waits for them, and re-layouts, spread_parts(): quarters[:, :, quarter]  6.71 us
    reshape x3, local copies, waits for them, and re-layouts, body(): grad_frames.reshape(clip_count, frame_count, 4, stride)  5.21 us
  transfers between devices with their start and end apart: 6, of which 2 were waited for; matrix products, arithmetic and copies ran while one was open for 31% of the time, Pallas kernels for 0%

profile of v3, /device:TPU:0, one launch (start us, length us, event | category | flops | bytes accessed | tf_op | source)
XLA Modules:
  0.0 149.6 jit_solution(4565234268649374519)
XLA Ops:
  7.3 0.5 cosine_multiply_fusion.3
  7.8 1.1 fusion.95
  9.0 0.2 add_convert_fusion.2
  9.2 2.0 %convolution_bitcast_fusion = f32[195,4,2048]{2,0,1:T(8,128)S(1)} fusion(bf16[2,128,2048]{2,1,0:T(8,128)(2,1)S(1)} %bitcast.273, bf16[4,2,128,192]{2,3,1,0:T(8,128)(2,1)} %param.3), kind=kOutput, calls=%fused_computation.6 | convolution fusion | flops 817889280 | bytes 7831552 | tf_op jit(solution)/shard_map/crbf,rbm->fcm/dot_general | solution.py:118
  11.3 2.0 %slice_add_fusion = f32[192,4,512]{2,0,1:T(8,128)} fusion(f32[195,4,2048]{2,0,1:T(8,128)S(1)} %convolution_bitcast_fusion), kind=kLoop, calls=%fused_computation.20 | loop fusion | flops 1179648 | bytes 7864320 | tf_op jit(solution)/shard_map/add | solution.py:122
  13.7 0.2 fusion.112
  13.9 0.2 fusion.105
  14.1 1.1 cosine_multiply_fusion.2
  15.2 2.1 %cosine_multiply_fusion.1 = (f32[128,1024]{1,0:T(8,128)S(1)}, f32[128,1024]{1,0:T(8,128)S(1)}) fusion(f32[1024]{0:T(1024)S(1)} %subtract_multiply_fusion), kind=kLoop, calls=%fused_computation.62 | loop fusion | flops 2097152 | bytes 1052672 | tf_op jit(solution)/shard_map/mul | solution.py:44
  17.3 0.1 add_convert_fusion.3
  17.4 1.9 %add_convert_fusion.1 = bf16[8,128,1024]{2,1,0:T(8,128)(2,1)} fusion(f32[128,1024]{1,0:T(8,128)S(1)} %get-tuple-element.84, f32[8,1024]{1,0:T(8,128)S(1)} %get-tuple-element.93, f32[128,1024]{1,0:T(8,128)S(1)} %get-tuple-element.83, f32[8,1024]{1,0:T(8,128)S(1)} %get-tuple-element.92), kind=kLoop, calls=%fused_computation.5 | loop fusion | flops 4194304 | bytes 3211264 | tf_op jit(solution)/shard_map/convert_element_type | solution.py:46
  19.3 4.3 %cosine_multiply_fusion = (f32[128,2048]{1,0:T(8,128)S(1)}, f32[128,2048]{1,0:T(8,128)S(1)}) fusion(f32[2048]{0:T(1024)S(1)} %fusion.110), kind=kLoop, calls=%fused_computation.34 | loop fusion | flops 4194304 | bytes 2105344 | tf_op jit(solution)/shard_map/mul | solution.py:44
  23.7 5.7 %add_convert_fusion = bf16[16,128,2048]{2,1,0:T(8,128)(2,1)} fusion(f32[128,2048]{1,0:T(8,128)S(1)} %get-tuple-element.80, f32[16,2048]{1,0:T(8,128)S(1)} %get-tuple-element.105, f32[128,2048]{1,0:T(8,128)S(1)} %get-tuple-element.79, f32[16,2048]{1,0:T(8,128)S(1)} %get-tuple-element.106), kind=kLoop, calls=%fused_computation | loop fusion | flops 16777216 | bytes 10747904 | tf_op jit(solution)/shard_map/convert_element_type | solution.py:46
  29.4 25.2 %reduce-scatter.2.cloned.1.call-done = f32[24,4,512]{2,0,1:T(8,128)} async-done(((f32[192,4,512]{2,0,1:T(8,128)}), f32[24,4,512]{2,0,1:T(8,128)}) %reduce-scatter.2.cloned.1.call-update) | async-done | bytes 196624 | tf_op jit(solution)/shard_map/reduce_scatter | solution.py:121
  54.6 1.1 copy.45
  55.7 0.2 fusion.72
  55.9 1.3 collective-permute-start
  57.2 0.6 broadcast_compare_fusion.1
  57.8 1.2 collective-permute-done
  59.5 0.8 fusion.137
  60.4 0.8 fusion.136
  61.4 0.8 fusion.135
  62.6 0.6 fusion.25
  63.2 1.3 select_reduce_fusion.5
  64.7 1.0 fusion.11
  65.8 1.4 select_reduce_fusion.4
  67.3 0.9 slice-done.1
  68.2 2.9 %fusion = f32[2,4,24,2048]{3,2,1,0:T(8,128)S(1)} fusion(bf16[2048,2048]{1,0:T(8,128)(2,1)S(1)} %bitcast.268, bf16[1,4,24,2048]{3,2,1,0:T(8,128)(2,1)S(1)} %maximum_bitcast_fusion.11, bf16[1,4,24,2048]{3,2,1,0:T(8,128)(2,1)S(1)} %maximum_bitcast_fusion.10), kind=kOutput, calls=%fused_computation.1 | convolution fusion | flops 1611005952 | bytes 10747904 | tf_op jit(solution)/shard_map/ecfm,jm->ecfj/dot_general | solution.py:157
  71.1 1.4 select_reduce_fusion.3
  72.6 14.5 %all-reduce.17 = (f32[3,4]{1,0:T(4,128)}, f32[3,4]{1,0:T(4,128)}, f32[3,4]{1,0:T(4,128)}) all-reduce(f32[3,4]{1,0:T(4,128)S(1)} %pad_maximum_fusion.9, f32[3,4]{1,0:T(4,128)S(1)} %pad_maximum_fusion.8, f32[3,4]{1,0:T(4,128)S(1)} %pad_maximum_fusion.7), channel_id=1, replica_groups=mesh['clip'=4,'seg'=8] {'seg'}, use_global_device_ids=true, to_apply=%region_12.13 | all-reduce | flops 36 | bytes 288 | tf_op jit(solution)/shard_map/psum | solution.py:181
  87.0 1.3 multiply_rsqrt_fusion
  88.4 3.4 %collective-permute-start.3 = (f32[]{:T(128)}, f32[]{:T(128)}, u32[]{:S(2)}, u32[]{:S(2)}) collective-permute-start(f32[]{:T(128)} %get-tuple-element.82), channel_id=1, source_target_pairs={{0,24},{8,0},{16,8},{24,16},{1,25},{9,1},{17,9},{25,17},{2,26},{10... | collective-permute-start | bytes 20 | tf_op jit(solution)/shard_map/ppermute | solution.py:79
  91.7 1.1 collective-permute-start.1
  92.8 0.6 slice_bitcast_fusion.17
  93.4 1.8 %divide_convert_fusion.1 = (bf16[4,24,1024]{2,1,0:T(8,128)(2,1)S(1)}, bf16[4,24,1024]{2,1,0:T(8,128)(2,1)S(1)}) fusion(f32[2,4,24,2048]{3,2,1,0:T(8,128)} %copy-done.4, f32[4,24,1024]{2,1,0:T(8,128)} %get-tuple-element.22, f32[1,4,24,1024]{3,2,1,0:T(8,128)} %get-tuple-element.23, f32[4]{0:T(128)S(1)} %get-tuple-element.98, f32[4]{0:T(128)S(1)} %get-tuple-element.86, ...), kind=kLoop, calls=%fused_computation.116 | loop fusion | flops 1671168 | bytes 1966208 | tf_op jit(solution)/shard_map/convert
  95.2 5.8 %fusion.2 = f32[4,24,2048]{2,1,0:T(8,128)} fusion(bf16[2048,2048]{1,0:T(8,128)(2,1)} %bitcast.265, bf16[4,24,1024]{2,1,0:T(8,128)(2,1)S(1)} %get-tuple-element.29, bf16[4,24,1024]{2,1,0:T(8,128)(2,1)S(1)} %get-tuple-element.28), kind=kOutput, calls=%fused_computation.3 | convolution fusion | flops 806092800 | bytes 9568256 | tf_op jit(solution)/shard_map/cfj,jm->cfm/dot_general | solution.py:200
  101.0 2.6 %reshape.924 = f32[4,24,4,512]{3,2,1,0:T(4,128)} reshape(f32[4,24,2048]{2,1,0:T(8,128)} %fusion.2) | data formatting | bytes 1572864 | tf_op jit(solution)/shard_map/reshape | solution.py:203
  103.6 3.2 %fusion.133 = (f32[4,24,1,512]{3,2,1,0:T(1,128)S(1)}, f32[4,24,1,512]{3,2,1,0:T(1,128)S(1)}, f32[4,24,1,512]{3,2,1,0:T(1,128)S(1)}, f32[4,24,1,512]{3,2,1,0:T(1,128)S(1)}) fusion(f32[4,24,4,512]{3,2,1,0:T(4,128)} %reshape.924), kind=kLoop, calls=%fused_computation.303 | loop fusion | bytes 1572864 | tf_op jit(solution)/shard_map/slice | solution.py:92
  106.8 0.1 copy.60
  106.9 0.1 copy.61
  107.1 0.1 copy.62
  107.2 0.1 copy.63
  107.3 0.8 pad_add_fusion
  108.1 0.6 pad_add_fusion.3
  108.7 0.5 divide_convert_fusion.3
  109.3 1.5 %fusion.13 = f32[4,48,1024]{2,1,0:T(8,128)} fusion(bf16[1024,1024]{1,0:T(8,128)(2,1)S(1)} %bitcast.270, bf16[4,48,512]{2,1,0:T(8,128)(2,1)S(1)} %get-tuple-element.27, bf16[4,48,512]{2,1,0:T(8,128)(2,1)S(1)} %get-tuple-element.26), kind=kOutput, calls=%fused_computation.17 | convolution fusion | flops 403439616 | bytes 3276800 | tf_op jit(solution)/shard_map/cfj,jm->cfm/dot_general | solution.py:200
  110.8 2.4 %reshape.922 = f32[4,48,4,256]{3,2,1,0:T(4,128)} reshape(f32[4,48,1024]{2,1,0:T(8,128)} %fusion.13) | data formatting | bytes 1572864 | tf_op jit(solution)/shard_map/reshape | solution.py:203
  113.1 3.0 %fusion.132 = (f32[4,48,1,256]{3,2,1,0:T(1,128)S(1)}, f32[4,48,1,256]{3,2,1,0:T(1,128)S(1)}, f32[4,48,1,256]{3,2,1,0:T(1,128)S(1)}, f32[4,48,1,256]{3,2,1,0:T(1,128)S(1)}) fusion(f32[4,48,4,256]{3,2,1,0:T(4,128)} %reshape.922), kind=kLoop, calls=%fused_computation.302 | loop fusion | bytes 1572864 | tf_op jit(solution)/shard_map/slice | solution.py:92
  116.1 0.1 copy.64
  116.3 0.1 copy.65
  116.4 0.1 copy.66
  116.6 0.1 copy.67
  116.7 0.8 pad_add_fusion.1
  117.5 0.5 divide_convert_fusion.5
  118.0 0.4 fusion.39
  118.4 0.3 reshape.920
  118.7 0.6 fusion.131
  119.2 0.1 copy.68
  119.8 1.3 collective-permute-start.4
  121.3 3.0 %fusion.119 = f32[]{:T(128)} fusion(f32[]{:T(128)} %collective-permute-done.3, s32[]{:T(128)S(6)} %select_n.332, f32[]{:T(128)} %collective-permute-done.2, s32[]{:T(128)S(6)} %select_n.330, f32[]{:T(128)} %collective-permute-done.1, s32[]{:T(128)S(6)} %select_n.328, f32[]{:T(128)} %get-tuple-element.82, s32[]{:T(128)S(6)} %select_n.293), kind=kLoop, calls=%fused_computation.277 | loop fusion | flops 47 | bytes 36 | tf_op jit(solution)/shard_map/reduce_sum | solution.py:86
  125.2 13.9 %all_gather.3 = bf16[4,192,512]{2,1,0:T(8,128)(2,1)S(1)} all-gather(bf16[4,24,512]{2,1,0:T(8,128)(2,1)S(1)} %bitcast.301), channel_id=1, replica_groups=mesh['clip'=4,'seg'=8] {'seg'}, dimensions={1}, use_global_device_ids=true | all-gather | bytes 884736 | tf_op jit(solution)/shard_map/all_gather | solution.py:212
  139.1 0.5 pad_slice_fusion.2
  139.6 1.3 fusion.16
  140.8 0.8 copy.27
  (138 shorter events, 2.5 us)
Async XLA Ops:
  7.2 47.4 %reduce-scatter.2.cloned.1.call-start = ((), (), s32[]{:S(2)}) async-start(), calls=%async_computation.1 | async-start | bytes 1769472 | tf_op jit(solution)/shard_map/reduce_scatter | solution.py:121
  11.3 2.3 %copy-start.26 = (s32[4]{0:T(128)S(1)}, s32[4]{0:T(128)}, u32[]{:S(2)}) copy-start(s32[4]{0:T(128)} %param.5) | copy-start | bytes 52
  13.3 42.4 %copy-start.8 = (s32[12288]{0:T(1024)}, s32[12288]{0:T(1024)S(1)}, u32[]{:S(2)}) copy-start(s32[12288]{0:T(1024)S(1)} %iota_add_fusion) | copy-start | bytes 147460
  13.5 42.1 %copy-start.24 = (s32[4]{0:T(128)}, s32[4]{0:T(128)S(1)}, u32[]{:S(2)}) copy-start(s32[4]{0:T(128)S(1)} %get-tuple-element.100) | copy-start | bytes 52
  13.7 57.4 %copy-start.30 = (pred[4,24]{1,0:T(4,128)(4,1)}, pred[4,24]{1,0:T(4,128)(4,1)S(1)}, u32[]{:S(2)}) copy-start(pred[4,24]{1,0:T(4,128)(4,1)S(1)} %broadcast_compare_fusion) | copy-start | bytes 292
  13.7 49.5 %copy-start.28 = (pred[4,96]{1,0:T(4,128)(4,1)}, pred[4,96]{1,0:T(4,128)(4,1)S(1)}, u32[]{:S(2)}) copy-start(pred[4,96]{1,0:T(4,128)(4,1)S(1)} %broadcast_compare_fusion.2) | copy-start | bytes 1156
  23.7 32.0 %copy-start.23 = (bf16[4,12288]{1,0:T(4,128)(2,1)S(1)}, bf16[4,12288]{1,0:T(4,128)(2,1)}, u32[]{:S(2)}) copy-start(bf16[4,12288]{1,0:T(4,128)(2,1)} %param.4) | copy-start | bytes 294916
  55.9 3.1 %collective-permute-start = (bf16[2,4,1536]{2,1,0:T(4,128)(2,1)S(1)}, bf16[2,4,1536]{2,1,0:T(4,128)(2,1)S(1)}, u32[]{:S(2)}, u32[]{:S(2)}) collective-permute-start(bf16[2,4,1536]{2,1,0:T(4,128)(2,1)S(1)} %pad_maximum_fusion.6), channel_id=1, source_target_pairs={{1,0},{2,1},{3,2},{4,3},{5,4},{6,5},{7,6},{9,8},{10,9},{11,10},{12... | collective-permute-start | bytes 73736 | tf_op jit(solution)/shard_map/ppermute | solution.py:20
  62.4 2.1 %copy-start.10 = (bf16[4,48,256]{2,1,0:T(8,128)(2,1)S(1)}, bf16[4,48,256]{2,1,0:T(8,128)(2,1)}, u32[]{:S(2)}) copy-start(bf16[4,48,256]{2,1,0:T(8,128)(2,1)} %get-tuple-element.57) | copy-start | bytes 294916
  62.4 2.1 %copy-start.11 = (bf16[4,48,256]{2,1,0:T(8,128)(2,1)S(1)}, bf16[4,48,256]{2,1,0:T(8,128)(2,1)}, u32[]{:S(2)}) copy-start(bf16[4,48,256]{2,1,0:T(8,128)(2,1)} %get-tuple-element.58) | copy-start | bytes 294916
  62.4 2.1 %copy-start.12 = (bf16[4,48,256]{2,1,0:T(8,128)(2,1)S(1)}, bf16[4,48,256]{2,1,0:T(8,128)(2,1)}, u32[]{:S(2)}) copy-start(bf16[4,48,256]{2,1,0:T(8,128)(2,1)} %get-tuple-element.59) | copy-start | bytes 294916
  62.4 2.1 %copy-start.13 = (bf16[4,48,256]{2,1,0:T(8,128)(2,1)S(1)}, bf16[4,48,256]{2,1,0:T(8,128)(2,1)}, u32[]{:S(2)}) copy-start(bf16[4,48,256]{2,1,0:T(8,128)(2,1)} %get-tuple-element.60) | copy-start | bytes 294916
  62.5 2.1 %copy-start.14 = (bf16[4,48,256]{2,1,0:T(8,128)(2,1)S(1)}, bf16[4,48,256]{2,1,0:T(8,128)(2,1)}, u32[]{:S(2)}) copy-start(bf16[4,48,256]{2,1,0:T(8,128)(2,1)} %get-tuple-element.53) | copy-start | bytes 294916
  62.5 2.1 %copy-start.15 = (bf16[4,48,256]{2,1,0:T(8,128)(2,1)S(1)}, bf16[4,48,256]{2,1,0:T(8,128)(2,1)}, u32[]{:S(2)}) copy-start(bf16[4,48,256]{2,1,0:T(8,128)(2,1)} %get-tuple-element.54) | copy-start | bytes 294916
  62.5 2.1 %copy-start.16 = (bf16[4,48,256]{2,1,0:T(8,128)(2,1)S(1)}, bf16[4,48,256]{2,1,0:T(8,128)(2,1)}, u32[]{:S(2)}) copy-start(bf16[4,48,256]{2,1,0:T(8,128)(2,1)} %get-tuple-element.55) | copy-start | bytes 294916
  62.5 2.1 %copy-start.17 = (bf16[4,48,256]{2,1,0:T(8,128)(2,1)S(1)}, bf16[4,48,256]{2,1,0:T(8,128)(2,1)}, u32[]{:S(2)}) copy-start(bf16[4,48,256]{2,1,0:T(8,128)(2,1)} %get-tuple-element.56) | copy-start | bytes 294916
  62.5 2.1 %copy-start = (bf16[8,128,1024]{2,1,0:T(8,128)(2,1)S(1)}, bf16[8,128,1024]{2,1,0:T(8,128)(2,1)}, u32[]{:S(2)}) copy-start(bf16[8,128,1024]{2,1,0:T(8,128)(2,1)} %add_convert_fusion.1) | copy-start | bytes 6291460
  62.6 4.7 %slice-start = ((s8[8388608]{0:T(1024)(128)(4,1)}), s8[4194304]{0:T(1024)(128)(4,1)S(1)}, s32[]{:S(2)}) async-start(s8[8388608]{0:T(1024)(128)(4,1)} %bitcast.266), calls=%async_computation.2 | async-start | bytes 8388608
  64.6 1.2 copy-start.31
  64.7 2.5 %copy-start.18 = (bf16[4,24,512]{2,1,0:T(8,128)(2,1)S(1)}, bf16[4,24,512]{2,1,0:T(8,128)(2,1)}, u32[]{:S(2)}) copy-start(bf16[4,24,512]{2,1,0:T(8,128)(2,1)} %get-tuple-element.49) | copy-start | bytes 294916
  64.7 2.5 %copy-start.19 = (bf16[4,24,512]{2,1,0:T(8,128)(2,1)S(1)}, bf16[4,24,512]{2,1,0:T(8,128)(2,1)}, u32[]{:S(2)}) copy-start(bf16[4,24,512]{2,1,0:T(8,128)(2,1)} %get-tuple-element.50) | copy-start | bytes 294916
  64.7 2.5 %copy-start.20 = (bf16[4,24,512]{2,1,0:T(8,128)(2,1)S(1)}, bf16[4,24,512]{2,1,0:T(8,128)(2,1)}, u32[]{:S(2)}) copy-start(bf16[4,24,512]{2,1,0:T(8,128)(2,1)} %get-tuple-element.51) | copy-start | bytes 294916
  64.7 2.5 %copy-start.21 = (bf16[4,24,512]{2,1,0:T(8,128)(2,1)S(1)}, bf16[4,24,512]{2,1,0:T(8,128)(2,1)}, u32[]{:S(2)}) copy-start(bf16[4,24,512]{2,1,0:T(8,128)(2,1)} %get-tuple-element.52) | copy-start | bytes 294916
  64.7 3.5 %slice-start.1 = ((s8[8388608]{0:T(1024)(128)(4,1)}), s8[4194304]{0:T(1024)(128)(4,1)S(1)}, s32[]{:S(2)}) async-start(s8[8388608]{0:T(1024)(128)(4,1)} %bitcast.266), calls=%async_computation.3 | async-start | bytes 8388608
  65.7 5.3 %copy-start.2 = (f32[2,4,48,1024]{3,2,1,0:T(8,128)}, f32[2,4,48,1024]{3,2,1,0:T(8,128)S(1)}, u32[]{:S(2)}) copy-start(f32[2,4,48,1024]{3,2,1,0:T(8,128)S(1)} %fusion.11) | copy-start | bytes 4718596
  71.1 1.4 copy-start.4
  88.4 32.9 %collective-permute-start.3 = (f32[]{:T(128)}, f32[]{:T(128)}, u32[]{:S(2)}, u32[]{:S(2)}) collective-permute-start(f32[]{:T(128)} %get-tuple-element.82), channel_id=1, source_target_pairs={{0,24},{8,0},{16,8},{24,16},{1,25},{9,1},{17,9},{25,17},{2,26},{10... | collective-permute-start | bytes 20 | tf_op jit(solution)/shard_map/ppermute | solution.py:79
  91.7 29.5 %collective-permute-start.2 = (f32[]{:T(128)}, f32[]{:T(128)}, u32[]{:S(2)}, u32[]{:S(2)}) collective-permute-start(f32[]{:T(128)} %get-tuple-element.82), channel_id=1, source_target_pairs={{0,16},{8,24},{16,0},{24,8},{1,17},{9,25},{17,1},{25,9},{2,18},{10... | collective-permute-start | bytes 20 | tf_op jit(solution)/shard_map/ppermute | solution.py:79
  91.7 29.5 %collective-permute-start.1 = (f32[]{:T(128)}, f32[]{:T(128)}, u32[]{:S(2)}, u32[]{:S(2)}) collective-permute-start(f32[]{:T(128)} %get-tuple-element.82), channel_id=1, source_target_pairs={{0,8},{8,16},{16,24},{24,0},{1,9},{9,17},{17,25},{25,1},{2,10},{10... | collective-permute-start | bytes 20 | tf_op jit(solution)/shard_map/ppermute | solution.py:79
  101.0 7.7 %copy-start.32 = (pred[4,48]{1,0:T(4,128)(4,1)S(1)}, pred[4,48]{1,0:T(4,128)(4,1)}, u32[]{:S(2)}) copy-start(pred[4,48]{1,0:T(4,128)(4,1)} %broadcast_compare_fusion.1) | copy-start | bytes 580
  103.6 5.1 %copy-start.3 = (f32[2,4,48,1024]{3,2,1,0:T(8,128)S(1)}, f32[2,4,48,1024]{3,2,1,0:T(8,128)}, u32[]{:S(2)}) copy-start(f32[2,4,48,1024]{3,2,1,0:T(8,128)} %copy-done.2) | copy-start | bytes 4718596
  103.6 5.1 %copy-start.6 = (f32[4,48,512]{2,1,0:T(8,128)S(1)}, f32[4,48,512]{2,1,0:T(8,128)}, u32[]{:S(2)}) copy-start(f32[4,48,512]{2,1,0:T(8,128)} %get-tuple-element.20) | copy-start | bytes 1179652
  103.6 5.1 %copy-start.7 = (f32[1,4,48,512]{3,2,1,0:T(8,128)S(1)}, f32[1,4,48,512]{3,2,1,0:T(8,128)}, u32[]{:S(2)}) copy-start(f32[1,4,48,512]{3,2,1,0:T(8,128)} %get-tuple-element.21) | copy-start | bytes 1179652
  103.6 5.6 %copy-start.1 = (bf16[8,128,1024]{2,1,0:T(8,128)(2,1)S(1)}, bf16[8,128,1024]{2,1,0:T(8,128)(2,1)}, u32[]{:S(2)}) copy-start(bf16[8,128,1024]{2,1,0:T(8,128)(2,1)} %add_convert_fusion.1) | copy-start | bytes 6291460
  113.1 4.3 %copy-start.5 = (f32[1,4,96,256]{3,2,1,0:T(8,128)S(1)}, f32[1,4,96,256]{3,2,1,0:T(8,128)}, u32[]{:S(2)}) copy-start(f32[1,4,96,256]{3,2,1,0:T(8,128)} %get-tuple-element.19) | copy-start | bytes 1179652
  113.1 4.3 %copy-start.27 = (f32[4]{0:T(128)S(1)}, f32[4]{0:T(128)}, u32[]{:S(2)}) copy-start(f32[4]{0:T(128)} %get-tuple-element.85) | copy-start | bytes 52
  113.1 4.3 %copy-start.29 = (pred[4,96]{1,0:T(4,128)(4,1)S(1)}, pred[4,96]{1,0:T(4,128)(4,1)}, u32[]{:S(2)}) copy-start(pred[4,96]{1,0:T(4,128)(4,1)} %copy-done.28) | copy-start | bytes 1156
  118.3 1.5 copy-start.22
  118.6 6.3 %slice-start.2 = ((f32[4,27,512]{2,0,1:T(4,128)}), f32[4,24,512]{2,0,1:T(4,128)S(1)}, s32[]{:S(2)}) async-start(f32[4,27,512]{2,0,1:T(4,128)} %pad_add_fusion), calls=%async_computation.4 | async-start | bytes 393216 | tf_op jit(solution)/shard_map/slice | solution.py:204
  118.6 6.3 %slice-start.3 = ((f32[4,51,256]{2,0,1:T(4,128)}), f32[4,48,256]{2,0,1:T(4,128)S(1)}, s32[]{:S(2)}) async-start(f32[4,51,256]{2,0,1:T(4,128)} %pad_add_fusion.1), calls=%async_computation.5 | async-start | bytes 393216 | tf_op jit(solution)/shard_map/slice | solution.py:204
  118.7 6.3 %copy-start.9 = (s32[12288]{0:T(1024)S(1)}, s32[12288]{0:T(1024)}, u32[]{:S(2)}) copy-start(s32[12288]{0:T(1024)} %copy-done.8) | copy-start | bytes 147460
  118.7 6.3 %copy-start.25 = (s32[4]{0:T(128)S(1)}, s32[4]{0:T(128)}, u32[]{:S(2)}) copy-start(s32[4]{0:T(128)} %copy-done.24) | copy-start | bytes 52
  119.8 5.1 %collective-permute-start.4 = (f32[4,1536]{1,0:T(4,128)S(1)}, f32[4,1536]{1,0:T(4,128)S(1)}, u32[]{:S(2)}, u32[]{:S(2)}) collective-permute-start(f32[4,1536]{1,0:T(4,128)S(1)} %add_add_fusion.3), channel_id=1, source_target_pairs={{0,1},{1,2},{2,3},{3,4},{4,5},{5,6},{6,7},{8,9},{9,10},{10,11},{11... | collective-permute-start | bytes 73736 | tf_op jit(solution)/shard_map/ppermute | solution.py:20
Sparse Core Ops, SparseCore 0:
  13.4 41.1 reduce-scatter.1

commit v4 on v3

--- a/solution.py
+++ b/solution.py
@@ -114,6 +114,10 @@
     seg_index = lax.axis_index("seg")
     start_sample = seg_index * samples
     local_table = synthesis_rows(seg_index * band_count, band_count)
+    sample_index = start_sample + jnp.arange(samples, dtype=jnp.int32)
+    inside = sample_index[None, :] < (lengths * HOP)[:, None]
+    clean = jnp.where(inside, target, jnp.zeros_like(target))
+    clean, local_table = lax.optimization_barrier((clean, local_table))
     padded_spec = jnp.pad(spectra, ((0, 0), (0, 0), (0, 0), (3, 0)))
     framed_sig = jnp.einsum(
         "crbf,rbm->fcm", padded_spec, local_table, preferred_element_type=jnp.float32
@@ -134,33 +138,36 @@
         tiled=True,
     )
     estimate = jnp.transpose(hop_rows, (1, 0, 2)).reshape(clip_count, samples)
-    sample_index = start_sample + jnp.arange(samples, dtype=jnp.int32)
-    inside = sample_index[None, :] < (lengths * HOP)[:, None]
     est_wave = jnp.where(inside, estimate, 0.0).astype(jnp.bfloat16)
-    clean = jnp.where(inside, target, jnp.zeros_like(target))
     sizes_list = (NFFT // 4, NFFT // 2, NFFT)
     halo = 3 * NFFT // 4
-    beyond_all = shifted(jnp.stack([est_wave[:, :halo], clean[:, :halo]]), "seg", -1)
-    beyond_list = [beyond_all[:, :, : 3 * points // 4] for points in sizes_list]
+    clean_beyond = shifted(clean[:, :halo], "seg", -1)
+    est_beyond = shifted(est_wave[:, :halo], "seg", -1)
     saved = []
     spread_list = []
     energy_list = []
     logterm_list = []
-    for points, beyond_pair in zip(sizes_list, beyond_list):
+    for points in sizes_list:
         stride = points // 4
         halfway = points // 2
         frame_count = samples // stride
-        paired = jnp.stack(
-            [framed(est_wave, beyond_pair[0], stride), framed(clean, beyond_pair[1], stride)]
-        )
         table = analysis_table(points)
-        spectra_pair = jnp.einsum(
-            "ecfm,jm->ecfj", paired, table, preferred_element_type=jnp.float32
-        )
-        est_real = spectra_pair[0, :, :, :halfway]
-        est_imag = spectra_pair[0, :, :, halfway:]
-        tgt_real = spectra_pair[1, :, :, :halfway]
-        tgt_imag = spectra_pair[1, :, :, halfway:]
+        tgt_x = jnp.einsum(
+            "cfm,jm->cfj",
+            framed(clean, clean_beyond[:, : 3 * stride], stride),
+            table,
+            preferred_element_type=jnp.float32,
+        )
+        est_x = jnp.einsum(
+            "cfm,jm->cfj",
+            framed(est_wave, est_beyond[:, : 3 * stride], stride),
+            table,
+            preferred_element_type=jnp.float32,
+        )
+        est_real = est_x[:, :, :halfway]
+        est_imag = est_x[:, :, halfway:]
+        tgt_real = tgt_x[:, :, :halfway]
+        tgt_imag = tgt_x[:, :, halfway:]
         est_mag = jnp.sqrt(est_real * est_real + est_imag * est_imag + EPS_MAG)
         tgt_mag = jnp.sqrt(tgt_real * tgt_real + tgt_imag * tgt_imag + EPS_MAG)
         usable_count = lengths * (HOP // stride)

time: 150 us -> 145 us (0.967)
  waiting for transfers between devices: 26.5 us -> 5.79 us
  matrix products: 15.4 us -> 28.4 us
  other arithmetic: 34.9 us -> 43.8 us
  local copies, waits for them, and re-layouts: 20.5 us -> 14 us
  starting transfers between devices: 7.07 us -> 9.29 us
  blocking collectives: 28.4 us -> 26.5 us
    reduce_scatter x1, waiting for transfers between devices: 25.2 us -> 3.51 us  [body(): lax.psum_scatter(sum((framed_sig[3 - quarter:3 - quarter + rows_here * la...]
    dot_general x3 -> x6, matrix products: 4.47 us -> 18.4 us  [the longest x3 10.9 us: body(): jnp.einsum('cfm,jm->cfj', framed(clean, clean_beyond[:, :3 * stride], str...]
    slice x3, local copies, waits for them, and re-layouts: 6.71 us -> 1.88 us  [spread_parts(): quarters[:, :, quarter]]
    reshape x3, local copies, waits for them, and re-layouts: 5.21 us -> 2.36 us  [body(): grad_frames.reshape(clip_count, frame_count, 4, stride)]
    ppermute x3, waiting for transfers between devices: 0.01 us -> 2.25 us  [gathered_sum(): arrived = lax.ppermute(value, axis, route)]
    slice x0 -> x6, local copies, waits for them, and re-layouts: none -> 1.99 us  [the longest x2 1.38 us: body(): clean_beyond[:, :3 * stride]]
    all_gather x1, blocking collectives: 13.9 us -> 12 us  [body(): portion = lax.all_gather(grad_hops, 'seg', axis=1, tiled=True)]
    lt x3, other arithmetic: 0.73 us -> 2.54 us  [body(): usable = frame_index[None, :, None] < usable_count[:, None, None]]
  transfers between devices with their start and end apart: 6 -> 7, of which waited for: 2 -> 4; matrix products, arithmetic and copies ran while one was open for 31% -> 29% of each run, Pallas kernels for 0% -> 0%
where the time goes in v4:
time: 145 us; the launch traced here: 144 us
  other arithmetic  43.8 us (30%)
  matrix products  28.4 us (20%)
  blocking collectives  26.5 us (18%)
  between operations  16.7 us (12%)
  local copies, waits for them, and re-layouts  14 us (10%)
  starting transfers between devices  9.29 us (6%)
  waiting for transfers between devices  5.79 us (4%)
    psum x1, blocking collectives, body(): spreads, energies, logterms = lax.psum((spreads, energies, logterms), 'seg')  14.4 us
    all_gather x1, blocking collectives, body(): portion = lax.all_gather(grad_hops, 'seg', axis=1, tiled=True)  12 us
    dot_general x3, matrix products, body(): jnp.einsum('cfm,jm->cfj', framed(clean, clean_beyond[:, :3 * stride], str...  10.9 us
    mul x3, other arithmetic, analysis_table(): fine_cos, fine_sin = (part * scale for part in fine)  8.63 us
    dot_general x3, matrix products, body(): jnp.einsum('cfm,jm->cfj', framed(est_wave, est_beyond[:, :3 * stride], st...  7.52 us
    convert_element_type x3, other arithmetic, analysis_table(): table = entry_value.astype(jnp.bfloat16)  7.4 us
    dot_general x3, matrix products, body(): jnp.einsum('cfj,jm->cfm', grad_x, table, preferred_element_type=jnp.float32)  6.71 us
    ppermute x3, starting transfers between devices, gathered_sum(): arrived = lax.ppermute(value, axis, route)  5.39 us
  transfers between devices with their start and end apart: 7, of which 4 were waited for; matrix products, arithmetic and copies ran while one was open for 29% of the time, Pallas kernels for 0%

profile of v4, /device:TPU:0, one launch (start us, length us, event | category | flops | bytes accessed | tf_op | source)
XLA Modules:
  0.0 144.5 jit_solution(9374658757925993402)
XLA Ops:
  7.3 0.5 cosine_multiply_fusion.3
  7.8 1.9 %fusion.128 = (f32[16,2048]{1,0:T(8,128)S(1)}, f32[16,2048]{1,0:T(8,128)S(1)}, f32[16,2048]{1,0:T(8,128)}, f32[16,2048]{1,0:T(8,128)}) fusion(s32[16]{0:T(128)S(1)} %get-tuple-element.103, pred[16]{0:T(512)(128)(4,1)S(1)} %iota_compare_fusion.2, s32[16]{0:T(128)S(1)} %get-tuple-element.104), kind=kLoop, calls=%fused_computation.222 | loop fusion | flops 1179648 | bytes 524432 | tf_op jit(solution)/shard_map/jit(_where)/select_n | solution.py:62
  10.1 1.3 multiply_convert_fusion
  11.3 1.0 compare_select_fusion.2
  12.4 2.0 %convolution_bitcast_fusion = f32[195,4,2048]{2,0,1:T(8,128)S(1)} fusion(bf16[2,128,2048]{2,1,0:T(8,128)(2,1)S(1)} %bitcast.129, bf16[4,2,128,192]{2,3,1,0:T(8,128)(2,1)} %param.3), kind=kOutput, calls=%fused_computation.8 | convolution fusion | flops 817889280 | bytes 7831552 | tf_op jit(solution)/shard_map/crbf,rbm->fcm/dot_general | solution.py:122
  14.4 2.0 %slice_add_fusion = f32[192,4,512]{2,0,1:T(8,128)} fusion(f32[195,4,2048]{2,0,1:T(8,128)S(1)} %convolution_bitcast_fusion), kind=kLoop, calls=%fused_computation.24 | loop fusion | flops 1179648 | bytes 7864320 | tf_op jit(solution)/shard_map/add | solution.py:126
  16.4 0.6 slice.222
  17.0 1.3 collective-permute-start.1
  18.4 0.5 fusion.150
  18.9 0.6 iota_compare_fusion
  19.5 0.6 subtract_multiply_fusion.1
  20.1 0.5 fusion.149
  20.7 0.6 iota_compare_fusion.1
  21.2 4.1 %cosine_multiply_fusion = (f32[128,2048]{1,0:T(8,128)S(1)}, f32[128,2048]{1,0:T(8,128)S(1)}) fusion(f32[2048]{0:T(1024)S(1)} %fusion.143), kind=kLoop, calls=%fused_computation.38 | loop fusion | flops 4194304 | bytes 2105344 | tf_op jit(solution)/shard_map/mul | solution.py:44
  25.4 0.6 broadcast_compare_fusion
  26.0 2.1 %cosine_multiply_fusion.1 = (f32[128,1024]{1,0:T(8,128)S(1)}, f32[128,1024]{1,0:T(8,128)S(1)}) fusion(f32[1024]{0:T(1024)S(1)} %subtract_multiply_fusion), kind=kLoop, calls=%fused_computation.59 | loop fusion | flops 2097152 | bytes 1052672 | tf_op jit(solution)/shard_map/mul | solution.py:44
  28.1 0.5 iota_add_fusion.2
  28.6 2.4 %cosine_multiply_fusion.2 = (f32[128,512]{1,0:T(8,128)S(1)}, f32[128,512]{1,0:T(8,128)}) fusion(f32[512]{0:T(512)} %subtract_multiply_fusion.1), kind=kLoop, calls=%fused_computation.161 | loop fusion | flops 1048576 | bytes 526336 | tf_op jit(solution)/shard_map/mul | solution.py:44
  31.1 0.9 fusion.138
  32.0 1.3 broadcast_compare_fusion.1
  33.2 0.8 fusion.145
  34.1 6.7 %add_convert_fusion = bf16[16,128,2048]{2,1,0:T(8,128)(2,1)} fusion(f32[128,2048]{1,0:T(8,128)S(1)} %get-tuple-element.76, f32[16,2048]{1,0:T(8,128)} %get-tuple-element.101, f32[128,2048]{1,0:T(8,128)S(1)} %get-tuple-element.75, f32[16,2048]{1,0:T(8,128)} %get-tuple-element.102), kind=kLoop, calls=%fused_computation | loop fusion | flops 16777216 | bytes 10747904 | tf_op jit(solution)/shard_map/convert_element_type | solution.py:46
  40.8 0.6 add_convert_fusion.1
  41.5 0.7 broadcast_compare_fusion.2
  42.2 0.8 pad_maximum_fusion.1
  43.0 0.7 slice.306
  43.8 0.7 slice.292
  44.7 0.7 fusion.174
  45.5 1.7 %fusion.15 = f32[4,48,1024]{2,1,0:T(8,128)} fusion(bf16[1024,1024]{1,0:T(8,128)(2,1)S(1)} %bitcast.126, bf16[4,48,256]{2,1,0:T(8,128)(2,1)S(1)} %get-tuple-element.58, bf16[4,48,256]{2,1,0:T(8,128)(2,1)S(1)} %get-tuple-element.59, bf16[4,48,256]{2,1,0:T(8,128)(2,1)S(1)} %get-tuple-element.60, bf16[4,48,256]{2,1,0:T(8,128)(2,1)S(1)} %get-tuple-element.57), kind=kOutput, calls=%fused_computation.19 | convolution fusion | flops 404226048 | bytes 3276800 | tf_op jit(solution)/shard_map/cfm,jm->cfj/dot_general | solution.py:155
  47.2 7.0 %fusion.2 = f32[4,24,2048]{2,1,0:T(8,128)} fusion(bf16[2048,2048]{1,0:T(8,128)(2,1)} %bitcast.123, bf16[4,24,512]{2,1,0:T(8,128)(2,1)S(1)} %get-tuple-element.50, bf16[4,24,512]{2,1,0:T(8,128)(2,1)S(1)} %get-tuple-element.51, bf16[4,24,512]{2,1,0:T(8,128)(2,1)S(1)} %get-tuple-element.52, bf16[4,24,512]{2,1,0:T(8,128)(2,1)S(1)} %get-tuple-element.49), kind=kOutput, calls=%fused_computation.3 | convolution fusion | flops 806879232 | bytes 9568256 | tf_op jit(solution)/shard_map/cfm,jm->cfj/dot_general | solution.py:155
  54.2 3.5 %reduce-scatter.2.cloned.1.call-done = f32[24,4,512]{2,0,1:T(8,128)} async-done(((f32[192,4,512]{2,0,1:T(8,128)}), f32[24,4,512]{2,0,1:T(8,128)}) %reduce-scatter.2.cloned.1.call-update) | async-done | bytes 196624 | tf_op jit(solution)/shard_map/reduce_scatter | solution.py:125
  57.7 1.1 copy.42
  58.9 1.3 collective-permute-start
  60.2 2.2 %fusion.34 = f32[4,96,512]{2,1,0:T(8,128)} fusion(bf16[512,512]{1,0:T(8,128)(2,1)S(1)} %bitcast.131, bf16[4,96,128]{2,1,0:T(8,128)(2,1)S(1)} %get-tuple-element.66, bf16[4,96,128]{2,1,0:T(8,128)(2,1)S(1)} %copy-done.17, bf16[4,96,128]{2,1,0:T(8,128)(2,1)} %get-tuple-element.68, bf16[4,96,128]{2,1,0:T(8,128)(2,1)S(1)} %get-tuple-element.65), kind=kOutput, calls=%fused_computation.54 | convolution fusion | flops 202899456 | bytes 1703936 | tf_op jit(solution)/shard_map/cfm,jm->cfj/dot_general | solution.py:155
  62.6 0.7 fusion.171
  63.4 0.8 fusion.173
  64.5 6.3 %fusion.4 = f32[4,24,2048]{2,1,0:T(8,128)S(1)} fusion(bf16[2048,2048]{1,0:T(8,128)(2,1)} %bitcast.124, bf16[4,24,512]{2,1,0:T(8,128)(2,1)} %get-tuple-element.54, bf16[4,24,512]{2,1,0:T(8,128)(2,1)} %get-tuple-element.55, bf16[4,24,512]{2,1,0:T(8,128)(2,1)} %get-tuple-element.56, bf16[4,24,512]{2,1,0:T(8,128)(2,1)S(1)} %get-tuple-element.53), kind=kOutput, calls=%fused_computation.5 | convolution fusion | flops 806879232 | bytes 9568256 | tf_op jit(solution)/shard_map/cfm,jm->cfj/dot_general | solution.py:161
  70.8 1.4 select_reduce_fusion.6
  72.2 0.9 fusion.17
  73.1 1.5 %select_reduce_fusion.7 = (f32[4]{0:T(128)S(1)}, f32[4]{0:T(128)S(1)}, f32[4]{0:T(128)S(1)}, f32[4,48,512]{2,1,0:T(8,128)}, f32[4,48,512]{2,1,0:T(8,128)}) fusion(pred[4,48]{1,0:T(4,128)(4,1)S(1)} %copy-done.27, f32[4,48,1024]{2,1,0:T(8,128)S(1)} %fusion.17, f32[4,48,1024]{2,1,0:T(8,128)S(1)} %copy-done.11), kind=kLoop, calls=%fused_computation.147 | loop fusion | flops 2064372 | bytes 2359536 | tf_op jit(solution)/shard_map/reduce_sum | solution.py:179
  75.0 0.9 copy-done.3
  75.9 1.4 select_reduce_fusion.8
  77.4 14.4 %all-reduce.17 = (f32[3,4]{1,0:T(4,128)S(1)}, f32[3,4]{1,0:T(4,128)S(1)}, f32[3,4]{1,0:T(4,128)S(1)}) all-reduce(f32[3,4]{1,0:T(4,128)S(1)} %pad_maximum_fusion.8, f32[3,4]{1,0:T(4,128)S(1)} %pad_maximum_fusion.7, f32[3,4]{1,0:T(4,128)S(1)} %pad_maximum_fusion.6), channel_id=1, replica_groups=mesh['clip'=4,'seg'=8] {'seg'}, use_global_device_ids=true, to_apply=%region_12.13 | all-reduce | flops 36 | bytes 288 | tf_op jit(solution)/shard_map/psum | solution.py:188
  91.8 0.6 multiply_rsqrt_fusion
  92.4 1.8 %divide_convert_fusion.3 = (bf16[4,48,512]{2,1,0:T(8,128)(2,1)S(1)}, bf16[4,48,512]{2,1,0:T(8,128)(2,1)S(1)}) fusion(f32[4,48,1024]{2,1,0:T(8,128)} %copy-done.5, f32[4,48,512]{2,1,0:T(8,128)} %get-tuple-element.24, f32[4,48,512]{2,1,0:T(8,128)} %get-tuple-element.25, f32[4]{0:T(128)S(1)} %copy-done.21, f32[4]{0:T(128)S(1)} %get-tuple-element.83, ...), kind=kLoop, calls=%fused_computation.131 | loop fusion | flops 1671168 | bytes 1966304 | tf_op jit(solution)/shard_map/convert.2
  94.3 1.5 %fusion.13 = f32[4,48,1024]{2,1,0:T(8,128)} fusion(bf16[1024,1024]{1,0:T(8,128)(2,1)S(1)} %bitcast.128, bf16[4,48,512]{2,1,0:T(8,128)(2,1)S(1)} %get-tuple-element.31, bf16[4,48,512]{2,1,0:T(8,128)(2,1)S(1)} %get-tuple-element.30), kind=kOutput, calls=%fused_computation.17 | convolution fusion | flops 403439616 | bytes 3276800 | tf_op jit(solution)/shard_map/cfj,jm->cfm/dot_general | solution.py:207
  95.8 1.6 %reshape.901 = f32[4,48,4,256]{3,2,1,0:T(4,128)S(1)} reshape(f32[4,48,1024]{2,1,0:T(8,128)} %fusion.13) | data formatting | bytes 1572864 | tf_op jit(solution)/shard_map/reshape | solution.py:210
  97.3 0.6 fusion.168
  98.5 0.8 pad_add_fusion.1
  99.8 4.9 %fusion = f32[4,24,2048]{2,1,0:T(8,128)S(1)} fusion(bf16[2048,2048]{1,0:T(8,128)(2,1)} %bitcast.125, bf16[4,24,1024]{2,1,0:T(8,128)(2,1)S(1)} %get-tuple-element.33, bf16[4,24,1024]{2,1,0:T(8,128)(2,1)S(1)} %get-tuple-element.32), kind=kOutput, calls=%fused_computation.1 | convolution fusion | flops 806092800 | bytes 9568256 | tf_op jit(solution)/shard_map/cfj,jm->cfm/dot_general | solution.py:207
  104.6 0.5 reshape.903
  105.2 0.7 fusion.169
  106.6 0.5 divide_convert_fusion.5
  107.7 0.6 fusion.167
  109.0 1.3 collective-permute-start.5
  110.3 1.5 %collective-permute-start.2 = (f32[]{:T(128)}, f32[]{:T(128)}, u32[]{:S(2)}, u32[]{:S(2)}) collective-permute-start(f32[]{:T(128)} %get-tuple-element.78), channel_id=1, source_target_pairs={{0,8},{8,16},{16,24},{24,0},{1,9},{9,17},{17,25},{25,1},{2,10},{10... | collective-permute-start | bytes 20 | tf_op jit(solution)/shard_map/ppermute | solution.py:79
  111.9 2.4 %collective-permute-start.3 = (f32[]{:T(128)}, f32[]{:T(128)}, u32[]{:S(2)}, u32[]{:S(2)}) collective-permute-start(f32[]{:T(128)} %get-tuple-element.78), channel_id=1, source_target_pairs={{0,16},{8,24},{16,0},{24,8},{1,17},{9,25},{17,1},{25,9},{2,18},{10... | collective-permute-start | bytes 20 | tf_op jit(solution)/shard_map/ppermute | solution.py:79
  114.3 1.4 collective-permute-start.4
  116.5 1.5 %collective-permute-done.4 = f32[]{:T(128)} collective-permute-done((f32[]{:T(128)}, f32[]{:T(128)}, u32[]{:S(2)}, u32[]{:S(2)}) %collective-permute-start.4) | collective-permute-done | bytes 36 | tf_op jit(solution)/shard_map/ppermute | solution.py:79
  118.0 3.0 %fusion.152 = f32[]{:T(128)} fusion(f32[]{:T(128)} %collective-permute-done.4, s32[]{:T(128)S(6)} %select_n.332, f32[]{:T(128)} %collective-permute-done.3, s32[]{:T(128)S(6)} %select_n.330, f32[]{:T(128)} %collective-permute-done.2, s32[]{:T(128)S(6)} %select_n.328, f32[]{:T(128)} %get-tuple-element.78, s32[]{:T(128)S(6)} %select_n.293), kind=kLoop, calls=%fused_computation.289 | loop fusion | flops 47 | bytes 36 | tf_op jit(solution)/shard_map/reduce_sum | solution.py:86
  121.9 12.0 %all_gather.3 = bf16[4,192,512]{2,1,0:T(8,128)(2,1)S(1)} all-gather(bf16[4,24,512]{2,1,0:T(8,128)(2,1)S(1)} %bitcast.160), channel_id=1, replica_groups=mesh['clip'=4,'seg'=8] {'seg'}, dimensions={1}, use_global_device_ids=true | all-gather | bytes 884736 | tf_op jit(solution)/shard_map/all_gather | solution.py:219
  133.9 0.5 pad_slice_fusion.2
  134.5 1.2 fusion.20
  135.7 0.8 copy.27
  (124 shorter events, 5.9 us)
Async XLA Ops:
  7.2 50.6 %reduce-scatter.2.cloned.1.call-start = ((), (), s32[]{:S(2)}) async-start(), calls=%async_computation.1 | async-start | bytes 1769472 | tf_op jit(solution)/shard_map/reduce_scatter | solution.py:125
  10.0 6.3 %copy-start = (bf16[16,16,2048]{2,1,0:T(8,128)(2,1)}, bf16[16,16,2048]{2,1,0:T(8,128)(2,1)S(1)}, u32[]{:S(2)}) copy-start(bf16[16,16,2048]{2,1,0:T(8,128)(2,1)S(1)} %add_convert_fusion.2) | copy-start | bytes 3145732
  11.3 5.0 %copy-start.18 = (s32[4]{0:T(128)}, s32[4]{0:T(128)S(1)}, u32[]{:S(2)}) copy-start(s32[4]{0:T(128)S(1)} %get-tuple-element.96) | copy-start | bytes 52
  14.4 11.0 %copy-start.22 = (s32[4]{0:T(128)S(1)}, s32[4]{0:T(128)}, u32[]{:S(2)}) copy-start(s32[4]{0:T(128)} %param.5) | copy-start | bytes 52
  17.0 25.2 %collective-permute-start.1 = (bf16[4,1536]{1,0:T(4,128)(2,1)}, bf16[4,1536]{1,0:T(4,128)(2,1)}, u32[]{:S(2)}, u32[]{:S(2)}) collective-permute-start(bf16[4,1536]{1,0:T(4,128)(2,1)} %slice.222), channel_id=1, source_target_pairs={{1,0},{2,1},{3,2},{4,3},{5,4},{6,5},{7,6},{9,8},{10,9},{11,10},{12... | collective-permute-start | bytes 36872 | tf_op jit(solution)/shard_map/ppermute | solution.py:20
  34.1 7.3 %copy-start.10 = (f32[128,512]{1,0:T(8,128)S(1)}, f32[128,512]{1,0:T(8,128)}, u32[]{:S(2)}) copy-start(f32[128,512]{1,0:T(8,128)} %get-tuple-element.85) | copy-start | bytes 786436
  40.8 0.7 copy-start.28
  47.2 11.6 %copy-start.19 = (s32[4]{0:T(128)S(1)}, s32[4]{0:T(128)}, u32[]{:S(2)}) copy-start(s32[4]{0:T(128)} %copy-done.18) | copy-start | bytes 52
  47.2 13.0 %copy-start.17 = (bf16[4,96,128]{2,1,0:T(8,128)(2,1)S(1)}, bf16[4,96,128]{2,1,0:T(8,128)(2,1)}, u32[]{:S(2)}) copy-start(bf16[4,96,128]{2,1,0:T(8,128)(2,1)} %get-tuple-element.67) | copy-start | bytes 294916
  58.9 3.5 %collective-permute-start = (bf16[4,1536]{1,0:T(4,128)(2,1)S(1)}, bf16[4,1536]{1,0:T(4,128)(2,1)S(1)}, u32[]{:S(2)}, u32[]{:S(2)}) collective-permute-start(bf16[4,1536]{1,0:T(4,128)(2,1)S(1)} %slice.284), channel_id=1, source_target_pairs={{1,0},{2,1},{3,2},{4,3},{5,4},{6,5},{7,6},{9,8},{10,9},{11,10},{12... | collective-permute-start | bytes 36872 | tf_op jit(solution)/shard_map/ppermute | solution.py:20
  64.4 6.3 %copy-start.2 = (f32[4,24,2048]{2,1,0:T(8,128)S(1)}, f32[4,24,2048]{2,1,0:T(8,128)}, u32[]{:S(2)}) copy-start(f32[4,24,2048]{2,1,0:T(8,128)} %fusion.2) | copy-start | bytes 2359300
  64.4 6.3 %copy-start.24 = (pred[4,24]{1,0:T(4,128)(4,1)S(1)}, pred[4,24]{1,0:T(4,128)(4,1)}, u32[]{:S(2)}) copy-start(pred[4,24]{1,0:T(4,128)(4,1)} %broadcast_compare_fusion) | copy-start | bytes 292
  64.4 7.7 %copy-start.13 = (bf16[4,48,256]{2,1,0:T(8,128)(2,1)S(1)}, bf16[4,48,256]{2,1,0:T(8,128)(2,1)}, u32[]{:S(2)}) copy-start(bf16[4,48,256]{2,1,0:T(8,128)(2,1)} %get-tuple-element.61) | copy-start | bytes 294916
  64.4 7.7 %copy-start.14 = (bf16[4,48,256]{2,1,0:T(8,128)(2,1)S(1)}, bf16[4,48,256]{2,1,0:T(8,128)(2,1)}, u32[]{:S(2)}) copy-start(bf16[4,48,256]{2,1,0:T(8,128)(2,1)} %get-tuple-element.62) | copy-start | bytes 294916
  64.4 7.7 %copy-start.15 = (bf16[4,48,256]{2,1,0:T(8,128)(2,1)S(1)}, bf16[4,48,256]{2,1,0:T(8,128)(2,1)}, u32[]{:S(2)}) copy-start(bf16[4,48,256]{2,1,0:T(8,128)(2,1)} %get-tuple-element.63) | copy-start | bytes 294916
  64.4 7.7 %copy-start.16 = (bf16[4,48,256]{2,1,0:T(8,128)(2,1)S(1)}, bf16[4,48,256]{2,1,0:T(8,128)(2,1)}, u32[]{:S(2)}) copy-start(bf16[4,48,256]{2,1,0:T(8,128)(2,1)} %get-tuple-element.64) | copy-start | bytes 294916
  70.8 2.3 %copy-start.11 = (f32[4,48,1024]{2,1,0:T(8,128)S(1)}, f32[4,48,1024]{2,1,0:T(8,128)}, u32[]{:S(2)}) copy-start(f32[4,48,1024]{2,1,0:T(8,128)} %fusion.15) | copy-start | bytes 2359300
  70.8 2.3 %copy-start.27 = (pred[4,48]{1,0:T(4,128)(4,1)S(1)}, pred[4,48]{1,0:T(4,128)(4,1)}, u32[]{:S(2)}) copy-start(pred[4,48]{1,0:T(4,128)(4,1)} %broadcast_compare_fusion.1) | copy-start | bytes 580
  72.1 3.7 %copy-start.12 = (f32[4,96,512]{2,1,0:T(8,128)S(1)}, f32[4,96,512]{2,1,0:T(8,128)}, u32[]{:S(2)}) copy-start(f32[4,96,512]{2,1,0:T(8,128)} %fusion.34) | copy-start | bytes 2359300
  72.2 3.7 %copy-start.26 = (pred[4,96]{1,0:T(4,128)(4,1)S(1)}, pred[4,96]{1,0:T(4,128)(4,1)}, u32[]{:S(2)}) copy-start(pred[4,96]{1,0:T(4,128)(4,1)} %broadcast_compare_fusion.2) | copy-start | bytes 1156
  73.1 4.2 %copy-start.5 = (f32[4,48,1024]{2,1,0:T(8,128)}, f32[4,48,1024]{2,1,0:T(8,128)S(1)}, u32[]{:S(2)}) copy-start(f32[4,48,1024]{2,1,0:T(8,128)S(1)} %fusion.17) | copy-start | bytes 2359300
  73.1 4.3 %copy-start.23 = (s32[4]{0:T(128)S(1)}, s32[4]{0:T(128)}, u32[]{:S(2)}) copy-start(s32[4]{0:T(128)} %param.5) | copy-start | bytes 52
  73.1 19.4 %copy-start.21 = (f32[4]{0:T(128)S(1)}, f32[4]{0:T(128)}, u32[]{:S(2)}) copy-start(f32[4]{0:T(128)} %get-tuple-element.94) | copy-start | bytes 52
  75.0 0.9 copy-start.3
  94.3 5.0 %copy-start.25 = (pred[4,24]{1,0:T(4,128)(4,1)S(1)}, pred[4,24]{1,0:T(4,128)(4,1)}, u32[]{:S(2)}) copy-start(pred[4,24]{1,0:T(4,128)(4,1)} %broadcast_compare_fusion) | copy-start | bytes 292
  95.8 3.5 %copy-start.8 = (f32[4,24,1024]{2,1,0:T(8,128)S(1)}, f32[4,24,1024]{2,1,0:T(8,128)}, u32[]{:S(2)}) copy-start(f32[4,24,1024]{2,1,0:T(8,128)} %get-tuple-element.26) | copy-start | bytes 1179652
  95.8 3.5 %copy-start.9 = (f32[4,24,1024]{2,1,0:T(8,128)S(1)}, f32[4,24,1024]{2,1,0:T(8,128)}, u32[]{:S(2)}) copy-start(f32[4,24,1024]{2,1,0:T(8,128)} %get-tuple-element.27) | copy-start | bytes 1179652
  104.6 1.9 %copy-start.4 = (f32[4,96,512]{2,1,0:T(8,128)S(1)}, f32[4,96,512]{2,1,0:T(8,128)}, u32[]{:S(2)}) copy-start(f32[4,96,512]{2,1,0:T(8,128)} %copy-done.3) | copy-start | bytes 2359300
  104.6 1.9 %copy-start.6 = (f32[4,96,256]{2,1,0:T(8,128)S(1)}, f32[4,96,256]{2,1,0:T(8,128)}, u32[]{:S(2)}) copy-start(f32[4,96,256]{2,1,0:T(8,128)} %get-tuple-element.22) | copy-start | bytes 1179652
  105.2 1.4 copy-start.7
  107.0 14.7 %slice-start = ((f32[4,51,256]{2,0,1:T(4,128)}), f32[4,48,256]{2,0,1:T(4,128)S(1)}, s32[]{:S(2)}) async-start(f32[4,51,256]{2,0,1:T(4,128)} %pad_add_fusion.1), calls=%async_computation.2 | async-start | bytes 393216 | tf_op jit(solution)/shard_map/slice | solution.py:211
  107.1 14.7 %copy-start.20 = (s32[4]{0:T(128)S(1)}, s32[4]{0:T(128)}, u32[]{:S(2)}) copy-start(s32[4]{0:T(128)} %copy-done.18) | copy-start | bytes 52
  108.6 25.8 %copy-start.1 = (bf16[16,16,2048]{2,1,0:T(8,128)(2,1)S(1)}, bf16[16,16,2048]{2,1,0:T(8,128)(2,1)}, u32[]{:S(2)}) copy-start(bf16[16,16,2048]{2,1,0:T(8,128)(2,1)} %copy-done) | copy-start | bytes 3145732
  109.0 12.8 %collective-permute-start.5 = (f32[4,1536]{1,0:T(4,128)S(1)}, f32[4,1536]{1,0:T(4,128)S(1)}, u32[]{:S(2)}, u32[]{:S(2)}) collective-permute-start(f32[4,1536]{1,0:T(4,128)S(1)} %add_add_fusion.3), channel_id=1, source_target_pairs={{0,1},{1,2},{2,3},{3,4},{4,5},{5,6},{6,7},{8,9},{9,10},{10,11},{11... | collective-permute-start | bytes 73736 | tf_op jit(solution)/shard_map/ppermute | solution.py:20
  110.3 5.7 %collective-permute-start.2 = (f32[]{:T(128)}, f32[]{:T(128)}, u32[]{:S(2)}, u32[]{:S(2)}) collective-permute-start(f32[]{:T(128)} %get-tuple-element.78), channel_id=1, source_target_pairs={{0,8},{8,16},{16,24},{24,0},{1,9},{9,17},{17,25},{25,1},{2,10},{10... | collective-permute-start | bytes 20 | tf_op jit(solution)/shard_map/ppermute | solution.py:79
  111.9 4.6 %collective-permute-start.3 = (f32[]{:T(128)}, f32[]{:T(128)}, u32[]{:S(2)}, u32[]{:S(2)}) collective-permute-start(f32[]{:T(128)} %get-tuple-element.78), channel_id=1, source_target_pairs={{0,16},{8,24},{16,0},{24,8},{1,17},{9,25},{17,1},{25,9},{2,18},{10... | collective-permute-start | bytes 20 | tf_op jit(solution)/shard_map/ppermute | solution.py:79
  114.3 3.7 %collective-permute-start.4 = (f32[]{:T(128)}, f32[]{:T(128)}, u32[]{:S(2)}, u32[]{:S(2)}) collective-permute-start(f32[]{:T(128)} %get-tuple-element.78), channel_id=1, source_target_pairs={{0,24},{8,0},{16,8},{24,16},{1,25},{9,1},{17,9},{25,17},{2,26},{10... | collective-permute-start | bytes 20 | tf_op jit(solution)/shard_map/ppermute | solution.py:79
Sparse Core Ops, SparseCore 0:
  16.5 41.1 reduce-scatter.1

commit v5 on v4

--- a/solution.py
+++ b/solution.py
@@ -69,20 +69,25 @@
 def gathered_sum(value, axis):
     size = lax.axis_size(axis)
     here = lax.axis_index(axis)
-    devices = range(size)
-    slots = jnp.zeros((size,) + value.shape, value.dtype)
-    for distance in range(size):
-        if distance == 0:
-            arrived = value
-        else:
-            route = [(i, (i + distance) % size) for i in devices]
-            arrived = lax.ppermute(value, axis, route)
-        source = (here - distance) % size
-        slots = slots + jnp.where(
-            (jnp.arange(size, dtype=jnp.int32) == source).reshape((size,) + (1,) * value.ndim),
-            arrived[None],
+    held = value[None]
+    while held.shape[0] < size and size % (2 * held.shape[0]) == 0:
+        distance = held.shape[0]
+        route = [(i, (i + distance) % size) for i in range(size)]
+        held = jnp.concatenate([held, lax.ppermute(held, axis, route)], axis=0)
+    for distance in range(held.shape[0], size):
+        route = [(i, (i + distance) % size) for i in range(size)]
+        held = jnp.concatenate([held, lax.ppermute(value, axis, route)[None]], axis=0)
+    source = (here - jnp.arange(size, dtype=jnp.int32)) % size
+    slots = jnp.sum(
+        jnp.where(
+            (source[:, None] == jnp.arange(size, dtype=jnp.int32)[None, :]).reshape(
+                (size, size) + (1,) * value.ndim
+            ),
+            held[:, None],
             0.0,
-        )
+        ),
+        axis=0,
+    )
     return jnp.sum(slots, axis=0)
 
 
@@ -185,7 +190,8 @@
     spreads = jnp.stack(spread_list)
     energies = jnp.stack(energy_list)
     logterms = jnp.stack(logterm_list)
-    spreads, energies, logterms = lax.psum((spreads, energies, logterms), "seg")
+    parts = lax.all_gather(jnp.stack([spreads, energies, logterms]), "seg", axis=0, tiled=False)
+    spreads, energies, logterms = jnp.sum(parts, axis=0)
     own_loss = jnp.sum(jnp.sqrt((spreads + EPS_RATIO) / energies) + logterms)
     loss = gathered_sum(own_loss, "clip") / (3 * clip_count * lax.axis_size("clip"))
     ratio_weight = 1.0 / jnp.sqrt((spreads + EPS_RATIO) * energies)

time: 145 us -> 144 us (level)
  waiting for transfers between devices: 5.79 us -> 13.8 us
  blocking collectives: 26.5 us -> 20.9 us
  starting transfers between devices: 9.29 us -> 7.14 us
    psum x1 -> x0, blocking collectives: 14.4 us -> none  [body(): spreads, energies, logterms = lax.psum((spreads, energies, logterms), 'seg')]
    all_gather x0 -> x1, blocking collectives: none -> 10.6 us  [body(): lax.all_gather(jnp.stack([spreads, energies, logterms]), 'seg', axis=0, t...]
    reduce_scatter x1, waiting for transfers between devices: 3.51 us -> 7.88 us  [body(): lax.psum_scatter(sum((framed_sig[3 - quarter:3 - quarter + rows_here * la...]
    ppermute x3 -> x2, waiting for transfers between devices: 2.25 us -> 5.69 us  [gathered_sum(): held = jnp.concatenate([held, lax.ppermute(held, axis, route)], axis=0)]
    ppermute x3 -> x2, starting transfers between devices: 5.39 us -> 2.17 us  [gathered_sum(): held = jnp.concatenate([held, lax.ppermute(held, axis, route)], axis=0)]
    concatenate x0 -> x2, other arithmetic: none -> 2.87 us  [gathered_sum(): held = jnp.concatenate([held, lax.ppermute(held, axis, route)], axis=0)]
    reduce_sum x1, other arithmetic: 3.05 us -> 0.67 us  [gathered_sum(): return jnp.sum(slots, axis=0)]
    slice x3, local copies, waits for them, and re-layouts: 1.88 us -> 4.24 us  [spread_parts(): quarters[:, :, quarter]]
  transfers between devices with their start and end apart: 7 -> 6, of which waited for: 4 -> 4; matrix products, arithmetic and copies ran while one was open for 29% -> 26% of each run, Pallas kernels for 0% -> 0%
where the time goes in v5:
time: 144 us; the launch traced here: 143 us
  other arithmetic  42.7 us (30%)
  matrix products  27.6 us (19%)
  blocking collectives  20.9 us (15%)
  between operations  16.7 us (12%)
  local copies, waits for them, and re-layouts  14.1 us (10%)
  waiting for transfers between devices  13.8 us (10%)
  starting transfers between devices  7.14 us (5%)
    all_gather x1, blocking collectives, body(): lax.all_gather(jnp.stack([spreads, energies, logterms]), 'seg', axis=0, t...  10.6 us
    all_gather x1, blocking collectives, body(): portion = lax.all_gather(grad_hops, 'seg', axis=1, tiled=True)  10.3 us
    dot_general x3, matrix products, body(): jnp.einsum('cfm,jm->cfj', framed(clean, clean_beyond[:, :3 * stride], str...  10.1 us
    mul x3, other arithmetic, analysis_table(): fine_cos, fine_sin = (part * scale for part in fine)  9.54 us
    convert_element_type x3, other arithmetic, analysis_table(): table = entry_value.astype(jnp.bfloat16)  9.29 us
    dot_general x3, matrix products, body(): jnp.einsum('cfm,jm->cfj', framed(est_wave, est_beyond[:, :3 * stride], st...  8.46 us
    reduce_scatter x1, waiting for transfers between devices, body(): lax.psum_scatter(sum((framed_sig[3 - quarter:3 - quarter + rows_here * la...  7.88 us
    dot_general x3, matrix products, body(): jnp.einsum('cfj,jm->cfm', grad_x, table, preferred_element_type=jnp.float32)  5.81 us
  transfers between devices with their start and end apart: 6, of which 4 were waited for; matrix products, arithmetic and copies ran while one was open for 26% of the time, Pallas kernels for 0%

profile of v5, /device:TPU:0, one launch (start us, length us, event | category | flops | bytes accessed | tf_op | source)
XLA Modules:
  0.0 143.0 jit_solution(16491448133786597606)
XLA Ops:
  7.3 1.2 multiply_convert_fusion
  8.5 0.5 cosine_multiply_fusion.3
  9.0 1.9 %fusion.128 = (f32[16,2048]{1,0:T(8,128)S(1)}, f32[16,2048]{1,0:T(8,128)S(1)}, f32[16,2048]{1,0:T(8,128)S(1)}, f32[16,2048]{1,0:T(8,128)}) fusion(s32[16]{0:T(128)S(1)} %get-tuple-element.104, pred[16]{0:T(512)(128)(4,1)S(1)} %iota_compare_fusion.3, s32[16]{0:T(128)S(1)} %get-tuple-element.105), kind=kLoop, calls=%fused_computation.222 | loop fusion | flops 1179648 | bytes 524432 | tf_op jit(solution)/shard_map/jit(_where)/select_n | solution.py:62
  10.9 0.2 add_convert_fusion.2
  11.2 1.1 compare_select_fusion.2
  12.3 2.0 %convolution_bitcast_fusion = f32[195,4,2048]{2,0,1:T(8,128)S(1)} fusion(bf16[2,128,2048]{2,1,0:T(8,128)(2,1)S(1)} %bitcast.137, bf16[4,2,128,192]{2,3,1,0:T(8,128)(2,1)} %param.3), kind=kOutput, calls=%fused_computation.8 | convolution fusion | flops 817889280 | bytes 7831552 | tf_op jit(solution)/shard_map/crbf,rbm->fcm/dot_general | solution.py:127
  14.4 2.0 %slice_add_fusion = f32[192,4,512]{2,0,1:T(8,128)} fusion(f32[195,4,2048]{2,0,1:T(8,128)S(1)} %convolution_bitcast_fusion), kind=kLoop, calls=%fused_computation.24 | loop fusion | flops 1179648 | bytes 7864320 | tf_op jit(solution)/shard_map/add | solution.py:131
  16.4 1.5 %collective-permute-start.1 = (bf16[4,1536]{1,0:T(4,128)(2,1)S(1)}, bf16[4,1536]{1,0:T(4,128)(2,1)S(1)}, u32[]{:S(2)}, u32[]{:S(2)}) collective-permute-start(bf16[4,1536]{1,0:T(4,128)(2,1)S(1)} %slice.225), channel_id=1, source_target_pairs={{1,0},{2,1},{3,2},{4,3},{5,4},{6,5},{7,6},{9,8},{10,9},{11,10},{12... | collective-permute-start | bytes 36872 | tf_op jit(solution)/shard_map/ppermute | solution.py:20
  18.1 1.1 cosine_multiply_fusion.2
  19.2 3.1 %cosine_multiply_fusion.1 = (f32[128,1024]{1,0:T(8,128)}, f32[128,1024]{1,0:T(8,128)}) fusion(f32[1024]{0:T(1024)S(1)} %subtract_multiply_fusion), kind=kLoop, calls=%fused_computation.59 | loop fusion | flops 2097152 | bytes 1052672 | tf_op jit(solution)/shard_map/mul | solution.py:44
  22.3 0.7 broadcast_compare_fusion
  23.0 5.4 %cosine_multiply_fusion = (f32[128,2048]{1,0:T(8,128)S(1)}, f32[128,2048]{1,0:T(8,128)}) fusion(f32[2048]{0:T(1024)S(1)} %fusion.143), kind=kLoop, calls=%fused_computation.38 | loop fusion | flops 4194304 | bytes 2105344 | tf_op jit(solution)/shard_map/mul | solution.py:44
  28.4 0.7 broadcast_compare_fusion.2
  29.0 0.2 fusion.145
  29.2 0.6 broadcast_compare_fusion.1
  29.8 0.2 fusion.138
  30.0 1.0 add_convert_fusion.3
  31.0 1.8 %add_convert_fusion.1 = bf16[8,128,1024]{2,1,0:T(8,128)(2,1)S(1)} fusion(f32[128,1024]{1,0:T(8,128)} %get-tuple-element.81, f32[8,1024]{1,0:T(8,128)S(1)} %get-tuple-element.90, f32[128,1024]{1,0:T(8,128)} %get-tuple-element.80, f32[8,1024]{1,0:T(8,128)S(1)} %get-tuple-element.89), kind=kLoop, calls=%fused_computation.7 | loop fusion | flops 4194304 | bytes 3211264 | tf_op jit(solution)/shard_map/convert_element_type | solution.py:46
  32.8 6.5 %add_convert_fusion = bf16[16,128,2048]{2,1,0:T(8,128)(2,1)} fusion(f32[128,2048]{1,0:T(8,128)S(1)} %copy-done.2, f32[16,2048]{1,0:T(8,128)S(1)} %get-tuple-element.102, f32[128,2048]{1,0:T(8,128)S(1)} %get-tuple-element.76, f32[16,2048]{1,0:T(8,128)} %get-tuple-element.103), kind=kLoop, calls=%fused_computation | loop fusion | flops 16777216 | bytes 10747904 | tf_op jit(solution)/shard_map/convert_element_type | solution.py:46
  39.3 0.6 and_select_fusion.3
  40.2 0.7 fusion.172
  41.1 1.8 %fusion.15 = f32[4,48,1024]{2,1,0:T(8,128)} fusion(bf16[1024,1024]{1,0:T(8,128)(2,1)S(1)} %bitcast.134, bf16[4,48,256]{2,1,0:T(8,128)(2,1)S(1)} %get-tuple-element.59, bf16[4,48,256]{2,1,0:T(8,128)(2,1)S(1)} %get-tuple-element.60, bf16[4,48,256]{2,1,0:T(8,128)(2,1)S(1)} %get-tuple-element.61, bf16[4,48,256]{2,1,0:T(8,128)(2,1)S(1)} %get-tuple-element.58), kind=kOutput, calls=%fused_computation.19 | convolution fusion | flops 404226048 | bytes 3276800 | tf_op jit(solution)/shard_map/cfm,jm->cfj/dot_general | solution.py:160
  42.9 7.0 %fusion.2 = f32[4,24,2048]{2,1,0:T(8,128)} fusion(bf16[2048,2048]{1,0:T(8,128)(2,1)} %bitcast.131, bf16[4,24,512]{2,1,0:T(8,128)(2,1)S(1)} %get-tuple-element.51, bf16[4,24,512]{2,1,0:T(8,128)(2,1)S(1)} %get-tuple-element.52, bf16[4,24,512]{2,1,0:T(8,128)(2,1)S(1)} %get-tuple-element.53, bf16[4,24,512]{2,1,0:T(8,128)(2,1)S(1)} %get-tuple-element.50), kind=kOutput, calls=%fused_computation.3 | convolution fusion | flops 806879232 | bytes 9568256 | tf_op jit(solution)/shard_map/cfm,jm->cfj/dot_general | solution.py:160
  49.9 7.9 %reduce-scatter.2.cloned.1.call-done = f32[24,4,512]{2,0,1:T(8,128)} async-done(((f32[192,4,512]{2,0,1:T(8,128)}), f32[24,4,512]{2,0,1:T(8,128)}) %reduce-scatter.2.cloned.1.call-update) | async-done | bytes 196624 | tf_op jit(solution)/shard_map/reduce_scatter | solution.py:130
  57.8 1.1 copy.68
  59.0 1.5 %collective-permute-start = (bf16[4,1536]{1,0:T(4,128)(2,1)S(1)}, bf16[4,1536]{1,0:T(4,128)(2,1)S(1)}, u32[]{:S(2)}, u32[]{:S(2)}) collective-permute-start(bf16[4,1536]{1,0:T(4,128)(2,1)S(1)} %slice.287), channel_id=1, source_target_pairs={{1,0},{2,1},{3,2},{4,3},{5,4},{6,5},{7,6},{9,8},{10,9},{11,10},{12... | collective-permute-start | bytes 36872 | tf_op jit(solution)/shard_map/ppermute | solution.py:20
  60.5 1.3 fusion.34
  61.8 0.2 collective-permute-done
  62.2 0.8 fusion.173
  63.1 0.8 fusion.171
  64.1 1.5 %fusion.36 = f32[4,96,512]{2,1,0:T(8,128)S(1)} fusion(bf16[512,512]{1,0:T(8,128)(2,1)S(1)} %bitcast.140, bf16[4,96,128]{2,1,0:T(8,128)(2,1)} %get-tuple-element.71, bf16[4,96,128]{2,1,0:T(8,128)(2,1)} %get-tuple-element.72, bf16[4,96,128]{2,1,0:T(8,128)(2,1)} %get-tuple-element.73, bf16[4,96,128]{2,1,0:T(8,128)(2,1)} %get-tuple-element.70), kind=kOutput, calls=%fused_computation.56 | convolution fusion | flops 202899456 | bytes 1703936 | tf_op jit(solution)/shard_map/cfm,jm->cfj/dot_general | solution.py:166
  65.6 1.0 copy-done.4
  66.6 2.6 %select_reduce_fusion.8 = (f32[4]{0:T(128)S(1)}, f32[4]{0:T(128)S(1)}, f32[4]{0:T(128)S(1)}, f32[4,96,256]{2,1,0:T(8,128)}, f32[4,96,256]{2,1,0:T(8,128)}) fusion(pred[4,96]{1,0:T(4,128)(4,1)} %broadcast_compare_fusion.2, f32[4,96,512]{2,1,0:T(8,128)S(1)} %fusion.36, f32[4,96,512]{2,1,0:T(8,128)} %fusion.34), kind=kLoop, calls=%fused_computation.149 | loop fusion | flops 2064372 | bytes 2359728 | tf_op jit(solution)/shard_map/reduce_sum | solution.py:184
  69.2 0.9 fusion.17
  70.0 1.5 %select_reduce_fusion.7 = (f32[4]{0:T(128)S(1)}, f32[4]{0:T(128)S(1)}, f32[4]{0:T(128)S(1)}, f32[4,48,512]{2,1,0:T(8,128)}, f32[4,48,512]{2,1,0:T(8,128)}) fusion(pred[4,48]{1,0:T(4,128)(4,1)S(1)} %copy-done.25, f32[4,48,1024]{2,1,0:T(8,128)S(1)} %fusion.17, f32[4,48,1024]{2,1,0:T(8,128)S(1)} %copy-done.13), kind=kLoop, calls=%fused_computation.147 | loop fusion | flops 2064372 | bytes 2359536 | tf_op jit(solution)/shard_map/reduce_sum | solution.py:184
  71.5 6.1 %fusion.4 = f32[4,24,2048]{2,1,0:T(8,128)S(1)} fusion(bf16[2048,2048]{1,0:T(8,128)(2,1)} %bitcast.132, bf16[4,24,512]{2,1,0:T(8,128)(2,1)S(1)} %get-tuple-element.55, bf16[4,24,512]{2,1,0:T(8,128)(2,1)S(1)} %get-tuple-element.56, bf16[4,24,512]{2,1,0:T(8,128)(2,1)S(1)} %get-tuple-element.57, bf16[4,24,512]{2,1,0:T(8,128)(2,1)S(1)} %get-tuple-element.54), kind=kOutput, calls=%fused_computation.5 | convolution fusion | flops 806879232 | bytes 9568256 | tf_op jit(solution)/shard_map/cfm,jm->cfj/dot_general | solution.py:166
  77.7 1.4 select_reduce_fusion.6
  79.1 10.6 %all-gather = f32[24,3,4]{2,1,0:T(4,128)S(1)} all-gather(f32[3,3,4]{2,1,0:T(4,128)S(1)} %pad_maximum_fusion.6), channel_id=2, replica_groups=mesh['clip'=4,'seg'=8] {'seg'}, dimensions={0}, use_global_device_ids=true | all-gather | bytes 1296 | tf_op jit(solution)/shard_map/all_gather | solution.py:193
  89.7 0.7 multiply_rsqrt_fusion
  90.4 1.6 %divide_convert_fusion.1 = (bf16[4,24,1024]{2,1,0:T(8,128)(2,1)S(1)}, bf16[4,24,1024]{2,1,0:T(8,128)(2,1)S(1)}) fusion(f32[4,24,2048]{2,1,0:T(8,128)S(1)} %fusion.4, f32[4,24,1024]{2,1,0:T(8,128)} %get-tuple-element.27, f32[4,24,1024]{2,1,0:T(8,128)} %get-tuple-element.28, f32[4]{0:T(128)S(1)} %copy-done.21, f32[4]{0:T(128)S(1)} %get-tuple-element.83, ...), kind=kLoop, calls=%fused_computation.128 | loop fusion | flops 1671168 | bytes 1966208 | tf_op jit(solution)/shard_map/convert
  92.0 4.9 %fusion = f32[4,24,2048]{2,1,0:T(8,128)S(1)} fusion(bf16[2048,2048]{1,0:T(8,128)(2,1)} %bitcast.133, bf16[4,24,1024]{2,1,0:T(8,128)(2,1)S(1)} %get-tuple-element.34, bf16[4,24,1024]{2,1,0:T(8,128)(2,1)S(1)} %get-tuple-element.33), kind=kOutput, calls=%fused_computation.1 | convolution fusion | flops 806092800 | bytes 9568256 | tf_op jit(solution)/shard_map/cfj,jm->cfm/dot_general | solution.py:213
  96.9 1.4 reshape.928
  98.3 3.0 %fusion.167 = (f32[4,24,1,512]{3,2,1,0:T(1,128)S(1)}, f32[4,24,1,512]{3,2,1,0:T(1,128)S(1)}, f32[4,24,1,512]{3,2,1,0:T(1,128)S(1)}, f32[4,24,1,512]{3,2,1,0:T(1,128)S(1)}) fusion(f32[4,24,4,512]{3,2,1,0:T(4,128)} %reshape.928), kind=kLoop, calls=%fused_computation.321 | loop fusion | bytes 1572864 | tf_op jit(solution)/shard_map/slice | solution.py:97
  101.9 0.8 pad_add_fusion
  102.7 0.5 divide_convert_fusion.3
  103.2 0.6 fusion.13
  103.8 0.4 reshape.926
  104.2 0.6 fusion.166
  105.5 0.5 divide_convert_fusion.5
  106.0 0.4 fusion.32
  106.4 0.3 reshape.924
  106.6 0.6 fusion.165
  108.0 1.5 %collective-permute-start.2 = (f32[1]{0:T(128)}, f32[1]{0:T(128)}, u32[]{:S(2)}, u32[]{:S(2)}) collective-permute-start(f32[1]{0:T(128)} %bitcast.26), channel_id=1, source_target_pairs={{0,8},{8,16},{16,24},{24,0},{1,9},{9,17},{17,25},{25,1},{2,10},{10... | collective-permute-start | bytes 20 | tf_op jit(solution)/shard_map/ppermute | solution.py:76
  109.5 1.9 %collective-permute-start.4 = (f32[4,1536]{1,0:T(4,128)S(1)}, f32[4,1536]{1,0:T(4,128)S(1)}, u32[]{:S(2)}, u32[]{:S(2)}) collective-permute-start(f32[4,1536]{1,0:T(4,128)S(1)} %add_add_fusion.3), channel_id=1, source_target_pairs={{0,1},{1,2},{2,3},{3,4},{4,5},{5,6},{6,7},{8,9},{9,10},{10,11},{11... | collective-permute-start | bytes 73736 | tf_op jit(solution)/shard_map/ppermute | solution.py:20
  111.5 1.9 %collective-permute-done.2 = f32[1]{0:T(128)} collective-permute-done((f32[1]{0:T(128)}, f32[1]{0:T(128)}, u32[]{:S(2)}, u32[]{:S(2)}) %collective-permute-start.2) | collective-permute-done | bytes 36 | tf_op jit(solution)/shard_map/ppermute | solution.py:76
  113.4 1.4 %pad_maximum_fusion.7 = f32[2]{0:T(128)S(1)} fusion(f32[1]{0:T(128)} %collective-permute-done.2, f32[1]{0:T(128)} %bitcast.26), kind=kLoop, calls=%fused_computation.288 | loop fusion | flops 2 | bytes 16 | tf_op jit(solution)/shard_map/concatenate | solution.py:76
  114.8 0.6 collective-permute-start.3
  115.4 3.8 %collective-permute-done.3 = f32[2]{0:T(128)S(1)} collective-permute-done((f32[2]{0:T(128)S(1)}, f32[2]{0:T(128)S(1)}, u32[]{:S(2)}, u32[]{:S(2)}) %collective-permute-start.3) | collective-permute-done | bytes 40 | tf_op jit(solution)/shard_map/ppermute | solution.py:76
  119.2 1.4 %pad_maximum_fusion.8 = f32[4]{0:T(128)S(1)} fusion(f32[2]{0:T(128)S(1)} %collective-permute-done.3, f32[1]{0:T(128)} %collective-permute-done.2, f32[1]{0:T(128)} %bitcast.26), kind=kLoop, calls=%fused_computation.289 | loop fusion | flops 8 | bytes 32 | tf_op jit(solution)/shard_map/concatenate | solution.py:76
  120.7 0.7 select_reduce_fusion.9
  122.2 10.3 %all_gather.11 = bf16[4,192,512]{2,1,0:T(8,128)(2,1)S(1)} all-gather(bf16[4,24,512]{2,1,0:T(8,128)(2,1)S(1)} %bitcast.168), channel_id=1, replica_groups=mesh['clip'=4,'seg'=8] {'seg'}, dimensions={1}, use_global_device_ids=true | all-gather | bytes 884736 | tf_op jit(solution)/shard_map/all_gather | solution.py:225
  132.5 0.5 pad_slice_fusion.2
  133.0 1.3 fusion.20
  134.2 0.8 copy.53
  (127 shorter events, 3.4 us)
Async XLA Ops:
  7.2 50.6 %reduce-scatter.2.cloned.1.call-start = ((), (), s32[]{:S(2)}) async-start(), calls=%async_computation.1 | async-start | bytes 1769472 | tf_op jit(solution)/shard_map/reduce_scatter | solution.py:130
  8.5 5.9 %copy-start.18 = (s32[4]{0:T(128)}, s32[4]{0:T(128)S(1)}, u32[]{:S(2)}) copy-start(s32[4]{0:T(128)S(1)} %get-tuple-element.97) | copy-start | bytes 52
  11.2 1.1 copy-start
  14.4 7.9 %copy-start.22 = (s32[4]{0:T(128)S(1)}, s32[4]{0:T(128)}, u32[]{:S(2)}) copy-start(s32[4]{0:T(128)} %param.5) | copy-start | bytes 52
  16.4 23.4 %collective-permute-start.1 = (bf16[4,1536]{1,0:T(4,128)(2,1)S(1)}, bf16[4,1536]{1,0:T(4,128)(2,1)S(1)}, u32[]{:S(2)}, u32[]{:S(2)}) collective-permute-start(bf16[4,1536]{1,0:T(4,128)(2,1)S(1)} %slice.225), channel_id=1, source_target_pairs={{1,0},{2,1},{3,2},{4,3},{5,4},{6,5},{7,6},{9,8},{10,9},{11,10},{12... | collective-permute-start | bytes 36872 | tf_op jit(solution)/shard_map/ppermute | solution.py:20
  28.4 4.4 %copy-start.2 = (f32[128,2048]{1,0:T(8,128)S(1)}, f32[128,2048]{1,0:T(8,128)}, u32[]{:S(2)}) copy-start(f32[128,2048]{1,0:T(8,128)} %get-tuple-element.77) | copy-start | bytes 3145732
  42.9 16.0 %copy-start.19 = (s32[4]{0:T(128)S(1)}, s32[4]{0:T(128)}, u32[]{:S(2)}) copy-start(s32[4]{0:T(128)} %copy-done.18) | copy-start | bytes 52
  42.9 17.7 %copy-start.8 = (bf16[4,128,512]{2,1,0:T(8,128)(2,1)S(1)}, bf16[4,128,512]{2,1,0:T(8,128)(2,1)}, u32[]{:S(2)}) copy-start(bf16[4,128,512]{2,1,0:T(8,128)(2,1)} %add_convert_fusion.3) | copy-start | bytes 1572868
  42.9 17.7 %copy-start.14 = (bf16[4,96,128]{2,1,0:T(8,128)(2,1)S(1)}, bf16[4,96,128]{2,1,0:T(8,128)(2,1)}, u32[]{:S(2)}) copy-start(bf16[4,96,128]{2,1,0:T(8,128)(2,1)} %get-tuple-element.69) | copy-start | bytes 294916
  59.0 3.1 %collective-permute-start = (bf16[4,1536]{1,0:T(4,128)(2,1)S(1)}, bf16[4,1536]{1,0:T(4,128)(2,1)S(1)}, u32[]{:S(2)}, u32[]{:S(2)}) collective-permute-start(bf16[4,1536]{1,0:T(4,128)(2,1)S(1)} %slice.287), channel_id=1, source_target_pairs={{1,0},{2,1},{3,2},{4,3},{5,4},{6,5},{7,6},{9,8},{10,9},{11,10},{12... | collective-permute-start | bytes 36872 | tf_op jit(solution)/shard_map/ppermute | solution.py:20
  64.0 5.2 %copy-start.15 = (bf16[4,48,256]{2,1,0:T(8,128)(2,1)S(1)}, bf16[4,48,256]{2,1,0:T(8,128)(2,1)}, u32[]{:S(2)}) copy-start(bf16[4,48,256]{2,1,0:T(8,128)(2,1)} %get-tuple-element.63) | copy-start | bytes 294916
  64.0 5.2 %copy-start.16 = (bf16[4,48,256]{2,1,0:T(8,128)(2,1)S(1)}, bf16[4,48,256]{2,1,0:T(8,128)(2,1)}, u32[]{:S(2)}) copy-start(bf16[4,48,256]{2,1,0:T(8,128)(2,1)} %get-tuple-element.64) | copy-start | bytes 294916
  64.0 5.2 %copy-start.17 = (bf16[4,48,256]{2,1,0:T(8,128)(2,1)S(1)}, bf16[4,48,256]{2,1,0:T(8,128)(2,1)}, u32[]{:S(2)}) copy-start(bf16[4,48,256]{2,1,0:T(8,128)(2,1)} %get-tuple-element.65) | copy-start | bytes 294916
  64.1 6.0 %copy-start.13 = (f32[4,48,1024]{2,1,0:T(8,128)S(1)}, f32[4,48,1024]{2,1,0:T(8,128)}, u32[]{:S(2)}) copy-start(f32[4,48,1024]{2,1,0:T(8,128)} %fusion.15) | copy-start | bytes 2359300
  64.1 6.0 %copy-start.25 = (pred[4,48]{1,0:T(4,128)(4,1)S(1)}, pred[4,48]{1,0:T(4,128)(4,1)}, u32[]{:S(2)}) copy-start(pred[4,48]{1,0:T(4,128)(4,1)} %broadcast_compare_fusion.1) | copy-start | bytes 580
  65.6 1.0 copy-start.4
  70.0 1.5 %copy-start.6 = (f32[4,48,1024]{2,1,0:T(8,128)}, f32[4,48,1024]{2,1,0:T(8,128)S(1)}, u32[]{:S(2)}) copy-start(f32[4,48,1024]{2,1,0:T(8,128)S(1)} %fusion.17) | copy-start | bytes 2359300
  71.5 6.1 %copy-start.3 = (f32[4,24,2048]{2,1,0:T(8,128)S(1)}, f32[4,24,2048]{2,1,0:T(8,128)}, u32[]{:S(2)}) copy-start(f32[4,24,2048]{2,1,0:T(8,128)} %fusion.2) | copy-start | bytes 2359300
  71.5 6.1 %copy-start.27 = (pred[4,24]{1,0:T(4,128)(4,1)S(1)}, pred[4,24]{1,0:T(4,128)(4,1)}, u32[]{:S(2)}) copy-start(pred[4,24]{1,0:T(4,128)(4,1)} %broadcast_compare_fusion) | copy-start | bytes 292
  71.5 7.5 %copy-start.23 = (s32[4]{0:T(128)S(1)}, s32[4]{0:T(128)}, u32[]{:S(2)}) copy-start(s32[4]{0:T(128)} %param.5) | copy-start | bytes 52
  71.5 18.9 %copy-start.21 = (f32[4]{0:T(128)S(1)}, f32[4]{0:T(128)}, u32[]{:S(2)}) copy-start(f32[4]{0:T(128)} %get-tuple-element.95) | copy-start | bytes 52
  96.8 5.8 %copy-start.26 = (pred[4,48]{1,0:T(4,128)(4,1)S(1)}, pred[4,48]{1,0:T(4,128)(4,1)}, u32[]{:S(2)}) copy-start(pred[4,48]{1,0:T(4,128)(4,1)} %broadcast_compare_fusion.1) | copy-start | bytes 580
  98.3 4.4 %copy-start.7 = (f32[4,48,1024]{2,1,0:T(8,128)S(1)}, f32[4,48,1024]{2,1,0:T(8,128)}, u32[]{:S(2)}) copy-start(f32[4,48,1024]{2,1,0:T(8,128)} %copy-done.6) | copy-start | bytes 2359300
  98.3 4.4 %copy-start.11 = (f32[4,48,512]{2,1,0:T(8,128)S(1)}, f32[4,48,512]{2,1,0:T(8,128)}, u32[]{:S(2)}) copy-start(f32[4,48,512]{2,1,0:T(8,128)} %get-tuple-element.25) | copy-start | bytes 1179652
  98.3 4.4 %copy-start.12 = (f32[4,48,512]{2,1,0:T(8,128)S(1)}, f32[4,48,512]{2,1,0:T(8,128)}, u32[]{:S(2)}) copy-start(f32[4,48,512]{2,1,0:T(8,128)} %get-tuple-element.26) | copy-start | bytes 1179652
  103.2 2.3 %copy-start.24 = (pred[4,96]{1,0:T(4,128)(4,1)S(1)}, pred[4,96]{1,0:T(4,128)(4,1)}, u32[]{:S(2)}) copy-start(pred[4,96]{1,0:T(4,128)(4,1)} %broadcast_compare_fusion.2) | copy-start | bytes 1156
  103.8 1.7 %copy-start.5 = (f32[4,96,512]{2,1,0:T(8,128)S(1)}, f32[4,96,512]{2,1,0:T(8,128)}, u32[]{:S(2)}) copy-start(f32[4,96,512]{2,1,0:T(8,128)} %copy-done.4) | copy-start | bytes 2359300
  103.8 1.7 %copy-start.9 = (f32[4,96,256]{2,1,0:T(8,128)S(1)}, f32[4,96,256]{2,1,0:T(8,128)}, u32[]{:S(2)}) copy-start(f32[4,96,256]{2,1,0:T(8,128)} %get-tuple-element.23) | copy-start | bytes 1179652
  104.2 1.3 copy-start.10
  106.0 14.7 %copy-start.28 = (s32[4]{0:T(128)S(1)}, s32[4]{0:T(128)}, u32[]{:S(2)}) copy-start(s32[4]{0:T(128)} %and_select_fusion.3) | copy-start | bytes 52
  106.0 16.0 %slice-start = ((f32[4,27,512]{2,0,1:T(4,128)}), f32[4,24,512]{2,0,1:T(4,128)S(1)}, s32[]{:S(2)}) async-start(f32[4,27,512]{2,0,1:T(4,128)} %pad_add_fusion), calls=%async_computation.2 | async-start | bytes 393216 | tf_op jit(solution)/shard_map/slice | solution.py:217
  106.0 16.0 %copy-start.20 = (s32[4]{0:T(128)S(1)}, s32[4]{0:T(128)}, u32[]{:S(2)}) copy-start(s32[4]{0:T(128)} %copy-done.18) | copy-start | bytes 52
  107.6 25.4 %copy-start.1 = (bf16[16,16,2048]{2,1,0:T(8,128)(2,1)S(1)}, bf16[16,16,2048]{2,1,0:T(8,128)(2,1)}, u32[]{:S(2)}) copy-start(bf16[16,16,2048]{2,1,0:T(8,128)(2,1)} %copy-done) | copy-start | bytes 3145732
  108.0 5.4 %collective-permute-start.2 = (f32[1]{0:T(128)}, f32[1]{0:T(128)}, u32[]{:S(2)}, u32[]{:S(2)}) collective-permute-start(f32[1]{0:T(128)} %bitcast.26), channel_id=1, source_target_pairs={{0,8},{8,16},{16,24},{24,0},{1,9},{9,17},{17,25},{25,1},{2,10},{10... | collective-permute-start | bytes 20 | tf_op jit(solution)/shard_map/ppermute | solution.py:76
  109.5 12.5 %collective-permute-start.4 = (f32[4,1536]{1,0:T(4,128)S(1)}, f32[4,1536]{1,0:T(4,128)S(1)}, u32[]{:S(2)}, u32[]{:S(2)}) collective-permute-start(f32[4,1536]{1,0:T(4,128)S(1)} %add_add_fusion.3), channel_id=1, source_target_pairs={{0,1},{1,2},{2,3},{3,4},{4,5},{5,6},{6,7},{8,9},{9,10},{10,11},{11... | collective-permute-start | bytes 73736 | tf_op jit(solution)/shard_map/ppermute | solution.py:20
  114.8 4.4 %collective-permute-start.3 = (f32[2]{0:T(128)S(1)}, f32[2]{0:T(128)S(1)}, u32[]{:S(2)}, u32[]{:S(2)}) collective-permute-start(f32[2]{0:T(128)S(1)} %pad_maximum_fusion.7), channel_id=1, source_target_pairs={{0,16},{8,24},{16,0},{24,8},{1,17},{9,25},{17,1},{25,9},{2,18},{10... | collective-permute-start | bytes 32 | tf_op jit(solution)/shard_map/ppermute | solution.py:76
Sparse Core Ops, SparseCore 0:
  16.5 41.2 reduce-scatter.1

commit v6 on v5

--- a/solution.py
+++ b/solution.py
@@ -66,29 +66,19 @@
     return lax.optimization_barrier(table.reshape(2, band_count, NFFT))
 
 
-def gathered_sum(value, axis):
+def ring_gathered(value, axis):
     size = lax.axis_size(axis)
     here = lax.axis_index(axis)
-    held = value[None]
-    while held.shape[0] < size and size % (2 * held.shape[0]) == 0:
-        distance = held.shape[0]
+    held = [value]
+    for distance in range(1, size):
         route = [(i, (i + distance) % size) for i in range(size)]
-        held = jnp.concatenate([held, lax.ppermute(held, axis, route)], axis=0)
-    for distance in range(held.shape[0], size):
-        route = [(i, (i + distance) % size) for i in range(size)]
-        held = jnp.concatenate([held, lax.ppermute(value, axis, route)[None]], axis=0)
+        held.append(lax.ppermute(value, axis, route))
+    held = jnp.stack(held)
     source = (here - jnp.arange(size, dtype=jnp.int32)) % size
-    slots = jnp.sum(
-        jnp.where(
-            (source[:, None] == jnp.arange(size, dtype=jnp.int32)[None, :]).reshape(
-                (size, size) + (1,) * value.ndim
-            ),
-            held[:, None],
-            0.0,
-        ),
-        axis=0,
-    )
-    return jnp.sum(slots, axis=0)
+    pick = source[:, None] == jnp.arange(size, dtype=jnp.int32)[None, :]
+    return jnp.sum(
+        jnp.where(pick.reshape((size, size) + (1,) * value.ndim), held[:, None], 0.0), axis=0
+    )
 
 
 def spread_parts(quarters):
@@ -190,10 +180,12 @@
     spreads = jnp.stack(spread_list)
     energies = jnp.stack(energy_list)
     logterms = jnp.stack(logterm_list)
-    parts = lax.all_gather(jnp.stack([spreads, energies, logterms]), "seg", axis=0, tiled=False)
-    spreads, energies, logterms = jnp.sum(parts, axis=0)
-    own_loss = jnp.sum(jnp.sqrt((spreads + EPS_RATIO) / energies) + logterms)
-    loss = gathered_sum(own_loss, "clip") / (3 * clip_count * lax.axis_size("clip"))
+    groups = ring_gathered(jnp.stack([spreads, energies, logterms]), "clip")
+    totals = jnp.sum(lax.all_gather(groups, "seg", axis=0, tiled=False), axis=0)
+    loss = jnp.sum(jnp.sqrt((totals[:, 0] + EPS_RATIO) / totals[:, 1]) + totals[:, 2]) / (
+        3 * clip_count * lax.axis_size("clip")
+    )
+    spreads, energies, logterms = totals[lax.axis_index("clip")]
     ratio_weight = 1.0 / jnp.sqrt((spreads + EPS_RATIO) * energies)
     gradient = jnp.zeros((clip_count, samples), jnp.float32)
     extras = []

time: 144 us -> 145 us (level)
  blocking collectives: 20.9 us -> 23.6 us
  starting transfers between devices: 7.14 us -> 9.77 us
  other arithmetic: 42.7 us -> 40.2 us
    concatenate x2 -> x0, other arithmetic: 2.87 us -> none  [gathered_sum(): held = jnp.concatenate([held, lax.ppermute(held, axis, route)], axis=0)]
    ppermute x2 -> x3, starting transfers between devices: 2.17 us -> 4.49 us  [ring_gathered(): held.append(lax.ppermute(value, axis, route))]
    all_gather x1, blocking collectives: 10.3 us -> 12 us  [body(): portion = lax.all_gather(grad_hops, 'seg', axis=1, tiled=True)]
    ppermute x2 -> x3, waiting for transfers between devices: 5.69 us -> 4.33 us  [ring_gathered(): held.append(lax.ppermute(value, axis, route))]
  transfers between devices with their start and end apart: 6 -> 7, of which waited for: 4 -> 5; matrix products, arithmetic and copies ran while one was open for 26% -> 23% of each run, Pallas kernels for 0% -> 0%
where the time goes in v6:
time: 145 us
  other arithmetic  40.2 us (28%)
  matrix products  27.6 us (19%)
  blocking collectives  23.6 us (16%)
  between operations  16.8 us (12%)
  local copies, waits for them, and re-layouts  14.1 us (10%)
  waiting for transfers between devices  12.4 us (9%)
  starting transfers between devices  9.77 us (7%)
    all_gather x1, blocking collectives, body(): portion = lax.all_gather(grad_hops, 'seg', axis=1, tiled=True)  12 us
    all_gather x1, blocking collectives, body(): totals = jnp.sum(lax.all_gather(groups, 'seg', axis=0, tiled=False), axis=0)  11.6 us
    dot_general x3, matrix products, body(): jnp.einsum('cfm,jm->cfj', framed(clean, clean_beyond[:, :3 * stride], str...  10.1 us
    mul x3, other arithmetic, analysis_table(): fine_cos, fine_sin = (part * scale for part in fine)  9.56 us
    convert_element_type x3, other arithmetic, analysis_table(): table = entry_value.astype(jnp.bfloat16)  9.28 us
    dot_general x3, matrix products, body(): jnp.einsum('cfm,jm->cfj', framed(est_wave, est_beyond[:, :3 * stride], st...  8.44 us
    reduce_scatter x1, waiting for transfers between devices, body(): lax.psum_scatter(sum((framed_sig[3 - quarter:3 - quarter + rows_here * la...  7.86 us
    dot_general x3, matrix products, body(): jnp.einsum('cfj,jm->cfm', grad_x, table, preferred_element_type=jnp.float32)  5.81 us
  transfers between devices with their start and end apart: 7, of which 5 were waited for; matrix products, arithmetic and copies ran while one was open for 23% of the time, Pallas kernels for 0%

profile of v6, /device:TPU:0, one launch (start us, length us, event | category | flops | bytes accessed | tf_op | source)
XLA Modules:
  0.0 144.6 jit_solution(7291212851724479341)
XLA Ops:
  7.3 1.2 multiply_convert_fusion
  8.5 0.5 cosine_multiply_fusion.3
  9.0 1.9 %fusion.128 = (f32[16,2048]{1,0:T(8,128)S(1)}, f32[16,2048]{1,0:T(8,128)S(1)}, f32[16,2048]{1,0:T(8,128)S(1)}, f32[16,2048]{1,0:T(8,128)}) fusion(s32[16]{0:T(128)S(1)} %get-tuple-element.104, pred[16]{0:T(512)(128)(4,1)S(1)} %iota_compare_fusion.3, s32[16]{0:T(128)S(1)} %get-tuple-element.105), kind=kLoop, calls=%fused_computation.222 | loop fusion | flops 1179648 | bytes 524432 | tf_op jit(solution)/shard_map/jit(_where)/select_n | solution.py:62
  10.9 0.2 add_convert_fusion.2
  11.2 1.1 compare_select_fusion.2
  12.3 2.0 %convolution_bitcast_fusion = f32[195,4,2048]{2,0,1:T(8,128)S(1)} fusion(bf16[2,128,2048]{2,1,0:T(8,128)(2,1)S(1)} %bitcast.141, bf16[4,2,128,192]{2,3,1,0:T(8,128)(2,1)} %param.3), kind=kOutput, calls=%fused_computation.8 | convolution fusion | flops 817889280 | bytes 7831552 | tf_op jit(solution)/shard_map/crbf,rbm->fcm/dot_general | solution.py:117
  14.4 2.0 %slice_add_fusion = f32[192,4,512]{2,0,1:T(8,128)} fusion(f32[195,4,2048]{2,0,1:T(8,128)S(1)} %convolution_bitcast_fusion), kind=kLoop, calls=%fused_computation.24 | loop fusion | flops 1179648 | bytes 7864320 | tf_op jit(solution)/shard_map/add | solution.py:121
  16.4 1.5 %collective-permute-start.1 = (bf16[4,1536]{1,0:T(4,128)(2,1)S(1)}, bf16[4,1536]{1,0:T(4,128)(2,1)S(1)}, u32[]{:S(2)}, u32[]{:S(2)}) collective-permute-start(bf16[4,1536]{1,0:T(4,128)(2,1)S(1)} %slice.236), channel_id=1, source_target_pairs={{1,0},{2,1},{3,2},{4,3},{5,4},{6,5},{7,6},{9,8},{10,9},{11,10},{12... | collective-permute-start | bytes 36872 | tf_op jit(solution)/shard_map/ppermute | solution.py:20
  18.1 1.1 cosine_multiply_fusion.2
  19.2 3.1 %cosine_multiply_fusion.1 = (f32[128,1024]{1,0:T(8,128)}, f32[128,1024]{1,0:T(8,128)}) fusion(f32[1024]{0:T(1024)S(1)} %subtract_multiply_fusion), kind=kLoop, calls=%fused_computation.59 | loop fusion | flops 2097152 | bytes 1052672 | tf_op jit(solution)/shard_map/mul | solution.py:44
  22.3 0.7 broadcast_compare_fusion
  22.9 5.4 %cosine_multiply_fusion = (f32[128,2048]{1,0:T(8,128)S(1)}, f32[128,2048]{1,0:T(8,128)}) fusion(f32[2048]{0:T(1024)S(1)} %fusion.144), kind=kLoop, calls=%fused_computation.38 | loop fusion | flops 4194304 | bytes 2105344 | tf_op jit(solution)/shard_map/mul | solution.py:44
  28.4 0.6 broadcast_compare_fusion.2
  29.0 0.2 fusion.146
  29.2 0.6 broadcast_compare_fusion.1
  29.7 0.2 fusion.138
  30.0 1.0 add_convert_fusion.3
  30.9 1.8 %add_convert_fusion.1 = bf16[8,128,1024]{2,1,0:T(8,128)(2,1)S(1)} fusion(f32[128,1024]{1,0:T(8,128)} %get-tuple-element.81, f32[8,1024]{1,0:T(8,128)S(1)} %get-tuple-element.90, f32[128,1024]{1,0:T(8,128)} %get-tuple-element.80, f32[8,1024]{1,0:T(8,128)S(1)} %get-tuple-element.89), kind=kLoop, calls=%fused_computation.7 | loop fusion | flops 4194304 | bytes 3211264 | tf_op jit(solution)/shard_map/convert_element_type | solution.py:46
  32.7 6.5 %add_convert_fusion = bf16[16,128,2048]{2,1,0:T(8,128)(2,1)} fusion(f32[128,2048]{1,0:T(8,128)S(1)} %copy-done.2, f32[16,2048]{1,0:T(8,128)S(1)} %get-tuple-element.102, f32[128,2048]{1,0:T(8,128)S(1)} %get-tuple-element.76, f32[16,2048]{1,0:T(8,128)} %get-tuple-element.103), kind=kLoop, calls=%fused_computation | loop fusion | flops 16777216 | bytes 10747904 | tf_op jit(solution)/shard_map/convert_element_type | solution.py:46
  39.3 0.6 iota_compare_fusion
  40.2 0.7 fusion.174
  41.1 1.8 %fusion.15 = f32[4,48,1024]{2,1,0:T(8,128)} fusion(bf16[1024,1024]{1,0:T(8,128)(2,1)S(1)} %bitcast.138, bf16[4,48,256]{2,1,0:T(8,128)(2,1)S(1)} %get-tuple-element.59, bf16[4,48,256]{2,1,0:T(8,128)(2,1)S(1)} %get-tuple-element.60, bf16[4,48,256]{2,1,0:T(8,128)(2,1)S(1)} %get-tuple-element.61, bf16[4,48,256]{2,1,0:T(8,128)(2,1)S(1)} %get-tuple-element.58), kind=kOutput, calls=%fused_computation.19 | convolution fusion | flops 404226048 | bytes 3276800 | tf_op jit(solution)/shard_map/cfm,jm->cfj/dot_general | solution.py:150
  42.9 7.1 %fusion.2 = f32[4,24,2048]{2,1,0:T(8,128)} fusion(bf16[2048,2048]{1,0:T(8,128)(2,1)} %bitcast.135, bf16[4,24,512]{2,1,0:T(8,128)(2,1)S(1)} %get-tuple-element.51, bf16[4,24,512]{2,1,0:T(8,128)(2,1)S(1)} %get-tuple-element.52, bf16[4,24,512]{2,1,0:T(8,128)(2,1)S(1)} %get-tuple-element.53, bf16[4,24,512]{2,1,0:T(8,128)(2,1)S(1)} %get-tuple-element.50), kind=kOutput, calls=%fused_computation.3 | convolution fusion | flops 806879232 | bytes 9568256 | tf_op jit(solution)/shard_map/cfm,jm->cfj/dot_general | solution.py:150
  49.9 7.9 %reduce-scatter.2.cloned.1.call-done = f32[24,4,512]{2,0,1:T(8,128)} async-done(((f32[192,4,512]{2,0,1:T(8,128)}), f32[24,4,512]{2,0,1:T(8,128)}) %reduce-scatter.2.cloned.1.call-update) | async-done | bytes 196624 | tf_op jit(solution)/shard_map/reduce_scatter | solution.py:120
  57.8 1.1 copy.69
  59.0 1.5 %collective-permute-start = (bf16[4,1536]{1,0:T(4,128)(2,1)S(1)}, bf16[4,1536]{1,0:T(4,128)(2,1)S(1)}, u32[]{:S(2)}, u32[]{:S(2)}) collective-permute-start(bf16[4,1536]{1,0:T(4,128)(2,1)S(1)} %slice.301), channel_id=1, source_target_pairs={{1,0},{2,1},{3,2},{4,3},{5,4},{6,5},{7,6},{9,8},{10,9},{11,10},{12... | collective-permute-start | bytes 36872 | tf_op jit(solution)/shard_map/ppermute | solution.py:20
  60.5 1.3 fusion.34
  61.8 0.2 collective-permute-done
  62.2 0.8 fusion.175
  63.1 0.8 fusion.173
  64.0 1.5 %fusion.36 = f32[4,96,512]{2,1,0:T(8,128)S(1)} fusion(bf16[512,512]{1,0:T(8,128)(2,1)S(1)} %bitcast.144, bf16[4,96,128]{2,1,0:T(8,128)(2,1)} %get-tuple-element.71, bf16[4,96,128]{2,1,0:T(8,128)(2,1)} %get-tuple-element.72, bf16[4,96,128]{2,1,0:T(8,128)(2,1)} %get-tuple-element.73, bf16[4,96,128]{2,1,0:T(8,128)(2,1)} %get-tuple-element.70), kind=kOutput, calls=%fused_computation.56 | convolution fusion | flops 202899456 | bytes 1703936 | tf_op jit(solution)/shard_map/cfm,jm->cfj/dot_general | solution.py:156
  65.6 1.0 copy-done.4
  66.5 2.6 %select_reduce_fusion.8 = (f32[4]{0:T(128)S(1)}, f32[4]{0:T(128)S(1)}, f32[4]{0:T(128)S(1)}, f32[4,96,256]{2,1,0:T(8,128)}, f32[4,96,256]{2,1,0:T(8,128)}) fusion(pred[4,96]{1,0:T(4,128)(4,1)} %broadcast_compare_fusion.2, f32[4,96,512]{2,1,0:T(8,128)S(1)} %fusion.36, f32[4,96,512]{2,1,0:T(8,128)} %fusion.34), kind=kLoop, calls=%fused_computation.149 | loop fusion | flops 2064372 | bytes 2359728 | tf_op jit(solution)/shard_map/reduce_sum | solution.py:174
  69.1 0.8 fusion.17
  70.0 1.5 %select_reduce_fusion.7 = (f32[4]{0:T(128)S(1)}, f32[4]{0:T(128)S(1)}, f32[4]{0:T(128)S(1)}, f32[4,48,512]{2,1,0:T(8,128)}, f32[4,48,512]{2,1,0:T(8,128)}) fusion(pred[4,48]{1,0:T(4,128)(4,1)S(1)} %copy-done.25, f32[4,48,1024]{2,1,0:T(8,128)S(1)} %fusion.17, f32[4,48,1024]{2,1,0:T(8,128)S(1)} %copy-done.13), kind=kLoop, calls=%fused_computation.147 | loop fusion | flops 2064372 | bytes 2359536 | tf_op jit(solution)/shard_map/reduce_sum | solution.py:174
  71.5 6.1 %fusion.4 = f32[4,24,2048]{2,1,0:T(8,128)S(1)} fusion(bf16[2048,2048]{1,0:T(8,128)(2,1)} %bitcast.136, bf16[4,24,512]{2,1,0:T(8,128)(2,1)S(1)} %get-tuple-element.55, bf16[4,24,512]{2,1,0:T(8,128)(2,1)S(1)} %get-tuple-element.56, bf16[4,24,512]{2,1,0:T(8,128)(2,1)S(1)} %get-tuple-element.57, bf16[4,24,512]{2,1,0:T(8,128)(2,1)S(1)} %get-tuple-element.54), kind=kOutput, calls=%fused_computation.5 | convolution fusion | flops 806879232 | bytes 9568256 | tf_op jit(solution)/shard_map/cfm,jm->cfj/dot_general | solution.py:156
  77.7 1.4 select_reduce_fusion.6
  79.1 3.4 %collective-permute-start.4 = (f32[3,3,4]{2,1,0:T(4,128)S(1)}, f32[3,3,4]{2,1,0:T(4,128)S(1)}, u32[]{:S(2)}, u32[]{:S(2)}) collective-permute-start(f32[3,3,4]{2,1,0:T(4,128)S(1)} %get-tuple-element.79), channel_id=1, source_target_pairs={{0,24},{8,0},{16,8},{24,16},{1,25},{9,1},{17,9},{25,17},{2,26},{10... | collective-permute-start | bytes 440 | tf_op jit(solution)/shard_map/ppermute | solution.py:75
  82.5 1.1 collective-permute-start.2
  83.6 0.2 collective-permute-done.4
  83.8 3.2 %collective-permute-done.3 = f32[3,3,4]{2,1,0:T(4,128)S(1)} collective-permute-done((f32[3,3,4]{2,1,0:T(4,128)S(1)}, f32[3,3,4]{2,1,0:T(4,128)S(1)}, u32[]{:S(2)}, u32[]{:S(2)}) %collective-permute-start.3) | collective-permute-done | bytes 176 | tf_op jit(solution)/shard_map/ppermute | solution.py:75
  87.0 0.9 collective-permute-done.2
  88.1 11.6 %all-gather = f32[32,3,3,4]{3,2,1,0:T(4,128)} all-gather(f32[4,3,3,4]{3,2,1,0:T(4,128)S(1)} %copy.41), channel_id=2, replica_groups=mesh['clip'=4,'seg'=8] {'seg'}, dimensions={0}, use_global_device_ids=true | all-gather | bytes 5184 | tf_op jit(solution)/shard_map/all_gather | solution.py:184
  99.7 1.0 reduce_sum.118
  100.7 1.6 %divide_convert_fusion.1 = (bf16[4,24,1024]{2,1,0:T(8,128)(2,1)S(1)}, bf16[4,24,1024]{2,1,0:T(8,128)(2,1)S(1)}) fusion(f32[4,24,2048]{2,1,0:T(8,128)S(1)} %fusion.4, f32[4,24,1024]{2,1,0:T(8,128)} %get-tuple-element.27, f32[4,24,1024]{2,1,0:T(8,128)} %get-tuple-element.28, f32[4]{0:T(128)S(1)} %copy-done.21, f32[4]{0:T(128)S(1)} %get-tuple-element.83, ...), kind=kLoop, calls=%fused_computation.128 | loop fusion | flops 1671168 | bytes 1966208 | tf_op jit(solution)/shard_map/convert
  102.3 4.9 %fusion = f32[4,24,2048]{2,1,0:T(8,128)S(1)} fusion(bf16[2048,2048]{1,0:T(8,128)(2,1)} %bitcast.137, bf16[4,24,1024]{2,1,0:T(8,128)(2,1)S(1)} %get-tuple-element.34, bf16[4,24,1024]{2,1,0:T(8,128)(2,1)S(1)} %get-tuple-element.33), kind=kOutput, calls=%fused_computation.1 | convolution fusion | flops 806092800 | bytes 9568256 | tf_op jit(solution)/shard_map/cfj,jm->cfm/dot_general | solution.py:205
  107.2 1.4 reshape.955
  108.6 3.0 %fusion.169 = (f32[4,24,1,512]{3,2,1,0:T(1,128)S(1)}, f32[4,24,1,512]{3,2,1,0:T(1,128)S(1)}, f32[4,24,1,512]{3,2,1,0:T(1,128)S(1)}, f32[4,24,1,512]{3,2,1,0:T(1,128)S(1)}) fusion(f32[4,24,4,512]{3,2,1,0:T(4,128)} %reshape.955), kind=kLoop, calls=%fused_computation.324 | loop fusion | bytes 1572864 | tf_op jit(solution)/shard_map/slice | solution.py:87
  111.7 0.1 copy.84
  112.2 0.8 pad_add_fusion
  113.0 0.5 divide_convert_fusion.3
  113.5 0.6 fusion.13
  114.2 0.4 reshape.953
  114.5 0.6 fusion.168
  115.8 0.5 divide_convert_fusion.5
  116.3 0.4 fusion.32
  116.7 0.3 reshape.951
  117.0 0.6 fusion.167
  118.3 2.3 %collective-permute-start.5 = (f32[4,1536]{1,0:T(4,128)S(1)}, f32[4,1536]{1,0:T(4,128)S(1)}, u32[]{:S(2)}, u32[]{:S(2)}) collective-permute-start(f32[4,1536]{1,0:T(4,128)S(1)} %add_add_fusion.3), channel_id=1, source_target_pairs={{0,1},{1,2},{2,3},{3,4},{4,5},{5,6},{6,7},{8,9},{9,10},{10,11},{11... | collective-permute-start | bytes 73736 | tf_op jit(solution)/shard_map/ppermute | solution.py:20
  120.6 0.6 fusion.143
  122.1 12.0 %all_gather.11 = bf16[4,192,512]{2,1,0:T(8,128)(2,1)S(1)} all-gather(bf16[4,24,512]{2,1,0:T(8,128)(2,1)S(1)} %bitcast.173), channel_id=1, replica_groups=mesh['clip'=4,'seg'=8] {'seg'}, dimensions={1}, use_global_device_ids=true | all-gather | bytes 884736 | tf_op jit(solution)/shard_map/all_gather | solution.py:217
  134.0 0.5 pad_slice_fusion.2
  134.5 1.3 fusion.20
  135.8 0.8 copy.54
  (131 shorter events, 3.4 us)
Async XLA Ops:
  7.2 50.6 %reduce-scatter.2.cloned.1.call-start = ((), (), s32[]{:S(2)}) async-start(), calls=%async_computation.1 | async-start | bytes 1769472 | tf_op jit(solution)/shard_map/reduce_scatter | solution.py:120
  8.5 5.9 %copy-start.18 = (s32[4]{0:T(128)}, s32[4]{0:T(128)S(1)}, u32[]{:S(2)}) copy-start(s32[4]{0:T(128)S(1)} %get-tuple-element.97) | copy-start | bytes 52
  11.2 1.1 copy-start
  14.4 7.9 %copy-start.22 = (s32[4]{0:T(128)S(1)}, s32[4]{0:T(128)}, u32[]{:S(2)}) copy-start(s32[4]{0:T(128)} %param.5) | copy-start | bytes 52
  16.4 23.4 %collective-permute-start.1 = (bf16[4,1536]{1,0:T(4,128)(2,1)S(1)}, bf16[4,1536]{1,0:T(4,128)(2,1)S(1)}, u32[]{:S(2)}, u32[]{:S(2)}) collective-permute-start(bf16[4,1536]{1,0:T(4,128)(2,1)S(1)} %slice.236), channel_id=1, source_target_pairs={{1,0},{2,1},{3,2},{4,3},{5,4},{6,5},{7,6},{9,8},{10,9},{11,10},{12... | collective-permute-start | bytes 36872 | tf_op jit(solution)/shard_map/ppermute | solution.py:20
  28.4 4.4 %copy-start.2 = (f32[128,2048]{1,0:T(8,128)S(1)}, f32[128,2048]{1,0:T(8,128)}, u32[]{:S(2)}) copy-start(f32[128,2048]{1,0:T(8,128)} %get-tuple-element.77) | copy-start | bytes 3145732
  42.8 16.0 %copy-start.19 = (s32[4]{0:T(128)S(1)}, s32[4]{0:T(128)}, u32[]{:S(2)}) copy-start(s32[4]{0:T(128)} %copy-done.18) | copy-start | bytes 52
  42.8 17.7 %copy-start.8 = (bf16[4,128,512]{2,1,0:T(8,128)(2,1)S(1)}, bf16[4,128,512]{2,1,0:T(8,128)(2,1)}, u32[]{:S(2)}) copy-start(bf16[4,128,512]{2,1,0:T(8,128)(2,1)} %add_convert_fusion.3) | copy-start | bytes 1572868
  42.8 17.7 %copy-start.14 = (bf16[4,96,128]{2,1,0:T(8,128)(2,1)S(1)}, bf16[4,96,128]{2,1,0:T(8,128)(2,1)}, u32[]{:S(2)}) copy-start(bf16[4,96,128]{2,1,0:T(8,128)(2,1)} %get-tuple-element.69) | copy-start | bytes 294916
  59.0 3.1 %collective-permute-start = (bf16[4,1536]{1,0:T(4,128)(2,1)S(1)}, bf16[4,1536]{1,0:T(4,128)(2,1)S(1)}, u32[]{:S(2)}, u32[]{:S(2)}) collective-permute-start(bf16[4,1536]{1,0:T(4,128)(2,1)S(1)} %slice.301), channel_id=1, source_target_pairs={{1,0},{2,1},{3,2},{4,3},{5,4},{6,5},{7,6},{9,8},{10,9},{11,10},{12... | collective-permute-start | bytes 36872 | tf_op jit(solution)/shard_map/ppermute | solution.py:20
  63.9 5.2 %copy-start.15 = (bf16[4,48,256]{2,1,0:T(8,128)(2,1)S(1)}, bf16[4,48,256]{2,1,0:T(8,128)(2,1)}, u32[]{:S(2)}) copy-start(bf16[4,48,256]{2,1,0:T(8,128)(2,1)} %get-tuple-element.63) | copy-start | bytes 294916
  63.9 5.2 %copy-start.16 = (bf16[4,48,256]{2,1,0:T(8,128)(2,1)S(1)}, bf16[4,48,256]{2,1,0:T(8,128)(2,1)}, u32[]{:S(2)}) copy-start(bf16[4,48,256]{2,1,0:T(8,128)(2,1)} %get-tuple-element.64) | copy-start | bytes 294916
  64.0 5.2 %copy-start.17 = (bf16[4,48,256]{2,1,0:T(8,128)(2,1)S(1)}, bf16[4,48,256]{2,1,0:T(8,128)(2,1)}, u32[]{:S(2)}) copy-start(bf16[4,48,256]{2,1,0:T(8,128)(2,1)} %get-tuple-element.65) | copy-start | bytes 294916
  64.0 6.0 %copy-start.13 = (f32[4,48,1024]{2,1,0:T(8,128)S(1)}, f32[4,48,1024]{2,1,0:T(8,128)}, u32[]{:S(2)}) copy-start(f32[4,48,1024]{2,1,0:T(8,128)} %fusion.15) | copy-start | bytes 2359300
  64.0 6.0 %copy-start.25 = (pred[4,48]{1,0:T(4,128)(4,1)S(1)}, pred[4,48]{1,0:T(4,128)(4,1)}, u32[]{:S(2)}) copy-start(pred[4,48]{1,0:T(4,128)(4,1)} %broadcast_compare_fusion.1) | copy-start | bytes 580
  65.6 1.0 copy-start.4
  70.0 1.5 %copy-start.6 = (f32[4,48,1024]{2,1,0:T(8,128)}, f32[4,48,1024]{2,1,0:T(8,128)S(1)}, u32[]{:S(2)}) copy-start(f32[4,48,1024]{2,1,0:T(8,128)S(1)} %fusion.17) | copy-start | bytes 2359300
  71.5 6.1 %copy-start.3 = (f32[4,24,2048]{2,1,0:T(8,128)S(1)}, f32[4,24,2048]{2,1,0:T(8,128)}, u32[]{:S(2)}) copy-start(f32[4,24,2048]{2,1,0:T(8,128)} %fusion.2) | copy-start | bytes 2359300
  71.5 6.1 %copy-start.27 = (pred[4,24]{1,0:T(4,128)(4,1)S(1)}, pred[4,24]{1,0:T(4,128)(4,1)}, u32[]{:S(2)}) copy-start(pred[4,24]{1,0:T(4,128)(4,1)} %broadcast_compare_fusion) | copy-start | bytes 292
  71.5 7.5 %copy-start.23 = (s32[4]{0:T(128)S(1)}, s32[4]{0:T(128)}, u32[]{:S(2)}) copy-start(s32[4]{0:T(128)} %param.5) | copy-start | bytes 52
  71.5 16.4 %copy-start.28 = (pred[4,4]{1,0:T(4,128)(4,1)S(1)}, pred[4,4]{1,0:T(4,128)(4,1)}, u32[]{:S(2)}) copy-start(pred[4,4]{1,0:T(4,128)(4,1)} %iota_compare_fusion) | copy-start | bytes 52
  71.5 29.2 %copy-start.21 = (f32[4]{0:T(128)S(1)}, f32[4]{0:T(128)}, u32[]{:S(2)}) copy-start(f32[4]{0:T(128)} %get-tuple-element.95) | copy-start | bytes 52
  79.1 4.7 %collective-permute-start.4 = (f32[3,3,4]{2,1,0:T(4,128)S(1)}, f32[3,3,4]{2,1,0:T(4,128)S(1)}, u32[]{:S(2)}, u32[]{:S(2)}) collective-permute-start(f32[3,3,4]{2,1,0:T(4,128)S(1)} %get-tuple-element.79), channel_id=1, source_target_pairs={{0,24},{8,0},{16,8},{24,16},{1,25},{9,1},{17,9},{25,17},{2,26},{10... | collective-permute-start | bytes 440 | tf_op jit(solution)/shard_map/ppermute | solution.py:75
  82.5 4.5 %collective-permute-start.3 = (f32[3,3,4]{2,1,0:T(4,128)S(1)}, f32[3,3,4]{2,1,0:T(4,128)S(1)}, u32[]{:S(2)}, u32[]{:S(2)}) collective-permute-start(f32[3,3,4]{2,1,0:T(4,128)S(1)} %get-tuple-element.79), channel_id=1, source_target_pairs={{0,16},{8,24},{16,0},{24,8},{1,17},{9,25},{17,1},{25,9},{2,18},{10... | collective-permute-start | bytes 440 | tf_op jit(solution)/shard_map/ppermute | solution.py:75
  82.5 5.4 %collective-permute-start.2 = (f32[3,3,4]{2,1,0:T(4,128)S(1)}, f32[3,3,4]{2,1,0:T(4,128)S(1)}, u32[]{:S(2)}, u32[]{:S(2)}) collective-permute-start(f32[3,3,4]{2,1,0:T(4,128)S(1)} %get-tuple-element.79), channel_id=1, source_target_pairs={{0,8},{8,16},{16,24},{24,0},{1,9},{9,17},{17,25},{25,1},{2,10},{10... | collective-permute-start | bytes 440 | tf_op jit(solution)/shard_map/ppermute | solution.py:75
  107.2 5.8 %copy-start.26 = (pred[4,48]{1,0:T(4,128)(4,1)S(1)}, pred[4,48]{1,0:T(4,128)(4,1)}, u32[]{:S(2)}) copy-start(pred[4,48]{1,0:T(4,128)(4,1)} %broadcast_compare_fusion.1) | copy-start | bytes 580
  108.6 4.4 %copy-start.7 = (f32[4,48,1024]{2,1,0:T(8,128)S(1)}, f32[4,48,1024]{2,1,0:T(8,128)}, u32[]{:S(2)}) copy-start(f32[4,48,1024]{2,1,0:T(8,128)} %copy-done.6) | copy-start | bytes 2359300
  108.6 4.4 %copy-start.11 = (f32[4,48,512]{2,1,0:T(8,128)S(1)}, f32[4,48,512]{2,1,0:T(8,128)}, u32[]{:S(2)}) copy-start(f32[4,48,512]{2,1,0:T(8,128)} %get-tuple-element.25) | copy-start | bytes 1179652
  108.6 4.4 %copy-start.12 = (f32[4,48,512]{2,1,0:T(8,128)S(1)}, f32[4,48,512]{2,1,0:T(8,128)}, u32[]{:S(2)}) copy-start(f32[4,48,512]{2,1,0:T(8,128)} %get-tuple-element.26) | copy-start | bytes 1179652
  113.5 2.3 %copy-start.24 = (pred[4,96]{1,0:T(4,128)(4,1)S(1)}, pred[4,96]{1,0:T(4,128)(4,1)}, u32[]{:S(2)}) copy-start(pred[4,96]{1,0:T(4,128)(4,1)} %broadcast_compare_fusion.2) | copy-start | bytes 1156
  114.1 1.7 %copy-start.5 = (f32[4,96,512]{2,1,0:T(8,128)S(1)}, f32[4,96,512]{2,1,0:T(8,128)}, u32[]{:S(2)}) copy-start(f32[4,96,512]{2,1,0:T(8,128)} %copy-done.4) | copy-start | bytes 2359300
  114.1 1.7 %copy-start.9 = (f32[4,96,256]{2,1,0:T(8,128)S(1)}, f32[4,96,256]{2,1,0:T(8,128)}, u32[]{:S(2)}) copy-start(f32[4,96,256]{2,1,0:T(8,128)} %get-tuple-element.23) | copy-start | bytes 1179652
  114.5 1.3 copy-start.10
  116.3 5.6 %slice-start = ((f32[4,27,512]{2,0,1:T(4,128)}), f32[4,24,512]{2,0,1:T(4,128)S(1)}, s32[]{:S(2)}) async-start(f32[4,27,512]{2,0,1:T(4,128)} %pad_add_fusion), calls=%async_computation.2 | async-start | bytes 393216 | tf_op jit(solution)/shard_map/slice | solution.py:209
  116.3 5.6 %copy-start.20 = (s32[4]{0:T(128)S(1)}, s32[4]{0:T(128)}, u32[]{:S(2)}) copy-start(s32[4]{0:T(128)} %copy-done.18) | copy-start | bytes 52
  117.9 16.6 %copy-start.1 = (bf16[16,16,2048]{2,1,0:T(8,128)(2,1)S(1)}, bf16[16,16,2048]{2,1,0:T(8,128)(2,1)}, u32[]{:S(2)}) copy-start(bf16[16,16,2048]{2,1,0:T(8,128)(2,1)} %copy-done) | copy-start | bytes 3145732
  118.3 3.6 %collective-permute-start.5 = (f32[4,1536]{1,0:T(4,128)S(1)}, f32[4,1536]{1,0:T(4,128)S(1)}, u32[]{:S(2)}, u32[]{:S(2)}) collective-permute-start(f32[4,1536]{1,0:T(4,128)S(1)} %add_add_fusion.3), channel_id=1, source_target_pairs={{0,1},{1,2},{2,3},{3,4},{4,5},{5,6},{6,7},{8,9},{9,10},{10,11},{11... | collective-permute-start | bytes 73736 | tf_op jit(solution)/shard_map/ppermute | solution.py:20
Sparse Core Ops, SparseCore 0:
  16.5 41.2 reduce-scatter.1

commit v7 on v5

--- a/solution.py
+++ b/solution.py
@@ -124,19 +124,15 @@
     clean = jnp.where(inside, target, jnp.zeros_like(target))
     clean, local_table = lax.optimization_barrier((clean, local_table))
     padded_spec = jnp.pad(spectra, ((0, 0), (0, 0), (0, 0), (3, 0)))
-    framed_sig = jnp.einsum(
-        "crbf,rbm->fcm", padded_spec, local_table, preferred_element_type=jnp.float32
-    )
+    hop_count = rows_here * lax.axis_size("seg")
+    shifted_spec = jnp.stack(
+        [padded_spec[:, :, :, 3 - quarter : 3 - quarter + hop_count] for quarter in range(4)],
+        axis=1,
+    )
+    quarter_table = local_table.reshape(2, band_count, 4, HOP)
     hop_rows = lax.psum_scatter(
-        sum(
-            (
-                framed_sig[
-                    3 - quarter : 3 - quarter + rows_here * lax.axis_size("seg"),
-                    :,
-                    quarter * HOP : (quarter + 1) * HOP,
-                ]
-                for quarter in range(4)
-            )
+        jnp.einsum(
+            "cqrbh,rbqi->hci", shifted_spec, quarter_table, preferred_element_type=jnp.float32
         ),
         "seg",
         scatter_dimension=0,

time: 144 us -> 150 us (1.042)
  local copies, waits for them, and re-layouts: 14.1 us -> 19.7 us
  matrix products: 27.6 us -> 29.7 us
  waiting for transfers between devices: 13.8 us -> 12.3 us
    reduce_scatter x1, waiting for transfers between devices: 7.88 us -> 4.34 us  [body(): lax.psum_scatter(jnp.einsum('cqrbh,rbqi->hci', shifted_spec, quarter_tabl...]
    convert_element_type x3, other arithmetic: 9.29 us -> 6.37 us  [analysis_table(): table = entry_value.astype(jnp.bfloat16)]
    reshape x3, local copies, waits for them, and re-layouts: 2.07 us -> 4.41 us  [body(): grad_frames.reshape(clip_count, frame_count, 4, stride)]
    ppermute x2, waiting for transfers between devices: 5.69 us -> 7.97 us  [gathered_sum(): held = jnp.concatenate([held, lax.ppermute(held, axis, route)], axis=0)]
    add x1 -> x0, other arithmetic: 2.01 us -> none  [body(): sum((framed_sig[3 - quarter:3 - quarter + rows_here * lax.axis_size('seg'...]
    dot_general x3, matrix products: 5.81 us -> 7.74 us  [body(): jnp.einsum('cfj,jm->cfm', grad_x, table, preferred_element_type=jnp.float32)]
    another operation x0 -> x1, local copies, waits for them, and re-layouts: none -> 1.72 us  [body(): jnp.stack([padded_spec[:, :, :, 3 - quarter:3 - quarter + hop_count] for...]
    unnamed x73 -> x81, local copies, waits for them, and re-layouts: 4.5 us -> 4.02 us
  transfers between devices with their start and end apart: 6 -> 6, of which waited for: 4 -> 3; matrix products, arithmetic and copies ran while one was open for 26% -> 32% of each run, Pallas kernels for 0% -> 0%
where the time goes in v7:
time: 150 us; the launch traced here: 149 us
  other arithmetic  43.2 us (29%)
  matrix products  29.7 us (20%)
  blocking collectives  20.3 us (14%)
  local copies, waits for them, and re-layouts  19.7 us (13%)
  between operations  16.7 us (11%)
  waiting for transfers between devices  12.3 us (8%)
  starting transfers between devices  7.09 us (5%)
    dot_general x3, matrix products, body(): jnp.einsum('cfm,jm->cfj', framed(clean, clean_beyond[:, :3 * stride], str...  11 us
    all_gather x1, blocking collectives, body(): lax.all_gather(jnp.stack([spreads, energies, logterms]), 'seg', axis=0, t...  10.8 us
    all_gather x1, blocking collectives, body(): portion = lax.all_gather(grad_hops, 'seg', axis=1, tiled=True)  9.53 us
    mul x3, other arithmetic, analysis_table(): fine_cos, fine_sin = (part * scale for part in fine)  9.33 us
    ppermute x2, waiting for transfers between devices, gathered_sum(): held = jnp.concatenate([held, lax.ppermute(held, axis, route)], axis=0)  7.97 us
    dot_general x3, matrix products, body(): jnp.einsum('cfj,jm->cfm', grad_x, table, preferred_element_type=jnp.float32)  7.74 us
    dot_general x3, matrix products, body(): jnp.einsum('cfm,jm->cfj', framed(est_wave, est_beyond[:, :3 * stride], st...  7.52 us
    convert_element_type x3, other arithmetic, analysis_table(): table = entry_value.astype(jnp.bfloat16)  6.37 us
  transfers between devices with their start and end apart: 6, of which 3 were waited for; matrix products, arithmetic and copies ran while one was open for 32% of the time, Pallas kernels for 0%

profile of v7, /device:TPU:0, one launch (start us, length us, event | category | flops | bytes accessed | tf_op | source)
XLA Modules:
  0.0 149.0 jit_solution(2327112961058580676)
XLA Ops:
  7.3 0.5 cosine_multiply_fusion.3
  7.8 1.1 fusion.138
  9.3 1.3 multiply_convert_fusion
  10.6 1.0 compare_select_fusion.2
  11.6 0.6 slice.222
  12.2 1.3 collective-permute-start.1
  13.5 1.7 %slice_bitcast_fusion.2 = (bf16[4,1,2,128,192]{3,4,2,1,0:T(8,128)(2,1)S(1)}, bf16[4,1,2,128,192]{3,4,2,1,0:T(8,128)(2,1)S(1)}, bf16[4,1,2,128,192]{3,4,2,1,0:T(8,128)(2,1)S(1)}) fusion(bf16[4,2,128,192]{2,3,1,0:T(8,128)(2,1)} %param.3), kind=kLoop, calls=%fused_computation.161 | loop fusion | bytes 1572864 | tf_op jit(solution)/shard_map/stack | solution.py:128
  15.2 2.2 %fusion.27 = f32[192,4,512]{2,0,1:T(8,128)} fusion(bf16[4,1,2,128,192]{3,4,2,1,0:T(8,128)(2,1)S(1)} %get-tuple-element.52, bf16[4,1,2,128,192]{3,4,2,1,0:T(8,128)(2,1)S(1)} %get-tuple-element.51, bf16[4,1,2,128,192]{3,4,2,1,0:T(8,128)(2,1)S(1)} %get-tuple-element.50, bf16[4,1,2,128,192]{3,4,2,1,0:T(8,128)(2,1)S(1)} %bitcast.187, ...), kind=kOutput, calls=%fused_computation.34 | convolution fusion | flops 811597824 | bytes 4194304 | tf_op jit(solution)/shard_map/cqrbh,rbqi->hci/dot_general | solution.py:134
  17.5 0.6 subtract_multiply_fusion
  18.1 0.6 fusion.159
  18.7 0.6 iota_compare_fusion.1
  19.3 0.6 subtract_multiply_fusion.1
  20.4 0.6 iota_compare_fusion.2
  21.0 4.1 %cosine_multiply_fusion = (f32[128,2048]{1,0:T(8,128)S(1)}, f32[128,2048]{1,0:T(8,128)S(1)}) fusion(f32[2048]{0:T(1024)S(1)} %fusion.153), kind=kLoop, calls=%fused_computation.44 | loop fusion | flops 4194304 | bytes 2105344 | tf_op jit(solution)/shard_map/mul | solution.py:44
  25.2 0.6 broadcast_compare_fusion
  25.7 2.8 %cosine_multiply_fusion.1 = (f32[128,1024]{1,0:T(8,128)S(1)}, f32[128,1024]{1,0:T(8,128)S(1)}) fusion(f32[1024]{0:T(1024)} %subtract_multiply_fusion), kind=kLoop, calls=%fused_computation.65 | loop fusion | flops 2097152 | bytes 1052672 | tf_op jit(solution)/shard_map/mul | solution.py:44
  29.0 2.4 %cosine_multiply_fusion.2 = (f32[128,512]{1,0:T(8,128)}, f32[128,512]{1,0:T(8,128)}) fusion(f32[512]{0:T(512)} %subtract_multiply_fusion.1), kind=kLoop, calls=%fused_computation.169 | loop fusion | flops 1048576 | bytes 526336 | tf_op jit(solution)/shard_map/mul | solution.py:44
  32.0 0.9 fusion.148
  32.9 1.2 broadcast_compare_fusion.1
  34.1 0.8 fusion.155
  34.9 1.3 broadcast_compare_fusion.2
  36.3 5.7 %add_convert_fusion = bf16[16,128,2048]{2,1,0:T(8,128)(2,1)} fusion(f32[128,2048]{1,0:T(8,128)S(1)} %get-tuple-element.80, f32[16,2048]{1,0:T(8,128)S(1)} %get-tuple-element.105, f32[128,2048]{1,0:T(8,128)S(1)} %get-tuple-element.79, f32[16,2048]{1,0:T(8,128)S(1)} %get-tuple-element.106), kind=kLoop, calls=%fused_computation | loop fusion | flops 16777216 | bytes 10747904 | tf_op jit(solution)/shard_map/convert_element_type | solution.py:46
  41.9 0.6 add_convert_fusion.1
  43.1 0.6 and_select_fusion.3
  43.7 0.8 pad_maximum_fusion.1
  44.6 0.7 slice.302
  45.4 0.7 slice.288
  46.3 0.7 fusion.182
  47.1 1.7 %fusion.15 = f32[4,48,1024]{2,1,0:T(8,128)} fusion(bf16[1024,1024]{1,0:T(8,128)(2,1)S(1)} %bitcast.152, bf16[4,48,256]{2,1,0:T(8,128)(2,1)S(1)} %get-tuple-element.62, bf16[4,48,256]{2,1,0:T(8,128)(2,1)S(1)} %get-tuple-element.63, bf16[4,48,256]{2,1,0:T(8,128)(2,1)S(1)} %get-tuple-element.64, bf16[4,48,256]{2,1,0:T(8,128)(2,1)S(1)} %get-tuple-element.61), kind=kOutput, calls=%fused_computation.18 | convolution fusion | flops 404226048 | bytes 3276800 | tf_op jit(solution)/shard_map/cfm,jm->cfj/dot_general | solution.py:156
  48.8 7.0 %fusion.2 = f32[4,24,2048]{2,1,0:T(8,128)} fusion(bf16[2048,2048]{1,0:T(8,128)(2,1)} %bitcast.149, bf16[4,24,512]{2,1,0:T(8,128)(2,1)S(1)} %get-tuple-element.54, bf16[4,24,512]{2,1,0:T(8,128)(2,1)S(1)} %get-tuple-element.55, bf16[4,24,512]{2,1,0:T(8,128)(2,1)S(1)} %get-tuple-element.56, bf16[4,24,512]{2,1,0:T(8,128)(2,1)S(1)} %get-tuple-element.53), kind=kOutput, calls=%fused_computation.3 | convolution fusion | flops 806879232 | bytes 9568256 | tf_op jit(solution)/shard_map/cfm,jm->cfj/dot_general | solution.py:156
  55.8 4.3 %reduce-scatter.2.cloned.1.call-done = f32[24,4,512]{2,0,1:T(8,128)} async-done(((f32[192,4,512]{2,0,1:T(8,128)}), f32[24,4,512]{2,0,1:T(8,128)}) %reduce-scatter.2.cloned.1.call-update) | async-done | bytes 196624 | tf_op jit(solution)/shard_map/reduce_scatter | solution.py:133
  60.1 1.1 copy.81
  61.3 1.3 collective-permute-start
  62.7 2.3 %fusion.45 = f32[4,96,512]{2,1,0:T(8,128)} fusion(bf16[512,512]{1,0:T(8,128)(2,1)S(1)} %bitcast.155, bf16[4,96,128]{2,1,0:T(8,128)(2,1)S(1)} %get-tuple-element.70, bf16[4,96,128]{2,1,0:T(8,128)(2,1)S(1)} %copy-done.19, bf16[4,96,128]{2,1,0:T(8,128)(2,1)} %get-tuple-element.72, bf16[4,96,128]{2,1,0:T(8,128)(2,1)S(1)} %get-tuple-element.69), kind=kOutput, calls=%fused_computation.60 | convolution fusion | flops 202899456 | bytes 1703936 | tf_op jit(solution)/shard_map/cfm,jm->cfj/dot_general | solution.py:156
  65.0 0.8 fusion.179
  65.9 0.8 fusion.181
  66.9 6.3 %fusion.4 = f32[4,24,2048]{2,1,0:T(8,128)S(1)} fusion(bf16[2048,2048]{1,0:T(8,128)(2,1)} %bitcast.150, bf16[4,24,512]{2,1,0:T(8,128)(2,1)} %get-tuple-element.58, bf16[4,24,512]{2,1,0:T(8,128)(2,1)} %get-tuple-element.59, bf16[4,24,512]{2,1,0:T(8,128)(2,1)} %get-tuple-element.60, bf16[4,24,512]{2,1,0:T(8,128)(2,1)S(1)} %get-tuple-element.57), kind=kOutput, calls=%fused_computation.5 | convolution fusion | flops 806879232 | bytes 9568256 | tf_op jit(solution)/shard_map/cfm,jm->cfj/dot_general | solution.py:162
  73.2 1.4 select_reduce_fusion.6
  74.6 0.9 fusion.17
  75.6 1.5 %select_reduce_fusion.7 = (f32[4]{0:T(128)S(1)}, f32[4]{0:T(128)S(1)}, f32[4]{0:T(128)S(1)}, f32[4,48,512]{2,1,0:T(8,128)}, f32[4,48,512]{2,1,0:T(8,128)}) fusion(pred[4,48]{1,0:T(4,128)(4,1)S(1)} %copy-done.29, f32[4,48,1024]{2,1,0:T(8,128)S(1)} %fusion.17, f32[4,48,1024]{2,1,0:T(8,128)S(1)} %copy-done.12), kind=kLoop, calls=%fused_computation.152 | loop fusion | flops 2064372 | bytes 2359536 | tf_op jit(solution)/shard_map/reduce_sum | solution.py:180
  77.5 1.5 select_reduce_fusion.8
  79.1 10.8 %all-gather = f32[24,3,4]{2,1,0:T(4,128)S(1)} all-gather(f32[3,3,4]{2,1,0:T(4,128)S(1)} %pad_maximum_fusion.6), channel_id=2, replica_groups=mesh['clip'=4,'seg'=8] {'seg'}, dimensions={0}, use_global_device_ids=true | all-gather | bytes 1296 | tf_op jit(solution)/shard_map/all_gather | solution.py:189
  89.9 0.6 multiply_rsqrt_fusion
  90.5 1.8 %divide_convert_fusion.5 = (bf16[4,96,256]{2,1,0:T(8,128)(2,1)S(1)}, bf16[4,96,256]{2,1,0:T(8,128)(2,1)S(1)}) fusion(f32[4,96,512]{2,1,0:T(8,128)} %copy-done.3, f32[4,96,256]{2,1,0:T(8,128)} %get-tuple-element.23, f32[4,96,256]{2,1,0:T(8,128)} %get-tuple-element.24, f32[4]{0:T(128)S(1)} %copy-done.24, f32[4]{0:T(128)S(1)} %get-tuple-element.85, ...), kind=kLoop, calls=%fused_computation.139 | loop fusion | flops 1671168 | bytes 1966496 | tf_op jit(solution)/shard_map/convert.4
  92.3 1.3 fusion.43
  93.7 2.3 %reshape.928 = f32[4,96,4,128]{3,2,1,0:T(4,128)} reshape(f32[4,96,512]{2,1,0:T(8,128)} %fusion.43) | data formatting | bytes 1572864 | tf_op jit(solution)/shard_map/reshape | solution.py:212
  96.0 2.9 %fusion.175 = (f32[4,96,1,128]{3,2,1,0:T(1,128)S(1)}, f32[4,96,1,128]{3,2,1,0:T(1,128)S(1)}, f32[4,96,1,128]{3,2,1,0:T(1,128)S(1)}, f32[4,96,1,128]{3,2,1,0:T(1,128)S(1)}) fusion(f32[4,96,4,128]{3,2,1,0:T(4,128)} %reshape.928), kind=kLoop, calls=%fused_computation.327 | loop fusion | bytes 1572864 | tf_op jit(solution)/shard_map/slice | solution.py:97
  99.4 0.6 add_bitcast_fusion
  100.6 1.5 %fusion.13 = f32[4,48,1024]{2,1,0:T(8,128)} fusion(bf16[1024,1024]{1,0:T(8,128)(2,1)S(1)} %bitcast.154, bf16[4,48,512]{2,1,0:T(8,128)(2,1)S(1)} %get-tuple-element.32, bf16[4,48,512]{2,1,0:T(8,128)(2,1)S(1)} %get-tuple-element.31), kind=kOutput, calls=%fused_computation.16 | convolution fusion | flops 403439616 | bytes 3276800 | tf_op jit(solution)/shard_map/cfj,jm->cfm/dot_general | solution.py:209
  102.2 1.6 %reshape.930 = f32[4,48,4,256]{3,2,1,0:T(4,128)S(1)} reshape(f32[4,48,1024]{2,1,0:T(8,128)} %fusion.13) | data formatting | bytes 1572864 | tf_op jit(solution)/shard_map/reshape | solution.py:212
  103.7 0.7 fusion.176
  105.6 4.9 %fusion = f32[4,24,2048]{2,1,0:T(8,128)S(1)} fusion(bf16[2048,2048]{1,0:T(8,128)(2,1)} %bitcast.151, bf16[4,24,1024]{2,1,0:T(8,128)(2,1)S(1)} %get-tuple-element.34, bf16[4,24,1024]{2,1,0:T(8,128)(2,1)S(1)} %get-tuple-element.33), kind=kOutput, calls=%fused_computation.1 | convolution fusion | flops 806092800 | bytes 9568256 | tf_op jit(solution)/shard_map/cfj,jm->cfm/dot_general | solution.py:209
  111.0 0.7 fusion.177
  112.4 2.4 %collective-permute-start.4 = (f32[4,1536]{1,0:T(4,128)S(1)}, f32[4,1536]{1,0:T(4,128)S(1)}, u32[]{:S(2)}, u32[]{:S(2)}) collective-permute-start(f32[4,1536]{1,0:T(4,128)S(1)} %add_add_fusion.3), channel_id=1, source_target_pairs={{0,1},{1,2},{2,3},{3,4},{4,5},{5,6},{6,7},{8,9},{9,10},{10,11},{11... | collective-permute-start | bytes 73736 | tf_op jit(solution)/shard_map/ppermute | solution.py:20
  114.8 1.5 %collective-permute-start.2 = (f32[1]{0:T(128)}, f32[1]{0:T(128)}, u32[]{:S(2)}, u32[]{:S(2)}) collective-permute-start(f32[1]{0:T(128)} %bitcast.32), channel_id=1, source_target_pairs={{0,8},{8,16},{16,24},{24,0},{1,9},{9,17},{17,25},{25,1},{2,10},{10... | collective-permute-start | bytes 20 | tf_op jit(solution)/shard_map/ppermute | solution.py:76
  116.3 4.1 %collective-permute-done.2 = f32[1]{0:T(128)} collective-permute-done((f32[1]{0:T(128)}, f32[1]{0:T(128)}, u32[]{:S(2)}, u32[]{:S(2)}) %collective-permute-start.2) | collective-permute-done | bytes 36 | tf_op jit(solution)/shard_map/ppermute | solution.py:76
  120.4 1.3 pad_maximum_fusion.7
  121.7 0.6 collective-permute-start.3
  122.3 3.8 %collective-permute-done.3 = f32[2]{0:T(128)S(1)} collective-permute-done((f32[2]{0:T(128)S(1)}, f32[2]{0:T(128)S(1)}, u32[]{:S(2)}, u32[]{:S(2)}) %collective-permute-start.3) | collective-permute-done | bytes 40 | tf_op jit(solution)/shard_map/ppermute | solution.py:76
  126.2 1.3 pad_maximum_fusion.8
  127.4 0.7 select_reduce_fusion.9
  128.9 9.5 %all_gather.11 = bf16[4,192,512]{2,1,0:T(8,128)(2,1)S(1)} all-gather(bf16[4,24,512]{2,1,0:T(8,128)(2,1)S(1)} %bitcast.186), channel_id=1, replica_groups=mesh['clip'=4,'seg'=8] {'seg'}, dimensions={1}, use_global_device_ids=true | all-gather | bytes 884736 | tf_op jit(solution)/shard_map/all_gather | solution.py:221
  139.0 1.3 fusion.31
  140.2 0.8 copy.65
  (134 shorter events, 8.2 us)
Async XLA Ops:
  7.2 8.1 %copy-start.14 = (bf16[4,2,128,192]{2,3,1,0:T(8,128)(2,1)S(1)}, bf16[4,2,128,192]{2,3,1,0:T(8,128)(2,1)}, u32[]{:S(2)}) copy-start(bf16[4,2,128,192]{2,3,1,0:T(8,128)(2,1)} %param.3) | copy-start | bytes 1179652
  7.2 53.0 %reduce-scatter.2.cloned.1.call-start = ((), (), s32[]{:S(2)}) async-start(), calls=%async_computation.1 | async-start | bytes 1769472 | tf_op jit(solution)/shard_map/reduce_scatter | solution.py:133
  9.2 8.2 %copy-start.8 = (bf16[16,16,2048]{2,1,0:T(8,128)(2,1)}, bf16[16,16,2048]{2,1,0:T(8,128)(2,1)S(1)}, u32[]{:S(2)}) copy-start(bf16[16,16,2048]{2,1,0:T(8,128)(2,1)S(1)} %add_convert_fusion.2) | copy-start | bytes 3145732
  10.6 1.6 %copy-start.21 = (s32[4]{0:T(128)}, s32[4]{0:T(128)S(1)}, u32[]{:S(2)}) copy-start(s32[4]{0:T(128)S(1)} %get-tuple-element.100) | copy-start | bytes 52
  12.2 31.5 %collective-permute-start.1 = (bf16[4,1536]{1,0:T(4,128)(2,1)}, bf16[4,1536]{1,0:T(4,128)(2,1)}, u32[]{:S(2)}, u32[]{:S(2)}) collective-permute-start(bf16[4,1536]{1,0:T(4,128)(2,1)} %slice.222), channel_id=1, source_target_pairs={{1,0},{2,1},{3,2},{4,3},{5,4},{6,5},{7,6},{9,8},{10,9},{11,10},{12... | collective-permute-start | bytes 36872 | tf_op jit(solution)/shard_map/ppermute | solution.py:20
  17.4 7.8 %copy-start.25 = (s32[4]{0:T(128)S(1)}, s32[4]{0:T(128)}, u32[]{:S(2)}) copy-start(s32[4]{0:T(128)} %param.5) | copy-start | bytes 52
  41.9 1.0 copy-start.10
  41.9 1.0 copy-start.11
  48.8 12.4 %copy-start.22 = (s32[4]{0:T(128)S(1)}, s32[4]{0:T(128)}, u32[]{:S(2)}) copy-start(s32[4]{0:T(128)} %copy-done.21) | copy-start | bytes 52
  48.8 13.9 %copy-start.19 = (bf16[4,96,128]{2,1,0:T(8,128)(2,1)S(1)}, bf16[4,96,128]{2,1,0:T(8,128)(2,1)}, u32[]{:S(2)}) copy-start(bf16[4,96,128]{2,1,0:T(8,128)(2,1)} %get-tuple-element.71) | copy-start | bytes 294916
  61.3 3.6 %collective-permute-start = (bf16[4,1536]{1,0:T(4,128)(2,1)S(1)}, bf16[4,1536]{1,0:T(4,128)(2,1)S(1)}, u32[]{:S(2)}, u32[]{:S(2)}) collective-permute-start(bf16[4,1536]{1,0:T(4,128)(2,1)S(1)} %slice.280), channel_id=1, source_target_pairs={{1,0},{2,1},{3,2},{4,3},{5,4},{6,5},{7,6},{9,8},{10,9},{11,10},{12... | collective-permute-start | bytes 36872 | tf_op jit(solution)/shard_map/ppermute | solution.py:20
  66.9 6.3 %copy-start = (f32[4,24,2048]{2,1,0:T(8,128)S(1)}, f32[4,24,2048]{2,1,0:T(8,128)}, u32[]{:S(2)}) copy-start(f32[4,24,2048]{2,1,0:T(8,128)} %fusion.2) | copy-start | bytes 2359300
  66.9 6.3 %copy-start.27 = (pred[4,24]{1,0:T(4,128)(4,1)S(1)}, pred[4,24]{1,0:T(4,128)(4,1)}, u32[]{:S(2)}) copy-start(pred[4,24]{1,0:T(4,128)(4,1)} %broadcast_compare_fusion) | copy-start | bytes 292
  66.9 7.7 %copy-start.15 = (bf16[4,48,256]{2,1,0:T(8,128)(2,1)S(1)}, bf16[4,48,256]{2,1,0:T(8,128)(2,1)}, u32[]{:S(2)}) copy-start(bf16[4,48,256]{2,1,0:T(8,128)(2,1)} %get-tuple-element.65) | copy-start | bytes 294916
  66.9 7.7 %copy-start.16 = (bf16[4,48,256]{2,1,0:T(8,128)(2,1)S(1)}, bf16[4,48,256]{2,1,0:T(8,128)(2,1)}, u32[]{:S(2)}) copy-start(bf16[4,48,256]{2,1,0:T(8,128)(2,1)} %get-tuple-element.66) | copy-start | bytes 294916
  66.9 7.7 %copy-start.17 = (bf16[4,48,256]{2,1,0:T(8,128)(2,1)S(1)}, bf16[4,48,256]{2,1,0:T(8,128)(2,1)}, u32[]{:S(2)}) copy-start(bf16[4,48,256]{2,1,0:T(8,128)(2,1)} %get-tuple-element.67) | copy-start | bytes 294916
  66.9 7.7 %copy-start.18 = (bf16[4,48,256]{2,1,0:T(8,128)(2,1)S(1)}, bf16[4,48,256]{2,1,0:T(8,128)(2,1)}, u32[]{:S(2)}) copy-start(bf16[4,48,256]{2,1,0:T(8,128)(2,1)} %get-tuple-element.68) | copy-start | bytes 294916
  73.2 2.3 %copy-start.12 = (f32[4,48,1024]{2,1,0:T(8,128)S(1)}, f32[4,48,1024]{2,1,0:T(8,128)}, u32[]{:S(2)}) copy-start(f32[4,48,1024]{2,1,0:T(8,128)} %fusion.15) | copy-start | bytes 2359300
  73.2 2.3 %copy-start.29 = (pred[4,48]{1,0:T(4,128)(4,1)S(1)}, pred[4,48]{1,0:T(4,128)(4,1)}, u32[]{:S(2)}) copy-start(pred[4,48]{1,0:T(4,128)(4,1)} %broadcast_compare_fusion.1) | copy-start | bytes 580
  75.5 3.4 %copy-start.1 = (f32[4,48,1024]{2,1,0:T(8,128)}, f32[4,48,1024]{2,1,0:T(8,128)S(1)}, u32[]{:S(2)}) copy-start(f32[4,48,1024]{2,1,0:T(8,128)S(1)} %fusion.17) | copy-start | bytes 2359300
  75.5 1.9 %copy-start.13 = (f32[4,96,512]{2,1,0:T(8,128)S(1)}, f32[4,96,512]{2,1,0:T(8,128)}, u32[]{:S(2)}) copy-start(f32[4,96,512]{2,1,0:T(8,128)} %fusion.45) | copy-start | bytes 2359300
  75.5 1.9 %copy-start.31 = (pred[4,96]{1,0:T(4,128)(4,1)S(1)}, pred[4,96]{1,0:T(4,128)(4,1)}, u32[]{:S(2)}) copy-start(pred[4,96]{1,0:T(4,128)(4,1)} %broadcast_compare_fusion.2) | copy-start | bytes 1156
  75.6 3.4 %copy-start.26 = (s32[4]{0:T(128)S(1)}, s32[4]{0:T(128)}, u32[]{:S(2)}) copy-start(s32[4]{0:T(128)} %param.5) | copy-start | bytes 52
  75.6 14.9 %copy-start.24 = (f32[4]{0:T(128)S(1)}, f32[4]{0:T(128)}, u32[]{:S(2)}) copy-start(f32[4]{0:T(128)} %get-tuple-element.98) | copy-start | bytes 52
  77.5 1.5 copy-start.3
  93.7 6.4 %copy-start.6 = (f32[4,48,512]{2,1,0:T(8,128)S(1)}, f32[4,48,512]{2,1,0:T(8,128)}, u32[]{:S(2)}) copy-start(f32[4,48,512]{2,1,0:T(8,128)} %get-tuple-element.25) | copy-start | bytes 1179652
  93.7 6.4 %copy-start.30 = (pred[4,48]{1,0:T(4,128)(4,1)S(1)}, pred[4,48]{1,0:T(4,128)(4,1)}, u32[]{:S(2)}) copy-start(pred[4,48]{1,0:T(4,128)(4,1)} %broadcast_compare_fusion.1) | copy-start | bytes 580
  96.0 4.1 %copy-start.2 = (f32[4,48,1024]{2,1,0:T(8,128)S(1)}, f32[4,48,1024]{2,1,0:T(8,128)}, u32[]{:S(2)}) copy-start(f32[4,48,1024]{2,1,0:T(8,128)} %copy-done.1) | copy-start | bytes 2359300
  96.0 4.1 %copy-start.7 = (f32[4,48,512]{2,1,0:T(8,128)S(1)}, f32[4,48,512]{2,1,0:T(8,128)}, u32[]{:S(2)}) copy-start(f32[4,48,512]{2,1,0:T(8,128)} %get-tuple-element.26) | copy-start | bytes 1179652
  102.2 2.9 %copy-start.4 = (f32[4,24,1024]{2,1,0:T(8,128)S(1)}, f32[4,24,1024]{2,1,0:T(8,128)}, u32[]{:S(2)}) copy-start(f32[4,24,1024]{2,1,0:T(8,128)} %get-tuple-element.27) | copy-start | bytes 1179652
  102.2 2.9 %copy-start.5 = (f32[4,24,1024]{2,1,0:T(8,128)S(1)}, f32[4,24,1024]{2,1,0:T(8,128)}, u32[]{:S(2)}) copy-start(f32[4,24,1024]{2,1,0:T(8,128)} %get-tuple-element.28) | copy-start | bytes 1179652
  102.2 2.9 %copy-start.28 = (pred[4,24]{1,0:T(4,128)(4,1)S(1)}, pred[4,24]{1,0:T(4,128)(4,1)}, u32[]{:S(2)}) copy-start(pred[4,24]{1,0:T(4,128)(4,1)} %broadcast_compare_fusion) | copy-start | bytes 292
  110.5 1.9 %copy-start.20 = (f32[4,384]{1,0:T(4,128)S(1)}, f32[4,384]{1,0:T(4,128)}, u32[]{:S(2)}) copy-start(f32[4,384]{1,0:T(4,128)} %add_bitcast_fusion) | copy-start | bytes 18436
  111.0 16.4 %copy-start.32 = (s32[4]{0:T(128)S(1)}, s32[4]{0:T(128)}, u32[]{:S(2)}) copy-start(s32[4]{0:T(128)} %and_select_fusion.3) | copy-start | bytes 52
  111.0 17.8 %copy-start.23 = (s32[4]{0:T(128)S(1)}, s32[4]{0:T(128)}, u32[]{:S(2)}) copy-start(s32[4]{0:T(128)} %copy-done.21) | copy-start | bytes 52
  112.4 26.6 %copy-start.9 = (bf16[16,16,2048]{2,1,0:T(8,128)(2,1)S(1)}, bf16[16,16,2048]{2,1,0:T(8,128)(2,1)}, u32[]{:S(2)}) copy-start(bf16[16,16,2048]{2,1,0:T(8,128)(2,1)} %copy-done.8) | copy-start | bytes 3145732
  112.4 16.4 %collective-permute-start.4 = (f32[4,1536]{1,0:T(4,128)S(1)}, f32[4,1536]{1,0:T(4,128)S(1)}, u32[]{:S(2)}, u32[]{:S(2)}) collective-permute-start(f32[4,1536]{1,0:T(4,128)S(1)} %add_add_fusion.3), channel_id=1, source_target_pairs={{0,1},{1,2},{2,3},{3,4},{4,5},{5,6},{6,7},{8,9},{9,10},{10,11},{11... | collective-permute-start | bytes 73736 | tf_op jit(solution)/shard_map/ppermute | solution.py:20
  114.8 5.6 %collective-permute-start.2 = (f32[1]{0:T(128)}, f32[1]{0:T(128)}, u32[]{:S(2)}, u32[]{:S(2)}) collective-permute-start(f32[1]{0:T(128)} %bitcast.32), channel_id=1, source_target_pairs={{0,8},{8,16},{16,24},{24,0},{1,9},{9,17},{17,25},{25,1},{2,10},{10... | collective-permute-start | bytes 20 | tf_op jit(solution)/shard_map/ppermute | solution.py:76
  121.7 4.4 %collective-permute-start.3 = (f32[2]{0:T(128)S(1)}, f32[2]{0:T(128)S(1)}, u32[]{:S(2)}, u32[]{:S(2)}) collective-permute-start(f32[2]{0:T(128)S(1)} %pad_maximum_fusion.7), channel_id=1, source_target_pairs={{0,16},{8,24},{16,0},{24,8},{1,17},{9,25},{17,1},{25,9},{2,18},{10... | collective-permute-start | bytes 32 | tf_op jit(solution)/shard_map/ppermute | solution.py:76
Sparse Core Ops, SparseCore 0:
  17.6 42.5 reduce-scatter.1

commit v8 on v4

--- a/solution.py
+++ b/solution.py
@@ -185,7 +185,8 @@
     spreads = jnp.stack(spread_list)
     energies = jnp.stack(energy_list)
     logterms = jnp.stack(logterm_list)
-    spreads, energies, logterms = lax.psum((spreads, energies, logterms), "seg")
+    parts = lax.all_gather(jnp.stack([spreads, energies, logterms]), "seg", axis=0, tiled=False)
+    spreads, energies, logterms = jnp.sum(parts, axis=0)
     own_loss = jnp.sum(jnp.sqrt((spreads + EPS_RATIO) / energies) + logterms)
     loss = gathered_sum(own_loss, "clip") / (3 * clip_count * lax.axis_size("clip"))
     ratio_weight = 1.0 / jnp.sqrt((spreads + EPS_RATIO) * energies)

time: 145 us -> 140 us (0.966)
  blocking collectives: 26.5 us -> 20.4 us
    psum x1 -> x0, blocking collectives: 14.4 us -> none  [body(): spreads, energies, logterms = lax.psum((spreads, energies, logterms), 'seg')]
    all_gather x0 -> x1, blocking collectives: none -> 10.8 us  [body(): lax.all_gather(jnp.stack([spreads, energies, logterms]), 'seg', axis=0, t...]
    all_gather x1, blocking collectives: 12 us -> 9.59 us  [body(): portion = lax.all_gather(grad_hops, 'seg', axis=1, tiled=True)]
    unnamed x73 -> x75, local copies, waits for them, and re-layouts: 4.41 us -> 4.42 us
  transfers between devices with their start and end apart: 7 -> 7, of which waited for: 4 -> 4; matrix products, arithmetic and copies ran while one was open for 29% -> 30% of each run, Pallas kernels for 0% -> 0%
where the time goes in v8:
time: 140 us; the launch traced here: 139 us
  other arithmetic  43.9 us (31%)
  matrix products  28.4 us (20%)
  blocking collectives  20.4 us (15%)
  between operations  16.7 us (12%)
  local copies, waits for them, and re-layouts  14 us (10%)
  starting transfers between devices  10.2 us (7%)
  waiting for transfers between devices  5.7 us (4%)
    dot_general x3, matrix products, body(): jnp.einsum('cfm,jm->cfj', framed(clean, clean_beyond[:, :3 * stride], str...  10.9 us
    all_gather x1, blocking collectives, body(): lax.all_gather(jnp.stack([spreads, energies, logterms]), 'seg', axis=0, t...  10.8 us
    all_gather x1, blocking collectives, body(): portion = lax.all_gather(grad_hops, 'seg', axis=1, tiled=True)  9.59 us
    mul x3, other arithmetic, analysis_table(): fine_cos, fine_sin = (part * scale for part in fine)  8.64 us
    dot_general x3, matrix products, body(): jnp.einsum('cfm,jm->cfj', framed(est_wave, est_beyond[:, :3 * stride], st...  7.52 us
    convert_element_type x3, other arithmetic, analysis_table(): table = entry_value.astype(jnp.bfloat16)  7.4 us
    dot_general x3, matrix products, body(): jnp.einsum('cfj,jm->cfm', grad_x, table, preferred_element_type=jnp.float32)  6.72 us
    ppermute x3, starting transfers between devices, gathered_sum(): arrived = lax.ppermute(value, axis, route)  5.4 us
  transfers between devices with their start and end apart: 7, of which 4 were waited for; matrix products, arithmetic and copies ran while one was open for 30% of the time, Pallas kernels for 0%

profile of v8, /device:TPU:0, one launch (start us, length us, event | category | flops | bytes accessed | tf_op | source)
XLA Modules:
  0.0 139.3 jit_solution(10493401880546571573)
XLA Ops:
  7.3 0.5 cosine_multiply_fusion.3
  7.8 1.9 %fusion.128 = (f32[16,2048]{1,0:T(8,128)S(1)}, f32[16,2048]{1,0:T(8,128)S(1)}, f32[16,2048]{1,0:T(8,128)}, f32[16,2048]{1,0:T(8,128)}) fusion(s32[16]{0:T(128)S(1)} %get-tuple-element.102, pred[16]{0:T(512)(128)(4,1)S(1)} %iota_compare_fusion.2, s32[16]{0:T(128)S(1)} %get-tuple-element.103), kind=kLoop, calls=%fused_computation.222 | loop fusion | flops 1179648 | bytes 524432 | tf_op jit(solution)/shard_map/jit(_where)/select_n | solution.py:62
  10.1 1.3 multiply_convert_fusion
  11.3 1.0 compare_select_fusion.2
  12.4 2.0 %convolution_bitcast_fusion = f32[195,4,2048]{2,0,1:T(8,128)S(1)} fusion(bf16[2,128,2048]{2,1,0:T(8,128)(2,1)S(1)} %bitcast.136, bf16[4,2,128,192]{2,3,1,0:T(8,128)(2,1)} %param.3), kind=kOutput, calls=%fused_computation.8 | convolution fusion | flops 817889280 | bytes 7831552 | tf_op jit(solution)/shard_map/crbf,rbm->fcm/dot_general | solution.py:122
  14.4 2.0 %slice_add_fusion = f32[192,4,512]{2,0,1:T(8,128)} fusion(f32[195,4,2048]{2,0,1:T(8,128)S(1)} %convolution_bitcast_fusion), kind=kLoop, calls=%fused_computation.24 | loop fusion | flops 1179648 | bytes 7864320 | tf_op jit(solution)/shard_map/add | solution.py:126
  16.4 0.6 slice.225
  17.0 1.3 collective-permute-start.1
  18.4 0.6 fusion.151
  19.5 0.6 subtract_multiply_fusion.1
  20.1 0.5 fusion.150
  20.6 0.6 iota_compare_fusion.1
  21.2 4.1 %cosine_multiply_fusion = (f32[128,2048]{1,0:T(8,128)S(1)}, f32[128,2048]{1,0:T(8,128)S(1)}) fusion(f32[2048]{0:T(1024)S(1)} %fusion.143), kind=kLoop, calls=%fused_computation.38 | loop fusion | flops 4194304 | bytes 2105344 | tf_op jit(solution)/shard_map/mul | solution.py:44
  25.4 0.6 broadcast_compare_fusion
  26.0 2.1 %cosine_multiply_fusion.1 = (f32[128,1024]{1,0:T(8,128)S(1)}, f32[128,1024]{1,0:T(8,128)S(1)}) fusion(f32[1024]{0:T(1024)S(1)} %subtract_multiply_fusion), kind=kLoop, calls=%fused_computation.59 | loop fusion | flops 2097152 | bytes 1052672 | tf_op jit(solution)/shard_map/mul | solution.py:44
  28.1 0.6 iota_add_fusion.2
  28.7 2.4 %cosine_multiply_fusion.2 = (f32[128,512]{1,0:T(8,128)S(1)}, f32[128,512]{1,0:T(8,128)}) fusion(f32[512]{0:T(512)} %subtract_multiply_fusion.1), kind=kLoop, calls=%fused_computation.161 | loop fusion | flops 1048576 | bytes 526336 | tf_op jit(solution)/shard_map/mul | solution.py:44
  31.1 0.9 fusion.138
  32.0 1.3 broadcast_compare_fusion.1
  33.4 0.8 fusion.145
  34.2 6.7 %add_convert_fusion = bf16[16,128,2048]{2,1,0:T(8,128)(2,1)} fusion(f32[128,2048]{1,0:T(8,128)S(1)} %get-tuple-element.75, f32[16,2048]{1,0:T(8,128)} %get-tuple-element.100, f32[128,2048]{1,0:T(8,128)S(1)} %get-tuple-element.74, f32[16,2048]{1,0:T(8,128)} %get-tuple-element.101), kind=kLoop, calls=%fused_computation | loop fusion | flops 16777216 | bytes 10747904 | tf_op jit(solution)/shard_map/convert_element_type | solution.py:46
  40.9 0.6 add_convert_fusion.1
  41.7 0.6 broadcast_compare_fusion.2
  42.2 0.8 pad_maximum_fusion.1
  43.1 0.7 slice.309
  43.9 0.7 slice.295
  44.8 0.7 fusion.175
  45.6 1.7 %fusion.15 = f32[4,48,1024]{2,1,0:T(8,128)} fusion(bf16[1024,1024]{1,0:T(8,128)(2,1)S(1)} %bitcast.133, bf16[4,48,256]{2,1,0:T(8,128)(2,1)S(1)} %get-tuple-element.57, bf16[4,48,256]{2,1,0:T(8,128)(2,1)S(1)} %get-tuple-element.58, bf16[4,48,256]{2,1,0:T(8,128)(2,1)S(1)} %get-tuple-element.59, bf16[4,48,256]{2,1,0:T(8,128)(2,1)S(1)} %get-tuple-element.56), kind=kOutput, calls=%fused_computation.19 | convolution fusion | flops 404226048 | bytes 3276800 | tf_op jit(solution)/shard_map/cfm,jm->cfj/dot_general | solution.py:155
  47.3 7.0 %fusion.2 = f32[4,24,2048]{2,1,0:T(8,128)} fusion(bf16[2048,2048]{1,0:T(8,128)(2,1)} %bitcast.130, bf16[4,24,512]{2,1,0:T(8,128)(2,1)S(1)} %get-tuple-element.49, bf16[4,24,512]{2,1,0:T(8,128)(2,1)S(1)} %get-tuple-element.50, bf16[4,24,512]{2,1,0:T(8,128)(2,1)S(1)} %get-tuple-element.51, bf16[4,24,512]{2,1,0:T(8,128)(2,1)S(1)} %get-tuple-element.48), kind=kOutput, calls=%fused_computation.3 | convolution fusion | flops 806879232 | bytes 9568256 | tf_op jit(solution)/shard_map/cfm,jm->cfj/dot_general | solution.py:155
  54.3 3.4 %reduce-scatter.2.cloned.1.call-done = f32[24,4,512]{2,0,1:T(8,128)} async-done(((f32[192,4,512]{2,0,1:T(8,128)}), f32[24,4,512]{2,0,1:T(8,128)}) %reduce-scatter.2.cloned.1.call-update) | async-done | bytes 196624 | tf_op jit(solution)/shard_map/reduce_scatter | solution.py:125
  57.7 1.1 copy.55
  58.9 1.3 collective-permute-start
  60.2 2.2 %fusion.34 = f32[4,96,512]{2,1,0:T(8,128)} fusion(bf16[512,512]{1,0:T(8,128)(2,1)S(1)} %bitcast.138, bf16[4,96,128]{2,1,0:T(8,128)(2,1)S(1)} %get-tuple-element.65, bf16[4,96,128]{2,1,0:T(8,128)(2,1)S(1)} %copy-done.17, bf16[4,96,128]{2,1,0:T(8,128)(2,1)} %get-tuple-element.67, bf16[4,96,128]{2,1,0:T(8,128)(2,1)S(1)} %get-tuple-element.64), kind=kOutput, calls=%fused_computation.54 | convolution fusion | flops 202899456 | bytes 1703936 | tf_op jit(solution)/shard_map/cfm,jm->cfj/dot_general | solution.py:155
  62.5 0.7 fusion.172
  63.4 0.8 fusion.174
  64.4 6.3 %fusion.4 = f32[4,24,2048]{2,1,0:T(8,128)S(1)} fusion(bf16[2048,2048]{1,0:T(8,128)(2,1)} %bitcast.131, bf16[4,24,512]{2,1,0:T(8,128)(2,1)} %get-tuple-element.53, bf16[4,24,512]{2,1,0:T(8,128)(2,1)} %get-tuple-element.54, bf16[4,24,512]{2,1,0:T(8,128)(2,1)} %get-tuple-element.55, bf16[4,24,512]{2,1,0:T(8,128)(2,1)S(1)} %get-tuple-element.52), kind=kOutput, calls=%fused_computation.5 | convolution fusion | flops 806879232 | bytes 9568256 | tf_op jit(solution)/shard_map/cfm,jm->cfj/dot_general | solution.py:161
  70.8 1.4 select_reduce_fusion.6
  72.2 0.9 fusion.17
  73.1 1.5 %select_reduce_fusion.7 = (f32[4]{0:T(128)S(1)}, f32[4]{0:T(128)S(1)}, f32[4]{0:T(128)S(1)}, f32[4,48,512]{2,1,0:T(8,128)}, f32[4,48,512]{2,1,0:T(8,128)}) fusion(pred[4,48]{1,0:T(4,128)(4,1)S(1)} %copy-done.28, f32[4,48,1024]{2,1,0:T(8,128)S(1)} %fusion.17, f32[4,48,1024]{2,1,0:T(8,128)S(1)} %copy-done.11), kind=kLoop, calls=%fused_computation.147 | loop fusion | flops 2064372 | bytes 2359536 | tf_op jit(solution)/shard_map/reduce_sum | solution.py:179
  75.0 0.9 copy-done.3
  75.9 1.4 %select_reduce_fusion.8 = (f32[4]{0:T(128)S(1)}, f32[4]{0:T(128)S(1)}, f32[4]{0:T(128)S(1)}, f32[4,96,256]{2,1,0:T(8,128)}, f32[4,96,256]{2,1,0:T(8,128)}) fusion(pred[4,96]{1,0:T(4,128)(4,1)S(1)} %copy-done.26, f32[4,96,512]{2,1,0:T(8,128)S(1)} %fusion.36, f32[4,96,512]{2,1,0:T(8,128)S(1)} %copy-done.12), kind=kLoop, calls=%fused_computation.149 | loop fusion | flops 2064372 | bytes 2359728 | tf_op jit(solution)/shard_map/reduce_sum | solution.py:179
  77.4 10.8 %all-gather = f32[24,3,4]{2,1,0:T(4,128)S(1)} all-gather(f32[3,3,4]{2,1,0:T(4,128)S(1)} %pad_maximum_fusion.6), channel_id=2, replica_groups=mesh['clip'=4,'seg'=8] {'seg'}, dimensions={0}, use_global_device_ids=true | all-gather | bytes 1296 | tf_op jit(solution)/shard_map/all_gather | solution.py:188
  88.2 0.6 multiply_rsqrt_fusion
  88.8 1.8 %divide_convert_fusion.3 = (bf16[4,48,512]{2,1,0:T(8,128)(2,1)S(1)}, bf16[4,48,512]{2,1,0:T(8,128)(2,1)S(1)}) fusion(f32[4,48,1024]{2,1,0:T(8,128)} %copy-done.5, f32[4,48,512]{2,1,0:T(8,128)} %get-tuple-element.23, f32[4,48,512]{2,1,0:T(8,128)} %get-tuple-element.24, f32[4]{0:T(128)S(1)} %copy-done.21, f32[4]{0:T(128)S(1)} %get-tuple-element.82, ...), kind=kLoop, calls=%fused_computation.131 | loop fusion | flops 1671168 | bytes 1966304 | tf_op jit(solution)/shard_map/convert.2
  90.7 1.5 %fusion.13 = f32[4,48,1024]{2,1,0:T(8,128)} fusion(bf16[1024,1024]{1,0:T(8,128)(2,1)S(1)} %bitcast.135, bf16[4,48,512]{2,1,0:T(8,128)(2,1)S(1)} %get-tuple-element.30, bf16[4,48,512]{2,1,0:T(8,128)(2,1)S(1)} %get-tuple-element.29), kind=kOutput, calls=%fused_computation.17 | convolution fusion | flops 403439616 | bytes 3276800 | tf_op jit(solution)/shard_map/cfj,jm->cfm/dot_general | solution.py:208
  92.2 1.6 %reshape.914 = f32[4,48,4,256]{3,2,1,0:T(4,128)S(1)} reshape(f32[4,48,1024]{2,1,0:T(8,128)} %fusion.13) | data formatting | bytes 1572864 | tf_op jit(solution)/shard_map/reshape | solution.py:211
  93.7 0.6 fusion.169
  94.9 0.8 pad_add_fusion.1
  95.7 0.5 divide_convert_fusion.1
  96.1 4.9 %fusion = f32[4,24,2048]{2,1,0:T(8,128)S(1)} fusion(bf16[2048,2048]{1,0:T(8,128)(2,1)} %bitcast.132, bf16[4,24,1024]{2,1,0:T(8,128)(2,1)S(1)} %get-tuple-element.32, bf16[4,24,1024]{2,1,0:T(8,128)(2,1)S(1)} %get-tuple-element.31), kind=kOutput, calls=%fused_computation.1 | convolution fusion | flops 806092800 | bytes 9568256 | tf_op jit(solution)/shard_map/cfj,jm->cfm/dot_general | solution.py:208
  101.0 0.5 reshape.916
  101.6 0.7 fusion.170
  103.0 0.5 divide_convert_fusion.5
  104.1 0.6 fusion.168
  105.4 2.2 %collective-permute-start.5 = (f32[4,1536]{1,0:T(4,128)S(1)}, f32[4,1536]{1,0:T(4,128)S(1)}, u32[]{:S(2)}, u32[]{:S(2)}) collective-permute-start(f32[4,1536]{1,0:T(4,128)S(1)} %add_add_fusion.3), channel_id=1, source_target_pairs={{0,1},{1,2},{2,3},{3,4},{4,5},{5,6},{6,7},{8,9},{9,10},{10,11},{11... | collective-permute-start | bytes 73736 | tf_op jit(solution)/shard_map/ppermute | solution.py:20
  107.7 1.5 %collective-permute-start.2 = (f32[]{:T(128)}, f32[]{:T(128)}, u32[]{:S(2)}, u32[]{:S(2)}) collective-permute-start(f32[]{:T(128)} %get-tuple-element.77), channel_id=1, source_target_pairs={{0,8},{8,16},{16,24},{24,0},{1,9},{9,17},{17,25},{25,1},{2,10},{10... | collective-permute-start | bytes 20 | tf_op jit(solution)/shard_map/ppermute | solution.py:79
  109.2 2.4 %collective-permute-start.3 = (f32[]{:T(128)}, f32[]{:T(128)}, u32[]{:S(2)}, u32[]{:S(2)}) collective-permute-start(f32[]{:T(128)} %get-tuple-element.77), channel_id=1, source_target_pairs={{0,16},{8,24},{16,0},{24,8},{1,17},{9,25},{17,1},{25,9},{2,18},{10... | collective-permute-start | bytes 20 | tf_op jit(solution)/shard_map/ppermute | solution.py:79
  111.7 1.4 %collective-permute-start.4 = (f32[]{:T(128)}, f32[]{:T(128)}, u32[]{:S(2)}, u32[]{:S(2)}) collective-permute-start(f32[]{:T(128)} %get-tuple-element.77), channel_id=1, source_target_pairs={{0,24},{8,0},{16,8},{24,16},{1,25},{9,1},{17,9},{25,17},{2,26},{10... | collective-permute-start | bytes 20 | tf_op jit(solution)/shard_map/ppermute | solution.py:79
  113.8 1.5 %collective-permute-done.4 = f32[]{:T(128)} collective-permute-done((f32[]{:T(128)}, f32[]{:T(128)}, u32[]{:S(2)}, u32[]{:S(2)}) %collective-permute-start.4) | collective-permute-done | bytes 36 | tf_op jit(solution)/shard_map/ppermute | solution.py:79
  115.4 3.0 %fusion.153 = f32[]{:T(128)} fusion(f32[]{:T(128)} %collective-permute-done.4, s32[]{:T(128)S(6)} %select_n.332, f32[]{:T(128)} %collective-permute-done.3, s32[]{:T(128)S(6)} %select_n.330, f32[]{:T(128)} %collective-permute-done.2, s32[]{:T(128)S(6)} %select_n.328, f32[]{:T(128)} %get-tuple-element.77, s32[]{:T(128)S(6)} %select_n.293), kind=kLoop, calls=%fused_computation.292 | loop fusion | flops 47 | bytes 36 | tf_op jit(solution)/shard_map/reduce_sum | solution.py:86
  119.2 9.6 %all_gather.11 = bf16[4,192,512]{2,1,0:T(8,128)(2,1)S(1)} all-gather(bf16[4,24,512]{2,1,0:T(8,128)(2,1)S(1)} %bitcast.167), channel_id=1, replica_groups=mesh['clip'=4,'seg'=8] {'seg'}, dimensions={1}, use_global_device_ids=true | all-gather | bytes 884736 | tf_op jit(solution)/shard_map/all_gather | solution.py:220
  128.8 0.5 pad_slice_fusion.2
  129.3 1.3 fusion.20
  130.6 0.8 copy.40
  (128 shorter events, 6.0 us)
Async XLA Ops:
  7.2 50.6 %reduce-scatter.2.cloned.1.call-start = ((), (), s32[]{:S(2)}) async-start(), calls=%async_computation.1 | async-start | bytes 1769472 | tf_op jit(solution)/shard_map/reduce_scatter | solution.py:125
  10.0 6.3 %copy-start = (bf16[16,16,2048]{2,1,0:T(8,128)(2,1)}, bf16[16,16,2048]{2,1,0:T(8,128)(2,1)S(1)}, u32[]{:S(2)}) copy-start(bf16[16,16,2048]{2,1,0:T(8,128)(2,1)S(1)} %add_convert_fusion.2) | copy-start | bytes 3145732
  11.3 5.0 %copy-start.18 = (s32[4]{0:T(128)}, s32[4]{0:T(128)S(1)}, u32[]{:S(2)}) copy-start(s32[4]{0:T(128)S(1)} %get-tuple-element.95) | copy-start | bytes 52
  14.4 11.0 %copy-start.22 = (s32[4]{0:T(128)S(1)}, s32[4]{0:T(128)}, u32[]{:S(2)}) copy-start(s32[4]{0:T(128)} %param.5) | copy-start | bytes 52
  17.0 25.3 %collective-permute-start.1 = (bf16[4,1536]{1,0:T(4,128)(2,1)}, bf16[4,1536]{1,0:T(4,128)(2,1)}, u32[]{:S(2)}, u32[]{:S(2)}) collective-permute-start(bf16[4,1536]{1,0:T(4,128)(2,1)} %slice.225), channel_id=1, source_target_pairs={{1,0},{2,1},{3,2},{4,3},{5,4},{6,5},{7,6},{9,8},{10,9},{11,10},{12... | collective-permute-start | bytes 36872 | tf_op jit(solution)/shard_map/ppermute | solution.py:20
  34.2 7.3 %copy-start.10 = (f32[128,512]{1,0:T(8,128)S(1)}, f32[128,512]{1,0:T(8,128)}, u32[]{:S(2)}) copy-start(f32[128,512]{1,0:T(8,128)} %get-tuple-element.84) | copy-start | bytes 786436
  40.9 0.7 copy-start.29
  47.3 11.5 %copy-start.19 = (s32[4]{0:T(128)S(1)}, s32[4]{0:T(128)}, u32[]{:S(2)}) copy-start(s32[4]{0:T(128)} %copy-done.18) | copy-start | bytes 52
  47.3 12.9 %copy-start.17 = (bf16[4,96,128]{2,1,0:T(8,128)(2,1)S(1)}, bf16[4,96,128]{2,1,0:T(8,128)(2,1)}, u32[]{:S(2)}) copy-start(bf16[4,96,128]{2,1,0:T(8,128)(2,1)} %get-tuple-element.66) | copy-start | bytes 294916
  58.9 3.5 %collective-permute-start = (bf16[4,1536]{1,0:T(4,128)(2,1)S(1)}, bf16[4,1536]{1,0:T(4,128)(2,1)S(1)}, u32[]{:S(2)}, u32[]{:S(2)}) collective-permute-start(bf16[4,1536]{1,0:T(4,128)(2,1)S(1)} %slice.287), channel_id=1, source_target_pairs={{1,0},{2,1},{3,2},{4,3},{5,4},{6,5},{7,6},{9,8},{10,9},{11,10},{12... | collective-permute-start | bytes 36872 | tf_op jit(solution)/shard_map/ppermute | solution.py:20
  64.4 6.3 %copy-start.2 = (f32[4,24,2048]{2,1,0:T(8,128)S(1)}, f32[4,24,2048]{2,1,0:T(8,128)}, u32[]{:S(2)}) copy-start(f32[4,24,2048]{2,1,0:T(8,128)} %fusion.2) | copy-start | bytes 2359300
  64.4 6.3 %copy-start.24 = (pred[4,24]{1,0:T(4,128)(4,1)S(1)}, pred[4,24]{1,0:T(4,128)(4,1)}, u32[]{:S(2)}) copy-start(pred[4,24]{1,0:T(4,128)(4,1)} %broadcast_compare_fusion) | copy-start | bytes 292
  64.4 7.7 %copy-start.13 = (bf16[4,48,256]{2,1,0:T(8,128)(2,1)S(1)}, bf16[4,48,256]{2,1,0:T(8,128)(2,1)}, u32[]{:S(2)}) copy-start(bf16[4,48,256]{2,1,0:T(8,128)(2,1)} %get-tuple-element.60) | copy-start | bytes 294916
  64.4 7.7 %copy-start.14 = (bf16[4,48,256]{2,1,0:T(8,128)(2,1)S(1)}, bf16[4,48,256]{2,1,0:T(8,128)(2,1)}, u32[]{:S(2)}) copy-start(bf16[4,48,256]{2,1,0:T(8,128)(2,1)} %get-tuple-element.61) | copy-start | bytes 294916
  64.4 7.7 %copy-start.15 = (bf16[4,48,256]{2,1,0:T(8,128)(2,1)S(1)}, bf16[4,48,256]{2,1,0:T(8,128)(2,1)}, u32[]{:S(2)}) copy-start(bf16[4,48,256]{2,1,0:T(8,128)(2,1)} %get-tuple-element.62) | copy-start | bytes 294916
  64.4 7.7 %copy-start.16 = (bf16[4,48,256]{2,1,0:T(8,128)(2,1)S(1)}, bf16[4,48,256]{2,1,0:T(8,128)(2,1)}, u32[]{:S(2)}) copy-start(bf16[4,48,256]{2,1,0:T(8,128)(2,1)} %get-tuple-element.63) | copy-start | bytes 294916
  70.7 2.3 %copy-start.11 = (f32[4,48,1024]{2,1,0:T(8,128)S(1)}, f32[4,48,1024]{2,1,0:T(8,128)}, u32[]{:S(2)}) copy-start(f32[4,48,1024]{2,1,0:T(8,128)} %fusion.15) | copy-start | bytes 2359300
  70.8 2.3 %copy-start.28 = (pred[4,48]{1,0:T(4,128)(4,1)S(1)}, pred[4,48]{1,0:T(4,128)(4,1)}, u32[]{:S(2)}) copy-start(pred[4,48]{1,0:T(4,128)(4,1)} %broadcast_compare_fusion.1) | copy-start | bytes 580
  72.1 3.7 %copy-start.12 = (f32[4,96,512]{2,1,0:T(8,128)S(1)}, f32[4,96,512]{2,1,0:T(8,128)}, u32[]{:S(2)}) copy-start(f32[4,96,512]{2,1,0:T(8,128)} %fusion.34) | copy-start | bytes 2359300
  72.1 3.7 %copy-start.26 = (pred[4,96]{1,0:T(4,128)(4,1)S(1)}, pred[4,96]{1,0:T(4,128)(4,1)}, u32[]{:S(2)}) copy-start(pred[4,96]{1,0:T(4,128)(4,1)} %broadcast_compare_fusion.2) | copy-start | bytes 1156
  73.1 4.2 %copy-start.5 = (f32[4,48,1024]{2,1,0:T(8,128)}, f32[4,48,1024]{2,1,0:T(8,128)S(1)}, u32[]{:S(2)}) copy-start(f32[4,48,1024]{2,1,0:T(8,128)S(1)} %fusion.17) | copy-start | bytes 2359300
  73.1 4.3 %copy-start.23 = (s32[4]{0:T(128)S(1)}, s32[4]{0:T(128)}, u32[]{:S(2)}) copy-start(s32[4]{0:T(128)} %param.5) | copy-start | bytes 52
  73.1 15.7 %copy-start.21 = (f32[4]{0:T(128)S(1)}, f32[4]{0:T(128)}, u32[]{:S(2)}) copy-start(f32[4]{0:T(128)} %get-tuple-element.93) | copy-start | bytes 52
  75.0 0.9 copy-start.3
  90.6 5.0 %copy-start.25 = (pred[4,24]{1,0:T(4,128)(4,1)S(1)}, pred[4,24]{1,0:T(4,128)(4,1)}, u32[]{:S(2)}) copy-start(pred[4,24]{1,0:T(4,128)(4,1)} %broadcast_compare_fusion) | copy-start | bytes 292
  92.1 3.5 %copy-start.8 = (f32[4,24,1024]{2,1,0:T(8,128)S(1)}, f32[4,24,1024]{2,1,0:T(8,128)}, u32[]{:S(2)}) copy-start(f32[4,24,1024]{2,1,0:T(8,128)} %get-tuple-element.25) | copy-start | bytes 1179652
  92.1 3.5 %copy-start.9 = (f32[4,24,1024]{2,1,0:T(8,128)S(1)}, f32[4,24,1024]{2,1,0:T(8,128)}, u32[]{:S(2)}) copy-start(f32[4,24,1024]{2,1,0:T(8,128)} %get-tuple-element.26) | copy-start | bytes 1179652
  101.0 1.9 %copy-start.4 = (f32[4,96,512]{2,1,0:T(8,128)S(1)}, f32[4,96,512]{2,1,0:T(8,128)}, u32[]{:S(2)}) copy-start(f32[4,96,512]{2,1,0:T(8,128)} %copy-done.3) | copy-start | bytes 2359300
  101.0 1.9 %copy-start.6 = (f32[4,96,256]{2,1,0:T(8,128)S(1)}, f32[4,96,256]{2,1,0:T(8,128)}, u32[]{:S(2)}) copy-start(f32[4,96,256]{2,1,0:T(8,128)} %get-tuple-element.21) | copy-start | bytes 1179652
  101.0 1.9 %copy-start.27 = (pred[4,96]{1,0:T(4,128)(4,1)S(1)}, pred[4,96]{1,0:T(4,128)(4,1)}, u32[]{:S(2)}) copy-start(pred[4,96]{1,0:T(4,128)(4,1)} %broadcast_compare_fusion.2) | copy-start | bytes 1156
  101.6 1.4 copy-start.7
  103.4 15.6 %slice-start = ((f32[4,51,256]{2,0,1:T(4,128)}), f32[4,48,256]{2,0,1:T(4,128)S(1)}, s32[]{:S(2)}) async-start(f32[4,51,256]{2,0,1:T(4,128)} %pad_add_fusion.1), calls=%async_computation.2 | async-start | bytes 393216 | tf_op jit(solution)/shard_map/slice | solution.py:212
  103.5 15.6 %copy-start.20 = (s32[4]{0:T(128)S(1)}, s32[4]{0:T(128)}, u32[]{:S(2)}) copy-start(s32[4]{0:T(128)} %copy-done.18) | copy-start | bytes 52
  105.0 24.3 %copy-start.1 = (bf16[16,16,2048]{2,1,0:T(8,128)(2,1)S(1)}, bf16[16,16,2048]{2,1,0:T(8,128)(2,1)}, u32[]{:S(2)}) copy-start(bf16[16,16,2048]{2,1,0:T(8,128)(2,1)} %copy-done) | copy-start | bytes 3145732
  105.4 13.7 %collective-permute-start.5 = (f32[4,1536]{1,0:T(4,128)S(1)}, f32[4,1536]{1,0:T(4,128)S(1)}, u32[]{:S(2)}, u32[]{:S(2)}) collective-permute-start(f32[4,1536]{1,0:T(4,128)S(1)} %add_add_fusion.3), channel_id=1, source_target_pairs={{0,1},{1,2},{2,3},{3,4},{4,5},{5,6},{6,7},{8,9},{9,10},{10,11},{11... | collective-permute-start | bytes 73736 | tf_op jit(solution)/shard_map/ppermute | solution.py:20
  107.7 5.7 %collective-permute-start.2 = (f32[]{:T(128)}, f32[]{:T(128)}, u32[]{:S(2)}, u32[]{:S(2)}) collective-permute-start(f32[]{:T(128)} %get-tuple-element.77), channel_id=1, source_target_pairs={{0,8},{8,16},{16,24},{24,0},{1,9},{9,17},{17,25},{25,1},{2,10},{10... | collective-permute-start | bytes 20 | tf_op jit(solution)/shard_map/ppermute | solution.py:79
  109.2 4.6 %collective-permute-start.3 = (f32[]{:T(128)}, f32[]{:T(128)}, u32[]{:S(2)}, u32[]{:S(2)}) collective-permute-start(f32[]{:T(128)} %get-tuple-element.77), channel_id=1, source_target_pairs={{0,16},{8,24},{16,0},{24,8},{1,17},{9,25},{17,1},{25,9},{2,18},{10... | collective-permute-start | bytes 20 | tf_op jit(solution)/shard_map/ppermute | solution.py:79
  111.7 3.7 %collective-permute-start.4 = (f32[]{:T(128)}, f32[]{:T(128)}, u32[]{:S(2)}, u32[]{:S(2)}) collective-permute-start(f32[]{:T(128)} %get-tuple-element.77), channel_id=1, source_target_pairs={{0,24},{8,0},{16,8},{24,16},{1,25},{9,1},{17,9},{25,17},{2,26},{10... | collective-permute-start | bytes 20 | tf_op jit(solution)/shard_map/ppermute | solution.py:79
Sparse Core Ops, SparseCore 0:
  16.5 41.1 reduce-scatter.1

commit v9 on v6

--- a/solution.py
+++ b/solution.py
@@ -66,19 +66,15 @@
     return lax.optimization_barrier(table.reshape(2, band_count, NFFT))
 
 
-def ring_gathered(value, axis):
+def gathered_sum(value, axis):
     size = lax.axis_size(axis)
     here = lax.axis_index(axis)
     held = [value]
     for distance in range(1, size):
         route = [(i, (i + distance) % size) for i in range(size)]
         held.append(lax.ppermute(value, axis, route))
-    held = jnp.stack(held)
-    source = (here - jnp.arange(size, dtype=jnp.int32)) % size
-    pick = source[:, None] == jnp.arange(size, dtype=jnp.int32)[None, :]
-    return jnp.sum(
-        jnp.where(pick.reshape((size, size) + (1,) * value.ndim), held[:, None], 0.0), axis=0
-    )
+    in_order = jnp.take(jnp.stack(held), (here - jnp.arange(size, dtype=jnp.int32)) % size, axis=0)
+    return jnp.sum(in_order, axis=0)
 
 
 def spread_parts(quarters):
@@ -180,12 +176,10 @@
     spreads = jnp.stack(spread_list)
     energies = jnp.stack(energy_list)
     logterms = jnp.stack(logterm_list)
-    groups = ring_gathered(jnp.stack([spreads, energies, logterms]), "clip")
-    totals = jnp.sum(lax.all_gather(groups, "seg", axis=0, tiled=False), axis=0)
-    loss = jnp.sum(jnp.sqrt((totals[:, 0] + EPS_RATIO) / totals[:, 1]) + totals[:, 2]) / (
-        3 * clip_count * lax.axis_size("clip")
-    )
-    spreads, energies, logterms = totals[lax.axis_index("clip")]
+    parts = lax.all_gather(jnp.stack([spreads, energies, logterms]), "seg", axis=0, tiled=False)
+    spreads, energies, logterms = jnp.sum(parts, axis=0)
+    own_loss = jnp.sum(jnp.sqrt((spreads + EPS_RATIO) / energies) + logterms)
+    loss = gathered_sum(own_loss, "clip") / (3 * clip_count * lax.axis_size("clip"))
     ratio_weight = 1.0 / jnp.sqrt((spreads + EPS_RATIO) * energies)
     gradient = jnp.zeros((clip_count, samples), jnp.float32)
     extras = []

time: 145 us -> 141 us (0.972)
  waiting for transfers between devices: 12.4 us -> 8.14 us
  other arithmetic: 40.2 us -> 42.4 us
  blocking collectives: 23.6 us -> 21.9 us
    ppermute x3, waiting for transfers between devices: 4.33 us -> 0.01 us  [gathered_sum(): held.append(lax.ppermute(value, axis, route))]
    another operation x8, other arithmetic: 2.63 us -> 5.22 us  [the longest x1 2.6 us: gathered_sum(): jnp.stack(held)]
    unnamed x73 -> x71, local copies, waits for them, and re-layouts: 4.5 us -> 4.5 us
  transfers between devices with their start and end apart: 7 -> 7, of which waited for: 5 -> 2; matrix products, arithmetic and copies ran while one was open for 23% -> 39% of each run, Pallas kernels for 0% -> 0%
where the time goes in v9:
time: 141 us
  other arithmetic  42.4 us (30%)
  matrix products  27.6 us (20%)
  blocking collectives  21.9 us (16%)
  between operations  16.7 us (12%)
  local copies, waits for them, and re-layouts  14.9 us (11%)
  starting transfers between devices  8.98 us (6%)
  waiting for transfers between devices  8.14 us (6%)
    all_gather x1, blocking collectives, body(): portion = lax.all_gather(grad_hops, 'seg', axis=1, tiled=True)  11.6 us
    all_gather x1, blocking collectives, body(): lax.all_gather(jnp.stack([spreads, energies, logterms]), 'seg', axis=0, t...  10.3 us
    dot_general x3, matrix products, body(): jnp.einsum('cfm,jm->cfj', framed(clean, clean_beyond[:, :3 * stride], str...  10.1 us
    mul x3, other arithmetic, analysis_table(): fine_cos, fine_sin = (part * scale for part in fine)  9.54 us
    convert_element_type x3, other arithmetic, analysis_table(): table = entry_value.astype(jnp.bfloat16)  9.29 us
    dot_general x3, matrix products, body(): jnp.einsum('cfm,jm->cfj', framed(est_wave, est_beyond[:, :3 * stride], st...  8.46 us
    reduce_scatter x1, waiting for transfers between devices, body(): lax.psum_scatter(sum((framed_sig[3 - quarter:3 - quarter + rows_here * la...  7.87 us
    dot_general x3, matrix products, body(): jnp.einsum('cfj,jm->cfm', grad_x, table, preferred_element_type=jnp.float32)  5.81 us
  transfers between devices with their start and end apart: 7, of which 2 were waited for; matrix products, arithmetic and copies ran while one was open for 39% of the time, Pallas kernels for 0%

profile of v9, /device:TPU:0, one launch (start us, length us, event | category | flops | bytes accessed | tf_op | source)
XLA Modules:
  0.0 140.7 jit_solution(4250436362426060738)
XLA Ops:
  7.3 1.2 multiply_convert_fusion
  8.5 0.5 cosine_multiply_fusion.3
  9.0 1.9 %fusion.128 = (f32[16,2048]{1,0:T(8,128)S(1)}, f32[16,2048]{1,0:T(8,128)S(1)}, f32[16,2048]{1,0:T(8,128)S(1)}, f32[16,2048]{1,0:T(8,128)}) fusion(s32[16]{0:T(128)S(1)} %get-tuple-element.102, pred[16]{0:T(512)(128)(4,1)S(1)} %iota_compare_fusion.2, s32[16]{0:T(128)S(1)} %get-tuple-element.103), kind=kLoop, calls=%fused_computation.223 | loop fusion | flops 1179648 | bytes 524432 | tf_op jit(solution)/shard_map/jit(_where)/select_n | solution.py:62
  10.9 0.2 add_convert_fusion.2
  11.2 1.1 compare_select_fusion.2
  12.3 2.0 %convolution_bitcast_fusion = f32[195,4,2048]{2,0,1:T(8,128)S(1)} fusion(bf16[2,128,2048]{2,1,0:T(8,128)(2,1)S(1)} %bitcast.142, bf16[4,2,128,192]{2,3,1,0:T(8,128)(2,1)} %param.3), kind=kOutput, calls=%fused_computation.9 | convolution fusion | flops 817889280 | bytes 7831552 | tf_op jit(solution)/shard_map/crbf,rbm->fcm/dot_general | solution.py:113
  14.4 2.0 %slice_add_fusion = f32[192,4,512]{2,0,1:T(8,128)} fusion(f32[195,4,2048]{2,0,1:T(8,128)S(1)} %convolution_bitcast_fusion), kind=kLoop, calls=%fused_computation.25 | loop fusion | flops 1179648 | bytes 7864320 | tf_op jit(solution)/shard_map/add | solution.py:117
  16.4 1.5 %collective-permute-start.1 = (bf16[4,1536]{1,0:T(4,128)(2,1)S(1)}, bf16[4,1536]{1,0:T(4,128)(2,1)S(1)}, u32[]{:S(2)}, u32[]{:S(2)}) collective-permute-start(bf16[4,1536]{1,0:T(4,128)(2,1)S(1)} %slice.225), channel_id=1, source_target_pairs={{1,0},{2,1},{3,2},{4,3},{5,4},{6,5},{7,6},{9,8},{10,9},{11,10},{12... | collective-permute-start | bytes 36872 | tf_op jit(solution)/shard_map/ppermute | solution.py:20
  18.1 1.1 cosine_multiply_fusion.2
  19.2 3.1 %cosine_multiply_fusion.1 = (f32[128,1024]{1,0:T(8,128)}, f32[128,1024]{1,0:T(8,128)}) fusion(f32[1024]{0:T(1024)S(1)} %subtract_multiply_fusion), kind=kLoop, calls=%fused_computation.60 | loop fusion | flops 2097152 | bytes 1052672 | tf_op jit(solution)/shard_map/mul | solution.py:44
  22.3 0.7 broadcast_compare_fusion
  23.0 5.4 %cosine_multiply_fusion = (f32[128,2048]{1,0:T(8,128)S(1)}, f32[128,2048]{1,0:T(8,128)}) fusion(f32[2048]{0:T(1024)S(1)} %fusion.143), kind=kLoop, calls=%fused_computation.39 | loop fusion | flops 4194304 | bytes 2105344 | tf_op jit(solution)/shard_map/mul | solution.py:44
  28.4 0.6 broadcast_compare_fusion.2
  29.0 0.2 fusion.145
  29.2 0.6 broadcast_compare_fusion.1
  29.7 0.2 fusion.138
  30.0 1.0 add_convert_fusion.3
  31.0 1.8 %add_convert_fusion.1 = bf16[8,128,1024]{2,1,0:T(8,128)(2,1)S(1)} fusion(f32[128,1024]{1,0:T(8,128)} %get-tuple-element.79, f32[8,1024]{1,0:T(8,128)S(1)} %get-tuple-element.88, f32[128,1024]{1,0:T(8,128)} %get-tuple-element.78, f32[8,1024]{1,0:T(8,128)S(1)} %get-tuple-element.87), kind=kLoop, calls=%fused_computation.8 | loop fusion | flops 4194304 | bytes 3211264 | tf_op jit(solution)/shard_map/convert_element_type | solution.py:46
  32.7 6.5 %add_convert_fusion = bf16[16,128,2048]{2,1,0:T(8,128)(2,1)} fusion(f32[128,2048]{1,0:T(8,128)S(1)} %copy-done.2, f32[16,2048]{1,0:T(8,128)S(1)} %get-tuple-element.100, f32[128,2048]{1,0:T(8,128)S(1)} %get-tuple-element.74, f32[16,2048]{1,0:T(8,128)} %get-tuple-element.101), kind=kLoop, calls=%fused_computation.1 | loop fusion | flops 16777216 | bytes 10747904 | tf_op jit(solution)/shard_map/convert_element_type | solution.py:46
  39.3 0.6 pad_clamp_fusion
  40.3 0.7 fusion.175
  41.1 1.8 %fusion.15 = f32[4,48,1024]{2,1,0:T(8,128)} fusion(bf16[1024,1024]{1,0:T(8,128)(2,1)S(1)} %bitcast.139, bf16[4,48,256]{2,1,0:T(8,128)(2,1)S(1)} %get-tuple-element.57, bf16[4,48,256]{2,1,0:T(8,128)(2,1)S(1)} %get-tuple-element.58, bf16[4,48,256]{2,1,0:T(8,128)(2,1)S(1)} %get-tuple-element.59, bf16[4,48,256]{2,1,0:T(8,128)(2,1)S(1)} %get-tuple-element.56), kind=kOutput, calls=%fused_computation.20 | convolution fusion | flops 404226048 | bytes 3276800 | tf_op jit(solution)/shard_map/cfm,jm->cfj/dot_general | solution.py:146
  42.9 7.0 %fusion.2 = f32[4,24,2048]{2,1,0:T(8,128)} fusion(bf16[2048,2048]{1,0:T(8,128)(2,1)} %bitcast.136, bf16[4,24,512]{2,1,0:T(8,128)(2,1)S(1)} %get-tuple-element.49, bf16[4,24,512]{2,1,0:T(8,128)(2,1)S(1)} %get-tuple-element.50, bf16[4,24,512]{2,1,0:T(8,128)(2,1)S(1)} %get-tuple-element.51, bf16[4,24,512]{2,1,0:T(8,128)(2,1)S(1)} %get-tuple-element.48), kind=kOutput, calls=%fused_computation.4 | convolution fusion | flops 806879232 | bytes 9568256 | tf_op jit(solution)/shard_map/cfm,jm->cfj/dot_general | solution.py:146
  49.9 7.9 %reduce-scatter.2.cloned.1.call-done = f32[24,4,512]{2,0,1:T(8,128)} async-done(((f32[192,4,512]{2,0,1:T(8,128)}), f32[24,4,512]{2,0,1:T(8,128)}) %reduce-scatter.2.cloned.1.call-update) | async-done | bytes 196624 | tf_op jit(solution)/shard_map/reduce_scatter | solution.py:116
  57.8 1.1 copy.55
  59.0 1.5 %collective-permute-start = (bf16[4,1536]{1,0:T(4,128)(2,1)S(1)}, bf16[4,1536]{1,0:T(4,128)(2,1)S(1)}, u32[]{:S(2)}, u32[]{:S(2)}) collective-permute-start(bf16[4,1536]{1,0:T(4,128)(2,1)S(1)} %slice.289), channel_id=1, source_target_pairs={{1,0},{2,1},{3,2},{4,3},{5,4},{6,5},{7,6},{9,8},{10,9},{11,10},{12... | collective-permute-start | bytes 36872 | tf_op jit(solution)/shard_map/ppermute | solution.py:20
  60.5 1.3 fusion.34
  61.8 0.2 collective-permute-done
  62.2 0.8 fusion.176
  63.1 0.8 fusion.174
  64.1 1.5 %fusion.36 = f32[4,96,512]{2,1,0:T(8,128)S(1)} fusion(bf16[512,512]{1,0:T(8,128)(2,1)S(1)} %bitcast.145, bf16[4,96,128]{2,1,0:T(8,128)(2,1)} %get-tuple-element.69, bf16[4,96,128]{2,1,0:T(8,128)(2,1)} %get-tuple-element.70, bf16[4,96,128]{2,1,0:T(8,128)(2,1)} %get-tuple-element.71, bf16[4,96,128]{2,1,0:T(8,128)(2,1)} %get-tuple-element.68), kind=kOutput, calls=%fused_computation.57 | convolution fusion | flops 202899456 | bytes 1703936 | tf_op jit(solution)/shard_map/cfm,jm->cfj/dot_general | solution.py:152
  65.6 1.0 copy-done.4
  66.6 2.6 %select_reduce_fusion.8 = (f32[4]{0:T(128)S(1)}, f32[4]{0:T(128)S(1)}, f32[4]{0:T(128)S(1)}, f32[4,96,256]{2,1,0:T(8,128)}, f32[4,96,256]{2,1,0:T(8,128)}) fusion(pred[4,96]{1,0:T(4,128)(4,1)} %broadcast_compare_fusion.2, f32[4,96,512]{2,1,0:T(8,128)S(1)} %fusion.36, f32[4,96,512]{2,1,0:T(8,128)} %fusion.34), kind=kLoop, calls=%fused_computation.150 | loop fusion | flops 2064372 | bytes 2359728 | tf_op jit(solution)/shard_map/reduce_sum | solution.py:170
  69.2 0.9 fusion.17
  70.0 1.5 %select_reduce_fusion.7 = (f32[4]{0:T(128)S(1)}, f32[4]{0:T(128)S(1)}, f32[4]{0:T(128)S(1)}, f32[4,48,512]{2,1,0:T(8,128)}, f32[4,48,512]{2,1,0:T(8,128)}) fusion(pred[4,48]{1,0:T(4,128)(4,1)S(1)} %copy-done.25, f32[4,48,1024]{2,1,0:T(8,128)S(1)} %fusion.17, f32[4,48,1024]{2,1,0:T(8,128)S(1)} %copy-done.13), kind=kLoop, calls=%fused_computation.148 | loop fusion | flops 2064372 | bytes 2359536 | tf_op jit(solution)/shard_map/reduce_sum | solution.py:170
  71.5 6.1 %fusion.4 = f32[4,24,2048]{2,1,0:T(8,128)S(1)} fusion(bf16[2048,2048]{1,0:T(8,128)(2,1)} %bitcast.137, bf16[4,24,512]{2,1,0:T(8,128)(2,1)S(1)} %get-tuple-element.53, bf16[4,24,512]{2,1,0:T(8,128)(2,1)S(1)} %get-tuple-element.54, bf16[4,24,512]{2,1,0:T(8,128)(2,1)S(1)} %get-tuple-element.55, bf16[4,24,512]{2,1,0:T(8,128)(2,1)S(1)} %get-tuple-element.52), kind=kOutput, calls=%fused_computation.6 | convolution fusion | flops 806879232 | bytes 9568256 | tf_op jit(solution)/shard_map/cfm,jm->cfj/dot_general | solution.py:152
  77.7 1.4 select_reduce_fusion.6
  79.1 10.3 %all-gather = f32[24,3,4]{2,1,0:T(4,128)S(1)} all-gather(f32[3,3,4]{2,1,0:T(4,128)S(1)} %pad_maximum_fusion.6), channel_id=2, replica_groups=mesh['clip'=4,'seg'=8] {'seg'}, dimensions={0}, use_global_device_ids=true | all-gather | bytes 1296 | tf_op jit(solution)/shard_map/all_gather | solution.py:179
  89.4 0.7 multiply_rsqrt_fusion
  90.1 3.3 %collective-permute-start.4 = (f32[]{:T(128)}, f32[]{:T(128)}, u32[]{:S(2)}, u32[]{:S(2)}) collective-permute-start(f32[]{:T(128)} %get-tuple-element.77), channel_id=1, source_target_pairs={{0,24},{8,0},{16,8},{24,16},{1,25},{9,1},{17,9},{25,17},{2,26},{10... | collective-permute-start | bytes 20 | tf_op jit(solution)/shard_map/ppermute | solution.py:75
  93.4 1.1 collective-permute-start.2
  94.6 1.6 %divide_convert_fusion.1 = (bf16[4,24,1024]{2,1,0:T(8,128)(2,1)S(1)}, bf16[4,24,1024]{2,1,0:T(8,128)(2,1)S(1)}) fusion(f32[4,24,2048]{2,1,0:T(8,128)S(1)} %fusion.4, f32[4,24,1024]{2,1,0:T(8,128)} %get-tuple-element.25, f32[4,24,1024]{2,1,0:T(8,128)} %get-tuple-element.26, f32[4]{0:T(128)S(1)} %copy-done.21, f32[4]{0:T(128)S(1)} %get-tuple-element.81, ...), kind=kLoop, calls=%fused_computation.129 | loop fusion | flops 1671168 | bytes 1966208 | tf_op jit(solution)/shard_map/convert
  96.2 4.9 %fusion = f32[4,24,2048]{2,1,0:T(8,128)S(1)} fusion(bf16[2048,2048]{1,0:T(8,128)(2,1)} %bitcast.138, bf16[4,24,1024]{2,1,0:T(8,128)(2,1)S(1)} %get-tuple-element.32, bf16[4,24,1024]{2,1,0:T(8,128)(2,1)S(1)} %get-tuple-element.31), kind=kOutput, calls=%fused_computation.2 | convolution fusion | flops 806092800 | bytes 9568256 | tf_op jit(solution)/shard_map/cfj,jm->cfm/dot_general | solution.py:199
  101.0 1.4 %reshape.966 = f32[4,24,4,512]{3,2,1,0:T(4,128)} reshape(f32[4,24,2048]{2,1,0:T(8,128)S(1)} %fusion) | data formatting | bytes 1572864 | tf_op jit(solution)/shard_map/reshape | solution.py:202
  102.5 3.0 %fusion.170 = (f32[4,24,1,512]{3,2,1,0:T(1,128)S(1)}, f32[4,24,1,512]{3,2,1,0:T(1,128)S(1)}, f32[4,24,1,512]{3,2,1,0:T(1,128)S(1)}, f32[4,24,1,512]{3,2,1,0:T(1,128)S(1)}) fusion(f32[4,24,4,512]{3,2,1,0:T(4,128)} %reshape.966), kind=kLoop, calls=%fused_computation.329 | loop fusion | bytes 1572864 | tf_op jit(solution)/shard_map/slice | solution.py:83
  105.5 0.1 copy.70
  106.0 0.8 pad_add_fusion
  106.9 0.5 divide_convert_fusion.3
  107.4 0.6 fusion.13
  108.0 0.4 reshape.964
  108.4 0.6 fusion.169
  109.7 0.5 divide_convert_fusion.5
  110.2 0.4 fusion.32
  110.5 0.3 reshape.962
  110.8 0.6 fusion.168
  112.2 1.5 %collective-permute-start.5 = (f32[4,1536]{1,0:T(4,128)S(1)}, f32[4,1536]{1,0:T(4,128)S(1)}, u32[]{:S(2)}, u32[]{:S(2)}) collective-permute-start(f32[4,1536]{1,0:T(4,128)S(1)} %add_add_fusion.3), channel_id=1, source_target_pairs={{0,1},{1,2},{2,3},{3,4},{4,5},{5,6},{6,7},{8,9},{9,10},{10,11},{11... | collective-permute-start | bytes 73736 | tf_op jit(solution)/shard_map/ppermute | solution.py:20
  113.7 2.6 %pad_maximum_fusion.7 = f32[4]{0:T(128)S(1)} fusion(f32[1]{0:T(128)} %bitcast.29, f32[1]{0:T(128)} %bitcast.28, f32[1]{0:T(128)} %bitcast.27, f32[1]{0:T(128)} %bitcast.26), kind=kLoop, calls=%fused_computation.296 | loop fusion | flops 12 | bytes 32 | tf_op jit(solution)/shard_map/stack | solution.py:76
  116.3 0.8 gather_fusion
  117.1 0.6 fusion.153
  118.4 0.1 fusion.106
  118.6 11.6 %all_gather.11 = bf16[4,192,512]{2,1,0:T(8,128)(2,1)S(1)} all-gather(bf16[4,24,512]{2,1,0:T(8,128)(2,1)S(1)} %bitcast.173), channel_id=1, replica_groups=mesh['clip'=4,'seg'=8] {'seg'}, dimensions={1}, use_global_device_ids=true | all-gather | bytes 884736 | tf_op jit(solution)/shard_map/all_gather | solution.py:211
  130.1 0.5 pad_slice_fusion.2
  130.7 1.3 fusion.20
  131.9 0.8 copy.40
  (128 shorter events, 3.2 us)
Async XLA Ops:
  7.2 50.6 %reduce-scatter.2.cloned.1.call-start = ((), (), s32[]{:S(2)}) async-start(), calls=%async_computation.1 | async-start | bytes 1769472 | tf_op jit(solution)/shard_map/reduce_scatter | solution.py:116
  8.5 5.9 %copy-start.18 = (s32[4]{0:T(128)}, s32[4]{0:T(128)S(1)}, u32[]{:S(2)}) copy-start(s32[4]{0:T(128)S(1)} %get-tuple-element.95) | copy-start | bytes 52
  11.2 1.1 copy-start
  14.4 7.9 %copy-start.22 = (s32[4]{0:T(128)S(1)}, s32[4]{0:T(128)}, u32[]{:S(2)}) copy-start(s32[4]{0:T(128)} %param.5) | copy-start | bytes 52
  16.4 23.5 %collective-permute-start.1 = (bf16[4,1536]{1,0:T(4,128)(2,1)S(1)}, bf16[4,1536]{1,0:T(4,128)(2,1)S(1)}, u32[]{:S(2)}, u32[]{:S(2)}) collective-permute-start(bf16[4,1536]{1,0:T(4,128)(2,1)S(1)} %slice.225), channel_id=1, source_target_pairs={{1,0},{2,1},{3,2},{4,3},{5,4},{6,5},{7,6},{9,8},{10,9},{11,10},{12... | collective-permute-start | bytes 36872 | tf_op jit(solution)/shard_map/ppermute | solution.py:20
  28.4 4.4 %copy-start.2 = (f32[128,2048]{1,0:T(8,128)S(1)}, f32[128,2048]{1,0:T(8,128)}, u32[]{:S(2)}) copy-start(f32[128,2048]{1,0:T(8,128)} %get-tuple-element.75) | copy-start | bytes 3145732
  42.9 16.0 %copy-start.19 = (s32[4]{0:T(128)S(1)}, s32[4]{0:T(128)}, u32[]{:S(2)}) copy-start(s32[4]{0:T(128)} %copy-done.18) | copy-start | bytes 52
  42.9 17.7 %copy-start.8 = (bf16[4,128,512]{2,1,0:T(8,128)(2,1)S(1)}, bf16[4,128,512]{2,1,0:T(8,128)(2,1)}, u32[]{:S(2)}) copy-start(bf16[4,128,512]{2,1,0:T(8,128)(2,1)} %add_convert_fusion.3) | copy-start | bytes 1572868
  42.9 17.7 %copy-start.14 = (bf16[4,96,128]{2,1,0:T(8,128)(2,1)S(1)}, bf16[4,96,128]{2,1,0:T(8,128)(2,1)}, u32[]{:S(2)}) copy-start(bf16[4,96,128]{2,1,0:T(8,128)(2,1)} %get-tuple-element.67) | copy-start | bytes 294916
  59.0 3.1 %collective-permute-start = (bf16[4,1536]{1,0:T(4,128)(2,1)S(1)}, bf16[4,1536]{1,0:T(4,128)(2,1)S(1)}, u32[]{:S(2)}, u32[]{:S(2)}) collective-permute-start(bf16[4,1536]{1,0:T(4,128)(2,1)S(1)} %slice.289), channel_id=1, source_target_pairs={{1,0},{2,1},{3,2},{4,3},{5,4},{6,5},{7,6},{9,8},{10,9},{11,10},{12... | collective-permute-start | bytes 36872 | tf_op jit(solution)/shard_map/ppermute | solution.py:20
  64.0 5.2 %copy-start.15 = (bf16[4,48,256]{2,1,0:T(8,128)(2,1)S(1)}, bf16[4,48,256]{2,1,0:T(8,128)(2,1)}, u32[]{:S(2)}) copy-start(bf16[4,48,256]{2,1,0:T(8,128)(2,1)} %get-tuple-element.61) | copy-start | bytes 294916
  64.0 5.2 %copy-start.16 = (bf16[4,48,256]{2,1,0:T(8,128)(2,1)S(1)}, bf16[4,48,256]{2,1,0:T(8,128)(2,1)}, u32[]{:S(2)}) copy-start(bf16[4,48,256]{2,1,0:T(8,128)(2,1)} %get-tuple-element.62) | copy-start | bytes 294916
  64.0 5.2 %copy-start.17 = (bf16[4,48,256]{2,1,0:T(8,128)(2,1)S(1)}, bf16[4,48,256]{2,1,0:T(8,128)(2,1)}, u32[]{:S(2)}) copy-start(bf16[4,48,256]{2,1,0:T(8,128)(2,1)} %get-tuple-element.63) | copy-start | bytes 294916
  64.1 6.0 %copy-start.13 = (f32[4,48,1024]{2,1,0:T(8,128)S(1)}, f32[4,48,1024]{2,1,0:T(8,128)}, u32[]{:S(2)}) copy-start(f32[4,48,1024]{2,1,0:T(8,128)} %fusion.15) | copy-start | bytes 2359300
  64.1 6.0 %copy-start.25 = (pred[4,48]{1,0:T(4,128)(4,1)S(1)}, pred[4,48]{1,0:T(4,128)(4,1)}, u32[]{:S(2)}) copy-start(pred[4,48]{1,0:T(4,128)(4,1)} %broadcast_compare_fusion.1) | copy-start | bytes 580
  65.6 1.0 copy-start.4
  70.0 1.5 %copy-start.6 = (f32[4,48,1024]{2,1,0:T(8,128)}, f32[4,48,1024]{2,1,0:T(8,128)S(1)}, u32[]{:S(2)}) copy-start(f32[4,48,1024]{2,1,0:T(8,128)S(1)} %fusion.17) | copy-start | bytes 2359300
  71.5 6.1 %copy-start.3 = (f32[4,24,2048]{2,1,0:T(8,128)S(1)}, f32[4,24,2048]{2,1,0:T(8,128)}, u32[]{:S(2)}) copy-start(f32[4,24,2048]{2,1,0:T(8,128)} %fusion.2) | copy-start | bytes 2359300
  71.5 6.1 %copy-start.27 = (pred[4,24]{1,0:T(4,128)(4,1)S(1)}, pred[4,24]{1,0:T(4,128)(4,1)}, u32[]{:S(2)}) copy-start(pred[4,24]{1,0:T(4,128)(4,1)} %broadcast_compare_fusion) | copy-start | bytes 292
  71.5 7.5 %copy-start.23 = (s32[4]{0:T(128)S(1)}, s32[4]{0:T(128)}, u32[]{:S(2)}) copy-start(s32[4]{0:T(128)} %param.5) | copy-start | bytes 52
  71.5 23.0 %copy-start.21 = (f32[4]{0:T(128)S(1)}, f32[4]{0:T(128)}, u32[]{:S(2)}) copy-start(f32[4]{0:T(128)} %get-tuple-element.93) | copy-start | bytes 52
  90.1 23.6 %collective-permute-start.4 = (f32[]{:T(128)}, f32[]{:T(128)}, u32[]{:S(2)}, u32[]{:S(2)}) collective-permute-start(f32[]{:T(128)} %get-tuple-element.77), channel_id=1, source_target_pairs={{0,24},{8,0},{16,8},{24,16},{1,25},{9,1},{17,9},{25,17},{2,26},{10... | collective-permute-start | bytes 20 | tf_op jit(solution)/shard_map/ppermute | solution.py:75
  93.4 20.3 %collective-permute-start.3 = (f32[]{:T(128)}, f32[]{:T(128)}, u32[]{:S(2)}, u32[]{:S(2)}) collective-permute-start(f32[]{:T(128)} %get-tuple-element.77), channel_id=1, source_target_pairs={{0,16},{8,24},{16,0},{24,8},{1,17},{9,25},{17,1},{25,9},{2,18},{10... | collective-permute-start | bytes 20 | tf_op jit(solution)/shard_map/ppermute | solution.py:75
  93.4 20.3 %collective-permute-start.2 = (f32[]{:T(128)}, f32[]{:T(128)}, u32[]{:S(2)}, u32[]{:S(2)}) collective-permute-start(f32[]{:T(128)} %get-tuple-element.77), channel_id=1, source_target_pairs={{0,8},{8,16},{16,24},{24,0},{1,9},{9,17},{17,25},{25,1},{2,10},{10... | collective-permute-start | bytes 20 | tf_op jit(solution)/shard_map/ppermute | solution.py:75
  101.0 5.8 %copy-start.26 = (pred[4,48]{1,0:T(4,128)(4,1)S(1)}, pred[4,48]{1,0:T(4,128)(4,1)}, u32[]{:S(2)}) copy-start(pred[4,48]{1,0:T(4,128)(4,1)} %broadcast_compare_fusion.1) | copy-start | bytes 580
  102.5 4.4 %copy-start.7 = (f32[4,48,1024]{2,1,0:T(8,128)S(1)}, f32[4,48,1024]{2,1,0:T(8,128)}, u32[]{:S(2)}) copy-start(f32[4,48,1024]{2,1,0:T(8,128)} %copy-done.6) | copy-start | bytes 2359300
  102.5 4.4 %copy-start.11 = (f32[4,48,512]{2,1,0:T(8,128)S(1)}, f32[4,48,512]{2,1,0:T(8,128)}, u32[]{:S(2)}) copy-start(f32[4,48,512]{2,1,0:T(8,128)} %get-tuple-element.23) | copy-start | bytes 1179652
  102.5 4.4 %copy-start.12 = (f32[4,48,512]{2,1,0:T(8,128)S(1)}, f32[4,48,512]{2,1,0:T(8,128)}, u32[]{:S(2)}) copy-start(f32[4,48,512]{2,1,0:T(8,128)} %get-tuple-element.24) | copy-start | bytes 1179652
  107.4 2.3 %copy-start.24 = (pred[4,96]{1,0:T(4,128)(4,1)S(1)}, pred[4,96]{1,0:T(4,128)(4,1)}, u32[]{:S(2)}) copy-start(pred[4,96]{1,0:T(4,128)(4,1)} %broadcast_compare_fusion.2) | copy-start | bytes 1156
  108.0 1.7 %copy-start.5 = (f32[4,96,512]{2,1,0:T(8,128)S(1)}, f32[4,96,512]{2,1,0:T(8,128)}, u32[]{:S(2)}) copy-start(f32[4,96,512]{2,1,0:T(8,128)} %copy-done.4) | copy-start | bytes 2359300
  108.0 1.7 %copy-start.9 = (f32[4,96,256]{2,1,0:T(8,128)S(1)}, f32[4,96,256]{2,1,0:T(8,128)}, u32[]{:S(2)}) copy-start(f32[4,96,256]{2,1,0:T(8,128)} %get-tuple-element.21) | copy-start | bytes 1179652
  108.4 1.3 copy-start.10
  110.5 7.9 %slice-start = ((f32[4,27,512]{2,0,1:T(4,128)}), f32[4,24,512]{2,0,1:T(4,128)S(1)}, s32[]{:S(2)}) async-start(f32[4,27,512]{2,0,1:T(4,128)} %pad_add_fusion), calls=%async_computation.2 | async-start | bytes 393216 | tf_op jit(solution)/shard_map/slice | solution.py:203
  110.5 7.9 %copy-start.20 = (s32[4]{0:T(128)S(1)}, s32[4]{0:T(128)}, u32[]{:S(2)}) copy-start(s32[4]{0:T(128)} %copy-done.18) | copy-start | bytes 52
  111.9 18.8 %copy-start.1 = (bf16[16,16,2048]{2,1,0:T(8,128)(2,1)S(1)}, bf16[16,16,2048]{2,1,0:T(8,128)(2,1)}, u32[]{:S(2)}) copy-start(bf16[16,16,2048]{2,1,0:T(8,128)(2,1)} %copy-done) | copy-start | bytes 3145732
  112.2 6.2 %collective-permute-start.5 = (f32[4,1536]{1,0:T(4,128)S(1)}, f32[4,1536]{1,0:T(4,128)S(1)}, u32[]{:S(2)}, u32[]{:S(2)}) collective-permute-start(f32[4,1536]{1,0:T(4,128)S(1)} %add_add_fusion.3), channel_id=1, source_target_pairs={{0,1},{1,2},{2,3},{3,4},{4,5},{5,6},{6,7},{8,9},{9,10},{10,11},{11... | collective-permute-start | bytes 73736 | tf_op jit(solution)/shard_map/ppermute | solution.py:20
Sparse Core Ops, SparseCore 0:
  16.5 41.2 reduce-scatter.1

commit v10 on v8

--- a/solution.py
+++ b/solution.py
@@ -86,10 +86,13 @@
     return jnp.sum(slots, axis=0)
 
 
-def spread_parts(quarters):
+def spread_parts(frames, stride):
     return sum(
         (
-            jnp.pad(quarters[:, :, quarter], ((0, 0), (quarter, 3 - quarter), (0, 0)))
+            jnp.pad(
+                frames[:, :, quarter * stride : (quarter + 1) * stride],
+                ((0, 0), (quarter, 3 - quarter), (0, 0)),
+            )
             for quarter in range(4)
         )
     )
@@ -208,7 +211,7 @@
         grad_frames = jnp.einsum(
             "cfj,jm->cfm", grad_x, table, preferred_element_type=jnp.float32
         )
-        spread_back = spread_parts(grad_frames.reshape(clip_count, frame_count, 4, stride))
+        spread_back = spread_parts(grad_frames, stride)
         gradient = gradient + spread_back[:, :frame_count].reshape(clip_count, samples)
         extras.append(spread_back[:, frame_count:].reshape(clip_count, 3 * stride))
     halo = 3 * NFFT // 4

time: 140 us -> 131 us (0.936)
  matrix products: 28.4 us -> 24.2 us
  local copies, waits for them, and re-layouts: 14 us -> 10.6 us
  waiting for transfers between devices: 5.7 us -> 4.14 us
    dot_general x3, matrix products: 6.72 us -> 2.45 us  [body(): jnp.einsum('cfj,jm->cfm', grad_x, table, preferred_element_type=jnp.float32)]
    reshape x3 -> x0, local copies, waits for them, and re-layouts: 2.36 us -> none  [body(): grad_frames.reshape(clip_count, frame_count, 4, stride)]
    ppermute x3, waiting for transfers between devices: 2.25 us -> 0.49 us  [gathered_sum(): arrived = lax.ppermute(value, axis, route)]
    slice x6 -> x3, local copies, waits for them, and re-layouts: 1.9 us -> 0.18 us  [spread_parts(): frames[:, :, quarter * stride:(quarter + 1) * stride]]
    unnamed x75 -> x73, local copies, waits for them, and re-layouts: 4.42 us -> 5.05 us
  transfers between devices with their start and end apart: 7 -> 7, of which waited for: 4 -> 2; matrix products, arithmetic and copies ran while one was open for 30% -> 32% of each run, Pallas kernels for 0% -> 0%
where the time goes in v10:
time: 131 us; the launch traced here: 130 us
  other arithmetic  44.3 us (34%)
  matrix products  24.2 us (18%)
  blocking collectives  20.9 us (16%)
  between operations  16.7 us (13%)
  local copies, waits for them, and re-layouts  10.6 us (8%)
  starting transfers between devices  9.61 us (7%)
  waiting for transfers between devices  4.14 us (3%)
    dot_general x3, matrix products, body(): jnp.einsum('cfm,jm->cfj', framed(clean, clean_beyond[:, :3 * stride], str...  11 us
    all_gather x1, blocking collectives, body(): lax.all_gather(jnp.stack([spreads, energies, logterms]), 'seg', axis=0, t...  10.6 us
    all_gather x1, blocking collectives, body(): portion = lax.all_gather(grad_hops, 'seg', axis=1, tiled=True)  10.3 us
    mul x3, other arithmetic, analysis_table(): fine_cos, fine_sin = (part * scale for part in fine)  8.59 us
    dot_general x3, matrix products, body(): jnp.einsum('cfm,jm->cfj', framed(est_wave, est_beyond[:, :3 * stride], st...  7.52 us
    convert_element_type x3, other arithmetic, analysis_table(): table = entry_value.astype(jnp.bfloat16)  7.32 us
    ppermute x3, starting transfers between devices, gathered_sum(): arrived = lax.ppermute(value, axis, route)  5.4 us
    unnamed x73, local copies, waits for them, and re-layouts  5.05 us
  transfers between devices with their start and end apart: 7, of which 2 were waited for; matrix products, arithmetic and copies ran while one was open for 32% of the time, Pallas kernels for 0%

profile of v10, /device:TPU:0, one launch (start us, length us, event | category | flops | bytes accessed | tf_op | source)
XLA Modules:
  0.0 130.3 jit_solution(2784609587687921686)
XLA Ops:
  7.3 0.5 cosine_multiply_fusion.3
  7.8 1.9 %fusion.127 = (f32[16,2048]{1,0:T(8,128)S(1)}, f32[16,2048]{1,0:T(8,128)S(1)}, f32[16,2048]{1,0:T(8,128)}, f32[16,2048]{1,0:T(8,128)}) fusion(s32[16]{0:T(128)S(1)} %get-tuple-element.102, pred[16]{0:T(512)(128)(4,1)S(1)} %iota_compare_fusion.2, s32[16]{0:T(128)S(1)} %get-tuple-element.103), kind=kLoop, calls=%fused_computation.212 | loop fusion | flops 1179648 | bytes 524432 | tf_op jit(solution)/shard_map/jit(_where)/select_n | solution.py:62
  9.8 0.2 add_convert_fusion.2
  10.0 1.2 multiply_convert_fusion
  11.3 1.0 compare_select_fusion.2
  12.3 2.0 %convolution_bitcast_fusion = f32[195,4,2048]{2,0,1:T(8,128)S(1)} fusion(bf16[2,128,2048]{2,1,0:T(8,128)(2,1)S(1)} %bitcast.113, bf16[4,2,128,192]{2,3,1,0:T(8,128)(2,1)} %param.3), kind=kOutput, calls=%fused_computation.8 | convolution fusion | flops 817889280 | bytes 7831552 | tf_op jit(solution)/shard_map/crbf,rbm->fcm/dot_general | solution.py:125
  14.4 2.0 %slice_add_fusion = f32[192,4,512]{2,0,1:T(8,128)} fusion(f32[195,4,2048]{2,0,1:T(8,128)S(1)} %convolution_bitcast_fusion), kind=kLoop, calls=%fused_computation.24 | loop fusion | flops 1179648 | bytes 7864320 | tf_op jit(solution)/shard_map/add | solution.py:129
  16.4 0.6 slice.225
  17.0 1.3 collective-permute-start.1
  18.4 0.6 fusion.150
  19.0 0.5 iota_compare_fusion
  19.5 0.6 subtract_multiply_fusion.1
  20.0 0.6 fusion.149
  20.6 0.6 iota_compare_fusion.1
  21.2 4.1 %cosine_multiply_fusion = (f32[128,2048]{1,0:T(8,128)S(1)}, f32[128,2048]{1,0:T(8,128)S(1)}) fusion(f32[2048]{0:T(1024)S(1)} %fusion.142), kind=kLoop, calls=%fused_computation.38 | loop fusion | flops 4194304 | bytes 2105344 | tf_op jit(solution)/shard_map/mul | solution.py:44
  25.4 0.6 broadcast_compare_fusion
  25.9 2.1 %cosine_multiply_fusion.1 = (f32[128,1024]{1,0:T(8,128)S(1)}, f32[128,1024]{1,0:T(8,128)S(1)}) fusion(f32[1024]{0:T(1024)S(1)} %subtract_multiply_fusion), kind=kLoop, calls=%fused_computation.59 | loop fusion | flops 2097152 | bytes 1052672 | tf_op jit(solution)/shard_map/mul | solution.py:44
  28.0 0.6 iota_add_fusion.2
  28.6 2.4 %cosine_multiply_fusion.2 = (f32[128,512]{1,0:T(8,128)S(1)}, f32[128,512]{1,0:T(8,128)}) fusion(f32[512]{0:T(512)} %subtract_multiply_fusion.1), kind=kLoop, calls=%fused_computation.162 | loop fusion | flops 1048576 | bytes 526336 | tf_op jit(solution)/shard_map/mul | solution.py:44
  31.0 0.9 fusion.137
  31.9 1.3 broadcast_compare_fusion.1
  33.2 0.8 fusion.144
  34.0 6.6 %add_convert_fusion = bf16[16,128,2048]{2,1,0:T(8,128)(2,1)} fusion(f32[128,2048]{1,0:T(8,128)S(1)} %get-tuple-element.75, f32[16,2048]{1,0:T(8,128)} %get-tuple-element.100, f32[128,2048]{1,0:T(8,128)S(1)} %get-tuple-element.74, f32[16,2048]{1,0:T(8,128)} %get-tuple-element.101), kind=kLoop, calls=%fused_computation | loop fusion | flops 16777216 | bytes 10747904 | tf_op jit(solution)/shard_map/convert_element_type | solution.py:46
  40.7 0.6 add_convert_fusion.1
  41.4 0.7 broadcast_compare_fusion.2
  42.1 0.8 pad_maximum_fusion.1
  42.9 0.7 slice.309
  43.7 0.7 slice.295
  44.6 0.7 fusion.174
  45.4 1.7 %fusion.15 = f32[4,48,1024]{2,1,0:T(8,128)} fusion(bf16[1024,1024]{1,0:T(8,128)(2,1)S(1)} %bitcast.110, bf16[4,48,256]{2,1,0:T(8,128)(2,1)S(1)} %get-tuple-element.57, bf16[4,48,256]{2,1,0:T(8,128)(2,1)S(1)} %get-tuple-element.58, bf16[4,48,256]{2,1,0:T(8,128)(2,1)S(1)} %get-tuple-element.59, bf16[4,48,256]{2,1,0:T(8,128)(2,1)S(1)} %get-tuple-element.56), kind=kOutput, calls=%fused_computation.19 | convolution fusion | flops 404226048 | bytes 3276800 | tf_op jit(solution)/shard_map/cfm,jm->cfj/dot_general | solution.py:158
  47.1 7.0 %fusion.2 = f32[4,24,2048]{2,1,0:T(8,128)} fusion(bf16[2048,2048]{1,0:T(8,128)(2,1)} %bitcast.105, bf16[4,24,512]{2,1,0:T(8,128)(2,1)S(1)} %get-tuple-element.49, bf16[4,24,512]{2,1,0:T(8,128)(2,1)S(1)} %get-tuple-element.50, bf16[4,24,512]{2,1,0:T(8,128)(2,1)S(1)} %get-tuple-element.51, bf16[4,24,512]{2,1,0:T(8,128)(2,1)S(1)} %get-tuple-element.48), kind=kOutput, calls=%fused_computation.3 | convolution fusion | flops 806879232 | bytes 9568256 | tf_op jit(solution)/shard_map/cfm,jm->cfj/dot_general | solution.py:158
  54.1 3.6 %reduce-scatter.2.cloned.1.call-done = f32[24,4,512]{2,0,1:T(8,128)} async-done(((f32[192,4,512]{2,0,1:T(8,128)}), f32[24,4,512]{2,0,1:T(8,128)}) %reduce-scatter.2.cloned.1.call-update) | async-done | bytes 196624 | tf_op jit(solution)/shard_map/reduce_scatter | solution.py:128
  57.7 1.1 copy.10
  58.9 1.5 %collective-permute-start = (bf16[4,1536]{1,0:T(4,128)(2,1)S(1)}, bf16[4,1536]{1,0:T(4,128)(2,1)S(1)}, u32[]{:S(2)}, u32[]{:S(2)}) collective-permute-start(bf16[4,1536]{1,0:T(4,128)(2,1)S(1)} %slice.287), channel_id=1, source_target_pairs={{1,0},{2,1},{3,2},{4,3},{5,4},{6,5},{7,6},{9,8},{10,9},{11,10},{12... | collective-permute-start | bytes 36872 | tf_op jit(solution)/shard_map/ppermute | solution.py:20
  60.4 2.3 %fusion.34 = f32[4,96,512]{2,1,0:T(8,128)} fusion(bf16[512,512]{1,0:T(8,128)(2,1)S(1)} %bitcast.115, bf16[4,96,128]{2,1,0:T(8,128)(2,1)S(1)} %get-tuple-element.65, bf16[4,96,128]{2,1,0:T(8,128)(2,1)S(1)} %copy-done.17, bf16[4,96,128]{2,1,0:T(8,128)(2,1)} %get-tuple-element.67, bf16[4,96,128]{2,1,0:T(8,128)(2,1)S(1)} %get-tuple-element.64), kind=kOutput, calls=%fused_computation.54 | convolution fusion | flops 202899456 | bytes 1703936 | tf_op jit(solution)/shard_map/cfm,jm->cfj/dot_general | solution.py:158
  62.8 0.8 fusion.171
  63.7 0.8 fusion.173
  64.7 6.3 %fusion.4 = f32[4,24,2048]{2,1,0:T(8,128)S(1)} fusion(bf16[2048,2048]{1,0:T(8,128)(2,1)} %bitcast.106, bf16[4,24,512]{2,1,0:T(8,128)(2,1)} %get-tuple-element.53, bf16[4,24,512]{2,1,0:T(8,128)(2,1)} %get-tuple-element.54, bf16[4,24,512]{2,1,0:T(8,128)(2,1)} %get-tuple-element.55, bf16[4,24,512]{2,1,0:T(8,128)(2,1)S(1)} %get-tuple-element.52), kind=kOutput, calls=%fused_computation.5 | convolution fusion | flops 806879232 | bytes 9568256 | tf_op jit(solution)/shard_map/cfm,jm->cfj/dot_general | solution.py:164
  71.0 1.4 %select_reduce_fusion.6 = (f32[4]{0:T(128)S(1)}, f32[4]{0:T(128)S(1)}, f32[4]{0:T(128)S(1)}, f32[4,24,1024]{2,1,0:T(8,128)}, f32[4,24,1024]{2,1,0:T(8,128)}) fusion(pred[4,24]{1,0:T(4,128)(4,1)S(1)} %copy-done.24, f32[4,24,2048]{2,1,0:T(8,128)S(1)} %fusion.4, f32[4,24,2048]{2,1,0:T(8,128)S(1)} %copy-done.2), kind=kLoop, calls=%fused_computation.145 | loop fusion | flops 2064372 | bytes 2359440 | tf_op jit(solution)/shard_map/reduce_sum | solution.py:182
  72.5 0.9 fusion.17
  73.3 0.9 copy-done.3
  74.2 1.5 %select_reduce_fusion.7 = (f32[4]{0:T(128)S(1)}, f32[4]{0:T(128)S(1)}, f32[4]{0:T(128)S(1)}, f32[4,48,512]{2,1,0:T(8,128)}, f32[4,48,512]{2,1,0:T(8,128)}) fusion(pred[4,48]{1,0:T(4,128)(4,1)S(1)} %copy-done.26, f32[4,48,1024]{2,1,0:T(8,128)S(1)} %fusion.17, f32[4,48,1024]{2,1,0:T(8,128)S(1)} %copy-done.11), kind=kLoop, calls=%fused_computation.147 | loop fusion | flops 2064372 | bytes 2359536 | tf_op jit(solution)/shard_map/reduce_sum | solution.py:182
  75.7 0.4 fusion.36
  76.1 0.9 copy-done.5
  77.0 1.5 %select_reduce_fusion.8 = (f32[4]{0:T(128)S(1)}, f32[4]{0:T(128)S(1)}, f32[4]{0:T(128)S(1)}, f32[4,96,256]{2,1,0:T(8,128)}, f32[4,96,256]{2,1,0:T(8,128)}) fusion(pred[4,96]{1,0:T(4,128)(4,1)S(1)} %copy-done.27, f32[4,96,512]{2,1,0:T(8,128)S(1)} %fusion.36, f32[4,96,512]{2,1,0:T(8,128)S(1)} %copy-done.12), kind=kLoop, calls=%fused_computation.149 | loop fusion | flops 2064372 | bytes 2359728 | tf_op jit(solution)/shard_map/reduce_sum | solution.py:182
  78.6 10.6 %all-gather = f32[24,3,4]{2,1,0:T(4,128)S(1)} all-gather(f32[3,3,4]{2,1,0:T(4,128)S(1)} %pad_maximum_fusion.6), channel_id=2, replica_groups=mesh['clip'=4,'seg'=8] {'seg'}, dimensions={0}, use_global_device_ids=true | all-gather | bytes 1296 | tf_op jit(solution)/shard_map/all_gather | solution.py:191
  89.2 0.7 multiply_rsqrt_fusion
  89.9 1.8 %divide_convert_fusion.5 = (bf16[4,96,256]{2,1,0:T(8,128)(2,1)S(1)}, bf16[4,96,256]{2,1,0:T(8,128)(2,1)S(1)}) fusion(f32[4,96,512]{2,1,0:T(8,128)} %copy-done.5, f32[4,96,256]{2,1,0:T(8,128)} %get-tuple-element.21, f32[4,96,256]{2,1,0:T(8,128)} %get-tuple-element.22, f32[4]{0:T(128)S(1)} %copy-done.21, f32[4]{0:T(128)S(1)} %get-tuple-element.80, ...), kind=kLoop, calls=%fused_computation.134 | loop fusion | flops 1671168 | bytes 1966496 | tf_op jit(solution)/shard_map/convert.4
  91.7 0.4 fusion.32
  92.3 1.4 %divide_convert_fusion.3 = (bf16[4,48,512]{2,1,0:T(8,128)(2,1)S(1)}, bf16[4,48,512]{2,1,0:T(8,128)(2,1)S(1)}) fusion(f32[4,48,1024]{2,1,0:T(8,128)S(1)} %copy-done.4, f32[4,48,512]{2,1,0:T(8,128)S(1)} %copy-done.8, f32[4,48,512]{2,1,0:T(8,128)S(1)} %copy-done.9, f32[4]{0:T(128)S(1)} %copy-done.21, f32[4]{0:T(128)S(1)} %get-tuple-element.82, ...), kind=kLoop, calls=%fused_computation.131 | loop fusion | flops 1671168 | bytes 1966304 | tf_op jit(solution)/shard_map/convert.2
  93.7 0.6 fusion.13
  94.5 0.5 divide_convert_fusion.1
  95.0 1.0 slice-done.1
  96.0 1.5 %fusion = f32[4,24,2048]{2,1,0:T(8,128)S(1)} fusion(bf16[2048,2048]{1,0:T(8,128)(2,1)S(1)} %bitcast.109, bf16[4,24,1024]{2,1,0:T(8,128)(2,1)S(1)} %get-tuple-element.32, bf16[4,24,1024]{2,1,0:T(8,128)(2,1)S(1)} %get-tuple-element.31), kind=kOutput, calls=%fused_computation.1 | convolution fusion | flops 806092800 | bytes 9568256 | tf_op jit(solution)/shard_map/cfj,jm->cfm/dot_general | solution.py:211
  97.7 1.5 %collective-permute-start.2 = (f32[]{:T(128)}, f32[]{:T(128)}, u32[]{:S(2)}, u32[]{:S(2)}) collective-permute-start(f32[]{:T(128)} %get-tuple-element.77), channel_id=1, source_target_pairs={{0,8},{8,16},{16,24},{24,0},{1,9},{9,17},{17,25},{25,1},{2,10},{10... | collective-permute-start | bytes 20 | tf_op jit(solution)/shard_map/ppermute | solution.py:79
  99.3 2.4 %collective-permute-start.3 = (f32[]{:T(128)}, f32[]{:T(128)}, u32[]{:S(2)}, u32[]{:S(2)}) collective-permute-start(f32[]{:T(128)} %get-tuple-element.77), channel_id=1, source_target_pairs={{0,16},{8,24},{16,0},{24,8},{1,17},{9,25},{17,1},{25,9},{2,18},{10... | collective-permute-start | bytes 20 | tf_op jit(solution)/shard_map/ppermute | solution.py:79
  101.7 1.4 %collective-permute-start.4 = (f32[]{:T(128)}, f32[]{:T(128)}, u32[]{:S(2)}, u32[]{:S(2)}) collective-permute-start(f32[]{:T(128)} %get-tuple-element.77), channel_id=1, source_target_pairs={{0,24},{8,0},{16,8},{24,16},{1,25},{9,1},{17,9},{25,17},{2,26},{10... | collective-permute-start | bytes 20 | tf_op jit(solution)/shard_map/ppermute | solution.py:79
  103.2 1.4 %collective-permute-start.5 = (f32[4,1536]{1,0:T(4,128)S(1)}, f32[4,1536]{1,0:T(4,128)S(1)}, u32[]{:S(2)}, u32[]{:S(2)}) collective-permute-start(f32[4,1536]{1,0:T(4,128)S(1)} %add_add_fusion.3), channel_id=1, source_target_pairs={{0,1},{1,2},{2,3},{3,4},{4,5},{5,6},{6,7},{8,9},{9,10},{10,11},{11... | collective-permute-start | bytes 73736 | tf_op jit(solution)/shard_map/ppermute | solution.py:20
  104.9 0.5 collective-permute-done.4
  105.4 3.2 %fusion.152 = f32[]{:T(128)} fusion(f32[]{:T(128)} %collective-permute-done.4, s32[]{:T(128)S(6)} %select_n.332, f32[]{:T(128)} %collective-permute-done.3, s32[]{:T(128)S(6)} %select_n.330, f32[]{:T(128)} %collective-permute-done.2, s32[]{:T(128)S(6)} %select_n.328, f32[]{:T(128)} %get-tuple-element.77, s32[]{:T(128)S(6)} %select_n.293), kind=kLoop, calls=%fused_computation.283 | loop fusion | flops 47 | bytes 36 | tf_op jit(solution)/shard_map/reduce_sum | solution.py:86
  109.5 10.3 %all_gather.11 = bf16[4,192,512]{2,1,0:T(8,128)(2,1)S(1)} all-gather(bf16[4,24,512]{2,1,0:T(8,128)(2,1)S(1)} %bitcast.120), channel_id=1, replica_groups=mesh['clip'=4,'seg'=8] {'seg'}, dimensions={1}, use_global_device_ids=true | all-gather | bytes 884736 | tf_op jit(solution)/shard_map/all_gather | solution.py:223
  119.8 0.5 pad_slice_fusion.2
  120.3 1.2 fusion.20
  121.6 0.8 copy.7
  (121 shorter events, 2.5 us)
Async XLA Ops:
  7.2 50.5 %reduce-scatter.2.cloned.1.call-start = ((), (), s32[]{:S(2)}) async-start(), calls=%async_computation.1 | async-start | bytes 1769472 | tf_op jit(solution)/shard_map/reduce_scatter | solution.py:128
  10.0 6.3 %copy-start = (bf16[16,16,2048]{2,1,0:T(8,128)(2,1)}, bf16[16,16,2048]{2,1,0:T(8,128)(2,1)S(1)}, u32[]{:S(2)}) copy-start(bf16[16,16,2048]{2,1,0:T(8,128)(2,1)S(1)} %add_convert_fusion.2) | copy-start | bytes 3145732
  11.3 5.1 %copy-start.18 = (s32[4]{0:T(128)}, s32[4]{0:T(128)S(1)}, u32[]{:S(2)}) copy-start(s32[4]{0:T(128)S(1)} %get-tuple-element.95) | copy-start | bytes 52
  14.3 11.0 %copy-start.22 = (s32[4]{0:T(128)S(1)}, s32[4]{0:T(128)}, u32[]{:S(2)}) copy-start(s32[4]{0:T(128)} %param.5) | copy-start | bytes 52
  17.0 25.1 %collective-permute-start.1 = (bf16[4,1536]{1,0:T(4,128)(2,1)}, bf16[4,1536]{1,0:T(4,128)(2,1)}, u32[]{:S(2)}, u32[]{:S(2)}) collective-permute-start(bf16[4,1536]{1,0:T(4,128)(2,1)} %slice.225), channel_id=1, source_target_pairs={{1,0},{2,1},{3,2},{4,3},{5,4},{6,5},{7,6},{9,8},{10,9},{11,10},{12... | collective-permute-start | bytes 36872 | tf_op jit(solution)/shard_map/ppermute | solution.py:20
  34.0 7.2 %copy-start.10 = (f32[128,512]{1,0:T(8,128)S(1)}, f32[128,512]{1,0:T(8,128)}, u32[]{:S(2)}) copy-start(f32[128,512]{1,0:T(8,128)} %get-tuple-element.84) | copy-start | bytes 786436
  40.7 0.7 copy-start.28
  47.1 11.7 %copy-start.19 = (s32[4]{0:T(128)S(1)}, s32[4]{0:T(128)}, u32[]{:S(2)}) copy-start(s32[4]{0:T(128)} %copy-done.18) | copy-start | bytes 52
  47.1 13.3 %copy-start.17 = (bf16[4,96,128]{2,1,0:T(8,128)(2,1)S(1)}, bf16[4,96,128]{2,1,0:T(8,128)(2,1)}, u32[]{:S(2)}) copy-start(bf16[4,96,128]{2,1,0:T(8,128)(2,1)} %get-tuple-element.66) | copy-start | bytes 294916
  58.9 3.8 %collective-permute-start = (bf16[4,1536]{1,0:T(4,128)(2,1)S(1)}, bf16[4,1536]{1,0:T(4,128)(2,1)S(1)}, u32[]{:S(2)}, u32[]{:S(2)}) collective-permute-start(bf16[4,1536]{1,0:T(4,128)(2,1)S(1)} %slice.287), channel_id=1, source_target_pairs={{1,0},{2,1},{3,2},{4,3},{5,4},{6,5},{7,6},{9,8},{10,9},{11,10},{12... | collective-permute-start | bytes 36872 | tf_op jit(solution)/shard_map/ppermute | solution.py:20
  64.7 6.3 %copy-start.2 = (f32[4,24,2048]{2,1,0:T(8,128)S(1)}, f32[4,24,2048]{2,1,0:T(8,128)}, u32[]{:S(2)}) copy-start(f32[4,24,2048]{2,1,0:T(8,128)} %fusion.2) | copy-start | bytes 2359300
  64.7 6.3 %copy-start.24 = (pred[4,24]{1,0:T(4,128)(4,1)S(1)}, pred[4,24]{1,0:T(4,128)(4,1)}, u32[]{:S(2)}) copy-start(pred[4,24]{1,0:T(4,128)(4,1)} %broadcast_compare_fusion) | copy-start | bytes 292
  64.7 7.7 %copy-start.13 = (bf16[4,48,256]{2,1,0:T(8,128)(2,1)S(1)}, bf16[4,48,256]{2,1,0:T(8,128)(2,1)}, u32[]{:S(2)}) copy-start(bf16[4,48,256]{2,1,0:T(8,128)(2,1)} %get-tuple-element.60) | copy-start | bytes 294916
  64.7 7.7 %copy-start.14 = (bf16[4,48,256]{2,1,0:T(8,128)(2,1)S(1)}, bf16[4,48,256]{2,1,0:T(8,128)(2,1)}, u32[]{:S(2)}) copy-start(bf16[4,48,256]{2,1,0:T(8,128)(2,1)} %get-tuple-element.61) | copy-start | bytes 294916
  64.7 7.7 %copy-start.15 = (bf16[4,48,256]{2,1,0:T(8,128)(2,1)S(1)}, bf16[4,48,256]{2,1,0:T(8,128)(2,1)}, u32[]{:S(2)}) copy-start(bf16[4,48,256]{2,1,0:T(8,128)(2,1)} %get-tuple-element.62) | copy-start | bytes 294916
  64.7 7.7 %copy-start.16 = (bf16[4,48,256]{2,1,0:T(8,128)(2,1)S(1)}, bf16[4,48,256]{2,1,0:T(8,128)(2,1)}, u32[]{:S(2)}) copy-start(bf16[4,48,256]{2,1,0:T(8,128)(2,1)} %get-tuple-element.63) | copy-start | bytes 294916
  71.0 3.2 %copy-start.11 = (f32[4,48,1024]{2,1,0:T(8,128)S(1)}, f32[4,48,1024]{2,1,0:T(8,128)}, u32[]{:S(2)}) copy-start(f32[4,48,1024]{2,1,0:T(8,128)} %fusion.15) | copy-start | bytes 2359300
  71.0 3.2 %copy-start.26 = (pred[4,48]{1,0:T(4,128)(4,1)S(1)}, pred[4,48]{1,0:T(4,128)(4,1)}, u32[]{:S(2)}) copy-start(pred[4,48]{1,0:T(4,128)(4,1)} %broadcast_compare_fusion.1) | copy-start | bytes 580
  72.4 4.6 %copy-start.12 = (f32[4,96,512]{2,1,0:T(8,128)S(1)}, f32[4,96,512]{2,1,0:T(8,128)}, u32[]{:S(2)}) copy-start(f32[4,96,512]{2,1,0:T(8,128)} %fusion.34) | copy-start | bytes 2359300
  72.4 4.6 %copy-start.27 = (pred[4,96]{1,0:T(4,128)(4,1)S(1)}, pred[4,96]{1,0:T(4,128)(4,1)}, u32[]{:S(2)}) copy-start(pred[4,96]{1,0:T(4,128)(4,1)} %broadcast_compare_fusion.2) | copy-start | bytes 1156
  73.3 0.9 copy-start.3
  74.2 4.3 %copy-start.23 = (s32[4]{0:T(128)S(1)}, s32[4]{0:T(128)}, u32[]{:S(2)}) copy-start(s32[4]{0:T(128)} %param.5) | copy-start | bytes 52
  74.2 15.7 %copy-start.21 = (f32[4]{0:T(128)S(1)}, f32[4]{0:T(128)}, u32[]{:S(2)}) copy-start(f32[4]{0:T(128)} %get-tuple-element.93) | copy-start | bytes 52
  76.1 0.9 copy-start.5
  89.2 3.1 %copy-start.4 = (f32[4,48,1024]{2,1,0:T(8,128)S(1)}, f32[4,48,1024]{2,1,0:T(8,128)}, u32[]{:S(2)}) copy-start(f32[4,48,1024]{2,1,0:T(8,128)} %copy-done.3) | copy-start | bytes 2359300
  89.2 3.1 %copy-start.8 = (f32[4,48,512]{2,1,0:T(8,128)S(1)}, f32[4,48,512]{2,1,0:T(8,128)}, u32[]{:S(2)}) copy-start(f32[4,48,512]{2,1,0:T(8,128)} %get-tuple-element.23) | copy-start | bytes 1179652
  89.2 3.1 %copy-start.9 = (f32[4,48,512]{2,1,0:T(8,128)S(1)}, f32[4,48,512]{2,1,0:T(8,128)}, u32[]{:S(2)}) copy-start(f32[4,48,512]{2,1,0:T(8,128)} %get-tuple-element.24) | copy-start | bytes 1179652
  91.7 3.3 %slice-start = ((s8[8388608]{0:T(1024)(128)(4,1)}), s8[4194304]{0:T(1024)(128)(4,1)S(1)}, s32[]{:S(2)}) async-start(s8[8388608]{0:T(1024)(128)(4,1)} %bitcast.107), calls=%async_computation.2 | async-start | bytes 8388608
  92.3 2.2 %copy-start.6 = (f32[4,24,1024]{2,1,0:T(8,128)S(1)}, f32[4,24,1024]{2,1,0:T(8,128)}, u32[]{:S(2)}) copy-start(f32[4,24,1024]{2,1,0:T(8,128)} %get-tuple-element.25) | copy-start | bytes 1179652
  92.3 2.2 %copy-start.7 = (f32[4,24,1024]{2,1,0:T(8,128)S(1)}, f32[4,24,1024]{2,1,0:T(8,128)}, u32[]{:S(2)}) copy-start(f32[4,24,1024]{2,1,0:T(8,128)} %get-tuple-element.26) | copy-start | bytes 1179652
  92.3 2.2 %copy-start.25 = (pred[4,24]{1,0:T(4,128)(4,1)S(1)}, pred[4,24]{1,0:T(4,128)(4,1)}, u32[]{:S(2)}) copy-start(pred[4,24]{1,0:T(4,128)(4,1)} %broadcast_compare_fusion) | copy-start | bytes 292
  93.7 2.3 %slice-start.1 = ((s8[8388608]{0:T(1024)(128)(4,1)}), s8[4194304]{0:T(1024)(128)(4,1)S(1)}, s32[]{:S(2)}) async-start(s8[8388608]{0:T(1024)(128)(4,1)} %bitcast.107), calls=%async_computation.3 | async-start | bytes 8388608
  97.5 11.7 %copy-start.20 = (s32[4]{0:T(128)S(1)}, s32[4]{0:T(128)}, u32[]{:S(2)}) copy-start(s32[4]{0:T(128)} %copy-done.18) | copy-start | bytes 52
  97.6 22.7 %copy-start.1 = (bf16[16,16,2048]{2,1,0:T(8,128)(2,1)S(1)}, bf16[16,16,2048]{2,1,0:T(8,128)(2,1)}, u32[]{:S(2)}) copy-start(bf16[16,16,2048]{2,1,0:T(8,128)(2,1)} %copy-done) | copy-start | bytes 3145732
  97.7 7.2 %collective-permute-start.2 = (f32[]{:T(128)}, f32[]{:T(128)}, u32[]{:S(2)}, u32[]{:S(2)}) collective-permute-start(f32[]{:T(128)} %get-tuple-element.77), channel_id=1, source_target_pairs={{0,8},{8,16},{16,24},{24,0},{1,9},{9,17},{17,25},{25,1},{2,10},{10... | collective-permute-start | bytes 20 | tf_op jit(solution)/shard_map/ppermute | solution.py:79
  99.3 5.6 %collective-permute-start.3 = (f32[]{:T(128)}, f32[]{:T(128)}, u32[]{:S(2)}, u32[]{:S(2)}) collective-permute-start(f32[]{:T(128)} %get-tuple-element.77), channel_id=1, source_target_pairs={{0,16},{8,24},{16,0},{24,8},{1,17},{9,25},{17,1},{25,9},{2,18},{10... | collective-permute-start | bytes 20 | tf_op jit(solution)/shard_map/ppermute | solution.py:79
  101.7 3.7 %collective-permute-start.4 = (f32[]{:T(128)}, f32[]{:T(128)}, u32[]{:S(2)}, u32[]{:S(2)}) collective-permute-start(f32[]{:T(128)} %get-tuple-element.77), channel_id=1, source_target_pairs={{0,24},{8,0},{16,8},{24,16},{1,25},{9,1},{17,9},{25,17},{2,26},{10... | collective-permute-start | bytes 20 | tf_op jit(solution)/shard_map/ppermute | solution.py:79
  103.2 6.0 %collective-permute-start.5 = (f32[4,1536]{1,0:T(4,128)S(1)}, f32[4,1536]{1,0:T(4,128)S(1)}, u32[]{:S(2)}, u32[]{:S(2)}) collective-permute-start(f32[4,1536]{1,0:T(4,128)S(1)} %add_add_fusion.3), channel_id=1, source_target_pairs={{0,1},{1,2},{2,3},{3,4},{4,5},{5,6},{6,7},{8,9},{9,10},{10,11},{11... | collective-permute-start | bytes 73736 | tf_op jit(solution)/shard_map/ppermute | solution.py:20
Sparse Core Ops, SparseCore 0:
  16.5 41.1 reduce-scatter.1

commit v11 on v10

--- a/solution.py
+++ b/solution.py
@@ -191,7 +191,7 @@
     parts = lax.all_gather(jnp.stack([spreads, energies, logterms]), "seg", axis=0, tiled=False)
     spreads, energies, logterms = jnp.sum(parts, axis=0)
     own_loss = jnp.sum(jnp.sqrt((spreads + EPS_RATIO) / energies) + logterms)
-    loss = gathered_sum(own_loss, "clip") / (3 * clip_count * lax.axis_size("clip"))
+    loss = lax.psum(own_loss, "clip") / (3 * clip_count * lax.axis_size("clip"))
     ratio_weight = 1.0 / jnp.sqrt((spreads + EPS_RATIO) * energies)
     gradient = jnp.zeros((clip_count, samples), jnp.float32)
     extras = []

time: 131 us -> 137 us (1.046)
  blocking collectives: 20.9 us -> 33.1 us
  other arithmetic: 44.3 us -> 34.9 us
  waiting for transfers between devices: 4.14 us -> 12.8 us
  local copies, waits for them, and re-layouts: 10.6 us -> 5.44 us
  starting transfers between devices: 9.61 us -> 5.17 us
  matrix products: 24.2 us -> 28 us
    psum x0 -> x1, blocking collectives: none -> 12.2 us  [body(): loss = lax.psum(own_loss, 'clip') / (3 * clip_count * lax.axis_size('clip'))]
    reduce_scatter x1, waiting for transfers between devices: 3.62 us -> 12.3 us  [body(): lax.psum_scatter(sum((framed_sig[3 - quarter:3 - quarter + rows_here * la...]
    ppermute x3 -> x0, starting transfers between devices: 5.4 us -> none  [gathered_sum(): arrived = lax.ppermute(value, axis, route)]
    dot_general x3, matrix products: 2.45 us -> 5.92 us  [body(): jnp.einsum('cfj,jm->cfm', grad_x, table, preferred_element_type=jnp.float32)]
    reduce_sum x1 -> x0, other arithmetic: 3.15 us -> none  [gathered_sum(): return jnp.sum(slots, axis=0)]
    unnamed x73 -> x57, local copies, waits for them, and re-layouts: 5.05 us -> 3.25 us
    slice x6, local copies, waits for them, and re-layouts: 2.45 us -> 1.07 us  [framed(): padded[:, quarter:quarter + frame_count]]
    slice x2, local copies, waits for them, and re-layouts: 1.38 us -> 0.01 us  [body(): clean_beyond[:, :3 * stride]]
  transfers between devices with their start and end apart: 7 -> 4, of which waited for: 2 -> 2; matrix products, arithmetic and copies ran while one was open for 32% -> 21% of each run, Pallas kernels for 0% -> 0%
where the time goes in v11:
time: 137 us; the launch traced here: 136 us
  other arithmetic  34.9 us (25%)
  blocking collectives  33.1 us (24%)
  matrix products  28 us (20%)
  between operations  16.7 us (12%)
  waiting for transfers between devices  12.8 us (9%)
  local copies, waits for them, and re-layouts  5.44 us (4%)
  starting transfers between devices  5.17 us (4%)
    reduce_scatter x1, waiting for transfers between devices, body(): lax.psum_scatter(sum((framed_sig[3 - quarter:3 - quarter + rows_here * la...  12.3 us
    psum x1, blocking collectives, body(): loss = lax.psum(own_loss, 'clip') / (3 * clip_count * lax.axis_size('clip'))  12.2 us
    dot_general x3, matrix products, body(): jnp.einsum('cfm,jm->cfj', framed(clean, clean_beyond[:, :3 * stride], str...  10.5 us
    all_gather x1, blocking collectives, body(): lax.all_gather(jnp.stack([spreads, energies, logterms]), 'seg', axis=0, t...  10.4 us
    all_gather x1, blocking collectives, body(): portion = lax.all_gather(grad_hops, 'seg', axis=1, tiled=True)  10.4 us
    dot_general x3, matrix products, body(): jnp.einsum('cfm,jm->cfj', framed(est_wave, est_beyond[:, :3 * stride], st...  8.35 us
    convert_element_type x3, other arithmetic, analysis_table(): table = entry_value.astype(jnp.bfloat16)  8.02 us
    mul x3, other arithmetic, analysis_table(): fine_cos, fine_sin = (part * scale for part in fine)  7.26 us
  transfers between devices with their start and end apart: 4, of which 2 were waited for; matrix products, arithmetic and copies ran while one was open for 21% of the time, Pallas kernels for 0%

profile of v11, /device:TPU:0, one launch (start us, length us, event | category | flops | bytes accessed | tf_op | source)
XLA Modules:
  0.0 136.1 jit_solution(3466466911043481477)
XLA Ops:
  7.3 1.2 multiply_convert_fusion
  8.5 0.5 cosine_multiply_fusion.3
  9.0 1.9 %fusion.127 = (f32[16,2048]{1,0:T(8,128)S(1)}, f32[16,2048]{1,0:T(8,128)S(1)}, f32[16,2048]{1,0:T(8,128)S(1)}, f32[16,2048]{1,0:T(8,128)}) fusion(s32[16]{0:T(128)S(1)} %get-tuple-element.102, pred[16]{0:T(512)(128)(4,1)S(1)} %iota_compare_fusion.2, s32[16]{0:T(128)S(1)} %get-tuple-element.103), kind=kLoop, calls=%fused_computation.212 | loop fusion | flops 1179648 | bytes 524432 | tf_op jit(solution)/shard_map/jit(_where)/select_n | solution.py:62
  10.9 0.2 add_convert_fusion.2
  11.2 1.1 compare_select_fusion.2
  12.3 2.0 %convolution_bitcast_fusion = f32[195,4,2048]{2,0,1:T(8,128)S(1)} fusion(bf16[2,128,2048]{2,1,0:T(8,128)(2,1)S(1)} %bitcast.111, bf16[4,2,128,192]{2,3,1,0:T(8,128)(2,1)} %param.3), kind=kOutput, calls=%fused_computation.8 | convolution fusion | flops 817889280 | bytes 7831552 | tf_op jit(solution)/shard_map/crbf,rbm->fcm/dot_general | solution.py:125
  14.4 2.0 %slice_add_fusion = f32[192,4,512]{2,0,1:T(8,128)} fusion(f32[195,4,2048]{2,0,1:T(8,128)S(1)} %convolution_bitcast_fusion), kind=kLoop, calls=%fused_computation.24 | loop fusion | flops 1179648 | bytes 7864320 | tf_op jit(solution)/shard_map/add | solution.py:129
  16.4 1.5 %collective-permute-start.1 = (bf16[4,1536]{1,0:T(4,128)(2,1)S(1)}, bf16[4,1536]{1,0:T(4,128)(2,1)S(1)}, u32[]{:S(2)}, u32[]{:S(2)}) collective-permute-start(bf16[4,1536]{1,0:T(4,128)(2,1)S(1)} %slice.225), channel_id=1, source_target_pairs={{1,0},{2,1},{3,2},{4,3},{5,4},{6,5},{7,6},{9,8},{10,9},{11,10},{12... | collective-permute-start | bytes 36872 | tf_op jit(solution)/shard_map/ppermute | solution.py:20
  18.1 1.1 cosine_multiply_fusion.2
  19.2 2.1 %cosine_multiply_fusion.1 = (f32[128,1024]{1,0:T(8,128)S(1)}, f32[128,1024]{1,0:T(8,128)S(1)}) fusion(f32[1024]{0:T(1024)S(1)} %subtract_multiply_fusion), kind=kLoop, calls=%fused_computation.59 | loop fusion | flops 2097152 | bytes 1052672 | tf_op jit(solution)/shard_map/mul | solution.py:44
  21.3 0.6 broadcast_compare_fusion
  21.9 4.1 %cosine_multiply_fusion = (f32[128,2048]{1,0:T(8,128)S(1)}, f32[128,2048]{1,0:T(8,128)S(1)}) fusion(f32[2048]{0:T(1024)S(1)} %fusion.142), kind=kLoop, calls=%fused_computation.38 | loop fusion | flops 4194304 | bytes 2105344 | tf_op jit(solution)/shard_map/mul | solution.py:44
  26.0 0.6 broadcast_compare_fusion.2
  26.6 0.2 fusion.144
  26.8 0.2 fusion.137
  27.0 1.0 add_convert_fusion.3
  28.0 0.6 add_convert_fusion.1
  28.5 6.5 %add_convert_fusion = bf16[16,128,2048]{2,1,0:T(8,128)(2,1)} fusion(f32[128,2048]{1,0:T(8,128)S(1)} %get-tuple-element.75, f32[16,2048]{1,0:T(8,128)S(1)} %get-tuple-element.100, f32[128,2048]{1,0:T(8,128)S(1)} %get-tuple-element.74, f32[16,2048]{1,0:T(8,128)} %get-tuple-element.101), kind=kLoop, calls=%fused_computation | loop fusion | flops 16777216 | bytes 10747904 | tf_op jit(solution)/shard_map/convert_element_type | solution.py:46
  35.0 0.6 broadcast_compare_fusion.1
  35.7 0.1 reshape.894
  36.0 0.1 fusion.170
  36.1 0.1 fusion.168
  36.2 2.0 %fusion.15 = f32[4,48,1024]{2,1,0:T(8,128)} fusion(bf16[1024,1024]{1,0:T(8,128)(2,1)S(1)} %bitcast.108, bf16[4,48,256]{2,1,0:T(8,128)(2,1)S(1)} %get-tuple-element.57, bf16[4,48,256]{2,1,0:T(8,128)(2,1)S(1)} %get-tuple-element.58, bf16[4,48,256]{2,1,0:T(8,128)(2,1)S(1)} %get-tuple-element.59, bf16[4,48,256]{2,1,0:T(8,128)(2,1)S(1)} %get-tuple-element.56), kind=kOutput, calls=%fused_computation.19 | convolution fusion | flops 404226048 | bytes 3276800 | tf_op jit(solution)/shard_map/cfm,jm->cfj/dot_general | solution.py:158
  38.2 7.2 %fusion.2 = f32[4,24,2048]{2,1,0:T(8,128)} fusion(bf16[2048,2048]{1,0:T(8,128)(2,1)} %bitcast.105, bf16[4,24,512]{2,1,0:T(8,128)(2,1)S(1)} %get-tuple-element.49, bf16[4,24,512]{2,1,0:T(8,128)(2,1)S(1)} %get-tuple-element.50, bf16[4,24,512]{2,1,0:T(8,128)(2,1)S(1)} %get-tuple-element.51, bf16[4,24,512]{2,1,0:T(8,128)(2,1)S(1)} %get-tuple-element.48), kind=kOutput, calls=%fused_computation.3 | convolution fusion | flops 806879232 | bytes 9568256 | tf_op jit(solution)/shard_map/cfm,jm->cfj/dot_general | solution.py:158
  45.4 12.3 %reduce-scatter.2.cloned.1.call-done = f32[24,4,512]{2,0,1:T(8,128)} async-done(((f32[192,4,512]{2,0,1:T(8,128)}), f32[24,4,512]{2,0,1:T(8,128)}) %reduce-scatter.2.cloned.1.call-update) | async-done | bytes 196624 | tf_op jit(solution)/shard_map/reduce_scatter | solution.py:128
  57.7 1.1 copy.10
  58.8 0.1 fusion.105
  58.9 1.3 collective-permute-start
  60.2 1.3 fusion.34
  61.5 0.5 collective-permute-done
  62.1 0.1 reshape.893
  62.1 0.7 fusion.171
  63.0 0.1 fusion.169
  63.1 0.8 pad_maximum_fusion
  64.0 1.4 %fusion.36 = f32[4,96,512]{2,1,0:T(8,128)S(1)} fusion(bf16[512,512]{1,0:T(8,128)(2,1)S(1)} %bitcast.114, bf16[4,96,128]{2,1,0:T(8,128)(2,1)S(1)} %get-tuple-element.69, bf16[4,96,128]{2,1,0:T(8,128)(2,1)} %get-tuple-element.70, bf16[4,96,128]{2,1,0:T(8,128)(2,1)} %get-tuple-element.71, bf16[4,96,128]{2,1,0:T(8,128)(2,1)S(1)} %get-tuple-element.68), kind=kOutput, calls=%fused_computation.56 | convolution fusion | flops 202899456 | bytes 1703936 | tf_op jit(solution)/shard_map/cfm,jm->cfj/dot_general | solution.py:164
  65.4 1.0 copy-done.3
  66.4 2.6 %select_reduce_fusion.8 = (f32[4]{0:T(128)S(1)}, f32[4]{0:T(128)S(1)}, f32[4]{0:T(128)S(1)}, f32[4,96,256]{2,1,0:T(8,128)}, f32[4,96,256]{2,1,0:T(8,128)}) fusion(pred[4,96]{1,0:T(4,128)(4,1)} %broadcast_compare_fusion.2, f32[4,96,512]{2,1,0:T(8,128)S(1)} %fusion.36, f32[4,96,512]{2,1,0:T(8,128)} %fusion.34), kind=kLoop, calls=%fused_computation.149 | loop fusion | flops 2064372 | bytes 2359728 | tf_op jit(solution)/shard_map/reduce_sum | solution.py:182
  69.0 0.8 fusion.17
  69.8 1.4 %select_reduce_fusion.7 = (f32[4]{0:T(128)S(1)}, f32[4]{0:T(128)S(1)}, f32[4]{0:T(128)S(1)}, f32[4,48,512]{2,1,0:T(8,128)}, f32[4,48,512]{2,1,0:T(8,128)}) fusion(pred[4,48]{1,0:T(4,128)(4,1)S(1)} %copy-done.21, f32[4,48,1024]{2,1,0:T(8,128)S(1)} %fusion.17, f32[4,48,1024]{2,1,0:T(8,128)S(1)} %copy-done.12), kind=kLoop, calls=%fused_computation.147 | loop fusion | flops 2064372 | bytes 2359536 | tf_op jit(solution)/shard_map/reduce_sum | solution.py:182
  71.3 6.1 %fusion.4 = f32[4,24,2048]{2,1,0:T(8,128)S(1)} fusion(bf16[2048,2048]{1,0:T(8,128)(2,1)} %bitcast.106, bf16[4,24,512]{2,1,0:T(8,128)(2,1)S(1)} %get-tuple-element.53, bf16[4,24,512]{2,1,0:T(8,128)(2,1)S(1)} %get-tuple-element.54, bf16[4,24,512]{2,1,0:T(8,128)(2,1)S(1)} %get-tuple-element.55, bf16[4,24,512]{2,1,0:T(8,128)(2,1)S(1)} %get-tuple-element.52), kind=kOutput, calls=%fused_computation.5 | convolution fusion | flops 806879232 | bytes 9568256 | tf_op jit(solution)/shard_map/cfm,jm->cfj/dot_general | solution.py:164
  77.4 1.3 select_reduce_fusion.6
  78.9 10.4 %all-gather = f32[24,3,4]{2,1,0:T(4,128)S(1)} all-gather(f32[3,3,4]{2,1,0:T(4,128)S(1)} %pad_maximum_fusion.6), channel_id=2, replica_groups=mesh['clip'=4,'seg'=8] {'seg'}, dimensions={0}, use_global_device_ids=true | all-gather | bytes 1296 | tf_op jit(solution)/shard_map/all_gather | solution.py:191
  89.3 0.6 multiply_rsqrt_fusion
  90.0 1.6 %divide_convert_fusion.1 = (bf16[4,24,1024]{2,1,0:T(8,128)(2,1)S(1)}, bf16[4,24,1024]{2,1,0:T(8,128)(2,1)S(1)}) fusion(f32[4,24,2048]{2,1,0:T(8,128)S(1)} %fusion.4, f32[4,24,1024]{2,1,0:T(8,128)} %get-tuple-element.25, f32[4,24,1024]{2,1,0:T(8,128)} %get-tuple-element.26, f32[4]{0:T(128)S(1)} %copy-done.16, f32[4]{0:T(128)S(1)} %get-tuple-element.81, ...), kind=kLoop, calls=%fused_computation.128 | loop fusion | flops 1671168 | bytes 1966208 | tf_op jit(solution)/shard_map/convert
  91.6 5.0 %fusion = f32[4,24,2048]{2,1,0:T(8,128)S(1)} fusion(bf16[2048,2048]{1,0:T(8,128)(2,1)} %bitcast.107, bf16[4,24,1024]{2,1,0:T(8,128)(2,1)S(1)} %get-tuple-element.32, bf16[4,24,1024]{2,1,0:T(8,128)(2,1)S(1)} %get-tuple-element.31), kind=kOutput, calls=%fused_computation.1 | convolution fusion | flops 806092800 | bytes 9568256 | tf_op jit(solution)/shard_map/cfj,jm->cfm/dot_general | solution.py:211
  96.6 0.1 fusion.165
  96.6 0.1 pad_add_fusion
  96.8 0.5 divide_convert_fusion.3
  97.4 0.6 fusion.13
  97.9 0.1 fusion.164
  98.0 0.1 pad_add_fusion.1
  98.2 0.5 divide_convert_fusion.5
  98.7 0.4 fusion.32
  99.0 0.1 fusion.163
  99.1 0.1 pad_add_fusion.2
  99.3 2.4 %collective-permute-start.2 = (f32[4,1536]{1,0:T(4,128)S(1)}, f32[4,1536]{1,0:T(4,128)S(1)}, u32[]{:S(2)}, u32[]{:S(2)}) collective-permute-start(f32[4,1536]{1,0:T(4,128)S(1)} %add_add_fusion.3), channel_id=1, source_target_pairs={{0,1},{1,2},{2,3},{3,4},{4,5},{5,6},{6,7},{8,9},{9,10},{10,11},{11... | collective-permute-start | bytes 73736 | tf_op jit(solution)/shard_map/ppermute | solution.py:20
  101.7 12.2 %psum.7 = f32[]{:T(128)} all-reduce(f32[]{:T(128)} %get-tuple-element.77), channel_id=1, replica_groups=mesh['clip'=4,'seg'=8] {'clip'}, use_global_device_ids=true, to_apply=%region_12.13 | all-reduce | flops 1 | bytes 8 | tf_op jit(solution)/shard_map/psum | solution.py:194
  113.9 0.1 copy.13
  114.1 0.1 copy.12
  114.9 0.2 fusion.106
  115.1 10.4 %all_gather.11 = bf16[4,192,512]{2,1,0:T(8,128)(2,1)S(1)} all-gather(bf16[4,24,512]{2,1,0:T(8,128)(2,1)S(1)} %bitcast.118), channel_id=1, replica_groups=mesh['clip'=4,'seg'=8] {'seg'}, dimensions={1}, use_global_device_ids=true | all-gather | bytes 884736 | tf_op jit(solution)/shard_map/all_gather | solution.py:223
  125.5 0.5 pad_slice_fusion.2
  126.1 1.2 fusion.20
  127.3 0.8 copy.7
  (98 shorter events, 1.2 us)
Async XLA Ops:
  7.2 50.6 %reduce-scatter.2.cloned.1.call-start = ((), (), s32[]{:S(2)}) async-start(), calls=%async_computation.1 | async-start | bytes 1769472 | tf_op jit(solution)/shard_map/reduce_scatter | solution.py:128
  8.5 50.3 %copy-start.14 = (s32[4]{0:T(128)}, s32[4]{0:T(128)S(1)}, u32[]{:S(2)}) copy-start(s32[4]{0:T(128)S(1)} %get-tuple-element.95) | copy-start | bytes 52
  11.2 1.1 copy-start
  14.4 7.0 %copy-start.17 = (s32[4]{0:T(128)S(1)}, s32[4]{0:T(128)}, u32[]{:S(2)}) copy-start(s32[4]{0:T(128)} %param.5) | copy-start | bytes 52
  16.4 19.2 %collective-permute-start.1 = (bf16[4,1536]{1,0:T(4,128)(2,1)S(1)}, bf16[4,1536]{1,0:T(4,128)(2,1)S(1)}, u32[]{:S(2)}, u32[]{:S(2)}) collective-permute-start(bf16[4,1536]{1,0:T(4,128)(2,1)S(1)} %slice.225), channel_id=1, source_target_pairs={{1,0},{2,1},{3,2},{4,3},{5,4},{6,5},{7,6},{9,8},{10,9},{11,10},{12... | collective-permute-start | bytes 36872 | tf_op jit(solution)/shard_map/ppermute | solution.py:20
  38.2 22.1 %copy-start.7 = (bf16[4,128,512]{2,1,0:T(8,128)(2,1)S(1)}, bf16[4,128,512]{2,1,0:T(8,128)(2,1)}, u32[]{:S(2)}) copy-start(bf16[4,128,512]{2,1,0:T(8,128)(2,1)} %add_convert_fusion.3) | copy-start | bytes 1572868
  58.9 3.1 %collective-permute-start = (bf16[4,1536]{1,0:T(4,128)(2,1)S(1)}, bf16[4,1536]{1,0:T(4,128)(2,1)S(1)}, u32[]{:S(2)}, u32[]{:S(2)}) collective-permute-start(bf16[4,1536]{1,0:T(4,128)(2,1)S(1)} %slice.287), channel_id=1, source_target_pairs={{1,0},{2,1},{3,2},{4,3},{5,4},{6,5},{7,6},{9,8},{10,9},{11,10},{12... | collective-permute-start | bytes 36872 | tf_op jit(solution)/shard_map/ppermute | solution.py:20
  62.0 0.9 copy-start.13
  64.0 5.8 %copy-start.12 = (f32[4,48,1024]{2,1,0:T(8,128)S(1)}, f32[4,48,1024]{2,1,0:T(8,128)}, u32[]{:S(2)}) copy-start(f32[4,48,1024]{2,1,0:T(8,128)} %fusion.15) | copy-start | bytes 2359300
  64.0 5.8 %copy-start.21 = (pred[4,48]{1,0:T(4,128)(4,1)S(1)}, pred[4,48]{1,0:T(4,128)(4,1)}, u32[]{:S(2)}) copy-start(pred[4,48]{1,0:T(4,128)(4,1)} %broadcast_compare_fusion.1) | copy-start | bytes 580
  65.4 1.0 copy-start.3
  69.8 1.5 %copy-start.5 = (f32[4,48,1024]{2,1,0:T(8,128)}, f32[4,48,1024]{2,1,0:T(8,128)S(1)}, u32[]{:S(2)}) copy-start(f32[4,48,1024]{2,1,0:T(8,128)S(1)} %fusion.17) | copy-start | bytes 2359300
  71.3 6.1 %copy-start.2 = (f32[4,24,2048]{2,1,0:T(8,128)S(1)}, f32[4,24,2048]{2,1,0:T(8,128)}, u32[]{:S(2)}) copy-start(f32[4,24,2048]{2,1,0:T(8,128)} %fusion.2) | copy-start | bytes 2359300
  71.3 6.1 %copy-start.20 = (pred[4,24]{1,0:T(4,128)(4,1)S(1)}, pred[4,24]{1,0:T(4,128)(4,1)}, u32[]{:S(2)}) copy-start(pred[4,24]{1,0:T(4,128)(4,1)} %broadcast_compare_fusion) | copy-start | bytes 292
  71.3 7.5 %copy-start.18 = (s32[4]{0:T(128)S(1)}, s32[4]{0:T(128)}, u32[]{:S(2)}) copy-start(s32[4]{0:T(128)} %param.5) | copy-start | bytes 52
  71.3 18.7 %copy-start.16 = (f32[4]{0:T(128)S(1)}, f32[4]{0:T(128)}, u32[]{:S(2)}) copy-start(f32[4]{0:T(128)} %get-tuple-element.93) | copy-start | bytes 52
  91.5 5.2 %copy-start.6 = (f32[4,48,1024]{2,1,0:T(8,128)S(1)}, f32[4,48,1024]{2,1,0:T(8,128)}, u32[]{:S(2)}) copy-start(f32[4,48,1024]{2,1,0:T(8,128)} %copy-done.5) | copy-start | bytes 2359300
  91.6 5.2 %copy-start.10 = (f32[4,48,512]{2,1,0:T(8,128)S(1)}, f32[4,48,512]{2,1,0:T(8,128)}, u32[]{:S(2)}) copy-start(f32[4,48,512]{2,1,0:T(8,128)} %get-tuple-element.23) | copy-start | bytes 1179652
  91.6 5.2 %copy-start.11 = (f32[4,48,512]{2,1,0:T(8,128)S(1)}, f32[4,48,512]{2,1,0:T(8,128)}, u32[]{:S(2)}) copy-start(f32[4,48,512]{2,1,0:T(8,128)} %get-tuple-element.24) | copy-start | bytes 1179652
  91.6 5.2 %copy-start.22 = (pred[4,48]{1,0:T(4,128)(4,1)S(1)}, pred[4,48]{1,0:T(4,128)(4,1)}, u32[]{:S(2)}) copy-start(pred[4,48]{1,0:T(4,128)(4,1)} %broadcast_compare_fusion.1) | copy-start | bytes 580
  96.8 1.3 copy-start.4
  96.8 1.3 copy-start.8
  96.8 1.3 copy-start.9
  96.8 1.3 copy-start.19
  98.2 16.7 %copy-start.15 = (s32[4]{0:T(128)S(1)}, s32[4]{0:T(128)}, u32[]{:S(2)}) copy-start(s32[4]{0:T(128)} %copy-done.14) | copy-start | bytes 52
  99.2 26.9 %copy-start.1 = (bf16[16,16,2048]{2,1,0:T(8,128)(2,1)S(1)}, bf16[16,16,2048]{2,1,0:T(8,128)(2,1)}, u32[]{:S(2)}) copy-start(bf16[16,16,2048]{2,1,0:T(8,128)(2,1)} %copy-done) | copy-start | bytes 3145732
  99.3 15.5 %collective-permute-start.2 = (f32[4,1536]{1,0:T(4,128)S(1)}, f32[4,1536]{1,0:T(4,128)S(1)}, u32[]{:S(2)}, u32[]{:S(2)}) collective-permute-start(f32[4,1536]{1,0:T(4,128)S(1)} %add_add_fusion.3), channel_id=1, source_target_pairs={{0,1},{1,2},{2,3},{3,4},{4,5},{5,6},{6,7},{8,9},{9,10},{10,11},{11... | collective-permute-start | bytes 73736 | tf_op jit(solution)/shard_map/ppermute | solution.py:20
Sparse Core Ops, SparseCore 0:
  16.5 41.1 reduce-scatter.1

commit v12 on v10

--- a/solution.py
+++ b/solution.py
@@ -100,8 +100,12 @@
 
 def framed(signal, beyond, stride):
     frame_count = signal.shape[1] // stride
-    padded = jnp.concatenate([signal, beyond], axis=1).reshape(
-        signal.shape[0], frame_count + 3, stride
+    padded = jnp.concatenate(
+        [
+            signal.reshape(signal.shape[0], frame_count, stride),
+            beyond.reshape(signal.shape[0], 3, stride),
+        ],
+        axis=1,
     )
     return jnp.concatenate(
         [padded[:, quarter : quarter + frame_count] for quarter in range(4)], axis=2

time: 131 us -> 132 us (level)
  waiting for transfers between devices: 4.14 us -> 1.54 us
  blocking collectives: 20.9 us -> 23.4 us
    reduce_scatter x1, waiting for transfers between devices: 3.62 us -> 0.04 us  [body(): lax.psum_scatter(sum((framed_sig[3 - quarter:3 - quarter + rows_here * la...]
    all_gather x1, blocking collectives: 10.6 us -> 12.3 us  [body(): lax.all_gather(jnp.stack([spreads, energies, logterms]), 'seg', axis=0, t...]
    reshape x6 -> x7, local copies, waits for them, and re-layouts: 0.36 us -> 1.98 us  [the longest x2 1.95 us: body(): estimate = jnp.transpose(hop_rows, (1, 0, 2)).reshape(clip_count, samples)]
    slice x2 -> x1, local copies, waits for them, and re-layouts: 1.38 us -> 0.01 us  [body(): clean_beyond[:, :3 * stride]]
    unnamed x73 -> x59, local copies, waits for them, and re-layouts: 5.05 us -> 5.29 us
  transfers between devices with their start and end apart: 7 -> 7, of which waited for: 2 -> 2; matrix products, arithmetic and copies ran while one was open for 32% -> 34% of each run, Pallas kernels for 0% -> 0%
where the time goes in v12:
time: 132 us; the launch traced here: 131 us
  other arithmetic  44.8 us (34%)
  matrix products  24.9 us (19%)
  blocking collectives  23.4 us (18%)
  between operations  16.6 us (13%)
  local copies, waits for them, and re-layouts  9.89 us (7%)
  starting transfers between devices  9.79 us (7%)
  waiting for transfers between devices  1.54 us (1%)
    all_gather x1, blocking collectives, body(): lax.all_gather(jnp.stack([spreads, energies, logterms]), 'seg', axis=0, t...  12.3 us
    dot_general x3, matrix products, body(): jnp.einsum('cfm,jm->cfj', framed(clean, clean_beyond[:, :3 * stride], str...  11.9 us
    all_gather x1, blocking collectives, body(): portion = lax.all_gather(grad_hops, 'seg', axis=1, tiled=True)  11.1 us
    mul x3, other arithmetic, analysis_table(): fine_cos, fine_sin = (part * scale for part in fine)  8 us
    convert_element_type x3, other arithmetic, analysis_table(): table = entry_value.astype(jnp.bfloat16)  7.32 us
    dot_general x3, matrix products, body(): jnp.einsum('cfm,jm->cfj', framed(est_wave, est_beyond[:, :3 * stride], st...  7.28 us
    ppermute x3, starting transfers between devices, gathered_sum(): arrived = lax.ppermute(value, axis, route)  5.56 us
    unnamed x59, local copies, waits for them, and re-layouts  5.29 us
  transfers between devices with their start and end apart: 7, of which 2 were waited for; matrix products, arithmetic and copies ran while one was open for 34% of the time, Pallas kernels for 0%

profile of v12, /device:TPU:0, one launch (start us, length us, event | category | flops | bytes accessed | tf_op | source)
XLA Modules:
  0.0 130.9 jit_solution(14579353394253820724)
XLA Ops:
  7.3 0.5 cosine_multiply_fusion.3
  7.8 1.9 %fusion.130 = (f32[16,2048]{1,0:T(8,128)S(1)}, f32[16,2048]{1,0:T(8,128)S(1)}, f32[16,2048]{1,0:T(8,128)}, f32[16,2048]{1,0:T(8,128)}) fusion(s32[16]{0:T(128)S(1)} %get-tuple-element.95, pred[16]{0:T(512)(128)(4,1)S(1)} %iota_compare_fusion.2, s32[16]{0:T(128)S(1)} %get-tuple-element.96), kind=kLoop, calls=%fused_computation.223 | loop fusion | flops 1179648 | bytes 524432 | tf_op jit(solution)/shard_map/jit(_where)/select_n | solution.py:62
  9.8 0.2 add_convert_fusion.2
  10.1 1.3 multiply_convert_fusion
  11.3 1.1 broadcast_select_fusion
  12.4 2.0 %convolution_bitcast_fusion = f32[195,4,2048]{2,0,1:T(8,128)S(1)} fusion(bf16[2,128,2048]{2,1,0:T(8,128)(2,1)S(1)} %bitcast.148, bf16[4,2,128,192]{2,3,1,0:T(8,128)(2,1)} %param.3), kind=kOutput, calls=%fused_computation.8 | convolution fusion | flops 817889280 | bytes 7831552 | tf_op jit(solution)/shard_map/crbf,rbm->fcm/dot_general | solution.py:129
  14.4 2.0 %slice_add_fusion = f32[192,4,512]{2,0,1:T(8,128)} fusion(f32[195,4,2048]{2,0,1:T(8,128)S(1)} %convolution_bitcast_fusion), kind=kLoop, calls=%fused_computation.24 | loop fusion | flops 1179648 | bytes 7864320 | tf_op jit(solution)/shard_map/add | solution.py:133
  16.5 1.3 collective-permute-start.1
  17.8 0.6 add_add_fusion.3
  18.5 0.6 add_add_fusion.4
  19.1 0.6 fusion.160
  19.8 0.5 iota_compare_fusion
  20.3 0.6 fusion.159
  20.9 0.6 iota_compare_fusion.1
  21.5 4.1 %cosine_multiply_fusion = (f32[128,2048]{1,0:T(8,128)S(1)}, f32[128,2048]{1,0:T(8,128)S(1)}) fusion(f32[2048]{0:T(1024)S(1)} %fusion.152), kind=kLoop, calls=%fused_computation.38 | loop fusion | flops 4194304 | bytes 2105344 | tf_op jit(solution)/shard_map/mul | solution.py:44
  25.6 0.7 constant_dynamic-update-slice_fusion.4
  26.4 2.1 %cosine_multiply_fusion.1 = (f32[128,1024]{1,0:T(8,128)S(1)}, f32[128,1024]{1,0:T(8,128)S(1)}) fusion(f32[1024]{0:T(1024)S(1)} %subtract_multiply_fusion), kind=kLoop, calls=%fused_computation.59 | loop fusion | flops 2097152 | bytes 1052672 | tf_op jit(solution)/shard_map/mul | solution.py:44
  28.5 0.5 iota_add_fusion.2
  29.0 1.8 %cosine_multiply_fusion.2 = (f32[128,512]{1,0:T(8,128)}, f32[128,512]{1,0:T(8,128)}) fusion(f32[512]{0:T(512)S(1)} %subtract_multiply_fusion.1), kind=kLoop, calls=%fused_computation.165 | loop fusion | flops 1048576 | bytes 526336 | tf_op jit(solution)/shard_map/mul | solution.py:44
  30.9 0.9 fusion.146
  31.8 1.3 %broadcast_compare_fusion.2 = pred[4,48]{1,0:T(4,128)(4,1)} fusion(s32[48]{0:T(128)} %iota_add_fusion.2, s32[4]{0:T(128)} %get-tuple-element.87), kind=kLoop, calls=%fused_computation.304 | loop fusion | flops 192 | bytes 400 | tf_op jit(solution)/shard_map/lt | solution.py:182
  33.1 0.8 fusion.154
  33.9 1.2 broadcast_compare_fusion.3
  35.2 6.6 %add_convert_fusion = bf16[16,128,2048]{2,1,0:T(8,128)(2,1)} fusion(f32[128,2048]{1,0:T(8,128)S(1)} %get-tuple-element.68, f32[16,2048]{1,0:T(8,128)} %get-tuple-element.93, f32[128,2048]{1,0:T(8,128)S(1)} %get-tuple-element.67, f32[16,2048]{1,0:T(8,128)} %get-tuple-element.94), kind=kLoop, calls=%fused_computation | loop fusion | flops 16777216 | bytes 10747904 | tf_op jit(solution)/shard_map/convert_element_type | solution.py:46
  41.8 0.6 add_convert_fusion.1
  42.6 0.7 copy.50
  43.2 0.7 copy.51
  43.9 0.6 copy_dynamic-update-slice_fusion
  44.6 1.1 fusion.180
  45.8 2.2 %fusion.34 = f32[4,96,512]{2,1,0:T(8,128)} fusion(bf16[512,512]{1,0:T(8,128)(2,1)S(1)} %bitcast.153, bf16[4,96,128]{2,1,0:T(8,128)(2,1)S(1)} %get-tuple-element.59, bf16[4,96,128]{2,1,0:T(8,128)(2,1)S(1)} %get-tuple-element.60, bf16[4,96,128]{2,1,0:T(8,128)(2,1)S(1)} %get-tuple-element.58, bf16[4,96,128]{2,1,0:T(8,128)(2,1)} %bitcast.164), kind=kOutput, calls=%fused_computation.54 | convolution fusion | flops 202899456 | bytes 1703936 | tf_op jit(solution)/shard_map/cfm,jm->cfj/dot_general | solution.py:162
  48.0 2.6 %fusion.15 = f32[4,48,1024]{2,1,0:T(8,128)} fusion(bf16[1024,1024]{1,0:T(8,128)(2,1)S(1)} %bitcast.139, bf16[4,48,256]{2,1,0:T(8,128)(2,1)S(1)} %get-tuple-element.54, bf16[4,48,256]{2,1,0:T(8,128)(2,1)S(1)} %get-tuple-element.55, bf16[4,48,256]{2,1,0:T(8,128)(2,1)S(1)} %get-tuple-element.53, bf16[4,48,256]{2,1,0:T(8,128)(2,1)} %bitcast.163), kind=kOutput, calls=%fused_computation.19 | convolution fusion | flops 404226048 | bytes 3276800 | tf_op jit(solution)/shard_map/cfm,jm->cfj/dot_general | solution.py:162
  50.7 7.1 %fusion.2 = f32[4,24,2048]{2,1,0:T(8,128)} fusion(bf16[2048,2048]{1,0:T(8,128)(2,1)} %bitcast.134, bf16[4,24,512]{2,1,0:T(8,128)(2,1)S(1)} %get-tuple-element.51, bf16[4,24,512]{2,1,0:T(8,128)(2,1)S(1)} %get-tuple-element.52, bf16[4,24,512]{2,1,0:T(8,128)(2,1)S(1)} %get-tuple-element.50, bf16[4,24,512]{2,1,0:T(8,128)(2,1)S(1)} %bitcast.158), kind=kOutput, calls=%fused_computation.3 | convolution fusion | flops 806879232 | bytes 9568256 | tf_op jit(solution)/shard_map/cfm,jm->cfj/dot_general | solution.py:162
  57.8 1.0 reshape.950
  58.8 1.0 reshape.945
  59.8 1.1 copy.22
  60.8 1.5 %collective-permute-start = (bf16[4,1536]{1,0:T(4,128)(2,1)S(1)}, bf16[4,1536]{1,0:T(4,128)(2,1)S(1)}, u32[]{:S(2)}, u32[]{:S(2)}) collective-permute-start(bf16[4,1536]{1,0:T(4,128)(2,1)S(1)} %fusion.147), channel_id=1, source_target_pairs={{1,0},{2,1},{3,2},{4,3},{5,4},{6,5},{7,6},{9,8},{10,9},{11,10},{12... | collective-permute-start | bytes 36872 | tf_op jit(solution)/shard_map/ppermute | solution.py:20
  62.5 1.0 select_convert_fusion
  63.6 0.9 collective-permute-done
  64.6 6.0 %fusion.4 = f32[4,24,2048]{2,1,0:T(8,128)S(1)} fusion(bf16[2048,2048]{1,0:T(8,128)(2,1)} %bitcast.135, bf16[4,3,512]{2,1,0:T(4,128)(2,1)S(1)} %copy.17, bf16[4,24,512]{2,1,0:T(8,128)(2,1)S(1)} %select_convert_fusion, bf16[4,24,512]{2,1,0:T(8,128)(2,1)S(1)} %get-tuple-element.57, bf16[4,24,512]{2,1,0:T(8,128)(2,1)S(1)} %get-tuple-element.56), kind=kOutput, calls=%fused_computation.5 | convolution fusion | flops 807272448 | bytes 9482240 | tf_op jit(solution)/shard_map/cfm,jm->cfj/dot_general | solution.py:168
  70.8 0.9 fusion.17
  71.7 0.4 fusion.36
  72.1 1.4 %select_reduce_fusion.6 = (f32[4]{0:T(128)S(1)}, f32[4]{0:T(128)S(1)}, f32[4]{0:T(128)S(1)}, f32[4,24,1024]{2,1,0:T(8,128)}, f32[4,24,1024]{2,1,0:T(8,128)}) fusion(pred[4,24]{1,0:T(4,128)(4,1)S(1)} %broadcast_compare_fusion.1, f32[4,24,2048]{2,1,0:T(8,128)S(1)} %fusion.4, f32[4,24,2048]{2,1,0:T(8,128)S(1)} %copy-done.2), kind=kLoop, calls=%fused_computation.148 | loop fusion | flops 2064372 | bytes 2359440 | tf_op jit(solution)/shard_map/reduce_sum | solution.py:186
  73.5 1.5 %select_reduce_fusion.7 = (f32[4]{0:T(128)S(1)}, f32[4]{0:T(128)S(1)}, f32[4]{0:T(128)S(1)}, f32[4,48,512]{2,1,0:T(8,128)}, f32[4,48,512]{2,1,0:T(8,128)}) fusion(pred[4,48]{1,0:T(4,128)(4,1)S(1)} %copy-done.17, f32[4,48,1024]{2,1,0:T(8,128)S(1)} %fusion.17, f32[4,48,1024]{2,1,0:T(8,128)S(1)} %copy-done.13), kind=kLoop, calls=%fused_computation.150 | loop fusion | flops 2064372 | bytes 2359536 | tf_op jit(solution)/shard_map/reduce_sum | solution.py:186
  75.0 1.4 %select_reduce_fusion.8 = (f32[4]{0:T(128)S(1)}, f32[4]{0:T(128)S(1)}, f32[4]{0:T(128)S(1)}, f32[4,96,256]{2,1,0:T(8,128)}, f32[4,96,256]{2,1,0:T(8,128)}) fusion(pred[4,96]{1,0:T(4,128)(4,1)S(1)} %copy-done.18, f32[4,96,512]{2,1,0:T(8,128)S(1)} %fusion.36, f32[4,96,512]{2,1,0:T(8,128)S(1)} %copy-done.12), kind=kLoop, calls=%fused_computation.152 | loop fusion | flops 2064372 | bytes 2359728 | tf_op jit(solution)/shard_map/reduce_sum | solution.py:186
  76.5 12.3 %all-gather = f32[24,3,4]{2,1,0:T(4,128)S(1)} all-gather(f32[3,3,4]{2,1,0:T(4,128)S(1)} %pad_maximum_fusion.3), channel_id=2, replica_groups=mesh['clip'=4,'seg'=8] {'seg'}, dimensions={0}, use_global_device_ids=true | all-gather | bytes 1296 | tf_op jit(solution)/shard_map/all_gather | solution.py:195
  88.9 0.6 multiply_rsqrt_fusion
  89.5 1.8 %divide_convert_fusion.5 = (bf16[4,96,256]{2,1,0:T(8,128)(2,1)S(1)}, bf16[4,96,256]{2,1,0:T(8,128)(2,1)S(1)}) fusion(f32[4,96,512]{2,1,0:T(8,128)} %copy-done.5, f32[4,96,256]{2,1,0:T(8,128)} %get-tuple-element.21, f32[4,96,256]{2,1,0:T(8,128)} %get-tuple-element.22, f32[4]{0:T(128)S(1)} %get-tuple-element.86, f32[4]{0:T(128)S(1)} %get-tuple-element.73, ...), kind=kLoop, calls=%fused_computation.137 | loop fusion | flops 1671168 | bytes 1966496 | tf_op jit(solution)/shard_map/convert.4
  91.3 0.4 fusion.32
  91.9 1.4 %divide_convert_fusion.3 = (bf16[4,48,512]{2,1,0:T(8,128)(2,1)S(1)}, bf16[4,48,512]{2,1,0:T(8,128)(2,1)S(1)}) fusion(f32[4,48,1024]{2,1,0:T(8,128)S(1)} %copy-done.4, f32[4,48,512]{2,1,0:T(8,128)S(1)} %copy-done.8, f32[4,48,512]{2,1,0:T(8,128)S(1)} %copy-done.9, f32[4]{0:T(128)S(1)} %get-tuple-element.86, f32[4]{0:T(128)S(1)} %get-tuple-element.75, ...), kind=kLoop, calls=%fused_computation.134 | loop fusion | flops 1671168 | bytes 1966304 | tf_op jit(solution)/shard_map/convert.2
  93.3 0.6 fusion.13
  94.1 0.5 divide_convert_fusion.1
  94.6 1.0 slice-done.1
  95.6 1.5 %fusion = f32[4,24,2048]{2,1,0:T(8,128)S(1)} fusion(bf16[2048,2048]{1,0:T(8,128)(2,1)S(1)} %bitcast.138, bf16[4,24,1024]{2,1,0:T(8,128)(2,1)S(1)} %get-tuple-element.34, bf16[4,24,1024]{2,1,0:T(8,128)(2,1)S(1)} %get-tuple-element.33), kind=kOutput, calls=%fused_computation.1 | convolution fusion | flops 806092800 | bytes 9568256 | tf_op jit(solution)/shard_map/cfj,jm->cfm/dot_general | solution.py:215
  97.4 1.6 %collective-permute-start.2 = (f32[]{:T(128)}, f32[]{:T(128)}, u32[]{:S(2)}, u32[]{:S(2)}) collective-permute-start(f32[]{:T(128)} %get-tuple-element.70), channel_id=1, source_target_pairs={{0,8},{8,16},{16,24},{24,0},{1,9},{9,17},{17,25},{25,1},{2,10},{10... | collective-permute-start | bytes 20 | tf_op jit(solution)/shard_map/ppermute | solution.py:79
  99.0 2.6 %collective-permute-start.3 = (f32[]{:T(128)}, f32[]{:T(128)}, u32[]{:S(2)}, u32[]{:S(2)}) collective-permute-start(f32[]{:T(128)} %get-tuple-element.70), channel_id=1, source_target_pairs={{0,16},{8,24},{16,0},{24,8},{1,17},{9,25},{17,1},{25,9},{2,18},{10... | collective-permute-start | bytes 20 | tf_op jit(solution)/shard_map/ppermute | solution.py:79
  101.6 1.3 %collective-permute-start.4 = (f32[]{:T(128)}, f32[]{:T(128)}, u32[]{:S(2)}, u32[]{:S(2)}) collective-permute-start(f32[]{:T(128)} %get-tuple-element.70), channel_id=1, source_target_pairs={{0,24},{8,0},{16,8},{24,16},{1,25},{9,1},{17,9},{25,17},{2,26},{10... | collective-permute-start | bytes 20 | tf_op jit(solution)/shard_map/ppermute | solution.py:79
  103.0 1.4 %collective-permute-start.5 = (f32[4,1536]{1,0:T(4,128)S(1)}, f32[4,1536]{1,0:T(4,128)S(1)}, u32[]{:S(2)}, u32[]{:S(2)}) collective-permute-start(f32[4,1536]{1,0:T(4,128)S(1)} %add_add_fusion.6), channel_id=1, source_target_pairs={{0,1},{1,2},{2,3},{3,4},{4,5},{5,6},{6,7},{8,9},{9,10},{10,11},{11... | collective-permute-start | bytes 73736 | tf_op jit(solution)/shard_map/ppermute | solution.py:20
  104.7 0.6 collective-permute-done.4
  105.3 3.1 %fusion.162 = f32[]{:T(128)} fusion(f32[]{:T(128)} %collective-permute-done.4, s32[]{:T(128)S(6)} %select_n.344, f32[]{:T(128)} %collective-permute-done.3, s32[]{:T(128)S(6)} %select_n.342, f32[]{:T(128)} %collective-permute-done.2, s32[]{:T(128)S(6)} %select_n.340, f32[]{:T(128)} %get-tuple-element.70, s32[]{:T(128)S(6)} %select_n.302), kind=kLoop, calls=%fused_computation.314 | loop fusion | flops 47 | bytes 36 | tf_op jit(solution)/shard_map/reduce_sum | solution.py:86
  109.1 0.2 fusion.111
  109.3 11.1 %all_gather.11 = bf16[4,192,512]{2,1,0:T(8,128)(2,1)S(1)} all-gather(bf16[4,24,512]{2,1,0:T(8,128)(2,1)S(1)} %bitcast.160), channel_id=1, replica_groups=mesh['clip'=4,'seg'=8] {'seg'}, dimensions={1}, use_global_device_ids=true | all-gather | bytes 884736 | tf_op jit(solution)/shard_map/all_gather | solution.py:227
  120.4 0.5 pad_slice_fusion.2
  120.9 1.3 fusion.20
  122.2 0.8 copy.19
  (108 shorter events, 2.2 us)
Async XLA Ops:
  7.2 50.6 %reduce-scatter.2.cloned.1.call-start = ((), (), s32[]{:S(2)}) async-start(), calls=%async_computation.1 | async-start | bytes 1769472 | tf_op jit(solution)/shard_map/reduce_scatter | solution.py:132
  10.0 6.4 %copy-start = (bf16[16,16,2048]{2,1,0:T(8,128)(2,1)}, bf16[16,16,2048]{2,1,0:T(8,128)(2,1)S(1)}, u32[]{:S(2)}) copy-start(bf16[16,16,2048]{2,1,0:T(8,128)(2,1)S(1)} %add_convert_fusion.2) | copy-start | bytes 3145732
  14.4 11.9 %copy-start.16 = (s32[4]{0:T(128)S(1)}, s32[4]{0:T(128)}, u32[]{:S(2)}) copy-start(s32[4]{0:T(128)} %param.5) | copy-start | bytes 52
  16.5 27.4 %collective-permute-start.1 = (bf16[4,1536]{1,0:T(4,128)(2,1)S(1)}, bf16[4,1536]{1,0:T(4,128)(2,1)S(1)}, u32[]{:S(2)}, u32[]{:S(2)}) collective-permute-start(bf16[4,1536]{1,0:T(4,128)(2,1)S(1)} %slice.206), channel_id=1, source_target_pairs={{1,0},{2,1},{3,2},{4,3},{5,4},{6,5},{7,6},{9,8},{10,9},{11,10},{12... | collective-permute-start | bytes 36872 | tf_op jit(solution)/shard_map/ppermute | solution.py:20
  35.2 7.2 %copy-start.10 = (f32[128,512]{1,0:T(8,128)S(1)}, f32[128,512]{1,0:T(8,128)}, u32[]{:S(2)}) copy-start(f32[128,512]{1,0:T(8,128)} %get-tuple-element.76) | copy-start | bytes 786436
  35.2 7.2 %copy-start.11 = (f32[128,512]{1,0:T(8,128)S(1)}, f32[128,512]{1,0:T(8,128)}, u32[]{:S(2)}) copy-start(f32[128,512]{1,0:T(8,128)} %get-tuple-element.77) | copy-start | bytes 786436
  50.6 11.7 %copy-start.15 = (s32[48,256]{1,0:T(8,128)S(1)}, s32[48,256]{1,0:T(8,128)}, u32[]{:S(2)}) copy-start(s32[48,256]{1,0:T(8,128)} %add_add_fusion.4) | copy-start | bytes 147460
  50.7 11.8 %copy-start.14 = (s32[24,512]{1,0:T(8,128)S(1)}, s32[24,512]{1,0:T(8,128)}, u32[]{:S(2)}) copy-start(s32[24,512]{1,0:T(8,128)} %add_add_fusion.3) | copy-start | bytes 147460
  60.8 3.7 %collective-permute-start = (bf16[4,1536]{1,0:T(4,128)(2,1)S(1)}, bf16[4,1536]{1,0:T(4,128)(2,1)S(1)}, u32[]{:S(2)}, u32[]{:S(2)}) collective-permute-start(bf16[4,1536]{1,0:T(4,128)(2,1)S(1)} %fusion.147), channel_id=1, source_target_pairs={{1,0},{2,1},{3,2},{4,3},{5,4},{6,5},{7,6},{9,8},{10,9},{11,10},{12... | collective-permute-start | bytes 36872 | tf_op jit(solution)/shard_map/ppermute | solution.py:20
  70.7 1.4 %copy-start.2 = (f32[4,24,2048]{2,1,0:T(8,128)S(1)}, f32[4,24,2048]{2,1,0:T(8,128)}, u32[]{:S(2)}) copy-start(f32[4,24,2048]{2,1,0:T(8,128)} %fusion.2) | copy-start | bytes 2359300
  70.7 2.8 %copy-start.13 = (f32[4,48,1024]{2,1,0:T(8,128)S(1)}, f32[4,48,1024]{2,1,0:T(8,128)}, u32[]{:S(2)}) copy-start(f32[4,48,1024]{2,1,0:T(8,128)} %fusion.15) | copy-start | bytes 2359300
  70.7 2.8 %copy-start.17 = (pred[4,48]{1,0:T(4,128)(4,1)S(1)}, pred[4,48]{1,0:T(4,128)(4,1)}, u32[]{:S(2)}) copy-start(pred[4,48]{1,0:T(4,128)(4,1)} %broadcast_compare_fusion.2) | copy-start | bytes 580
  71.6 4.8 %copy-start.3 = (f32[4,48,1024]{2,1,0:T(8,128)}, f32[4,48,1024]{2,1,0:T(8,128)S(1)}, u32[]{:S(2)}) copy-start(f32[4,48,1024]{2,1,0:T(8,128)S(1)} %fusion.17) | copy-start | bytes 2359300
  71.6 3.4 %copy-start.12 = (f32[4,96,512]{2,1,0:T(8,128)S(1)}, f32[4,96,512]{2,1,0:T(8,128)}, u32[]{:S(2)}) copy-start(f32[4,96,512]{2,1,0:T(8,128)} %fusion.34) | copy-start | bytes 2359300
  71.6 3.4 %copy-start.18 = (pred[4,96]{1,0:T(4,128)(4,1)S(1)}, pred[4,96]{1,0:T(4,128)(4,1)}, u32[]{:S(2)}) copy-start(pred[4,96]{1,0:T(4,128)(4,1)} %broadcast_compare_fusion.3) | copy-start | bytes 1156
  72.1 4.3 %copy-start.5 = (f32[4,96,512]{2,1,0:T(8,128)}, f32[4,96,512]{2,1,0:T(8,128)S(1)}, u32[]{:S(2)}) copy-start(f32[4,96,512]{2,1,0:T(8,128)S(1)} %fusion.36) | copy-start | bytes 2359300
  88.9 3.0 %copy-start.4 = (f32[4,48,1024]{2,1,0:T(8,128)S(1)}, f32[4,48,1024]{2,1,0:T(8,128)}, u32[]{:S(2)}) copy-start(f32[4,48,1024]{2,1,0:T(8,128)} %copy-done.3) | copy-start | bytes 2359300
  88.9 3.0 %copy-start.8 = (f32[4,48,512]{2,1,0:T(8,128)S(1)}, f32[4,48,512]{2,1,0:T(8,128)}, u32[]{:S(2)}) copy-start(f32[4,48,512]{2,1,0:T(8,128)} %get-tuple-element.23) | copy-start | bytes 1179652
  88.9 3.0 %copy-start.9 = (f32[4,48,512]{2,1,0:T(8,128)S(1)}, f32[4,48,512]{2,1,0:T(8,128)}, u32[]{:S(2)}) copy-start(f32[4,48,512]{2,1,0:T(8,128)} %get-tuple-element.24) | copy-start | bytes 1179652
  91.3 3.3 %slice-start = ((s8[8388608]{0:T(1024)(128)(4,1)}), s8[4194304]{0:T(1024)(128)(4,1)S(1)}, s32[]{:S(2)}) async-start(s8[8388608]{0:T(1024)(128)(4,1)} %bitcast.136), calls=%async_computation.2 | async-start | bytes 8388608
  91.9 2.2 %copy-start.6 = (f32[4,24,1024]{2,1,0:T(8,128)S(1)}, f32[4,24,1024]{2,1,0:T(8,128)}, u32[]{:S(2)}) copy-start(f32[4,24,1024]{2,1,0:T(8,128)} %get-tuple-element.25) | copy-start | bytes 1179652
  91.9 2.2 %copy-start.7 = (f32[4,24,1024]{2,1,0:T(8,128)S(1)}, f32[4,24,1024]{2,1,0:T(8,128)}, u32[]{:S(2)}) copy-start(f32[4,24,1024]{2,1,0:T(8,128)} %get-tuple-element.26) | copy-start | bytes 1179652
  93.3 2.3 %slice-start.1 = ((s8[8388608]{0:T(1024)(128)(4,1)}), s8[4194304]{0:T(1024)(128)(4,1)S(1)}, s32[]{:S(2)}) async-start(s8[8388608]{0:T(1024)(128)(4,1)} %bitcast.136), calls=%async_computation.3 | async-start | bytes 8388608
  97.3 23.7 %copy-start.1 = (bf16[16,16,2048]{2,1,0:T(8,128)(2,1)S(1)}, bf16[16,16,2048]{2,1,0:T(8,128)(2,1)}, u32[]{:S(2)}) copy-start(bf16[16,16,2048]{2,1,0:T(8,128)(2,1)} %copy-done) | copy-start | bytes 3145732
  97.4 7.3 %collective-permute-start.2 = (f32[]{:T(128)}, f32[]{:T(128)}, u32[]{:S(2)}, u32[]{:S(2)}) collective-permute-start(f32[]{:T(128)} %get-tuple-element.70), channel_id=1, source_target_pairs={{0,8},{8,16},{16,24},{24,0},{1,9},{9,17},{17,25},{25,1},{2,10},{10... | collective-permute-start | bytes 20 | tf_op jit(solution)/shard_map/ppermute | solution.py:79
  99.0 5.7 %collective-permute-start.3 = (f32[]{:T(128)}, f32[]{:T(128)}, u32[]{:S(2)}, u32[]{:S(2)}) collective-permute-start(f32[]{:T(128)} %get-tuple-element.70), channel_id=1, source_target_pairs={{0,16},{8,24},{16,0},{24,8},{1,17},{9,25},{17,1},{25,9},{2,18},{10... | collective-permute-start | bytes 20 | tf_op jit(solution)/shard_map/ppermute | solution.py:79
  101.6 3.7 %collective-permute-start.4 = (f32[]{:T(128)}, f32[]{:T(128)}, u32[]{:S(2)}, u32[]{:S(2)}) collective-permute-start(f32[]{:T(128)} %get-tuple-element.70), channel_id=1, source_target_pairs={{0,24},{8,0},{16,8},{24,16},{1,25},{9,1},{17,9},{25,17},{2,26},{10... | collective-permute-start | bytes 20 | tf_op jit(solution)/shard_map/ppermute | solution.py:79
  103.0 6.1 %collective-permute-start.5 = (f32[4,1536]{1,0:T(4,128)S(1)}, f32[4,1536]{1,0:T(4,128)S(1)}, u32[]{:S(2)}, u32[]{:S(2)}) collective-permute-start(f32[4,1536]{1,0:T(4,128)S(1)} %add_add_fusion.6), channel_id=1, source_target_pairs={{0,1},{1,2},{2,3},{3,4},{4,5},{5,6},{6,7},{8,9},{9,10},{10,11},{11... | collective-permute-start | bytes 73736 | tf_op jit(solution)/shard_map/ppermute | solution.py:20
Sparse Core Ops, SparseCore 0:
  16.6 41.1 reduce-scatter.1
